TPU v7x, 32 devices: a whole 2x2x4 slice. The times are simulated.
32 devices in a mesh: dp: 4 (over x, core), seq: 8 (over z, y).
Axes of the slice: x: 2, y: 2, z: 4, core: 2. Of those that a mesh axis runs over, the one named last changes fastest.
Arguments:
- queries: bfloat16 [4, 4096, 2048], P('dp', 'seq'), may hold values from -34 to 34
- neighbour_input: bfloat16 [4, 32, 64, 896], P('dp', 'seq'), may hold values from -6 to 6
- owner_list: int32 [4, 64, 2], P('dp', 'seq'), may hold values from 0 to 7, as said below
- block_list: int32 [4, 64, 2], P('dp', 'seq'), may hold values from 0 to 3
- enc_gain: float32 [896], replicated, may hold values from 0.5 to 8
- enc_attn: bfloat16 [4, 896, 896], P(None, 'dp'), may hold values from -0.1875 to 0.1875
- kv_weight: bfloat16 [2, 896, 2048], replicated, may hold values from -0.1875 to 0.1875
Outputs:
- context: bfloat16 [4, 4096, 2048], P('dp', 'seq')
Inputs may be any that keep to these rules, and one draw needn't show every extreme that they name: `owner_list`: within the spans of one device, no owner is named more than 2 times; every owner is named in every sequence.
All inputs are finite; a program needn't handle non-finite values.
Results may differ from a plain program's by a relative error of at most 0.025.
The roundings to bfloat16 on the way count: a program that leaves them out, or rounds other values in their place, can miss the bound.
Values may be sent and summed in bfloat16 or wider, within the bound.
No kernel may reach another device: no remote copies, remote signals or barrier semaphores. Data moves between devices by JAX's collectives and lax.ppermute only.
A program may use at most 128 MiB of HBM per device.

v0:
```python
import jax
import jax.numpy as jnp
from jax import lax
from jax.sharding import PartitionSpec as P

HEADS = 16
HEAD_DIM = 128
ENC_HEADS = 7
NLEN = 64
SPAN = 64
NEIGH = 2
NB_DEV = 4


epsilon = 1e-05


def softmax_rows(scores):
    highest = jnp.max(scores, axis=-1, keepdims=True)
    raised = jnp.exp(scores - highest)
    return raised / jnp.sum(raised, axis=-1, keepdims=True)


def encode(blocks, gain, attention):
    inputs = blocks.astype(jnp.float32)
    spread = jnp.mean(inputs * inputs, axis=-1, keepdims=True)
    normed = (inputs * lax.rsqrt(spread + epsilon) * gain).astype(jnp.bfloat16)
    count, length, width = blocks.shape
    head_size = width // ENC_HEADS
    projected = jnp.einsum(
        "nte,pef->pntf", normed, attention[:3], preferred_element_type=jnp.float32
    ).astype(jnp.bfloat16)
    split_heads = projected.reshape(3, count, length, ENC_HEADS, head_size)
    scores = jnp.einsum(
        "nqhd,nkhd->nhqk", split_heads[0], split_heads[1], preferred_element_type=jnp.float32
    ) * head_size ** (-0.5)
    weights = softmax_rows(scores).astype(jnp.bfloat16)
    mixture = jnp.einsum(
        "nhqk,nkhd->nqhd", weights, split_heads[2], preferred_element_type=jnp.float32
    ).astype(jnp.bfloat16)
    mixture = mixture.reshape(count, length, width)
    output = jnp.einsum("nte,ef->ntf", mixture, attention[3], preferred_element_type=jnp.float32)
    return (inputs + output).astype(jnp.bfloat16)


def shards(queries, neighbour_input, owner_list, block_list, enc_gain, enc_attn, kv_weight):
    full_weights = lax.all_gather(enc_attn, "dp", axis=1, tiled=True)
    encoded = encode(neighbour_input[0], enc_gain, full_weights)
    owners = owner_list.reshape(-1)
    indices = block_list.reshape(-1)
    global_ids = owners * NB_DEV + indices
    piece = lax.all_gather(encoded, "seq", axis=0, tiled=True)
    selector = (global_ids[:, None] == jnp.arange(piece.shape[0], dtype=jnp.int32)[None, :]).astype(
        jnp.bfloat16
    )
    chosen = jnp.einsum("rb,bte->rte", selector, piece, preferred_element_type=jnp.float32).astype(
        jnp.bfloat16
    )
    key_value = jnp.einsum(
        "rte,pef->prtf", chosen, kv_weight, preferred_element_type=jnp.float32
    ).astype(jnp.bfloat16)
    span_count = queries.shape[1] // SPAN
    memory_keys = key_value[0].reshape(span_count, NEIGH * NLEN, HEADS, HEAD_DIM)
    memory_values = key_value[1].reshape(span_count, NEIGH * NLEN, HEADS, HEAD_DIM)
    grouped = queries[0].reshape(span_count, SPAN, HEADS, HEAD_DIM)
    scores = jnp.einsum(
        "cqhd,ckhd->chqk", grouped, memory_keys, preferred_element_type=jnp.float32
    ) * HEAD_DIM ** (-0.5)
    weights = softmax_rows(scores).astype(jnp.bfloat16)
    mixture = jnp.einsum(
        "chqk,ckhd->cqhd", weights, memory_values, preferred_element_type=jnp.float32
    ).astype(jnp.bfloat16)
    return mixture.reshape(queries.shape)


def solution(mesh):
    return jax.shard_map(
        shards,
        mesh=mesh,
        in_specs=(
            P("dp", "seq", None),
            P("dp", "seq", None, None),
            P("dp", "seq", None),
            P("dp", "seq", None),
            P(),
            P(None, "dp", None),
            P(),
        ),
        out_specs=P("dp", "seq", None),
        check_vma=False,
    )
```

profile of v0, /device:TPU:0, one launch (start us, length us, event | category | flops | bytes accessed | tf_op | source)
XLA Modules:
  0.0 194.3 jit_solution(1259733458802943780)
XLA Ops:
  6.5 0.0 all-gather.3.cloned.1.call-start
  6.5 0.7 all-gather.3.cloned.1.call-update
  7.3 0.0 all-gather.5.cloned.1.call-start
  7.3 1.2 fusion.33
  8.5 50.3 %all-gather.3.cloned.1.call-done = bf16[4,896,896]{2,1,0:T(8,128)(2,1)} async-done(((bf16[4,224,896]{2,1,0:T(8,128)(2,1)}), bf16[4,896,896]{2,1,0:T(8,128)(2,1)}) %all-gather.3.cloned.1.call-update) | async-done | bytes 6422544 | tf_op jit(solution)/shard_map/all_gather | solution.py:47
  58.8 4.3 %fusion.28 = bf16[3,4,64,896]{3,2,0,1:T(8,128)(2,1)S(1)} fusion(bf16[4,896,896]{2,1,0:T(8,128)(2,1)} %all-gather.3.cloned.1.call-done, bf16[1,4,64,896]{3,2,1,0:T(8,128)(2,1)} %param.8, f32[896]{0:T(1024)} %param.11, f32[4,64]{1,0:T(4,128)S(1)} %add_rsqrt_fusion), kind=kOutput, calls=%fused_computation.28 | convolution fusion | flops 1234731008 | bytes 6657024 | tf_op jit(solution)/shard_map/nte,pef->pntf/dot_general | solution.py:30
  63.0 0.1 fusion.65
  63.2 0.5 squeeze.14
  63.7 0.5 squeeze.15
  64.2 0.4 convolution_multiply_fusion
  64.6 0.0 copy-start.1
  64.6 0.5 fusion.66
  65.1 0.5 squeeze.13
  65.6 0.0 copy-start.2
  65.6 0.0 copy-start.3
  65.6 0.4 fusion.32
  66.1 0.0 copy-done.1
  66.1 2.9 %fusion.31 = bf16[4,64,896]{2,1,0:T(8,128)(2,1)} fusion(bf16[4,896,896]{2,1,0:T(8,128)(2,1)} %all-gather.3.cloned.1.call-done, bf16[4,7,8,8,128]{4,3,2,1,0:T(8,128)(2,1)S(1)} %fusion.32, bf16[1,4,64,896]{3,2,1,0:T(8,128)(2,1)S(1)} %copy-done.1), kind=kOutput, calls=%fused_computation.36 | convolution fusion | flops 411729920 | bytes 2981888 | tf_op jit(solution)/shard_map/nte,ef->ntf/dot_general | solution.py:42
  69.0 0.0 all-gather.5.cloned.1.call-update
  69.0 0.0 copy-done.2
  69.0 0.0 copy-done.3
  69.0 0.1 copy.26
  69.1 0.1 add.25
  69.2 2.2 %copy.45 = bf16[64,8,16,128]{3,2,1,0:T(8,128)(2,1)S(1)} copy(bf16[64,8,16,128]{3,1,2,0:T(8,128)(2,1)} %bitcast.105) | data formatting | bytes 4194304
  71.4 64.6 %all-gather.5.cloned.1.call-done = bf16[32,64,896]{2,1,0:T(8,128)(2,1)} async-done(((bf16[4,64,896]{2,1,0:T(8,128)(2,1)}), bf16[32,64,896]{2,1,0:T(8,128)(2,1)}) %all-gather.5.cloned.1.call-update) | async-done | bytes 3670032 | tf_op jit(solution)/shard_map/all_gather | solution.py:52
  136.0 5.0 %convert_bitcast_fusion.2 = bf16[16,64,896,1]{2,0,1,3:T(8,128)(2,1)S(1)} fusion(bf16[32,64,896]{2,1,0:T(8,128)(2,1)} %all-gather.5.cloned.1.call-done, s32[16]{0:T(128)S(1)} %add.25), kind=kOutput, calls=%fused_computation.24 | convolution fusion | flops 59638272 | bytes 5505088 | tf_op jit(solution)/shard_map/rb,bte->rte/dot_general | solution.py:56
  141.0 11.3 %convert_bitcast_fusion = bf16[2,16,64,2048]{3,2,0,1:T(8,128)(2,1)S(1)} fusion(bf16[2,896,2048]{2,1,0:T(8,128)(2,1)} %param.13, bf16[16,64,896,1]{2,0,1,3:T(8,128)(2,1)S(1)} %convert_bitcast_fusion.2), kind=kOutput, calls=%fused_computation.2 | convolution fusion | flops 7520387072 | bytes 17563648 | tf_op jit(solution)/shard_map/rte,pef->prtf/dot_general | solution.py:59
  152.3 1.2 fusion.64
  153.5 1.4 copy.44
  154.9 3.0 %fusion.11 = f32[8,16,128,64]{2,3,1,0:T(8,128)S(1)} fusion(bf16[8,128,16,128]{3,2,1,0:T(8,128)(2,1)S(1)} %bitcast.100, bf16[8,64,16,128]{3,2,1,0:T(8,128)(2,1)S(1)} %bitcast.103), kind=kOutput, calls=%fused_computation.13 | convolution fusion | flops 268435456 | bytes 10485760 | tf_op jit(solution)/shard_map/cqhd,ckhd->chqk/dot_general | solution.py:66
  157.9 0.0 copy-start
  157.9 2.2 %fusion.71 = f32[8,16,64]{2,1,0:T(8,128)S(1)} fusion(f32[8,16,128,64]{2,3,1,0:T(8,128)S(1)} %fusion.11), kind=kOutput, calls=%fused_computation.65 | output fusion | flops 4194431 | bytes 4227072 | tf_op jit(solution)/shard_map/sub | solution.py:20
  160.1 3.3 %copy.46 = bf16[128,8,16,128]{3,2,1,0:T(8,128)(2,1)} copy(bf16[128,8,16,128]{3,1,2,0:T(8,128)(2,1)S(1)} %bitcast.101) | data formatting | bytes 8388608
  163.4 0.0 copy-done
  163.4 18.7 %convert_bitcast_fusion.1 = bf16[8,64,16,128]{3,1,2,0:T(8,128)(2,1)} fusion(bf16[8,128,16,128]{3,2,1,0:T(8,128)(2,1)} %bitcast.104, f32[8,16,64]{2,1,0:T(8,128)S(1)} %fusion.71, f32[8,16,128,64]{2,3,1,0:T(8,128)} %copy-done), kind=kOutput, calls=%fused_computation.20 | convolution fusion | flops 274735232 | bytes 10518528 | tf_op jit(solution)/shard_map/chqk,ckhd->cqhd/dot_general | solution.py:70
  182.2 3.0 %copy.37 = bf16[8,64,16,128]{3,2,1,0:T(8,128)(2,1)S(1)} copy(bf16[8,64,16,128]{3,1,2,0:T(8,128)(2,1)} %convert_bitcast_fusion.1) | data formatting | bytes 4194304 | tf_op jit(solution)/shard_map/convert_element_type | solution.py:72
  185.1 2.3 %reshape.44 = bf16[1,512,2048]{2,1,0:T(8,128)(2,1)} reshape(bf16[8,64,16,128]{3,2,1,0:T(8,128)(2,1)S(1)} %copy.37) | data formatting | bytes 4194304 | tf_op jit(solution)/shard_map/reshape | solution.py:73
  (2 shorter events, 0.0 us)
Async XLA Ops:
  6.5 52.2 %all-gather.3.cloned.1.call-start = ((), (), s32[]{:S(2)}) async-start(), calls=%async_computation | async-start | bytes 8028160 | tf_op jit(solution)/shard_map/all_gather | solution.py:47
  7.3 128.7 %all-gather.5.cloned.1.call-start = ((), (), s32[]{:S(2)}) async-start(), calls=%async_computation.1 | async-start | bytes 4128768 | tf_op jit(solution)/shard_map/all_gather | solution.py:52
  64.6 1.5 copy-start.1
  65.6 3.4 %copy-start.2 = (s32[1,8,2]{1,2,0:T(2,128)S(1)}, s32[1,8,2]{1,2,0:T(2,128)}, u32[]{:S(2)}) copy-start(s32[1,8,2]{1,2,0:T(2,128)} %param.10) | copy-start | bytes 196
  65.6 3.4 %copy-start.3 = (s32[1,8,2]{1,2,0:T(2,128)S(1)}, s32[1,8,2]{1,2,0:T(2,128)}, u32[]{:S(2)}) copy-start(s32[1,8,2]{1,2,0:T(2,128)} %param.9) | copy-start | bytes 196
  157.9 5.6 %copy-start = (f32[8,16,128,64]{2,3,1,0:T(8,128)}, f32[8,16,128,64]{2,3,1,0:T(8,128)S(1)}, u32[]{:S(2)}) copy-start(f32[8,16,128,64]{2,3,1,0:T(8,128)S(1)} %fusion.11) | copy-start | bytes 12582916
Sparse Core Ops, SparseCore 0:
  8.9 49.8 all-gather.2
  69.1 66.8 all-gather.4
where the time goes:
time: 195 us; the launch traced here: 194 us
  waiting for transfers between devices  116 us (59%)
  matrix products  46.4 us (24%)
  local copies, waits for them, and re-layouts  15.3 us (8%)
  between operations  13.5 us (7%)
  other arithmetic  3.45 us (2%)
    all_gather x1, waiting for transfers between devices, shards(): piece = lax.all_gather(encoded, 'seq', axis=0, tiled=True)  64.6 us
    all_gather x1, waiting for transfers between devices, shards(): full_weights = lax.all_gather(enc_attn, 'dp', axis=1, tiled=True)  50.3 us
    dot_general x1, matrix products, shards(): jnp.einsum('chqk,ckhd->cqhd', weights, memory_values, preferred_element_t...  18.7 us
    dot_general x1, matrix products, shards(): jnp.einsum('rte,pef->prtf', chosen, kv_weight, preferred_element_type=jnp...  11.3 us
    unnamed x11, local copies, waits for them, and re-layouts  6.96 us
    dot_general x1, matrix products, shards(): jnp.einsum('rb,bte->rte', selector, piece, preferred_element_type=jnp.flo...  5.01 us
    dot_general x1, matrix products, encode(): jnp.einsum('nte,pef->pntf', normed, attention[:3], preferred_element_type...  4.25 us
  transfers between devices with their start and end apart: 2, of which 2 were waited for; matrix products, arithmetic and copies ran while one was open for 2% of the time, Pallas kernels for 0%

commit v1 on v0

--- a/solution.py
+++ b/solution.py
@@ -43,39 +43,51 @@
     return (inputs + output).astype(jnp.bfloat16)
 
 
-def shards(queries, neighbour_input, owner_list, block_list, enc_gain, enc_attn, kv_weight):
-    full_weights = lax.all_gather(enc_attn, "dp", axis=1, tiled=True)
-    encoded = encode(neighbour_input[0], enc_gain, full_weights)
-    owners = owner_list.reshape(-1)
-    indices = block_list.reshape(-1)
-    global_ids = owners * NB_DEV + indices
-    piece = lax.all_gather(encoded, "seq", axis=0, tiled=True)
-    selector = (global_ids[:, None] == jnp.arange(piece.shape[0], dtype=jnp.int32)[None, :]).astype(
-        jnp.bfloat16
-    )
-    chosen = jnp.einsum("rb,bte->rte", selector, piece, preferred_element_type=jnp.float32).astype(
-        jnp.bfloat16
-    )
-    key_value = jnp.einsum(
-        "rte,pef->prtf", chosen, kv_weight, preferred_element_type=jnp.float32
-    ).astype(jnp.bfloat16)
-    span_count = queries.shape[1] // SPAN
-    memory_keys = key_value[0].reshape(span_count, NEIGH * NLEN, HEADS, HEAD_DIM)
-    memory_values = key_value[1].reshape(span_count, NEIGH * NLEN, HEADS, HEAD_DIM)
-    grouped = queries[0].reshape(span_count, SPAN, HEADS, HEAD_DIM)
-    scores = jnp.einsum(
-        "cqhd,ckhd->chqk", grouped, memory_keys, preferred_element_type=jnp.float32
-    ) * HEAD_DIM ** (-0.5)
-    weights = softmax_rows(scores).astype(jnp.bfloat16)
-    mixture = jnp.einsum(
-        "chqk,ckhd->cqhd", weights, memory_values, preferred_element_type=jnp.float32
-    ).astype(jnp.bfloat16)
-    return mixture.reshape(queries.shape)
+def make_shards(n_seq):
+    def shards(queries, neighbour_input, owner_list, block_list, enc_gain, enc_attn, kv_weight):
+        full_weights = lax.all_gather(enc_attn, "dp", axis=1, tiled=True)
+        me = lax.axis_index("seq")
+        owners = owner_list.reshape(-1)
+        indices = block_list.reshape(-1)
+        refs = owners.shape[0]
+        per_owner = -(-refs // n_seq)
+        same = owners[:, None] == owners[None, :]
+        earlier = jnp.arange(refs)[None, :] < jnp.arange(refs)[:, None]
+        rank = jnp.sum(same & earlier, axis=1).astype(jnp.int32)
+        asks = jnp.stack([owners, indices, rank])
+        asks = jnp.broadcast_to(asks[None], (n_seq, 3, refs))
+        asked = lax.all_to_all(asks, "seq", 0, 0, tiled=True)
+        slots = jnp.arange(per_owner, dtype=jnp.int32)
+        match = (asked[:, 0, None, :] == me) & (asked[:, 2, None, :] == slots[None, :, None])
+        picks = jnp.sum(jnp.where(match, asked[:, 1, None, :], 0), axis=-1)
+        sent = jnp.take(neighbour_input[0], picks.reshape(-1), axis=0, mode="clip")
+        sent = sent.reshape(n_seq, per_owner, NLEN, neighbour_input.shape[-1])
+        got = lax.all_to_all(sent, "seq", 0, 0, tiled=True)
+        got = got.reshape(n_seq * per_owner, NLEN, neighbour_input.shape[-1])
+        chosen_raw = jnp.take(got, owners * per_owner + rank, axis=0, mode="clip")
+        chosen = encode(chosen_raw, enc_gain, full_weights)
+        key_value = jnp.einsum(
+            "rte,pef->prtf", chosen, kv_weight, preferred_element_type=jnp.float32
+        ).astype(jnp.bfloat16)
+        span_count = queries.shape[1] // SPAN
+        memory_keys = key_value[0].reshape(span_count, NEIGH * NLEN, HEADS, HEAD_DIM)
+        memory_values = key_value[1].reshape(span_count, NEIGH * NLEN, HEADS, HEAD_DIM)
+        grouped = queries[0].reshape(span_count, SPAN, HEADS, HEAD_DIM)
+        scores = jnp.einsum(
+            "cqhd,ckhd->chqk", grouped, memory_keys, preferred_element_type=jnp.float32
+        ) * HEAD_DIM ** (-0.5)
+        weights = softmax_rows(scores).astype(jnp.bfloat16)
+        mixture = jnp.einsum(
+            "chqk,ckhd->cqhd", weights, memory_values, preferred_element_type=jnp.float32
+        ).astype(jnp.bfloat16)
+        return mixture.reshape(queries.shape)
+
+    return shards
 
 
 def solution(mesh):
     return jax.shard_map(
-        shards,
+        make_shards(mesh.shape["seq"]),
         mesh=mesh,
         in_specs=(
             P("dp", "seq", None),

time: 195 us -> 171 us (0.88)
  waiting for transfers between devices: 116 us -> 46.4 us
  local copies, waits for them, and re-layouts: 15.3 us -> 38 us
  starting transfers between devices: 0.04 us -> 11.7 us
  matrix products: 46.4 us -> 53.2 us
  other arithmetic: 3.45 us -> 7.5 us
    all_gather x1 -> x0, waiting for transfers between devices: 64.6 us -> none  [shards(): piece = lax.all_gather(encoded, 'seq', axis=0, tiled=True)]
    all_gather x1, waiting for transfers between devices: 50.3 us -> 0.02 us  [shards(): full_weights = lax.all_gather(enc_attn, 'dp', axis=1, tiled=True)]
    all_to_all x0 -> x2, waiting for transfers between devices: none -> 45.6 us  [the longest x1 39.1 us: shards(): got = lax.all_to_all(sent, 'seq', 0, 0, tiled=True)]
    all_to_all x0 -> x2, starting transfers between devices: none -> 11.7 us  [the longest x1 7.28 us: shards(): asked = lax.all_to_all(asks, 'seq', 0, 0, tiled=True)]
    gather x0 -> x2, local copies, waits for them, and re-layouts: none -> 5.48 us  [the longest x1 3.5 us: shards(): chosen_raw = jnp.take(got, owners * per_owner + rank, axis=0, mode='clip')]
    dot_general x1 -> x0, matrix products: 5.01 us -> none  [shards(): jnp.einsum('rb,bte->rte', selector, piece, preferred_element_type=jnp.flo...]
    dot_general x1, matrix products: 4.25 us -> 9.22 us  [encode(): jnp.einsum('nte,pef->pntf', normed, attention[:3], preferred_element_type...]
    squeeze x1, local copies, waits for them, and re-layouts: 0.53 us -> 4.6 us  [encode(): split_heads[0]]
  transfers between devices with their start and end apart: 2 -> 3, of which waited for: 2 -> 2; matrix products, arithmetic and copies ran while one was open for 2% -> 7% of each run, Pallas kernels for 0% -> 0%
where the time goes in v1:
time: 171 us; the launch traced here: 170 us
  matrix products  53.2 us (31%)
  waiting for transfers between devices  46.4 us (27%)
  local copies, waits for them, and re-layouts  38 us (22%)
  between operations  13.6 us (8%)
  starting transfers between devices  11.7 us (7%)
  other arithmetic  7.5 us (4%)
    all_to_all x1, waiting for transfers between devices, shards(): got = lax.all_to_all(sent, 'seq', 0, 0, tiled=True)  39.1 us
    dot_general x1, matrix products, shards(): jnp.einsum('chqk,ckhd->cqhd', weights, memory_values, preferred_element_t...  18.9 us
    dot_general x1, matrix products, shards(): jnp.einsum('rte,pef->prtf', chosen, kv_weight, preferred_element_type=jnp...  11.4 us
    dot_general x1, matrix products, encode(): jnp.einsum('nte,pef->pntf', normed, attention[:3], preferred_element_type...  9.22 us
    unnamed x17, local copies, waits for them, and re-layouts  8.49 us
    all_to_all x1, starting transfers between devices, shards(): asked = lax.all_to_all(asks, 'seq', 0, 0, tiled=True)  7.28 us
    all_to_all x1, waiting for transfers between devices, shards(): asked = lax.all_to_all(asks, 'seq', 0, 0, tiled=True)  6.58 us
    sub x2, other arithmetic, softmax_rows(): raised = jnp.exp(scores - highest)  5.2 us
  transfers between devices with their start and end apart: 3, of which 2 were waited for; matrix products, arithmetic and copies ran while one was open for 7% of the time, Pallas kernels for 0%

profile of v1, /device:TPU:0, one launch (start us, length us, event | category | flops | bytes accessed | tf_op | source)
XLA Modules:
  0.0 170.3 jit_solution(13675510612641703168)
XLA Ops:
  6.5 0.0 copy-start
  6.5 0.0 all-gather.2.cloned.1.call-start
  6.5 0.7 all-gather.2.cloned.1.call-update
  7.3 0.8 copy.48
  8.0 0.1 eq.36
  8.1 0.1 stack_reshape.6
  8.2 0.8 copy.49
  8.9 0.1 stack_reshape.7
  9.0 0.2 convert_reduce_fusion
  9.2 0.6 broadcast_in_dim.22
  9.8 7.3 %all-to-all-start = ((s32[8,3,16]{2,1,0:T(4,128)}), s32[8,3,16]{2,1,0:T(4,128)S(1)}, u32[]{:S(2)}, u32[]{:S(2)}) async-start(s32[8,3,16]{2,1,0:T(4,128)} %broadcast_in_dim.22), calls=%async_computation | async-start | bytes 32768 | tf_op jit(solution)/shard_map/all_to_all | solution.py:59
  17.1 6.6 %all-to-all-done = s32[8,3,16]{2,1,0:T(4,128)S(1)} async-done(((s32[8,3,16]{2,1,0:T(4,128)}), s32[8,3,16]{2,1,0:T(4,128)S(1)}, u32[]{:S(2)}, u32[]{:S(2)}) %all-to-all-start) | async-done | bytes 1568 | tf_op jit(solution)/shard_map/all_to_all | solution.py:59
  23.7 0.1 select_reduce_fusion
  23.9 0.1 copy.54
  23.9 0.1 reshape.63
  24.0 0.0 copy-done
  24.0 0.0 copy-start.4
  24.1 2.0 %gather_fusion = bf16[16,64,896]{2,1,0:T(8,128)(2,1)} fusion(bf16[4,64,896]{2,1,0:T(8,128)(2,1)S(1)} %bitcast.104, s32[1024]{0:T(1024)S(1)} %pad_clamp_fusion.1), kind=kCustom, calls=%fused_computation | custom fusion | bytes 3670080 | tf_op jit(solution)/shard_map/jit(_take)/gather | solution.py:63
  26.0 4.4 %all-to-all-start.1 = ((bf16[8,2,64,896]{3,2,1,0:T(8,128)(2,1)}), bf16[8,2,64,896]{3,2,1,0:T(8,128)(2,1)}, u32[]{:S(2)}, u32[]{:S(2)}) async-start(bf16[8,2,64,896]{3,2,1,0:T(8,128)(2,1)} %bitcast.5), calls=%async_computation.1 | async-start | bytes 3670016 | tf_op jit(solution)/shard_map/all_to_all | solution.py:65
  30.4 0.0 copy-done.4
  30.5 0.1 copy.55
  30.5 0.1 mul.48
  30.6 2.2 %copy.73 = bf16[64,8,16,128]{3,2,1,0:T(8,128)(2,1)S(1)} copy(bf16[64,8,16,128]{3,1,2,0:T(8,128)(2,1)} %bitcast.110) | data formatting | bytes 4194304
  32.8 0.0 copy-start.5
  32.9 39.1 %all-to-all-done.1 = bf16[8,2,64,896]{3,2,1,0:T(8,128)(2,1)} async-done(((bf16[8,2,64,896]{3,2,1,0:T(8,128)(2,1)}), bf16[8,2,64,896]{3,2,1,0:T(8,128)(2,1)}, u32[]{:S(2)}, u32[]{:S(2)}) %all-to-all-start.1) | async-done | bytes 1835040 | tf_op jit(solution)/shard_map/all_to_all | solution.py:65
  71.9 3.5 %gather_fusion.1 = bf16[16,64,896]{2,1,0:T(8,128)(2,1)} fusion(bf16[16,64,896]{2,1,0:T(8,128)(2,1)} %bitcast.6, s32[1024]{0:T(1024)S(1)} %pad_clamp_fusion), kind=kCustom, calls=%fused_computation.1 | custom fusion | bytes 3670080 | tf_op jit(solution)/shard_map/jit(_take)/gather | solution.py:67
  75.4 1.9 %fusion.14 = f32[16,64]{1,0:T(8,128)S(1)} fusion(bf16[16,64,896]{2,1,0:T(8,128)(2,1)} %gather_fusion.1), kind=kLoop, calls=%fused_computation.23 | loop fusion | flops 2751488 | bytes 1839104 | tf_op jit(solution)/shard_map/reduce_sum | solution.py:26
  77.4 0.0 all-gather.2.cloned.1.call-done
  77.4 0.0 copy-done.5
  77.4 9.2 %convert_bitcast_fusion.1 = bf16[3,16,64,896]{3,2,0,1:T(8,128)(2,1)S(1)} fusion(bf16[4,896,896]{2,1,0:T(8,128)(2,1)} %all-gather.2.cloned.1.call-done, bf16[16,64,896]{2,1,0:T(8,128)(2,1)} %gather_fusion.1, f32[896]{0:T(1024)S(1)} %copy-done.5, f32[16,64]{1,0:T(8,128)S(1)} %add_rsqrt_fusion), kind=kOutput, calls=%fused_computation.7 | convolution fusion | flops 4938924032 | bytes 12164608 | tf_op jit(solution)/shard_map/nte,pef->pntf/dot_general | solution.py:30
  86.6 2.6 %fusion.59 = (bf16[1,16,64,896]{3,2,0,1:T(8,128)(2,1)}, bf16[1,16,64,896]{3,2,0,1:T(8,128)(2,1)}, bf16[1,16,64,896]{3,2,0,1:T(8,128)(2,1)}) fusion(bf16[3,16,64,896]{3,2,0,1:T(8,128)(2,1)S(1)} %convert_bitcast_fusion.1), kind=kLoop, calls=%fused_computation.70 | loop fusion | bytes 11010048 | tf_op jit(solution)/shard_map/slice | solution.py:39
  89.2 4.6 %squeeze.17 = bf16[16,64,7,128]{3,2,1,0:T(8,128)(2,1)} reshape(bf16[1,16,64,896]{3,2,0,1:T(8,128)(2,1)} %get-tuple-element.9) | data formatting | bytes 3670016 | tf_op jit(solution)/shard_map/squeeze | solution.py:35
  93.8 4.6 %squeeze.18 = bf16[16,64,7,128]{3,2,1,0:T(8,128)(2,1)} reshape(bf16[1,16,64,896]{3,2,0,1:T(8,128)(2,1)} %get-tuple-element.8) | data formatting | bytes 3670016 | tf_op jit(solution)/shard_map/squeeze | solution.py:35
  98.4 3.3 %fusion.37 = f32[16,7,64,64]{2,3,1,0:T(8,128)S(1)} fusion(bf16[16,64,7,128]{3,2,1,0:T(8,128)(2,1)} %squeeze.18, bf16[16,64,7,128]{3,2,1,0:T(8,128)(2,1)} %squeeze.17), kind=kOutput, calls=%fused_computation.42 | convolution fusion | flops 117440512 | bytes 5505024 | tf_op jit(solution)/shard_map/nqhd,nkhd->nhqk/dot_general | solution.py:34
  101.7 3.0 %fusion.61 = (f32[16,7,64]{2,1,0:T(8,128)S(1)}, f32[16,7,64,64]{2,3,1,0:T(8,128)}) fusion(f32[16,7,64,64]{2,3,1,0:T(8,128)S(1)} %fusion.37), kind=kOutput, calls=%fused_computation.72 | output fusion | flops 1835071 | bytes 3698688 | tf_op jit(solution)/shard_map/sub | solution.py:20
  104.7 4.6 %squeeze.16 = bf16[16,64,7,128]{3,2,1,0:T(8,128)(2,1)} reshape(bf16[1,16,64,896]{3,2,0,1:T(8,128)(2,1)} %get-tuple-element.7) | data formatting | bytes 3670016 | tf_op jit(solution)/shard_map/squeeze | solution.py:39
  109.3 3.5 %convert_bitcast_fusion.3 = bf16[16,7,8,8,128]{4,3,2,1,0:T(8,128)(2,1)S(1)} fusion(f32[16,7,64,64]{2,3,1,0:T(8,128)} %get-tuple-element.14, f32[16,7,64]{2,1,0:T(8,128)S(1)} %get-tuple-element.13, bf16[16,64,7,128]{3,2,1,0:T(8,128)(2,1)} %squeeze.16), kind=kOutput, calls=%fused_computation.45 | convolution fusion | flops 119275520 | bytes 5533696 | tf_op jit(solution)/shard_map/nhqk,nkhd->nqhd/dot_general | solution.py:38
  112.8 3.8 %fusion.33 = f32[16,64,896]{2,1,0:T(8,128)S(1)} fusion(bf16[16,7,8,8,128]{4,3,2,1,0:T(8,128)(2,1)S(1)} %convert_bitcast_fusion.3, bf16[4,896,896]{2,1,0:T(8,128)(2,1)} %all-gather.2.cloned.1.call-done), kind=kOutput, calls=%fused_computation.38 | convolution fusion | flops 1644167168 | bytes 7110656 | tf_op jit(solution)/shard_map/nte,ef->ntf/dot_general | solution.py:42
  116.6 11.4 %convert_bitcast_fusion = bf16[2,16,64,2048]{3,2,0,1:T(8,128)(2,1)S(1)} fusion(bf16[2,896,2048]{2,1,0:T(8,128)(2,1)} %param.13, f32[16,64,896]{2,1,0:T(8,128)S(1)} %fusion.33, bf16[16,64,896]{2,1,0:T(8,128)(2,1)S(1)} %copy-done.2), kind=kOutput, calls=%fused_computation.4 | convolution fusion | flops 7523139584 | bytes 21233664 | tf_op jit(solution)/shard_map/rte,pef->prtf/dot_general | solution.py:69
  128.0 1.2 fusion.58
  129.2 1.4 copy.72
  130.6 3.0 %fusion.11 = f32[8,16,128,64]{2,3,1,0:T(8,128)S(1)} fusion(bf16[8,128,16,128]{3,2,1,0:T(8,128)(2,1)S(1)} %bitcast.105, bf16[8,64,16,128]{3,2,1,0:T(8,128)(2,1)S(1)} %bitcast.108), kind=kOutput, calls=%fused_computation.19 | convolution fusion | flops 268435456 | bytes 10485760 | tf_op jit(solution)/shard_map/cqhd,ckhd->chqk/dot_general | solution.py:76
  133.6 2.2 %fusion.62 = f32[8,16,64]{2,1,0:T(8,128)S(1)} fusion(f32[8,16,128,64]{2,3,1,0:T(8,128)S(1)} %fusion.11), kind=kOutput, calls=%fused_computation.73 | output fusion | flops 4194431 | bytes 4227072 | tf_op jit(solution)/shard_map/sub | solution.py:20
  135.9 3.3 %copy.74 = bf16[128,8,16,128]{3,2,1,0:T(8,128)(2,1)} copy(bf16[128,8,16,128]{3,1,2,0:T(8,128)(2,1)S(1)} %bitcast.106) | data formatting | bytes 8388608
  139.2 18.9 %convert_bitcast_fusion.2 = bf16[8,64,16,128]{3,1,2,0:T(8,128)(2,1)} fusion(bf16[8,128,16,128]{3,2,1,0:T(8,128)(2,1)} %bitcast.109, f32[8,16,64]{2,1,0:T(8,128)S(1)} %fusion.62, f32[8,16,128,64]{2,3,1,0:T(8,128)} %copy-done.3), kind=kOutput, calls=%fused_computation.32 | convolution fusion | flops 274735232 | bytes 10518528 | tf_op jit(solution)/shard_map/chqk,ckhd->cqhd/dot_general | solution.py:80
  158.2 3.0 %copy.64 = bf16[8,64,16,128]{3,2,1,0:T(8,128)(2,1)S(1)} copy(bf16[8,64,16,128]{3,1,2,0:T(8,128)(2,1)} %convert_bitcast_fusion.2) | data formatting | bytes 4194304 | tf_op jit(solution)/shard_map/convert_element_type | solution.py:82
  161.1 2.3 %reshape.60 = bf16[1,512,2048]{2,1,0:T(8,128)(2,1)} reshape(bf16[8,64,16,128]{3,2,1,0:T(8,128)(2,1)S(1)} %copy.64) | data formatting | bytes 4194304 | tf_op jit(solution)/shard_map/reshape | solution.py:83
  163.4 0.0 copy-done.1
  (13 shorter events, 0.1 us)
Async XLA Ops:
  6.5 17.5 %copy-start = (bf16[1,4,64,896]{3,2,1,0:T(8,128)(2,1)S(1)}, bf16[1,4,64,896]{3,2,1,0:T(8,128)(2,1)}, u32[]{:S(2)}) copy-start(bf16[1,4,64,896]{3,2,1,0:T(8,128)(2,1)} %param.8) | copy-start | bytes 1376260
  6.5 70.8 %all-gather.2.cloned.1.call-start = ((), (), s32[]{:S(2)}) async-start(), calls=%async_computation.2 | async-start | bytes 8028160 | tf_op jit(solution)/shard_map/all_gather | solution.py:48
  9.8 13.9 %all-to-all-start = ((s32[8,3,16]{2,1,0:T(4,128)}), s32[8,3,16]{2,1,0:T(4,128)S(1)}, u32[]{:S(2)}, u32[]{:S(2)}) async-start(s32[8,3,16]{2,1,0:T(4,128)} %broadcast_in_dim.22), calls=%async_computation | async-start | bytes 32768 | tf_op jit(solution)/shard_map/all_to_all | solution.py:59
  24.0 6.4 %copy-start.4 = (s32[1,8,2]{1,2,0:T(2,128)S(1)}, s32[1,8,2]{1,2,0:T(2,128)}, u32[]{:S(2)}) copy-start(s32[1,8,2]{1,2,0:T(2,128)} %param.9) | copy-start | bytes 196
  26.0 45.9 %all-to-all-start.1 = ((bf16[8,2,64,896]{3,2,1,0:T(8,128)(2,1)}), bf16[8,2,64,896]{3,2,1,0:T(8,128)(2,1)}, u32[]{:S(2)}, u32[]{:S(2)}) async-start(bf16[8,2,64,896]{3,2,1,0:T(8,128)(2,1)} %bitcast.5), calls=%async_computation.1 | async-start | bytes 3670016 | tf_op jit(solution)/shard_map/all_to_all | solution.py:65
  32.8 44.6 %copy-start.5 = (f32[896]{0:T(1024)S(1)}, f32[896]{0:T(1024)}, u32[]{:S(2)}) copy-start(f32[896]{0:T(1024)} %param.11) | copy-start | bytes 10756
  112.8 3.8 %copy-start.2 = (bf16[16,64,896]{2,1,0:T(8,128)(2,1)S(1)}, bf16[16,64,896]{2,1,0:T(8,128)(2,1)}, u32[]{:S(2)}) copy-start(bf16[16,64,896]{2,1,0:T(8,128)(2,1)} %gather_fusion.1) | copy-start | bytes 5505028
  133.6 5.6 %copy-start.3 = (f32[8,16,128,64]{2,3,1,0:T(8,128)}, f32[8,16,128,64]{2,3,1,0:T(8,128)S(1)}, u32[]{:S(2)}) copy-start(f32[8,16,128,64]{2,3,1,0:T(8,128)S(1)} %fusion.11) | copy-start | bytes 12582916
  139.2 24.2 %copy-start.1 = (bf16[1,4,64,896]{3,2,1,0:T(8,128)(2,1)S(1)}, bf16[1,4,64,896]{3,2,1,0:T(8,128)(2,1)}, u32[]{:S(2)}) copy-start(bf16[1,4,64,896]{3,2,1,0:T(8,128)(2,1)} %param.8) | copy-start | bytes 1376260
Sparse Core Ops, SparseCore 0:
  8.9 49.8 all-gather.1

commit v2 on v1

v2 whole, which is shorter than its diff:
```python
import jax
import jax.numpy as jnp
from jax import lax
from jax.experimental import pallas as pl
from jax.experimental.pallas import tpu as pltpu
from jax.sharding import PartitionSpec as P

HEADS = 16
HEAD_DIM = 128
ENC_HEADS = 7
NLEN = 64
SPAN = 64
NEIGH = 2
NB_DEV = 4


epsilon = 1e-05


def _softmax_bf16(scores):
    highest = jnp.max(scores, axis=-1, keepdims=True)
    raised = jnp.exp(scores - highest)
    return (raised / jnp.sum(raised, axis=-1, keepdims=True)).astype(jnp.bfloat16)


def _dot_t(a, b):
    return lax.dot_general(a, b, (((1,), (1,)), ((), ())), preferred_element_type=jnp.float32)


def _encoder_kernel(x_ref, gain_ref, w_ref, out_ref, qkv_ref, mix_ref):
    inputs = x_ref[...].astype(jnp.float32)
    spread = jnp.mean(inputs * inputs, axis=-1, keepdims=True)
    normed = (inputs * lax.rsqrt(spread + epsilon) * gain_ref[...]).astype(jnp.bfloat16)
    for p in range(3):
        qkv_ref[p] = jnp.dot(normed, w_ref[p], preferred_element_type=jnp.float32).astype(jnp.bfloat16)
    width = inputs.shape[-1]
    head_size = width // ENC_HEADS
    scale = head_size ** (-0.5)
    for b in range(inputs.shape[0] // NLEN):
        rows = pl.ds(b * NLEN, NLEN)
        for h in range(ENC_HEADS):
            cols = pl.ds(h * head_size, head_size)
            scores = _dot_t(qkv_ref[0, rows, cols], qkv_ref[1, rows, cols]) * scale
            weights = _softmax_bf16(scores)
            mix_ref[rows, cols] = jnp.dot(
                weights, qkv_ref[2, rows, cols], preferred_element_type=jnp.float32
            ).astype(jnp.bfloat16)
    output = jnp.dot(mix_ref[...], w_ref[3], preferred_element_type=jnp.float32)
    out_ref[...] = (inputs + output).astype(jnp.bfloat16)


def encode_blocks(blocks, gain, attention, group=4):
    count, length, width = blocks.shape
    rows = group * length
    flat = blocks.reshape(count * length, width)
    out = pl.pallas_call(
        _encoder_kernel,
        out_shape=jax.ShapeDtypeStruct(flat.shape, jnp.bfloat16),
        grid=(count // group,),
        in_specs=[
            pl.BlockSpec((rows, width), lambda i: (i, 0)),
            pl.BlockSpec((1, width), lambda i: (0, 0)),
            pl.BlockSpec(attention.shape, lambda i: (0, 0, 0)),
        ],
        out_specs=pl.BlockSpec((rows, width), lambda i: (i, 0)),
        scratch_shapes=[
            pltpu.VMEM((3, rows, width), jnp.bfloat16),
            pltpu.VMEM((rows, width), jnp.bfloat16),
        ],
    )(flat, gain.reshape(1, width), attention)
    return out


def _cross_kernel(q_ref, k_ref, v_ref, out_ref):
    scale = HEAD_DIM ** (-0.5)
    for h in range(q_ref.shape[-1] // HEAD_DIM):
        cols = pl.ds(h * HEAD_DIM, HEAD_DIM)
        scores = _dot_t(q_ref[:, cols], k_ref[:, cols]) * scale
        weights = _softmax_bf16(scores)
        out_ref[:, cols] = jnp.dot(
            weights, v_ref[:, cols], preferred_element_type=jnp.float32
        ).astype(jnp.bfloat16)


def cross_attend(queries, keys, values):
    length, width = queries.shape
    memory = NEIGH * NLEN
    return pl.pallas_call(
        _cross_kernel,
        out_shape=jax.ShapeDtypeStruct(queries.shape, jnp.bfloat16),
        grid=(length // SPAN,),
        in_specs=[
            pl.BlockSpec((SPAN, width), lambda c: (c, 0)),
            pl.BlockSpec((memory, width), lambda c: (c, 0)),
            pl.BlockSpec((memory, width), lambda c: (c, 0)),
        ],
        out_specs=pl.BlockSpec((SPAN, width), lambda c: (c, 0)),
    )(queries, keys, values)


def make_shards(n_seq):
    def shards(queries, neighbour_input, owner_list, block_list, enc_gain, enc_attn, kv_weight):
        full_weights = lax.all_gather(enc_attn, "dp", axis=1, tiled=True)
        me = lax.axis_index("seq")
        owners = owner_list.reshape(-1)
        indices = block_list.reshape(-1)
        refs = owners.shape[0]
        per_owner = -(-refs // n_seq)
        same = owners[:, None] == owners[None, :]
        earlier = jnp.arange(refs)[None, :] < jnp.arange(refs)[:, None]
        rank = jnp.sum(same & earlier, axis=1).astype(jnp.int32)
        asks = jnp.stack([owners, indices, rank])
        asks = jnp.broadcast_to(asks[None], (n_seq, 3, refs))
        asked = lax.all_to_all(asks, "seq", 0, 0, tiled=True)
        slots = jnp.arange(per_owner, dtype=jnp.int32)
        match = (asked[:, 0, None, :] == me) & (asked[:, 2, None, :] == slots[None, :, None])
        picks = jnp.sum(jnp.where(match, asked[:, 1, None, :], 0), axis=-1)
        sent = jnp.take(neighbour_input[0], picks.reshape(-1), axis=0, mode="clip")
        sent = sent.reshape(n_seq, per_owner, NLEN, neighbour_input.shape[-1])
        got = lax.all_to_all(sent, "seq", 0, 0, tiled=True)
        got = got.reshape(n_seq * per_owner, NLEN, neighbour_input.shape[-1])
        chosen_raw = jnp.take(got, owners * per_owner + rank, axis=0, mode="clip")
        chosen = encode_blocks(chosen_raw, enc_gain, full_weights)
        keys = jnp.dot(chosen, kv_weight[0], preferred_element_type=jnp.float32).astype(jnp.bfloat16)
        values = jnp.dot(chosen, kv_weight[1], preferred_element_type=jnp.float32).astype(jnp.bfloat16)
        return cross_attend(queries[0], keys, values)[None]

    return shards


def solution(mesh):
    return jax.shard_map(
        make_shards(mesh.shape["seq"]),
        mesh=mesh,
        in_specs=(
            P("dp", "seq", None),
            P("dp", "seq", None, None),
            P("dp", "seq", None),
            P("dp", "seq", None),
            P(),
            P(None, "dp", None),
            P(),
        ),
        out_specs=P("dp", "seq", None),
        check_vma=False,
    )
```

time: 171 us -> 187 us (1.094)
  Pallas kernels: 0 us -> 89.5 us
  matrix products: 53.2 us -> 17.4 us
  local copies, waits for them, and re-layouts: 38 us -> 7.29 us
  other arithmetic: 7.5 us -> 0.37 us
    pallas_call x0 -> x2, Pallas kernels: none -> 89.5 us  [the longest x1 45.9 us: encode_blocks(): pl.pallas_call(_encoder_kernel, out_shape=jax.ShapeDtypeStruct(flat.shape...]
    dot_general x7 -> x2, matrix products: 53.2 us -> 17.4 us  [the longest x1 9.17 us: shards(): jnp.dot(chosen, kv_weight[1], preferred_element_type=jnp.float32)]
    squeeze x3 -> x0, local copies, waits for them, and re-layouts: 13.8 us -> none  [the longest x1 4.6 us: encode(): split_heads[0]]
    unnamed x17 -> x10, local copies, waits for them, and re-layouts: 8.49 us -> 1.53 us
    sub x2 -> x0, other arithmetic: 5.2 us -> none  [softmax_rows(): raised = jnp.exp(scores - highest)]
    slice x2 -> x0, local copies, waits for them, and re-layouts: 3.78 us -> none  [the longest x1 2.58 us: encode(): split_heads[2]]
    convert_element_type x1 -> x0, local copies, waits for them, and re-layouts: 2.96 us -> none  [shards(): mixture = jnp.einsum('chqk,ckhd->cqhd', weights, memory_values, preferred...]
    reduce_sum x1 -> x0, other arithmetic: 1.93 us -> none  [encode(): spread = jnp.mean(inputs * inputs, axis=-1, keepdims=True)]
  transfers between devices with their start and end apart: 3 -> 3, of which waited for: 2 -> 2; matrix products, arithmetic and copies ran while one was open for 7% -> 4% of each run, Pallas kernels for 0% -> 0%
where the time goes in v2:
time: 187 us
  Pallas kernels  89.5 us (48%)
  waiting for transfers between devices  47.9 us (26%)
  matrix products  17.4 us (9%)
  between operations  13.5 us (7%)
  starting transfers between devices  11 us (6%)
  local copies, waits for them, and re-layouts  7.29 us (4%)
    pallas_call x1, Pallas kernels, encode_blocks(): pl.pallas_call(_encoder_kernel, out_shape=jax.ShapeDtypeStruct(flat.shape...  45.9 us
    pallas_call x1, Pallas kernels, cross_attend(): pl.pallas_call(_cross_kernel, out_shape=jax.ShapeDtypeStruct(queries.shap...  43.6 us
    all_to_all x1, waiting for transfers between devices, shards(): got = lax.all_to_all(sent, 'seq', 0, 0, tiled=True)  40.6 us
    dot_general x1, matrix products, shards(): jnp.dot(chosen, kv_weight[1], preferred_element_type=jnp.float32)  9.17 us
    dot_general x1, matrix products, shards(): jnp.dot(chosen, kv_weight[0], preferred_element_type=jnp.float32)  8.18 us
    all_to_all x1, starting transfers between devices, shards(): asked = lax.all_to_all(asks, 'seq', 0, 0, tiled=True)  7.28 us
    all_to_all x1, waiting for transfers between devices, shards(): asked = lax.all_to_all(asks, 'seq', 0, 0, tiled=True)  6.58 us
  transfers between devices with their start and end apart: 3, of which 2 were waited for; matrix products, arithmetic and copies ran while one was open for 4% of the time, Pallas kernels for 0%

profile of v2, /device:TPU:0, one launch (start us, length us, event | category | flops | bytes accessed | tf_op | source)
XLA Modules:
  0.0 186.9 jit_solution(11513416721398521813)
XLA Ops:
  6.5 0.0 copy-start
  6.5 0.0 all-gather.2.cloned.1.call-start
  6.5 0.7 all-gather.2.cloned.1.call-update
  7.3 0.8 copy.23
  8.0 0.1 eq.36
  8.1 0.1 stack_reshape.6
  8.2 0.8 copy.24
  8.9 0.1 stack_reshape.7
  9.0 0.2 convert_reduce_fusion
  9.2 0.6 broadcast_in_dim.32
  9.8 7.3 %all-to-all-start = ((s32[8,3,16]{2,1,0:T(4,128)}), s32[8,3,16]{2,1,0:T(4,128)S(1)}, u32[]{:S(2)}, u32[]{:S(2)}) async-start(s32[8,3,16]{2,1,0:T(4,128)} %broadcast_in_dim.32), calls=%async_computation | async-start | bytes 32768 | tf_op jit(solution)/shard_map/all_to_all | solution.py:114
  17.1 6.6 %all-to-all-done = s32[8,3,16]{2,1,0:T(4,128)S(1)} async-done(((s32[8,3,16]{2,1,0:T(4,128)}), s32[8,3,16]{2,1,0:T(4,128)S(1)}, u32[]{:S(2)}, u32[]{:S(2)}) %all-to-all-start) | async-done | bytes 1568 | tf_op jit(solution)/shard_map/all_to_all | solution.py:114
  23.7 0.1 select_reduce_fusion
  23.9 0.1 copy.29
  23.9 0.1 reshape.43
  24.0 0.0 copy-done
  24.0 2.0 %gather_fusion = bf16[16,64,896]{2,1,0:T(8,128)(2,1)} fusion(bf16[4,64,896]{2,1,0:T(8,128)(2,1)S(1)} %bitcast.30, s32[1024]{0:T(1024)S(1)} %pad_clamp_fusion.1), kind=kCustom, calls=%fused_computation | custom fusion | bytes 3670080 | tf_op jit(solution)/shard_map/jit(_take)/gather | solution.py:118
  26.0 0.0 copy-start.2
  26.0 0.0 copy-start.3
  26.0 3.7 %all-to-all-start.1 = ((bf16[8,2,64,896]{3,2,1,0:T(8,128)(2,1)}), bf16[8,2,64,896]{3,2,1,0:T(8,128)(2,1)S(1)}, u32[]{:S(2)}, u32[]{:S(2)}) async-start(bf16[8,2,64,896]{3,2,1,0:T(8,128)(2,1)} %bitcast.32), calls=%async_computation.1 | async-start | bytes 3670016 | tf_op jit(solution)/shard_map/all_to_all | solution.py:120
  29.8 0.0 copy-done.2
  29.8 0.1 copy.30
  29.9 0.1 mul.14
  30.0 0.0 copy-done.3
  30.0 0.6 reshape.40.gain_ref
  30.6 40.6 %all-to-all-done.1 = bf16[8,2,64,896]{3,2,1,0:T(8,128)(2,1)S(1)} async-done(((bf16[8,2,64,896]{3,2,1,0:T(8,128)(2,1)}), bf16[8,2,64,896]{3,2,1,0:T(8,128)(2,1)S(1)}, u32[]{:S(2)}, u32[]{:S(2)}) %all-to-all-start.1) | async-done | bytes 1835040 | tf_op jit(solution)/shard_map/all_to_all | solution.py:120
  71.2 2.0 %gather_fusion.1 = bf16[16,64,896]{2,1,0:T(8,128)(2,1)} fusion(bf16[16,64,896]{2,1,0:T(8,128)(2,1)S(1)} %bitcast.31, s32[1024]{0:T(1024)S(1)} %pad_clamp_fusion), kind=kCustom, calls=%fused_computation.1 | custom fusion | bytes 3670080 | tf_op jit(solution)/shard_map/jit(_take)/gather | solution.py:122
  73.2 0.0 all-gather.2.cloned.1.call-done.w_ref
  73.2 45.9 %shard_map.73 = bf16[1024,896]{1,0:T(8,128)(2,1)} custom-call(bf16[1024,896]{1,0:T(8,128)(2,1)} %bitcast.33, f32[1,896]{1,0:T(1,128)} %reshape.40.gain_ref, bf16[4,896,896]{2,1,0:T(8,128)(2,1)} %all-gather.2.cloned.1.call-done.w_ref), custom_call_target="tpu_custom_call" | custom-call | tf_op jit(solution)/shard_map/pallas_call | solution.py:56
  119.1 0.0 copy-start.1
  119.1 9.2 %convolution_convert_fusion.v_ref = bf16[1024,2048]{1,0:T(8,128)(2,1)} fusion(bf16[1024,896]{1,0:T(8,128)(2,1)} %shard_map.73, bf16[2,896,2048]{2,1,0:T(8,128)(2,1)} %param.13), kind=kOutput, calls=%fused_computation.2 | convolution fusion | flops 3760193536 | bytes 9699328 | tf_op jit(solution)/shard_map/dot_general | solution.py:125
  128.3 0.0 copy-done.1
  128.3 8.2 %convolution_convert_fusion.1.k_ref = bf16[1024,2048]{1,0:T(8,128)(2,1)} fusion(bf16[1024,896]{1,0:T(8,128)(2,1)S(1)} %copy-done.1, bf16[2,896,2048]{2,1,0:T(8,128)(2,1)} %param.13), kind=kOutput, calls=%fused_computation.3 | convolution fusion | flops 3760193536 | bytes 9699328 | tf_op jit(solution)/shard_map/dot_general | solution.py:124
  136.5 43.6 %shard_map.74 = bf16[512,2048]{1,0:T(8,128)(2,1)} custom-call(bf16[512,2048]{1,0:T(8,128)(2,1)} %bitcast.34, bf16[1024,2048]{1,0:T(8,128)(2,1)} %convolution_convert_fusion.1.k_ref, bf16[1024,2048]{1,0:T(8,128)(2,1)} %convolution_convert_fusion.v_ref), custom_call_target="tpu_custom_call" | custom-call | tf_op jit(solution)/shard_map/pallas_call | solution.py:88
  (7 shorter events, 0.1 us)
Async XLA Ops:
  6.5 17.5 %copy-start = (bf16[1,4,64,896]{3,2,1,0:T(8,128)(2,1)S(1)}, bf16[1,4,64,896]{3,2,1,0:T(8,128)(2,1)}, u32[]{:S(2)}) copy-start(bf16[1,4,64,896]{3,2,1,0:T(8,128)(2,1)} %param.8) | copy-start | bytes 1376260
  6.5 66.6 %all-gather.2.cloned.1.call-start = ((), (), s32[]{:S(2)}) async-start(), calls=%async_computation.2 | async-start | bytes 8028160 | tf_op jit(solution)/shard_map/all_gather | solution.py:103
  9.8 13.9 %all-to-all-start = ((s32[8,3,16]{2,1,0:T(4,128)}), s32[8,3,16]{2,1,0:T(4,128)S(1)}, u32[]{:S(2)}, u32[]{:S(2)}) async-start(s32[8,3,16]{2,1,0:T(4,128)} %broadcast_in_dim.32), calls=%async_computation | async-start | bytes 32768 | tf_op jit(solution)/shard_map/all_to_all | solution.py:114
  26.0 3.7 %copy-start.2 = (s32[1,8,2]{1,2,0:T(2,128)S(1)}, s32[1,8,2]{1,2,0:T(2,128)}, u32[]{:S(2)}) copy-start(s32[1,8,2]{1,2,0:T(2,128)} %param.9) | copy-start | bytes 196
  26.0 3.9 %copy-start.3 = (f32[896]{0:T(1024)S(1)}, f32[896]{0:T(1024)}, u32[]{:S(2)}) copy-start(f32[896]{0:T(1024)} %param.11) | copy-start | bytes 10756
  26.0 45.1 %all-to-all-start.1 = ((bf16[8,2,64,896]{3,2,1,0:T(8,128)(2,1)}), bf16[8,2,64,896]{3,2,1,0:T(8,128)(2,1)S(1)}, u32[]{:S(2)}, u32[]{:S(2)}) async-start(bf16[8,2,64,896]{3,2,1,0:T(8,128)(2,1)} %bitcast.32), calls=%async_computation.1 | async-start | bytes 3670016 | tf_op jit(solution)/shard_map/all_to_all | solution.py:120
  119.1 9.2 %copy-start.1 = (bf16[1024,896]{1,0:T(8,128)(2,1)S(1)}, bf16[1024,896]{1,0:T(8,128)(2,1)}, u32[]{:S(2)}) copy-start(bf16[1024,896]{1,0:T(8,128)(2,1)} %shard_map.73) | copy-start | bytes 5505028
Sparse Core Ops, SparseCore 0:
  8.9 49.8 all-gather.1

commit v3 on v2

--- a/solution.py
+++ b/solution.py
@@ -20,40 +20,42 @@
 def _softmax_bf16(scores):
     highest = jnp.max(scores, axis=-1, keepdims=True)
     raised = jnp.exp(scores - highest)
-    return (raised / jnp.sum(raised, axis=-1, keepdims=True)).astype(jnp.bfloat16)
+    return (raised * (1.0 / jnp.sum(raised, axis=-1, keepdims=True))).astype(jnp.bfloat16)
 
 
-def _dot_t(a, b):
-    return lax.dot_general(a, b, (((1,), (1,)), ((), ())), preferred_element_type=jnp.float32)
-
-
-def _encoder_kernel(x_ref, gain_ref, w_ref, out_ref, qkv_ref, mix_ref):
+def _encoder_kernel(x_ref, gain_ref, w_ref, out_ref, q_ref, kt_ref, v_ref, mix_ref):
     inputs = x_ref[...].astype(jnp.float32)
     spread = jnp.mean(inputs * inputs, axis=-1, keepdims=True)
     normed = (inputs * lax.rsqrt(spread + epsilon) * gain_ref[...]).astype(jnp.bfloat16)
-    for p in range(3):
-        qkv_ref[p] = jnp.dot(normed, w_ref[p], preferred_element_type=jnp.float32).astype(jnp.bfloat16)
+    q_ref[...] = jnp.dot(normed, w_ref[0], preferred_element_type=jnp.float32).astype(jnp.bfloat16)
+    v_ref[...] = jnp.dot(normed, w_ref[2], preferred_element_type=jnp.float32).astype(jnp.bfloat16)
+    kt_ref[...] = jnp.dot(normed, w_ref[1], preferred_element_type=jnp.float32).T.astype(jnp.bfloat16)
     width = inputs.shape[-1]
     head_size = width // ENC_HEADS
     scale = head_size ** (-0.5)
-    for b in range(inputs.shape[0] // NLEN):
-        rows = pl.ds(b * NLEN, NLEN)
+    pair = 2 * NLEN
+    rows_of = lax.broadcasted_iota(jnp.int32, (pair, pair), 0) // NLEN
+    cols_of = lax.broadcasted_iota(jnp.int32, (pair, pair), 1) // NLEN
+    same = rows_of == cols_of
+    for b in range(inputs.shape[0] // pair):
+        rows = pl.ds(b * pair, pair)
         for h in range(ENC_HEADS):
             cols = pl.ds(h * head_size, head_size)
-            scores = _dot_t(qkv_ref[0, rows, cols], qkv_ref[1, rows, cols]) * scale
-            weights = _softmax_bf16(scores)
+            scores = jnp.dot(q_ref[rows, cols], kt_ref[cols, rows], preferred_element_type=jnp.float32) * scale
+            weights = _softmax_bf16(jnp.where(same, scores, -jnp.inf))
             mix_ref[rows, cols] = jnp.dot(
-                weights, qkv_ref[2, rows, cols], preferred_element_type=jnp.float32
+                weights, v_ref[rows, cols], preferred_element_type=jnp.float32
             ).astype(jnp.bfloat16)
     output = jnp.dot(mix_ref[...], w_ref[3], preferred_element_type=jnp.float32)
     out_ref[...] = (inputs + output).astype(jnp.bfloat16)
 
 
-def encode_blocks(blocks, gain, attention, group=4):
+def encode_blocks(blocks, gain, attention, group=8):
     count, length, width = blocks.shape
+    group = min(group, count)
     rows = group * length
     flat = blocks.reshape(count * length, width)
-    out = pl.pallas_call(
+    return pl.pallas_call(
         _encoder_kernel,
         out_shape=jax.ShapeDtypeStruct(flat.shape, jnp.bfloat16),
         grid=(count // group,),
@@ -64,38 +66,44 @@
         ],
         out_specs=pl.BlockSpec((rows, width), lambda i: (i, 0)),
         scratch_shapes=[
-            pltpu.VMEM((3, rows, width), jnp.bfloat16),
+            pltpu.VMEM((rows, width), jnp.bfloat16),
+            pltpu.VMEM((width, rows), jnp.bfloat16),
+            pltpu.VMEM((rows, width), jnp.bfloat16),
             pltpu.VMEM((rows, width), jnp.bfloat16),
         ],
     )(flat, gain.reshape(1, width), attention)
-    return out
 
 
-def _cross_kernel(q_ref, k_ref, v_ref, out_ref):
+def _cross_kernel(q_ref, kt_ref, v_ref, out_ref):
     scale = HEAD_DIM ** (-0.5)
-    for h in range(q_ref.shape[-1] // HEAD_DIM):
-        cols = pl.ds(h * HEAD_DIM, HEAD_DIM)
-        scores = _dot_t(q_ref[:, cols], k_ref[:, cols]) * scale
-        weights = _softmax_bf16(scores)
-        out_ref[:, cols] = jnp.dot(
-            weights, v_ref[:, cols], preferred_element_type=jnp.float32
-        ).astype(jnp.bfloat16)
+    memory = NEIGH * NLEN
+    for s in range(q_ref.shape[0] // SPAN):
+        rq = pl.ds(s * SPAN, SPAN)
+        rk = pl.ds(s * memory, memory)
+        for h in range(q_ref.shape[-1] // HEAD_DIM):
+            cols = pl.ds(h * HEAD_DIM, HEAD_DIM)
+            scores = jnp.dot(q_ref[rq, cols], kt_ref[cols, rk], preferred_element_type=jnp.float32) * scale
+            weights = _softmax_bf16(scores)
+            out_ref[rq, cols] = jnp.dot(
+                weights, v_ref[rk, cols], preferred_element_type=jnp.float32
+            ).astype(jnp.bfloat16)
 
 
-def cross_attend(queries, keys, values):
+def cross_attend(queries, keys_t, values, group=4):
     length, width = queries.shape
     memory = NEIGH * NLEN
+    group = min(group, length // SPAN)
     return pl.pallas_call(
         _cross_kernel,
         out_shape=jax.ShapeDtypeStruct(queries.shape, jnp.bfloat16),
-        grid=(length // SPAN,),
+        grid=(length // (SPAN * group),),
         in_specs=[
-            pl.BlockSpec((SPAN, width), lambda c: (c, 0)),
-            pl.BlockSpec((memory, width), lambda c: (c, 0)),
-            pl.BlockSpec((memory, width), lambda c: (c, 0)),
+            pl.BlockSpec((SPAN * group, width), lambda c: (c, 0)),
+            pl.BlockSpec((width, memory * group), lambda c: (0, c)),
+            pl.BlockSpec((memory * group, width), lambda c: (c, 0)),
         ],
-        out_specs=pl.BlockSpec((SPAN, width), lambda c: (c, 0)),
-    )(queries, keys, values)
+        out_specs=pl.BlockSpec((SPAN * group, width), lambda c: (c, 0)),
+    )(queries, keys_t, values)
 
 
 def make_shards(n_seq):
@@ -121,9 +129,11 @@
         got = got.reshape(n_seq * per_owner, NLEN, neighbour_input.shape[-1])
         chosen_raw = jnp.take(got, owners * per_owner + rank, axis=0, mode="clip")
         chosen = encode_blocks(chosen_raw, enc_gain, full_weights)
-        keys = jnp.dot(chosen, kv_weight[0], preferred_element_type=jnp.float32).astype(jnp.bfloat16)
+        keys_t = jnp.einsum(
+            "ef,re->fr", kv_weight[0], chosen, preferred_element_type=jnp.float32
+        ).astype(jnp.bfloat16)
         values = jnp.dot(chosen, kv_weight[1], preferred_element_type=jnp.float32).astype(jnp.bfloat16)
-        return cross_attend(queries[0], keys, values)[None]
+        return cross_attend(queries[0], keys_t, values)[None]
 
     return shards
 

time: 187 us -> 122 us (0.65)
  Pallas kernels: 89.5 us -> 24.3 us
    pallas_call x1, Pallas kernels: 43.6 us -> 8.25 us  [cross_attend(): pl.pallas_call(_cross_kernel, out_shape=jax.ShapeDtypeStruct(queries.shap...]
    pallas_call x1, Pallas kernels: 45.9 us -> 16 us  [encode_blocks(): pl.pallas_call(_encoder_kernel, out_shape=jax.ShapeDtypeStruct(flat.shape...]
  transfers between devices with their start and end apart: 3 -> 3, of which waited for: 2 -> 2; matrix products, arithmetic and copies ran while one was open for 4% -> 6% of each run, Pallas kernels for 0% -> 0%
where the time goes in v3:
time: 122 us
  waiting for transfers between devices  47.9 us (39%)
  Pallas kernels  24.3 us (20%)
  matrix products  17.4 us (14%)
  between operations  13.5 us (11%)
  starting transfers between devices  11 us (9%)
  local copies, waits for them, and re-layouts  7.29 us (6%)
    all_to_all x1, waiting for transfers between devices, shards(): got = lax.all_to_all(sent, 'seq', 0, 0, tiled=True)  40.6 us
    pallas_call x1, Pallas kernels, encode_blocks(): pl.pallas_call(_encoder_kernel, out_shape=jax.ShapeDtypeStruct(flat.shape...  16 us
    dot_general x1, matrix products, shards(): jnp.dot(chosen, kv_weight[1], preferred_element_type=jnp.float32)  9.17 us
    pallas_call x1, Pallas kernels, cross_attend(): pl.pallas_call(_cross_kernel, out_shape=jax.ShapeDtypeStruct(queries.shap...  8.25 us
    dot_general x1, matrix products, shards(): jnp.einsum('ef,re->fr', kv_weight[0], chosen, preferred_element_type=jnp....  8.24 us
    all_to_all x1, starting transfers between devices, shards(): asked = lax.all_to_all(asks, 'seq', 0, 0, tiled=True)  7.28 us
    all_to_all x1, waiting for transfers between devices, shards(): asked = lax.all_to_all(asks, 'seq', 0, 0, tiled=True)  6.58 us
    all_to_all x1, starting transfers between devices, shards(): got = lax.all_to_all(sent, 'seq', 0, 0, tiled=True)  3.72 us
  transfers between devices with their start and end apart: 3, of which 2 were waited for; matrix products, arithmetic and copies ran while one was open for 6% of the time, Pallas kernels for 0%

profile of v3, /device:TPU:0, one launch (start us, length us, event | category | flops | bytes accessed | tf_op | source)
XLA Modules:
  0.0 121.7 jit_solution(989430405309559168)
XLA Ops:
  6.5 0.0 copy-start
  6.5 0.0 all-gather.2.cloned.1.call-start
  6.5 0.7 all-gather.2.cloned.1.call-update
  7.3 0.8 copy.26
  8.0 0.1 eq.36
  8.1 0.1 stack_reshape.6
  8.2 0.8 copy.27
  8.9 0.1 stack_reshape.7
  9.0 0.2 convert_reduce_fusion
  9.2 0.6 broadcast_in_dim.32
  9.8 7.3 %all-to-all-start = ((s32[8,3,16]{2,1,0:T(4,128)}), s32[8,3,16]{2,1,0:T(4,128)S(1)}, u32[]{:S(2)}, u32[]{:S(2)}) async-start(s32[8,3,16]{2,1,0:T(4,128)} %broadcast_in_dim.32), calls=%async_computation | async-start | bytes 32768 | tf_op jit(solution)/shard_map/all_to_all | solution.py:122
  17.1 6.6 %all-to-all-done = s32[8,3,16]{2,1,0:T(4,128)S(1)} async-done(((s32[8,3,16]{2,1,0:T(4,128)}), s32[8,3,16]{2,1,0:T(4,128)S(1)}, u32[]{:S(2)}, u32[]{:S(2)}) %all-to-all-start) | async-done | bytes 1568 | tf_op jit(solution)/shard_map/all_to_all | solution.py:122
  23.7 0.1 select_reduce_fusion
  23.9 0.1 copy.32
  23.9 0.1 reshape.43
  24.0 0.0 copy-done
  24.0 2.0 %gather_fusion = bf16[16,64,896]{2,1,0:T(8,128)(2,1)} fusion(bf16[4,64,896]{2,1,0:T(8,128)(2,1)S(1)} %bitcast.32, s32[1024]{0:T(1024)S(1)} %pad_clamp_fusion.1), kind=kCustom, calls=%fused_computation | custom fusion | bytes 3670080 | tf_op jit(solution)/shard_map/jit(_take)/gather | solution.py:126
  26.0 0.0 copy-start.2
  26.0 0.0 copy-start.3
  26.0 3.7 %all-to-all-start.1 = ((bf16[8,2,64,896]{3,2,1,0:T(8,128)(2,1)}), bf16[8,2,64,896]{3,2,1,0:T(8,128)(2,1)S(1)}, u32[]{:S(2)}, u32[]{:S(2)}) async-start(bf16[8,2,64,896]{3,2,1,0:T(8,128)(2,1)} %bitcast.34), calls=%async_computation.1 | async-start | bytes 3670016 | tf_op jit(solution)/shard_map/all_to_all | solution.py:128
  29.8 0.0 copy-done.2
  29.8 0.1 copy.33
  29.9 0.1 mul.14
  30.0 0.0 copy-done.3
  30.0 0.6 reshape.40.gain_ref
  30.6 40.6 %all-to-all-done.1 = bf16[8,2,64,896]{3,2,1,0:T(8,128)(2,1)S(1)} async-done(((bf16[8,2,64,896]{3,2,1,0:T(8,128)(2,1)}), bf16[8,2,64,896]{3,2,1,0:T(8,128)(2,1)S(1)}, u32[]{:S(2)}, u32[]{:S(2)}) %all-to-all-start.1) | async-done | bytes 1835040 | tf_op jit(solution)/shard_map/all_to_all | solution.py:128
  71.2 2.0 %gather_fusion.1 = bf16[16,64,896]{2,1,0:T(8,128)(2,1)} fusion(bf16[16,64,896]{2,1,0:T(8,128)(2,1)S(1)} %bitcast.33, s32[1024]{0:T(1024)S(1)} %pad_clamp_fusion), kind=kCustom, calls=%fused_computation.1 | custom fusion | bytes 3670080 | tf_op jit(solution)/shard_map/jit(_take)/gather | solution.py:130
  73.2 0.0 all-gather.2.cloned.1.call-done.w_ref
  73.2 16.0 %shard_map.73 = bf16[1024,896]{1,0:T(8,128)(2,1)} custom-call(bf16[1024,896]{1,0:T(8,128)(2,1)} %bitcast.35, f32[1,896]{1,0:T(1,128)} %reshape.40.gain_ref, bf16[4,896,896]{2,1,0:T(8,128)(2,1)} %all-gather.2.cloned.1.call-done.w_ref), custom_call_target="tpu_custom_call" | custom-call | tf_op jit(solution)/shard_map/pallas_call | solution.py:58
  89.2 0.0 copy-start.1
  89.2 9.2 %convolution_convert_fusion.v_ref = bf16[1024,2048]{1,0:T(8,128)(2,1)} fusion(bf16[1024,896]{1,0:T(8,128)(2,1)} %shard_map.73, bf16[2,896,2048]{2,1,0:T(8,128)(2,1)} %param.13), kind=kOutput, calls=%fused_computation.3 | convolution fusion | flops 3760193536 | bytes 9699328 | tf_op jit(solution)/shard_map/dot_general | solution.py:135
  98.3 0.0 copy-done.1
  98.4 8.2 %convert_bitcast_fusion.kt_ref = bf16[2048,1024]{1,0:T(8,128)(2,1)} fusion(bf16[1024,896]{1,0:T(8,128)(2,1)S(1)} %copy-done.1, bf16[2,896,2048]{2,1,0:T(8,128)(2,1)} %param.13), kind=kOutput, calls=%fused_computation.2 | convolution fusion | flops 3760193536 | bytes 9699328 | tf_op jit(solution)/shard_map/ef,re->fr/dot_general | solution.py:132
  106.6 8.2 %shard_map.74 = bf16[512,2048]{1,0:T(8,128)(2,1)} custom-call(bf16[512,2048]{1,0:T(8,128)(2,1)} %bitcast.36, bf16[2048,1024]{1,0:T(8,128)(2,1)} %convert_bitcast_fusion.kt_ref, bf16[1024,2048]{1,0:T(8,128)(2,1)} %convolution_convert_fusion.v_ref), custom_call_target="tpu_custom_call" | custom-call | tf_op jit(solution)/shard_map/pallas_call | solution.py:96
  (7 shorter events, 0.1 us)
Async XLA Ops:
  6.5 17.5 %copy-start = (bf16[1,4,64,896]{3,2,1,0:T(8,128)(2,1)S(1)}, bf16[1,4,64,896]{3,2,1,0:T(8,128)(2,1)}, u32[]{:S(2)}) copy-start(bf16[1,4,64,896]{3,2,1,0:T(8,128)(2,1)} %param.8) | copy-start | bytes 1376260
  6.5 66.6 %all-gather.2.cloned.1.call-start = ((), (), s32[]{:S(2)}) async-start(), calls=%async_computation.2 | async-start | bytes 8028160 | tf_op jit(solution)/shard_map/all_gather | solution.py:111
  9.8 13.9 %all-to-all-start = ((s32[8,3,16]{2,1,0:T(4,128)}), s32[8,3,16]{2,1,0:T(4,128)S(1)}, u32[]{:S(2)}, u32[]{:S(2)}) async-start(s32[8,3,16]{2,1,0:T(4,128)} %broadcast_in_dim.32), calls=%async_computation | async-start | bytes 32768 | tf_op jit(solution)/shard_map/all_to_all | solution.py:122
  26.0 3.7 %copy-start.2 = (s32[1,8,2]{1,2,0:T(2,128)S(1)}, s32[1,8,2]{1,2,0:T(2,128)}, u32[]{:S(2)}) copy-start(s32[1,8,2]{1,2,0:T(2,128)} %param.9) | copy-start | bytes 196
  26.0 3.9 %copy-start.3 = (f32[896]{0:T(1024)S(1)}, f32[896]{0:T(1024)}, u32[]{:S(2)}) copy-start(f32[896]{0:T(1024)} %param.11) | copy-start | bytes 10756
  26.0 45.1 %all-to-all-start.1 = ((bf16[8,2,64,896]{3,2,1,0:T(8,128)(2,1)}), bf16[8,2,64,896]{3,2,1,0:T(8,128)(2,1)S(1)}, u32[]{:S(2)}, u32[]{:S(2)}) async-start(bf16[8,2,64,896]{3,2,1,0:T(8,128)(2,1)} %bitcast.34), calls=%async_computation.1 | async-start | bytes 3670016 | tf_op jit(solution)/shard_map/all_to_all | solution.py:128
  89.2 9.2 %copy-start.1 = (bf16[1024,896]{1,0:T(8,128)(2,1)S(1)}, bf16[1024,896]{1,0:T(8,128)(2,1)}, u32[]{:S(2)}) copy-start(bf16[1024,896]{1,0:T(8,128)(2,1)} %shard_map.73) | copy-start | bytes 5505028
Sparse Core Ops, SparseCore 0:
  8.9 49.8 all-gather.1

commit v4 on v3

--- a/solution.py
+++ b/solution.py
@@ -108,8 +108,6 @@
 
 def make_shards(n_seq):
     def shards(queries, neighbour_input, owner_list, block_list, enc_gain, enc_attn, kv_weight):
-        full_weights = lax.all_gather(enc_attn, "dp", axis=1, tiled=True)
-        me = lax.axis_index("seq")
         owners = owner_list.reshape(-1)
         indices = block_list.reshape(-1)
         refs = owners.shape[0]
@@ -118,8 +116,10 @@
         earlier = jnp.arange(refs)[None, :] < jnp.arange(refs)[:, None]
         rank = jnp.sum(same & earlier, axis=1).astype(jnp.int32)
         asks = jnp.stack([owners, indices, rank])
-        asks = jnp.broadcast_to(asks[None], (n_seq, 3, refs))
-        asked = lax.all_to_all(asks, "seq", 0, 0, tiled=True)
+        asked = lax.all_gather(asks, "seq", axis=0, tiled=False)
+        asked, enc_attn = lax.optimization_barrier((asked, enc_attn))
+        full_weights = lax.all_gather(enc_attn, "dp", axis=1, tiled=True)
+        me = lax.axis_index("seq")
         slots = jnp.arange(per_owner, dtype=jnp.int32)
         match = (asked[:, 0, None, :] == me) & (asked[:, 2, None, :] == slots[None, :, None])
         picks = jnp.sum(jnp.where(match, asked[:, 1, None, :], 0), axis=-1)

time: 122 us -> 133 us (1.090)
  blocking collectives: 0 us -> 27.8 us
  waiting for transfers between devices: 47.9 us -> 38.1 us
  starting transfers between devices: 11 us -> 4.16 us
    all_gather x0 -> x1, blocking collectives: none -> 27.8 us  [shards(): asked = lax.all_gather(asks, 'seq', axis=0, tiled=False)]
    all_to_all x1 -> x0, starting transfers between devices: 7.28 us -> none  [shards(): asked = lax.all_to_all(asks, 'seq', 0, 0, tiled=True)]
    all_to_all x1 -> x0, waiting for transfers between devices: 6.58 us -> none  [shards(): asked = lax.all_to_all(asks, 'seq', 0, 0, tiled=True)]
    all_to_all x1, waiting for transfers between devices: 40.6 us -> 38.1 us  [shards(): got = lax.all_to_all(sent, 'seq', 0, 0, tiled=True)]
  transfers between devices with their start and end apart: 3 -> 2, of which waited for: 2 -> 1; matrix products, arithmetic and copies ran while one was open for 6% -> 4% of each run, Pallas kernels for 0% -> 0%
where the time goes in v4:
time: 133 us; the launch traced here: 132 us
  waiting for transfers between devices  38.1 us (29%)
  blocking collectives  27.8 us (21%)
  Pallas kernels  24.3 us (18%)
  matrix products  17.4 us (13%)
  between operations  13.5 us (10%)
  local copies, waits for them, and re-layouts  6.71 us (5%)
  starting transfers between devices  4.16 us (3%)
    all_to_all x1, waiting for transfers between devices, shards(): got = lax.all_to_all(sent, 'seq', 0, 0, tiled=True)  38.1 us
    all_gather x1, blocking collectives, shards(): asked = lax.all_gather(asks, 'seq', axis=0, tiled=False)  27.8 us
    pallas_call x1, Pallas kernels, encode_blocks(): pl.pallas_call(_encoder_kernel, out_shape=jax.ShapeDtypeStruct(flat.shape...  16 us
    dot_general x1, matrix products, shards(): jnp.dot(chosen, kv_weight[1], preferred_element_type=jnp.float32)  9.16 us
    dot_general x1, matrix products, shards(): jnp.einsum('ef,re->fr', kv_weight[0], chosen, preferred_element_type=jnp....  8.27 us
    pallas_call x1, Pallas kernels, cross_attend(): pl.pallas_call(_cross_kernel, out_shape=jax.ShapeDtypeStruct(queries.shap...  8.25 us
    all_to_all x1, starting transfers between devices, shards(): got = lax.all_to_all(sent, 'seq', 0, 0, tiled=True)  4.15 us
  transfers between devices with their start and end apart: 2, of which 1 were waited for; matrix products, arithmetic and copies ran while one was open for 4% of the time, Pallas kernels for 0%

profile of v4, /device:TPU:0, one launch (start us, length us, event | category | flops | bytes accessed | tf_op | source)
XLA Modules:
  0.0 132.2 jit_solution(6468110601116898498)
XLA Ops:
  6.5 0.0 copy-start
  6.5 0.0 all-gather.4.cloned.1.call-start
  6.5 0.8 copy.26
  7.3 0.1 eq.36
  7.4 0.1 stack_reshape.6
  7.5 0.2 convert_reduce_fusion
  7.7 0.8 copy.27
  8.5 0.1 stack_reshape.7
  8.5 27.8 %all-gather.1 = s32[8,3,16]{2,1,0:T(4,128)S(1)} all-gather(s32[1,3,16]{2,1,0:T(4,128)S(1)} %add_bitcast_fusion), channel_id=2, replica_groups=mesh['dp'=4,'seq'=8] {'seq'}, dimensions={0}, use_global_device_ids=true | all-gather | bytes 1728 | tf_op jit(solution)/shard_map/all_gather | solution.py:119
  36.3 0.0 all-gather.4.cloned.1.call-update
  36.4 0.1 select_reduce_fusion
  36.5 0.1 copy.32
  36.6 0.1 reshape.42
  36.7 0.0 copy-done
  36.7 2.0 %gather_fusion = bf16[16,64,896]{2,1,0:T(8,128)(2,1)} fusion(bf16[4,64,896]{2,1,0:T(8,128)(2,1)S(1)} %bitcast.31, s32[1024]{0:T(1024)S(1)} %pad_clamp_fusion.1), kind=kCustom, calls=%fused_computation | custom fusion | bytes 3670080 | tf_op jit(solution)/shard_map/jit(_take)/gather | solution.py:126
  38.7 0.0 copy-start.2
  38.7 0.0 copy-start.3
  38.7 4.2 %all-to-all-start = ((bf16[8,2,64,896]{3,2,1,0:T(8,128)(2,1)}), bf16[8,2,64,896]{3,2,1,0:T(8,128)(2,1)S(1)}, u32[]{:S(2)}, u32[]{:S(2)}) async-start(bf16[8,2,64,896]{3,2,1,0:T(8,128)(2,1)} %bitcast.33), calls=%async_computation | async-start | bytes 3670016 | tf_op jit(solution)/shard_map/all_to_all | solution.py:128
  42.9 0.0 copy-done.2
  42.9 0.1 copy.33
  43.0 0.1 mul.14
  43.1 0.0 copy-done.3
  43.1 0.6 reshape.39.gain_ref
  43.7 38.1 %all-to-all-done = bf16[8,2,64,896]{3,2,1,0:T(8,128)(2,1)S(1)} async-done(((bf16[8,2,64,896]{3,2,1,0:T(8,128)(2,1)}), bf16[8,2,64,896]{3,2,1,0:T(8,128)(2,1)S(1)}, u32[]{:S(2)}, u32[]{:S(2)}) %all-to-all-start) | async-done | bytes 1835040 | tf_op jit(solution)/shard_map/all_to_all | solution.py:128
  81.7 2.0 %gather_fusion.1 = bf16[16,64,896]{2,1,0:T(8,128)(2,1)} fusion(bf16[16,64,896]{2,1,0:T(8,128)(2,1)S(1)} %bitcast.32, s32[1024]{0:T(1024)S(1)} %pad_clamp_fusion), kind=kCustom, calls=%fused_computation.1 | custom fusion | bytes 3670080 | tf_op jit(solution)/shard_map/jit(_take)/gather | solution.py:130
  83.7 0.0 all-gather.4.cloned.1.call-done.w_ref
  83.7 16.0 %shard_map.73 = bf16[1024,896]{1,0:T(8,128)(2,1)} custom-call(bf16[1024,896]{1,0:T(8,128)(2,1)} %bitcast.34, f32[1,896]{1,0:T(1,128)} %reshape.39.gain_ref, bf16[4,896,896]{2,1,0:T(8,128)(2,1)} %all-gather.4.cloned.1.call-done.w_ref), custom_call_target="tpu_custom_call" | custom-call | tf_op jit(solution)/shard_map/pallas_call | solution.py:58
  99.7 0.0 copy-start.1
  99.7 9.2 %convolution_convert_fusion.v_ref = bf16[1024,2048]{1,0:T(8,128)(2,1)} fusion(bf16[1024,896]{1,0:T(8,128)(2,1)} %shard_map.73, bf16[2,896,2048]{2,1,0:T(8,128)(2,1)} %param.13), kind=kOutput, calls=%fused_computation.3 | convolution fusion | flops 3760193536 | bytes 9699328 | tf_op jit(solution)/shard_map/dot_general | solution.py:135
  108.9 0.0 copy-done.1
  108.9 8.3 %convert_bitcast_fusion.kt_ref = bf16[2048,1024]{1,0:T(8,128)(2,1)} fusion(bf16[1024,896]{1,0:T(8,128)(2,1)S(1)} %copy-done.1, bf16[2,896,2048]{2,1,0:T(8,128)(2,1)} %param.13), kind=kOutput, calls=%fused_computation.2 | convolution fusion | flops 3760193536 | bytes 9699328 | tf_op jit(solution)/shard_map/ef,re->fr/dot_general | solution.py:132
  117.1 8.2 %shard_map.74 = bf16[512,2048]{1,0:T(8,128)(2,1)} custom-call(bf16[512,2048]{1,0:T(8,128)(2,1)} %bitcast.35, bf16[2048,1024]{1,0:T(8,128)(2,1)} %convert_bitcast_fusion.kt_ref, bf16[1024,2048]{1,0:T(8,128)(2,1)} %convolution_convert_fusion.v_ref), custom_call_target="tpu_custom_call" | custom-call | tf_op jit(solution)/shard_map/pallas_call | solution.py:96
  (8 shorter events, 0.0 us)
Async XLA Ops:
  6.5 30.2 %copy-start = (bf16[1,4,64,896]{3,2,1,0:T(8,128)(2,1)S(1)}, bf16[1,4,64,896]{3,2,1,0:T(8,128)(2,1)}, u32[]{:S(2)}) copy-start(bf16[1,4,64,896]{3,2,1,0:T(8,128)(2,1)} %param.8) | copy-start | bytes 1376260
  6.5 77.2 %all-gather.4.cloned.1.call-start = ((), (), s32[]{:S(2)}) async-start(), calls=%async_computation.1 | async-start | bytes 8028160 | tf_op jit(solution)/shard_map/all_gather | solution.py:121
  38.7 4.2 %copy-start.2 = (s32[1,8,2]{1,2,0:T(2,128)S(1)}, s32[1,8,2]{1,2,0:T(2,128)}, u32[]{:S(2)}) copy-start(s32[1,8,2]{1,2,0:T(2,128)} %param.9) | copy-start | bytes 196
  38.7 4.3 %copy-start.3 = (f32[896]{0:T(1024)S(1)}, f32[896]{0:T(1024)}, u32[]{:S(2)}) copy-start(f32[896]{0:T(1024)} %param.11) | copy-start | bytes 10756
  38.7 43.0 %all-to-all-start = ((bf16[8,2,64,896]{3,2,1,0:T(8,128)(2,1)}), bf16[8,2,64,896]{3,2,1,0:T(8,128)(2,1)S(1)}, u32[]{:S(2)}, u32[]{:S(2)}) async-start(bf16[8,2,64,896]{3,2,1,0:T(8,128)(2,1)} %bitcast.33), calls=%async_computation | async-start | bytes 3670016 | tf_op jit(solution)/shard_map/all_to_all | solution.py:128
  99.7 9.2 %copy-start.1 = (bf16[1024,896]{1,0:T(8,128)(2,1)S(1)}, bf16[1024,896]{1,0:T(8,128)(2,1)}, u32[]{:S(2)}) copy-start(bf16[1024,896]{1,0:T(8,128)(2,1)} %shard_map.73) | copy-start | bytes 5505028
Sparse Core Ops, SparseCore 0:
  36.5 46.5 all-gather.3

commit v5 on v3

--- a/solution.py
+++ b/solution.py
@@ -118,8 +118,12 @@
         earlier = jnp.arange(refs)[None, :] < jnp.arange(refs)[:, None]
         rank = jnp.sum(same & earlier, axis=1).astype(jnp.int32)
         asks = jnp.stack([owners, indices, rank])
-        asks = jnp.broadcast_to(asks[None], (n_seq, 3, refs))
-        asked = lax.all_to_all(asks, "seq", 0, 0, tiled=True)
+        shifted = [asks]
+        for shift in range(1, n_seq):
+            ring = [(src, (src + shift) % n_seq) for src in range(n_seq)]
+            shifted.append(lax.ppermute(asks, "seq", ring))
+        shifted = jnp.stack(shifted)
+        asked = jnp.take(shifted, (me - jnp.arange(n_seq)) % n_seq, axis=0)
         slots = jnp.arange(per_owner, dtype=jnp.int32)
         match = (asked[:, 0, None, :] == me) & (asked[:, 2, None, :] == slots[None, :, None])
         picks = jnp.sum(jnp.where(match, asked[:, 1, None, :], 0), axis=-1)

time: 122 us -> 130 us (1.066)
  waiting for transfers between devices: 47.9 us -> 52.4 us
  starting transfers between devices: 11 us -> 14.6 us
    ppermute x0 -> x7, waiting for transfers between devices: none -> 13.6 us  [shards(): shifted.append(lax.ppermute(asks, 'seq', ring))]
    ppermute x0 -> x7, starting transfers between devices: none -> 10.5 us  [shards(): shifted.append(lax.ppermute(asks, 'seq', ring))]
    all_to_all x1 -> x0, starting transfers between devices: 7.28 us -> none  [shards(): asked = lax.all_to_all(asks, 'seq', 0, 0, tiled=True)]
    all_to_all x1 -> x0, waiting for transfers between devices: 6.58 us -> none  [shards(): asked = lax.all_to_all(asks, 'seq', 0, 0, tiled=True)]
    all_to_all x1, waiting for transfers between devices: 40.6 us -> 38 us  [shards(): got = lax.all_to_all(sent, 'seq', 0, 0, tiled=True)]
  transfers between devices with their start and end apart: 3 -> 9, of which waited for: 2 -> 4; matrix products, arithmetic and copies ran while one was open for 6% -> 6% of each run, Pallas kernels for 0% -> 0%
where the time goes in v5:
time: 130 us
  waiting for transfers between devices  52.4 us (40%)
  Pallas kernels  24.3 us (19%)
  matrix products  17.4 us (13%)
  starting transfers between devices  14.6 us (11%)
  between operations  13.5 us (10%)
  local copies, waits for them, and re-layouts  7.3 us (6%)
    all_to_all x1, waiting for transfers between devices, shards(): got = lax.all_to_all(sent, 'seq', 0, 0, tiled=True)  38 us
    pallas_call x1, Pallas kernels, encode_blocks(): pl.pallas_call(_encoder_kernel, out_shape=jax.ShapeDtypeStruct(flat.shape...  16 us
    ppermute x7, waiting for transfers between devices, shards(): shifted.append(lax.ppermute(asks, 'seq', ring))  13.6 us
    ppermute x7, starting transfers between devices, shards(): shifted.append(lax.ppermute(asks, 'seq', ring))  10.5 us
    dot_general x1, matrix products, shards(): jnp.dot(chosen, kv_weight[1], preferred_element_type=jnp.float32)  9.18 us
    dot_general x1, matrix products, shards(): jnp.einsum('ef,re->fr', kv_weight[0], chosen, preferred_element_type=jnp....  8.26 us
    pallas_call x1, Pallas kernels, cross_attend(): pl.pallas_call(_cross_kernel, out_shape=jax.ShapeDtypeStruct(queries.shap...  8.25 us
    all_to_all x1, starting transfers between devices, shards(): got = lax.all_to_all(sent, 'seq', 0, 0, tiled=True)  4.11 us
  transfers between devices with their start and end apart: 9, of which 4 were waited for; matrix products, arithmetic and copies ran while one was open for 6% of the time, Pallas kernels for 0%

profile of v5, /device:TPU:0, one launch (start us, length us, event | category | flops | bytes accessed | tf_op | source)
XLA Modules:
  0.0 130.0 jit_solution(4165400225521900072)
XLA Ops:
  6.5 0.0 copy-start
  6.5 0.0 all-gather.2.cloned.1.call-start
  6.5 0.7 all-gather.2.cloned.1.call-update
  7.3 0.8 copy.18
  8.0 0.1 stack_reshape.6
  8.1 0.1 eq.38
  8.2 0.8 copy.19
  8.9 0.1 stack_reshape.7
  9.0 0.2 convert_reduce_fusion
  9.2 5.1 %collective-permute-start.5 = (s32[3,16]{1,0:T(4,128)S(1)}, s32[3,16]{1,0:T(4,128)S(1)}, u32[]{:S(2)}, u32[]{:S(2)}) collective-permute-start(s32[3,16]{1,0:T(4,128)S(1)} %pad_add_fusion), channel_id=1, source_target_pairs={{0,6},{1,7},{2,0},{3,1},{4,2},{5,3},{6,4},{7,5},{8,14},{9,15},{10,... | collective-permute-start | bytes 584 | tf_op jit(solution)/shard_map/ppermute | solution.py:124
  14.3 0.4 collective-permute-start.4
  14.7 3.5 %collective-permute-start.3 = (s32[3,16]{1,0:T(4,128)S(1)}, s32[3,16]{1,0:T(4,128)S(1)}, u32[]{:S(2)}, u32[]{:S(2)}) collective-permute-start(s32[3,16]{1,0:T(4,128)S(1)} %pad_add_fusion), channel_id=1, source_target_pairs={{0,4},{1,5},{2,6},{3,7},{4,0},{5,1},{6,2},{7,3},{8,12},{9,13},{10,... | collective-permute-start | bytes 584 | tf_op jit(solution)/shard_map/ppermute | solution.py:124
  18.2 0.0 collective-permute-start.2
  18.2 1.5 %collective-permute-start = (s32[3,16]{1,0:T(4,128)S(1)}, s32[3,16]{1,0:T(4,128)S(1)}, u32[]{:S(2)}, u32[]{:S(2)}) collective-permute-start(s32[3,16]{1,0:T(4,128)S(1)} %pad_add_fusion), channel_id=1, source_target_pairs={{0,1},{1,2},{2,3},{3,4},{4,5},{5,6},{6,7},{7,0},{8,9},{9,10},{10,1... | collective-permute-start | bytes 584 | tf_op jit(solution)/shard_map/ppermute | solution.py:124
  19.7 4.8 %collective-permute-done = s32[3,16]{1,0:T(4,128)S(1)} collective-permute-done((s32[3,16]{1,0:T(4,128)S(1)}, s32[3,16]{1,0:T(4,128)S(1)}, u32[]{:S(2)}, u32[]{:S(2)}) %collective-permute-start) | collective-permute-done | bytes 224 | tf_op jit(solution)/shard_map/ppermute | solution.py:124
  24.5 0.0 collective-permute-start.1
  24.5 5.4 %collective-permute-done.1 = s32[3,16]{1,0:T(4,128)S(1)} collective-permute-done((s32[3,16]{1,0:T(4,128)S(1)}, s32[3,16]{1,0:T(4,128)S(1)}, u32[]{:S(2)}, u32[]{:S(2)}) %collective-permute-start.1) | collective-permute-done | bytes 224 | tf_op jit(solution)/shard_map/ppermute | solution.py:124
  29.9 0.0 collective-permute-start.6
  29.9 0.0 collective-permute-done.2
  29.9 0.0 collective-permute-done.3
  29.9 0.0 collective-permute-done.4
  29.9 0.0 collective-permute-done.5
  30.0 3.5 %collective-permute-done.6 = s32[3,16]{1,0:T(4,128)S(1)} collective-permute-done((s32[3,16]{1,0:T(4,128)S(1)}, s32[3,16]{1,0:T(4,128)S(1)}, u32[]{:S(2)}, u32[]{:S(2)}) %collective-permute-start.6) | collective-permute-done | bytes 224 | tf_op jit(solution)/shard_map/ppermute | solution.py:124
  33.5 0.6 gather_fusion
  34.0 0.1 broadcast_select_fusion
  34.2 0.1 select_reduce_fusion
  34.3 0.1 copy.21
  34.4 0.1 reshape.104
  34.5 0.0 copy-done
  34.5 2.0 %gather_fusion.1 = bf16[16,64,896]{2,1,0:T(8,128)(2,1)} fusion(bf16[4,64,896]{2,1,0:T(8,128)(2,1)S(1)} %bitcast.46, s32[1024]{0:T(1024)S(1)} %pad_clamp_fusion.1), kind=kCustom, calls=%fused_computation.1 | custom fusion | bytes 3670080 | tf_op jit(solution)/shard_map/jit(_take)/gather | solution.py:130
  36.5 0.0 copy-start.2
  36.5 0.0 copy-start.3
  36.5 4.1 %all-to-all-start = ((bf16[8,2,64,896]{3,2,1,0:T(8,128)(2,1)}), bf16[8,2,64,896]{3,2,1,0:T(8,128)(2,1)S(1)}, u32[]{:S(2)}, u32[]{:S(2)}) async-start(bf16[8,2,64,896]{3,2,1,0:T(8,128)(2,1)} %bitcast.48), calls=%async_computation | async-start | bytes 3670016 | tf_op jit(solution)/shard_map/all_to_all | solution.py:132
  40.6 0.0 copy-done.2
  40.6 0.1 copy.22
  40.7 0.1 mul.14
  40.8 0.0 copy-done.3
  40.8 0.6 reshape.93.gain_ref
  41.4 38.0 %all-to-all-done = bf16[8,2,64,896]{3,2,1,0:T(8,128)(2,1)S(1)} async-done(((bf16[8,2,64,896]{3,2,1,0:T(8,128)(2,1)}), bf16[8,2,64,896]{3,2,1,0:T(8,128)(2,1)S(1)}, u32[]{:S(2)}, u32[]{:S(2)}) %all-to-all-start) | async-done | bytes 1835040 | tf_op jit(solution)/shard_map/all_to_all | solution.py:132
  79.4 2.0 %gather_fusion.2 = bf16[16,64,896]{2,1,0:T(8,128)(2,1)} fusion(bf16[16,64,896]{2,1,0:T(8,128)(2,1)S(1)} %bitcast.47, s32[1024]{0:T(1024)S(1)} %pad_clamp_fusion), kind=kCustom, calls=%fused_computation.2 | custom fusion | bytes 3670080 | tf_op jit(solution)/shard_map/jit(_take)/gather | solution.py:134
  81.4 0.0 all-gather.2.cloned.1.call-done.w_ref
  81.4 16.0 %shard_map.73 = bf16[1024,896]{1,0:T(8,128)(2,1)} custom-call(bf16[1024,896]{1,0:T(8,128)(2,1)} %bitcast.49, f32[1,896]{1,0:T(1,128)} %reshape.93.gain_ref, bf16[4,896,896]{2,1,0:T(8,128)(2,1)} %all-gather.2.cloned.1.call-done.w_ref), custom_call_target="tpu_custom_call" | custom-call | tf_op jit(solution)/shard_map/pallas_call | solution.py:58
  97.5 0.0 copy-start.1
  97.5 9.2 %convolution_convert_fusion.v_ref = bf16[1024,2048]{1,0:T(8,128)(2,1)} fusion(bf16[1024,896]{1,0:T(8,128)(2,1)} %shard_map.73, bf16[2,896,2048]{2,1,0:T(8,128)(2,1)} %param.13), kind=kOutput, calls=%fused_computation.4 | convolution fusion | flops 3760193536 | bytes 9699328 | tf_op jit(solution)/shard_map/dot_general | solution.py:139
  106.6 0.0 copy-done.1
  106.6 8.3 %convert_bitcast_fusion.kt_ref = bf16[2048,1024]{1,0:T(8,128)(2,1)} fusion(bf16[1024,896]{1,0:T(8,128)(2,1)S(1)} %copy-done.1, bf16[2,896,2048]{2,1,0:T(8,128)(2,1)} %param.13), kind=kOutput, calls=%fused_computation.3 | convolution fusion | flops 3760193536 | bytes 9699328 | tf_op jit(solution)/shard_map/ef,re->fr/dot_general | solution.py:136
  114.9 8.2 %shard_map.74 = bf16[512,2048]{1,0:T(8,128)(2,1)} custom-call(bf16[512,2048]{1,0:T(8,128)(2,1)} %bitcast.50, bf16[2048,1024]{1,0:T(8,128)(2,1)} %convert_bitcast_fusion.kt_ref, bf16[1024,2048]{1,0:T(8,128)(2,1)} %convolution_convert_fusion.v_ref), custom_call_target="tpu_custom_call" | custom-call | tf_op jit(solution)/shard_map/pallas_call | solution.py:96
  (19 shorter events, 0.2 us)
Async XLA Ops:
  6.5 27.9 %copy-start = (bf16[1,4,64,896]{3,2,1,0:T(8,128)(2,1)S(1)}, bf16[1,4,64,896]{3,2,1,0:T(8,128)(2,1)}, u32[]{:S(2)}) copy-start(bf16[1,4,64,896]{3,2,1,0:T(8,128)(2,1)} %param.8) | copy-start | bytes 1376260
  6.5 74.9 %all-gather.2.cloned.1.call-start = ((), (), s32[]{:S(2)}) async-start(), calls=%async_computation.1 | async-start | bytes 8028160 | tf_op jit(solution)/shard_map/all_gather | solution.py:111
  9.2 20.7 %collective-permute-start.5 = (s32[3,16]{1,0:T(4,128)S(1)}, s32[3,16]{1,0:T(4,128)S(1)}, u32[]{:S(2)}, u32[]{:S(2)}) collective-permute-start(s32[3,16]{1,0:T(4,128)S(1)} %pad_add_fusion), channel_id=1, source_target_pairs={{0,6},{1,7},{2,0},{3,1},{4,2},{5,3},{6,4},{7,5},{8,14},{9,15},{10,... | collective-permute-start | bytes 584 | tf_op jit(solution)/shard_map/ppermute | solution.py:124
  14.3 15.6 %collective-permute-start.4 = (s32[3,16]{1,0:T(4,128)S(1)}, s32[3,16]{1,0:T(4,128)S(1)}, u32[]{:S(2)}, u32[]{:S(2)}) collective-permute-start(s32[3,16]{1,0:T(4,128)S(1)} %pad_add_fusion), channel_id=1, source_target_pairs={{0,5},{1,6},{2,7},{3,0},{4,1},{5,2},{6,3},{7,4},{8,13},{9,14},{10,... | collective-permute-start | bytes 584 | tf_op jit(solution)/shard_map/ppermute | solution.py:124
  14.7 15.2 %collective-permute-start.3 = (s32[3,16]{1,0:T(4,128)S(1)}, s32[3,16]{1,0:T(4,128)S(1)}, u32[]{:S(2)}, u32[]{:S(2)}) collective-permute-start(s32[3,16]{1,0:T(4,128)S(1)} %pad_add_fusion), channel_id=1, source_target_pairs={{0,4},{1,5},{2,6},{3,7},{4,0},{5,1},{6,2},{7,3},{8,12},{9,13},{10,... | collective-permute-start | bytes 584 | tf_op jit(solution)/shard_map/ppermute | solution.py:124
  18.2 11.7 %collective-permute-start.2 = (s32[3,16]{1,0:T(4,128)S(1)}, s32[3,16]{1,0:T(4,128)S(1)}, u32[]{:S(2)}, u32[]{:S(2)}) collective-permute-start(s32[3,16]{1,0:T(4,128)S(1)} %pad_add_fusion), channel_id=1, source_target_pairs={{0,3},{1,4},{2,5},{3,6},{4,7},{5,0},{6,1},{7,2},{8,11},{9,12},{10,... | collective-permute-start | bytes 584 | tf_op jit(solution)/shard_map/ppermute | solution.py:124
  18.2 6.3 %collective-permute-start = (s32[3,16]{1,0:T(4,128)S(1)}, s32[3,16]{1,0:T(4,128)S(1)}, u32[]{:S(2)}, u32[]{:S(2)}) collective-permute-start(s32[3,16]{1,0:T(4,128)S(1)} %pad_add_fusion), channel_id=1, source_target_pairs={{0,1},{1,2},{2,3},{3,4},{4,5},{5,6},{6,7},{7,0},{8,9},{9,10},{10,1... | collective-permute-start | bytes 584 | tf_op jit(solution)/shard_map/ppermute | solution.py:124
  24.5 5.4 %collective-permute-start.1 = (s32[3,16]{1,0:T(4,128)S(1)}, s32[3,16]{1,0:T(4,128)S(1)}, u32[]{:S(2)}, u32[]{:S(2)}) collective-permute-start(s32[3,16]{1,0:T(4,128)S(1)} %pad_add_fusion), channel_id=1, source_target_pairs={{0,2},{1,3},{2,4},{3,5},{4,6},{5,7},{6,0},{7,1},{8,10},{9,11},{10,... | collective-permute-start | bytes 584 | tf_op jit(solution)/shard_map/ppermute | solution.py:124
  29.9 3.6 %collective-permute-start.6 = (s32[3,16]{1,0:T(4,128)S(1)}, s32[3,16]{1,0:T(4,128)S(1)}, u32[]{:S(2)}, u32[]{:S(2)}) collective-permute-start(s32[3,16]{1,0:T(4,128)S(1)} %pad_add_fusion), channel_id=1, source_target_pairs={{0,7},{1,0},{2,1},{3,2},{4,3},{5,4},{6,5},{7,6},{8,15},{9,8},{10,9... | collective-permute-start | bytes 584 | tf_op jit(solution)/shard_map/ppermute | solution.py:124
  36.5 4.1 %copy-start.2 = (s32[1,8,2]{1,2,0:T(2,128)S(1)}, s32[1,8,2]{1,2,0:T(2,128)}, u32[]{:S(2)}) copy-start(s32[1,8,2]{1,2,0:T(2,128)} %param.9) | copy-start | bytes 196
  36.5 4.3 %copy-start.3 = (f32[896]{0:T(1024)S(1)}, f32[896]{0:T(1024)}, u32[]{:S(2)}) copy-start(f32[896]{0:T(1024)} %param.11) | copy-start | bytes 10756
  36.5 42.9 %all-to-all-start = ((bf16[8,2,64,896]{3,2,1,0:T(8,128)(2,1)}), bf16[8,2,64,896]{3,2,1,0:T(8,128)(2,1)S(1)}, u32[]{:S(2)}, u32[]{:S(2)}) async-start(bf16[8,2,64,896]{3,2,1,0:T(8,128)(2,1)} %bitcast.48), calls=%async_computation | async-start | bytes 3670016 | tf_op jit(solution)/shard_map/all_to_all | solution.py:132
  97.5 9.2 %copy-start.1 = (bf16[1024,896]{1,0:T(8,128)(2,1)S(1)}, bf16[1024,896]{1,0:T(8,128)(2,1)}, u32[]{:S(2)}) copy-start(bf16[1024,896]{1,0:T(8,128)(2,1)} %shard_map.73) | copy-start | bytes 5505028
Sparse Core Ops, SparseCore 0:
  8.9 49.8 all-gather.1

commit v6 on v3

--- a/solution.py
+++ b/solution.py
@@ -129,10 +129,11 @@
         got = got.reshape(n_seq * per_owner, NLEN, neighbour_input.shape[-1])
         chosen_raw = jnp.take(got, owners * per_owner + rank, axis=0, mode="clip")
         chosen = encode_blocks(chosen_raw, enc_gain, full_weights)
-        keys_t = jnp.einsum(
-            "ef,re->fr", kv_weight[0], chosen, preferred_element_type=jnp.float32
+        key_value = jnp.einsum(
+            "re,pef->prf", chosen, kv_weight, preferred_element_type=jnp.float32
         ).astype(jnp.bfloat16)
-        values = jnp.dot(chosen, kv_weight[1], preferred_element_type=jnp.float32).astype(jnp.bfloat16)
+        keys_t = key_value[0].T
+        values = key_value[1]
         return cross_attend(queries[0], keys_t, values)[None]
 
     return shards

time: 122 us -> 126 us (1.033)
  local copies, waits for them, and re-layouts: 7.29 us -> 17.2 us
  matrix products: 17.4 us -> 11.6 us
    transpose x0 -> x1, local copies, waits for them, and re-layouts: none -> 6.39 us  [shards(): keys_t = key_value[0].T]
    dot_general x2 -> x1, matrix products: 17.4 us -> 11.6 us  [shards(): jnp.einsum('re,pef->prf', chosen, kv_weight, preferred_element_type=jnp.f...]
    squeeze x0 -> x1, local copies, waits for them, and re-layouts: none -> 3.56 us  [shards(): values = key_value[1]]
where the time goes in v6:
time: 126 us
  waiting for transfers between devices  47.9 us (38%)
  Pallas kernels  24.3 us (19%)
  local copies, waits for them, and re-layouts  17.2 us (14%)
  between operations  13.5 us (11%)
  matrix products  11.6 us (9%)
  starting transfers between devices  11 us (9%)
    all_to_all x1, waiting for transfers between devices, shards(): got = lax.all_to_all(sent, 'seq', 0, 0, tiled=True)  40.6 us
    pallas_call x1, Pallas kernels, encode_blocks(): pl.pallas_call(_encoder_kernel, out_shape=jax.ShapeDtypeStruct(flat.shape...  16 us
    dot_general x1, matrix products, shards(): jnp.einsum('re,pef->prf', chosen, kv_weight, preferred_element_type=jnp.f...  11.6 us
    pallas_call x1, Pallas kernels, cross_attend(): pl.pallas_call(_cross_kernel, out_shape=jax.ShapeDtypeStruct(queries.shap...  8.25 us
    all_to_all x1, starting transfers between devices, shards(): asked = lax.all_to_all(asks, 'seq', 0, 0, tiled=True)  7.28 us
    all_to_all x1, waiting for transfers between devices, shards(): asked = lax.all_to_all(asks, 'seq', 0, 0, tiled=True)  6.58 us
    transpose x1, local copies, waits for them, and re-layouts, shards(): keys_t = key_value[0].T  6.39 us
    all_to_all x1, starting transfers between devices, shards(): got = lax.all_to_all(sent, 'seq', 0, 0, tiled=True)  3.72 us
  transfers between devices with their start and end apart: 3, of which 2 were waited for; matrix products, arithmetic and copies ran while one was open for 6% of the time, Pallas kernels for 0%

profile of v6, /device:TPU:0, one launch (start us, length us, event | category | flops | bytes accessed | tf_op | source)
XLA Modules:
  0.0 125.9 jit_solution(343281512956350697)
XLA Ops:
  6.5 0.0 copy-start
  6.5 0.0 all-gather.2.cloned.1.call-start
  6.5 0.7 all-gather.2.cloned.1.call-update
  7.3 0.8 copy.26
  8.0 0.1 eq.36
  8.1 0.1 stack_reshape.6
  8.2 0.8 copy.27
  8.9 0.1 stack_reshape.7
  9.0 0.2 convert_reduce_fusion
  9.2 0.6 broadcast_in_dim.32
  9.8 7.3 %all-to-all-start = ((s32[8,3,16]{2,1,0:T(4,128)}), s32[8,3,16]{2,1,0:T(4,128)S(1)}, u32[]{:S(2)}, u32[]{:S(2)}) async-start(s32[8,3,16]{2,1,0:T(4,128)} %broadcast_in_dim.32), calls=%async_computation | async-start | bytes 32768 | tf_op jit(solution)/shard_map/all_to_all | solution.py:122
  17.1 6.6 %all-to-all-done = s32[8,3,16]{2,1,0:T(4,128)S(1)} async-done(((s32[8,3,16]{2,1,0:T(4,128)}), s32[8,3,16]{2,1,0:T(4,128)S(1)}, u32[]{:S(2)}, u32[]{:S(2)}) %all-to-all-start) | async-done | bytes 1568 | tf_op jit(solution)/shard_map/all_to_all | solution.py:122
  23.7 0.1 select_reduce_fusion
  23.9 0.1 copy.32
  23.9 0.1 reshape.43
  24.0 0.0 copy-done
  24.0 2.0 %gather_fusion = bf16[16,64,896]{2,1,0:T(8,128)(2,1)} fusion(bf16[4,64,896]{2,1,0:T(8,128)(2,1)S(1)} %bitcast.34, s32[1024]{0:T(1024)S(1)} %pad_clamp_fusion.1), kind=kCustom, calls=%fused_computation | custom fusion | bytes 3670080 | tf_op jit(solution)/shard_map/jit(_take)/gather | solution.py:126
  26.0 0.0 copy-start.1
  26.0 0.0 copy-start.2
  26.0 3.7 %all-to-all-start.1 = ((bf16[8,2,64,896]{3,2,1,0:T(8,128)(2,1)}), bf16[8,2,64,896]{3,2,1,0:T(8,128)(2,1)S(1)}, u32[]{:S(2)}, u32[]{:S(2)}) async-start(bf16[8,2,64,896]{3,2,1,0:T(8,128)(2,1)} %bitcast.36), calls=%async_computation.1 | async-start | bytes 3670016 | tf_op jit(solution)/shard_map/all_to_all | solution.py:128
  29.8 0.0 copy-done.1
  29.8 0.1 copy.33
  29.9 0.1 mul.14
  30.0 0.0 copy-done.2
  30.0 0.6 reshape.40.gain_ref
  30.6 40.6 %all-to-all-done.1 = bf16[8,2,64,896]{3,2,1,0:T(8,128)(2,1)S(1)} async-done(((bf16[8,2,64,896]{3,2,1,0:T(8,128)(2,1)}), bf16[8,2,64,896]{3,2,1,0:T(8,128)(2,1)S(1)}, u32[]{:S(2)}, u32[]{:S(2)}) %all-to-all-start.1) | async-done | bytes 1835040 | tf_op jit(solution)/shard_map/all_to_all | solution.py:128
  71.2 2.0 %gather_fusion.1 = bf16[16,64,896]{2,1,0:T(8,128)(2,1)} fusion(bf16[16,64,896]{2,1,0:T(8,128)(2,1)S(1)} %bitcast.35, s32[1024]{0:T(1024)S(1)} %pad_clamp_fusion), kind=kCustom, calls=%fused_computation.1 | custom fusion | bytes 3670080 | tf_op jit(solution)/shard_map/jit(_take)/gather | solution.py:130
  73.2 0.0 all-gather.2.cloned.1.call-done.w_ref
  73.2 16.0 %shard_map.73 = bf16[1024,896]{1,0:T(8,128)(2,1)} custom-call(bf16[1024,896]{1,0:T(8,128)(2,1)} %bitcast.37, f32[1,896]{1,0:T(1,128)} %reshape.40.gain_ref, bf16[4,896,896]{2,1,0:T(8,128)(2,1)} %all-gather.2.cloned.1.call-done.w_ref), custom_call_target="tpu_custom_call" | custom-call | tf_op jit(solution)/shard_map/pallas_call | solution.py:58
  89.2 11.6 %convert_bitcast_fusion = bf16[2,1024,2048]{2,1,0:T(8,128)(2,1)S(1)} fusion(bf16[2,896,2048]{2,1,0:T(8,128)(2,1)} %param.13, bf16[1024,896]{1,0:T(8,128)(2,1)} %shard_map.73), kind=kOutput, calls=%fused_computation.2 | convolution fusion | flops 7520387072 | bytes 17563648 | tf_op jit(solution)/shard_map/re,pef->prf/dot_general | solution.py:132
  100.8 3.6 %slice_bitcast_fusion = (bf16[1024,2048]{1,0:T(8,128)(2,1)}, bf16[2048,1024]{0,1:T(8,128)(2,1)}) fusion(bf16[2,1024,2048]{2,1,0:T(8,128)(2,1)S(1)} %convert_bitcast_fusion), kind=kLoop, calls=%fused_computation.3 | loop fusion | bytes 16777216 | tf_op jit(solution)/shard_map/squeeze | solution.py:136
  104.4 6.4 %copy.34.kt_ref = bf16[2048,1024]{1,0:T(8,128)(2,1)} copy(bf16[2048,1024]{0,1:T(8,128)(2,1)} %get-tuple-element.6) | data formatting | bytes 8388608 | tf_op jit(solution)/shard_map/transpose | solution.py:135
  110.8 8.2 %shard_map.74 = bf16[512,2048]{1,0:T(8,128)(2,1)} custom-call(bf16[512,2048]{1,0:T(8,128)(2,1)} %bitcast.38, bf16[2048,1024]{1,0:T(8,128)(2,1)} %copy.34.kt_ref, bf16[1024,2048]{1,0:T(8,128)(2,1)} %get-tuple-element.5.v_ref), custom_call_target="tpu_custom_call" | custom-call | tf_op jit(solution)/shard_map/pallas_call | solution.py:96
  (7 shorter events, 0.1 us)
Async XLA Ops:
  6.5 17.5 %copy-start = (bf16[1,4,64,896]{3,2,1,0:T(8,128)(2,1)S(1)}, bf16[1,4,64,896]{3,2,1,0:T(8,128)(2,1)}, u32[]{:S(2)}) copy-start(bf16[1,4,64,896]{3,2,1,0:T(8,128)(2,1)} %param.8) | copy-start | bytes 1376260
  6.5 66.6 %all-gather.2.cloned.1.call-start = ((), (), s32[]{:S(2)}) async-start(), calls=%async_computation.2 | async-start | bytes 8028160 | tf_op jit(solution)/shard_map/all_gather | solution.py:111
  9.8 13.9 %all-to-all-start = ((s32[8,3,16]{2,1,0:T(4,128)}), s32[8,3,16]{2,1,0:T(4,128)S(1)}, u32[]{:S(2)}, u32[]{:S(2)}) async-start(s32[8,3,16]{2,1,0:T(4,128)} %broadcast_in_dim.32), calls=%async_computation | async-start | bytes 32768 | tf_op jit(solution)/shard_map/all_to_all | solution.py:122
  26.0 3.7 %copy-start.1 = (s32[1,8,2]{1,2,0:T(2,128)S(1)}, s32[1,8,2]{1,2,0:T(2,128)}, u32[]{:S(2)}) copy-start(s32[1,8,2]{1,2,0:T(2,128)} %param.9) | copy-start | bytes 196
  26.0 3.9 %copy-start.2 = (f32[896]{0:T(1024)S(1)}, f32[896]{0:T(1024)}, u32[]{:S(2)}) copy-start(f32[896]{0:T(1024)} %param.11) | copy-start | bytes 10756
  26.0 45.1 %all-to-all-start.1 = ((bf16[8,2,64,896]{3,2,1,0:T(8,128)(2,1)}), bf16[8,2,64,896]{3,2,1,0:T(8,128)(2,1)S(1)}, u32[]{:S(2)}, u32[]{:S(2)}) async-start(bf16[8,2,64,896]{3,2,1,0:T(8,128)(2,1)} %bitcast.36), calls=%async_computation.1 | async-start | bytes 3670016 | tf_op jit(solution)/shard_map/all_to_all | solution.py:128
Sparse Core Ops, SparseCore 0:
  8.9 49.8 all-gather.1

commit v7 on v3

--- a/solution.py
+++ b/solution.py
@@ -106,9 +106,27 @@
     )(queries, keys_t, values)
 
 
-def make_shards(n_seq):
+def gather_weights(shard, n_dp):
+    n_x = n_dp // 2
+    place = lax.axis_index("dp")
+    x, core = place // 2, place % 2
+    pieces = [shard]
+    for shift in range(1, n_x):
+        ring = [(src, ((src // 2 + shift) % n_x) * 2 + src % 2) for src in range(n_dp)]
+        pieces.append(lax.ppermute(shard, "dp", ring))
+    mine = jnp.stack(pieces)
+    other = lax.ppermute(mine, "dp", [(src, src ^ 1) for src in range(n_dp)])
+    order = (x - jnp.arange(n_x)) % n_x
+    mine = jnp.take(mine, order, axis=0)
+    other = jnp.take(other, order, axis=0)
+    both = jnp.where(core == 0, jnp.stack([mine, other], 1), jnp.stack([other, mine], 1))
+    count, rows, width = shard.shape
+    return both.transpose(2, 0, 1, 3, 4).reshape(count, n_dp * rows, width)
+
+
+def make_shards(n_seq, n_dp):
     def shards(queries, neighbour_input, owner_list, block_list, enc_gain, enc_attn, kv_weight):
-        full_weights = lax.all_gather(enc_attn, "dp", axis=1, tiled=True)
+        full_weights = gather_weights(enc_attn, n_dp)
         me = lax.axis_index("seq")
         owners = owner_list.reshape(-1)
         indices = block_list.reshape(-1)
@@ -140,7 +158,7 @@
 
 def solution(mesh):
     return jax.shard_map(
-        make_shards(mesh.shape["seq"]),
+        make_shards(mesh.shape["seq"], mesh.shape["dp"]),
         mesh=mesh,
         in_specs=(
             P("dp", "seq", None),

time: 122 us -> 122 us (level)
  between operations: 13.5 us -> 0.1 us
  local copies, waits for them, and re-layouts: 7.29 us -> 19.6 us
  waiting for transfers between devices: 47.9 us -> 38.6 us
  other arithmetic: 0.37 us -> 9.09 us
  starting transfers between devices: 11 us -> 12.4 us
    all_to_all x1, waiting for transfers between devices: 40.6 us -> 17.5 us  [shards(): got = lax.all_to_all(sent, 'seq', 0, 0, tiled=True)]
    ppermute x0 -> x2, waiting for transfers between devices: none -> 14.5 us  [the longest x1 14.5 us: gather_weights(): pieces.append(lax.ppermute(shard, 'dp', ring))]
    gather x0 -> x2, local copies, waits for them, and re-layouts: none -> 9.02 us  [the longest x1 4.54 us: gather_weights(): mine = jnp.take(mine, order, axis=0)]
    another operation x0 -> x2, other arithmetic: none -> 7.51 us  [the longest x1 3.9 us: gather_weights(): mine = jnp.stack(pieces)]
    transpose x0 -> x1, local copies, waits for them, and re-layouts: none -> 3.32 us  [gather_weights(): return both.transpose(2, 0, 1, 3, 4).reshape(count, n_dp * rows, width)]
    ppermute x0 -> x2, starting transfers between devices: none -> 2.94 us  [the longest x1 2.94 us: gather_weights(): pieces.append(lax.ppermute(shard, 'dp', ring))]
    all_to_all x1, starting transfers between devices: 7.28 us -> 5.83 us  [shards(): asked = lax.all_to_all(asks, 'seq', 0, 0, tiled=True)]
  transfers between devices with their start and end apart: 3 -> 4, of which waited for: 2 -> 3; matrix products, arithmetic and copies ran while one was open for 6% -> 13% of each run, Pallas kernels for 0% -> 0%
where the time goes in v7:
time: 122 us; the launch traced here: 121 us
  waiting for transfers between devices  38.6 us (32%)
  Pallas kernels  24.3 us (20%)
  local copies, waits for them, and re-layouts  19.6 us (16%)
  matrix products  17.3 us (14%)
  starting transfers between devices  12.4 us (10%)
  other arithmetic  9.09 us (7%)
    all_to_all x1, waiting for transfers between devices, shards(): got = lax.all_to_all(sent, 'seq', 0, 0, tiled=True)  17.5 us
    pallas_call x1, Pallas kernels, encode_blocks(): pl.pallas_call(_encoder_kernel, out_shape=jax.ShapeDtypeStruct(flat.shape...  16 us
    ppermute x1, waiting for transfers between devices, gather_weights(): pieces.append(lax.ppermute(shard, 'dp', ring))  14.5 us
    dot_general x1, matrix products, shards(): jnp.einsum('ef,re->fr', kv_weight[0], chosen, preferred_element_type=jnp....  9.22 us
    pallas_call x1, Pallas kernels, cross_attend(): pl.pallas_call(_cross_kernel, out_shape=jax.ShapeDtypeStruct(queries.shap...  8.25 us
    dot_general x1, matrix products, shards(): jnp.dot(chosen, kv_weight[1], preferred_element_type=jnp.float32)  8.07 us
    all_to_all x1, waiting for transfers between devices, shards(): asked = lax.all_to_all(asks, 'seq', 0, 0, tiled=True)  6.58 us
    all_to_all x1, starting transfers between devices, shards(): asked = lax.all_to_all(asks, 'seq', 0, 0, tiled=True)  5.83 us
  transfers between devices with their start and end apart: 4, of which 3 were waited for; matrix products, arithmetic and copies ran while one was open for 13% of the time, Pallas kernels for 0%

profile of v7, /device:TPU:0, one launch (start us, length us, event | category | flops | bytes accessed | tf_op | source)
XLA Modules:
  0.0 121.3 jit_solution(14595910248741154360)
XLA Ops:
  0.0 0.0 copy-start
  0.0 2.9 %collective-permute-start = (bf16[4,224,896]{2,1,0:T(8,128)(2,1)}, bf16[4,224,896]{2,1,0:T(8,128)(2,1)}, u32[]{:S(2)}, u32[]{:S(2)}) collective-permute-start(bf16[4,224,896]{2,1,0:T(8,128)(2,1)} %param.14), channel_id=1, source_target_pairs={{0,16},{8,24},{16,0},{24,8},{1,17},{9,25},{17,1},{25,9},{2,18},{10... | collective-permute-start | bytes 4816904 | tf_op jit(solution)/shard_map/ppermute | solution.py:116
  2.9 0.8 copy.29
  3.7 0.1 eq.43
  3.8 0.1 stack_reshape.6
  3.9 0.8 copy.30
  4.6 0.1 stack_reshape.7
  4.7 0.2 convert_reduce_fusion
  4.9 0.6 broadcast_in_dim.41
  5.5 5.8 %all-to-all-start = ((s32[8,3,16]{2,1,0:T(4,128)}), s32[8,3,16]{2,1,0:T(4,128)S(1)}, u32[]{:S(2)}, u32[]{:S(2)}) async-start(s32[8,3,16]{2,1,0:T(4,128)} %broadcast_in_dim.41), calls=%async_computation | async-start | bytes 32768 | tf_op jit(solution)/shard_map/all_to_all | solution.py:140
  11.3 6.6 %all-to-all-done = s32[8,3,16]{2,1,0:T(4,128)S(1)} async-done(((s32[8,3,16]{2,1,0:T(4,128)}), s32[8,3,16]{2,1,0:T(4,128)S(1)}, u32[]{:S(2)}, u32[]{:S(2)}) %all-to-all-start) | async-done | bytes 1568 | tf_op jit(solution)/shard_map/all_to_all | solution.py:140
  17.9 0.1 select_reduce_fusion
  18.1 0.1 copy.35
  18.2 0.1 reshape.68
  18.3 0.0 copy-done
  18.3 2.0 %gather_fusion = bf16[16,64,896]{2,1,0:T(8,128)(2,1)} fusion(bf16[4,64,896]{2,1,0:T(8,128)(2,1)S(1)} %bitcast.41, s32[1024]{0:T(1024)S(1)} %pad_clamp_fusion.2), kind=kCustom, calls=%fused_computation.2 | custom fusion | bytes 3670080 | tf_op jit(solution)/shard_map/jit(_take)/gather | solution.py:144
  20.3 3.6 %all-to-all-start.1 = ((bf16[8,2,64,896]{3,2,1,0:T(8,128)(2,1)}), bf16[8,2,64,896]{3,2,1,0:T(8,128)(2,1)S(1)}, u32[]{:S(2)}, u32[]{:S(2)}) async-start(bf16[8,2,64,896]{3,2,1,0:T(8,128)(2,1)} %bitcast.44), calls=%async_computation.1 | async-start | bytes 3670016 | tf_op jit(solution)/shard_map/all_to_all | solution.py:146
  23.9 14.5 %collective-permute-done = bf16[4,224,896]{2,1,0:T(8,128)(2,1)} collective-permute-done((bf16[4,224,896]{2,1,0:T(8,128)(2,1)}, bf16[4,224,896]{2,1,0:T(8,128)(2,1)}, u32[]{:S(2)}, u32[]{:S(2)}) %collective-permute-start) | collective-permute-done | bytes 1605664 | tf_op jit(solution)/shard_map/ppermute | solution.py:116
  38.4 0.0 copy-start.2
  38.4 0.0 copy-start.3
  38.4 3.9 %pad_maximum_fusion = bf16[2,4,224,896]{3,2,1,0:T(8,128)(2,1)} fusion(bf16[1,4,224,896]{3,2,1,0:T(8,128)(2,1)} %bitcast.12, bf16[1,4,224,896]{3,2,1,0:T(8,128)(2,1)} %bitcast.47), kind=kLoop, calls=%fused_computation.12 | loop fusion | flops 1605632 | bytes 6422528 | tf_op jit(solution)/shard_map/stack | solution.py:117
  42.3 0.0 collective-permute-start.1
  42.3 0.0 copy-done.2
  42.3 0.1 copy.36
  42.3 0.1 mul.14
  42.4 0.0 copy-done.3
  42.4 0.6 reshape.48.gain_ref
  43.1 4.5 %gather_fusion.2 = bf16[2,4,224,896]{3,2,1,0:T(8,128)(2,1)} fusion(bf16[2,4,224,896]{3,2,1,0:T(8,128)(2,1)} %pad_maximum_fusion, s32[1024]{0:T(1024)S(1)} %pad_clamp_fusion), kind=kCustom, calls=%fused_computation.clone | custom fusion | bytes 6422536 | tf_op jit(solution)/shard_map/jit(_take)/gather | solution.py:120
  47.6 17.5 %all-to-all-done.1 = bf16[8,2,64,896]{3,2,1,0:T(8,128)(2,1)S(1)} async-done(((bf16[8,2,64,896]{3,2,1,0:T(8,128)(2,1)}), bf16[8,2,64,896]{3,2,1,0:T(8,128)(2,1)S(1)}, u32[]{:S(2)}, u32[]{:S(2)}) %all-to-all-start.1) | async-done | bytes 1835040 | tf_op jit(solution)/shard_map/all_to_all | solution.py:146
  65.1 2.0 %gather_fusion.1 = bf16[16,64,896]{2,1,0:T(8,128)(2,1)} fusion(bf16[16,64,896]{2,1,0:T(8,128)(2,1)S(1)} %bitcast.43, s32[1024]{0:T(1024)S(1)} %pad_clamp_fusion.1), kind=kCustom, calls=%fused_computation.3 | custom fusion | bytes 3670080 | tf_op jit(solution)/shard_map/jit(_take)/gather | solution.py:148
  67.1 0.0 collective-permute-done.1
  67.1 4.5 %gather_fusion.3 = bf16[2,4,224,896]{3,2,1,0:T(8,128)(2,1)} fusion(bf16[2,4,224,896]{3,2,1,0:T(8,128)(2,1)} %collective-permute-done.1, s32[1024]{0:T(1024)S(1)} %pad_clamp_fusion), kind=kCustom, calls=%fused_computation.1.clone | custom fusion | bytes 6422536 | tf_op jit(solution)/shard_map/jit(_take)/gather | solution.py:121
  71.6 3.6 %select_bitcast_fusion.1 = (bf16[2,1,4,224,896]{4,3,2,0,1:T(8,128)(2,1)S(1)}, bf16[2,1,4,224,896]{4,3,2,0,1:T(8,128)(2,1)S(1)}) fusion(bf16[2,4,224,896]{3,2,1,0:T(8,128)(2,1)} %gather_fusion.2, pred[2]{0:T(512)(128)(4,1)S(1)} %compare_and_fusion, bf16[2,4,224,896]{3,2,1,0:T(8,128)(2,1)} %gather_fusion.3), kind=kLoop, calls=%fused_computation.14 | loop fusion | flops 3211264 | bytes 12845058 | tf_op jit(solution)/shard_map/stack | solution.py:122
  75.2 1.2 fusion
  76.4 3.3 %copy.37 = bf16[4,2,2,224,896]{4,3,2,1,0:T(8,128)(2,1)} copy(bf16[4,2,2,224,896]{4,3,0,1,2:T(8,128)(2,1)S(1)} %fusion) | data formatting | bytes 12845056 | tf_op jit(solution)/shard_map/transpose | solution.py:124
  79.7 16.0 %shard_map.73 = bf16[1024,896]{1,0:T(8,128)(2,1)} custom-call(bf16[1024,896]{1,0:T(8,128)(2,1)} %bitcast.45, f32[1,896]{1,0:T(1,128)} %reshape.48.gain_ref, bf16[4,896,896]{2,1,0:T(8,128)(2,1)} %bitcast.42), custom_call_target="tpu_custom_call" | custom-call | tf_op jit(solution)/shard_map/pallas_call | solution.py:58
  95.7 0.0 copy-start.1
  95.7 9.2 %convert_bitcast_fusion.kt_ref = bf16[2048,1024]{1,0:T(8,128)(2,1)} fusion(bf16[1024,896]{1,0:T(8,128)(2,1)} %shard_map.73, bf16[2,896,2048]{2,1,0:T(8,128)(2,1)} %param.15), kind=kOutput, calls=%fused_computation.6 | convolution fusion | flops 3760193536 | bytes 9699328 | tf_op jit(solution)/shard_map/ef,re->fr/dot_general | solution.py:150
  105.0 0.0 copy-done.1
  105.0 8.1 %convolution_convert_fusion.v_ref = bf16[1024,2048]{1,0:T(8,128)(2,1)} fusion(bf16[1024,896]{1,0:T(8,128)(2,1)S(1)} %copy-done.1, bf16[2,896,2048]{2,1,0:T(8,128)(2,1)} %param.15), kind=kOutput, calls=%fused_computation.7 | convolution fusion | flops 3760193536 | bytes 9699328 | tf_op jit(solution)/shard_map/dot_general | solution.py:153
  113.0 8.2 %shard_map.74 = bf16[512,2048]{1,0:T(8,128)(2,1)} custom-call(bf16[512,2048]{1,0:T(8,128)(2,1)} %bitcast.46, bf16[2048,1024]{1,0:T(8,128)(2,1)} %convert_bitcast_fusion.kt_ref, bf16[1024,2048]{1,0:T(8,128)(2,1)} %convolution_convert_fusion.v_ref), custom_call_target="tpu_custom_call" | custom-call | tf_op jit(solution)/shard_map/pallas_call | solution.py:96
  (10 shorter events, 0.1 us)
Async XLA Ops:
  0.0 18.3 %copy-start = (bf16[1,4,64,896]{3,2,1,0:T(8,128)(2,1)S(1)}, bf16[1,4,64,896]{3,2,1,0:T(8,128)(2,1)}, u32[]{:S(2)}) copy-start(bf16[1,4,64,896]{3,2,1,0:T(8,128)(2,1)} %param.10) | copy-start | bytes 1376260
  0.0 38.3 %collective-permute-start = (bf16[4,224,896]{2,1,0:T(8,128)(2,1)}, bf16[4,224,896]{2,1,0:T(8,128)(2,1)}, u32[]{:S(2)}, u32[]{:S(2)}) collective-permute-start(bf16[4,224,896]{2,1,0:T(8,128)(2,1)} %param.14), channel_id=1, source_target_pairs={{0,16},{8,24},{16,0},{24,8},{1,17},{9,25},{17,1},{25,9},{2,18},{10... | collective-permute-start | bytes 4816904 | tf_op jit(solution)/shard_map/ppermute | solution.py:116
  5.5 12.4 %all-to-all-start = ((s32[8,3,16]{2,1,0:T(4,128)}), s32[8,3,16]{2,1,0:T(4,128)S(1)}, u32[]{:S(2)}, u32[]{:S(2)}) async-start(s32[8,3,16]{2,1,0:T(4,128)} %broadcast_in_dim.41), calls=%async_computation | async-start | bytes 32768 | tf_op jit(solution)/shard_map/all_to_all | solution.py:140
  20.3 44.9 %all-to-all-start.1 = ((bf16[8,2,64,896]{3,2,1,0:T(8,128)(2,1)}), bf16[8,2,64,896]{3,2,1,0:T(8,128)(2,1)S(1)}, u32[]{:S(2)}, u32[]{:S(2)}) async-start(bf16[8,2,64,896]{3,2,1,0:T(8,128)(2,1)} %bitcast.44), calls=%async_computation.1 | async-start | bytes 3670016 | tf_op jit(solution)/shard_map/all_to_all | solution.py:146
  38.4 3.9 %copy-start.2 = (s32[1,8,2]{1,2,0:T(2,128)S(1)}, s32[1,8,2]{1,2,0:T(2,128)}, u32[]{:S(2)}) copy-start(s32[1,8,2]{1,2,0:T(2,128)} %param.11) | copy-start | bytes 196
  38.4 4.1 %copy-start.3 = (f32[896]{0:T(1024)S(1)}, f32[896]{0:T(1024)}, u32[]{:S(2)}) copy-start(f32[896]{0:T(1024)} %param.13) | copy-start | bytes 10756
  42.3 24.9 %collective-permute-start.1 = (bf16[2,4,224,896]{3,2,1,0:T(8,128)(2,1)}, bf16[2,4,224,896]{3,2,1,0:T(8,128)(2,1)}, u32[]{:S(2)}, u32[]{:S(2)}) collective-permute-start(bf16[2,4,224,896]{3,2,1,0:T(8,128)(2,1)} %pad_maximum_fusion), channel_id=1, source_target_pairs={{0,8},{8,0},{16,24},{24,16},{1,9},{9,1},{17,25},{25,17},{2,10},{10... | collective-permute-start | bytes 9633800 | tf_op jit(solution)/shard_map/ppermute | solution.py:118
  95.7 9.2 %copy-start.1 = (bf16[1024,896]{1,0:T(8,128)(2,1)S(1)}, bf16[1024,896]{1,0:T(8,128)(2,1)}, u32[]{:S(2)}) copy-start(bf16[1024,896]{1,0:T(8,128)(2,1)} %shard_map.73) | copy-start | bytes 5505028

commit v8 on v7

--- a/solution.py
+++ b/solution.py
@@ -110,18 +110,17 @@
     n_x = n_dp // 2
     place = lax.axis_index("dp")
     x, core = place // 2, place % 2
-    pieces = [shard]
+    pieces = [(shard, place)]
     for shift in range(1, n_x):
         ring = [(src, ((src // 2 + shift) % n_x) * 2 + src % 2) for src in range(n_dp)]
-        pieces.append(lax.ppermute(shard, "dp", ring))
-    mine = jnp.stack(pieces)
-    other = lax.ppermute(mine, "dp", [(src, src ^ 1) for src in range(n_dp)])
-    order = (x - jnp.arange(n_x)) % n_x
-    mine = jnp.take(mine, order, axis=0)
-    other = jnp.take(other, order, axis=0)
-    both = jnp.where(core == 0, jnp.stack([mine, other], 1), jnp.stack([other, mine], 1))
+        pieces.append((lax.ppermute(shard, "dp", ring), ((x - shift) % n_x) * 2 + core))
+    swap = [(src, src ^ 1) for src in range(n_dp)]
+    pieces += [(lax.ppermute(piece, "dp", swap), owner ^ 1) for piece, owner in pieces]
     count, rows, width = shard.shape
-    return both.transpose(2, 0, 1, 3, 4).reshape(count, n_dp * rows, width)
+    full = jnp.zeros((count, n_dp * rows, width), shard.dtype)
+    for piece, owner in pieces:
+        full = lax.dynamic_update_slice(full, piece, (0, owner * rows, 0))
+    return full
 
 
 def make_shards(n_seq, n_dp):

time: 122 us -> 108 us (0.89)
  other arithmetic: 9.09 us -> 0.37 us
  waiting for transfers between devices: 38.6 us -> 33 us
    all_to_all x1, waiting for transfers between devices: 17.5 us -> 3.65 us  [shards(): got = lax.all_to_all(sent, 'seq', 0, 0, tiled=True)]
    ppermute x2 -> x3, waiting for transfers between devices: 14.5 us -> 24.2 us  [the longest x1 24.2 us: gather_weights(): lax.ppermute(shard, 'dp', ring)]
    dynamic_update_slice x0 -> x4, local copies, waits for them, and re-layouts: none -> 9.45 us  [gather_weights(): full = lax.dynamic_update_slice(full, piece, (0, owner * rows, 0))]
    gather x2 -> x0, local copies, waits for them, and re-layouts: 9.02 us -> none  [the longest x1 4.54 us: gather_weights(): mine = jnp.take(mine, order, axis=0)]
    another operation x2 -> x0, other arithmetic: 7.51 us -> none  [the longest x1 3.9 us: gather_weights(): mine = jnp.stack(pieces)]
    transpose x1 -> x0, local copies, waits for them, and re-layouts: 3.32 us -> none  [gather_weights(): return both.transpose(2, 0, 1, 3, 4).reshape(count, n_dp * rows, width)]
    broadcast_in_dim x0 -> x1, local copies, waits for them, and re-layouts: none -> 3.17 us  [gather_weights(): full = jnp.zeros((count, n_dp * rows, width), shard.dtype)]
    all_to_all x1, waiting for transfers between devices: 6.58 us -> 5.08 us  [shards(): asked = lax.all_to_all(asks, 'seq', 0, 0, tiled=True)]
  transfers between devices with their start and end apart: 4 -> 5, of which waited for: 3 -> 3; matrix products, arithmetic and copies ran while one was open for 13% -> 15% of each run, Pallas kernels for 0% -> 0%
where the time goes in v8:
time: 108 us; the launch traced here: 107 us
  waiting for transfers between devices  33 us (31%)
  Pallas kernels  24.3 us (22%)
  local copies, waits for them, and re-layouts  20 us (19%)
  matrix products  17.3 us (16%)
  starting transfers between devices  12.4 us (11%)
    ppermute x1, waiting for transfers between devices, gather_weights(): lax.ppermute(shard, 'dp', ring)  24.2 us
    pallas_call x1, Pallas kernels, encode_blocks(): pl.pallas_call(_encoder_kernel, out_shape=jax.ShapeDtypeStruct(flat.shape...  16 us
    dynamic_update_slice x4, local copies, waits for them, and re-layouts, gather_weights(): full = lax.dynamic_update_slice(full, piece, (0, owner * rows, 0))  9.45 us
    dot_general x1, matrix products, shards(): jnp.einsum('ef,re->fr', kv_weight[0], chosen, preferred_element_type=jnp....  9.22 us
    pallas_call x1, Pallas kernels, cross_attend(): pl.pallas_call(_cross_kernel, out_shape=jax.ShapeDtypeStruct(queries.shap...  8.25 us
    dot_general x1, matrix products, shards(): jnp.dot(chosen, kv_weight[1], preferred_element_type=jnp.float32)  8.08 us
    all_to_all x1, starting transfers between devices, shards(): asked = lax.all_to_all(asks, 'seq', 0, 0, tiled=True)  7.28 us
    all_to_all x1, waiting for transfers between devices, shards(): asked = lax.all_to_all(asks, 'seq', 0, 0, tiled=True)  5.08 us
  transfers between devices with their start and end apart: 5, of which 3 were waited for; matrix products, arithmetic and copies ran while one was open for 15% of the time, Pallas kernels for 0%

profile of v8, /device:TPU:0, one launch (start us, length us, event | category | flops | bytes accessed | tf_op | source)
XLA Modules:
  0.0 107.4 jit_solution(15724862029557321123)
XLA Ops:
  0.0 0.0 copy-start
  0.0 0.8 copy.26
  0.8 0.1 eq.39
  0.9 0.1 stack_reshape.6
  1.0 0.2 convert_reduce_fusion
  1.2 0.8 copy.27
  1.9 0.1 stack_reshape.7
  2.0 0.6 broadcast_in_dim.35
  2.6 7.3 %all-to-all-start = ((s32[8,3,16]{2,1,0:T(4,128)}), s32[8,3,16]{2,1,0:T(4,128)S(1)}, u32[]{:S(2)}, u32[]{:S(2)}) async-start(s32[8,3,16]{2,1,0:T(4,128)} %broadcast_in_dim.35), calls=%async_computation | async-start | bytes 32768 | tf_op jit(solution)/shard_map/all_to_all | solution.py:139
  9.9 1.5 %collective-permute-start = (bf16[4,224,896]{2,1,0:T(8,128)(2,1)}, bf16[4,224,896]{2,1,0:T(8,128)(2,1)}, u32[]{:S(2)}, u32[]{:S(2)}) collective-permute-start(bf16[4,224,896]{2,1,0:T(8,128)(2,1)} %param.12), channel_id=1, source_target_pairs={{0,16},{8,24},{16,0},{24,8},{1,17},{9,25},{17,1},{25,9},{2,18},{10... | collective-permute-start | bytes 4816904 | tf_op jit(solution)/shard_map/ppermute | solution.py:116
  11.4 5.1 %all-to-all-done = s32[8,3,16]{2,1,0:T(4,128)S(1)} async-done(((s32[8,3,16]{2,1,0:T(4,128)}), s32[8,3,16]{2,1,0:T(4,128)S(1)}, u32[]{:S(2)}, u32[]{:S(2)}) %all-to-all-start) | async-done | bytes 1568 | tf_op jit(solution)/shard_map/all_to_all | solution.py:139
  16.5 0.1 select_reduce_fusion
  16.7 0.1 copy.32
  16.7 0.1 reshape.43
  16.8 0.0 copy-done
  16.8 0.0 copy-start.3
  16.9 0.0 copy-start.4
  16.9 2.0 %gather_fusion = bf16[16,64,896]{2,1,0:T(8,128)(2,1)} fusion(bf16[4,64,896]{2,1,0:T(8,128)(2,1)S(1)} %bitcast.32, s32[1024]{0:T(1024)S(1)} %pad_clamp_fusion.1), kind=kCustom, calls=%fused_computation | custom fusion | bytes 3670080 | tf_op jit(solution)/shard_map/jit(_take)/gather | solution.py:143
  18.9 3.6 %all-to-all-start.1 = ((bf16[8,2,64,896]{3,2,1,0:T(8,128)(2,1)}), bf16[8,2,64,896]{3,2,1,0:T(8,128)(2,1)S(1)}, u32[]{:S(2)}, u32[]{:S(2)}) async-start(bf16[8,2,64,896]{3,2,1,0:T(8,128)(2,1)} %bitcast.34), calls=%async_computation.1 | async-start | bytes 3670016 | tf_op jit(solution)/shard_map/all_to_all | solution.py:145
  22.5 0.1 collective-permute-start.1
  22.5 24.2 %collective-permute-done = bf16[4,224,896]{2,1,0:T(8,128)(2,1)} collective-permute-done((bf16[4,224,896]{2,1,0:T(8,128)(2,1)}, bf16[4,224,896]{2,1,0:T(8,128)(2,1)}, u32[]{:S(2)}, u32[]{:S(2)}) %collective-permute-start) | collective-permute-done | bytes 1605664 | tf_op jit(solution)/shard_map/ppermute | solution.py:116
  46.8 0.0 collective-permute-start.2
  46.8 0.0 copy-done.3
  46.8 0.1 copy.33
  46.9 0.1 mul.29
  47.0 0.0 copy-done.4
  47.0 0.6 reshape.40.gain_ref
  47.6 0.0 copy-start.2
  47.6 3.2 %broadcast_in_dim.40 = bf16[4,896,896]{2,1,0:T(8,128)(2,1)} broadcast(bf16[]{:T(256)} %constant.40.clone.1), dimensions={} | broadcast | bytes 6422530 | tf_op jit(solution)/shard_map/broadcast_in_dim | solution.py:120
  50.7 0.0 copy-done.2
  50.7 1.3 %constant_dynamic-update-slice_fusion.3 = bf16[4,896,896]{2,1,0:T(8,128)(2,1)} fusion(bf16[4,896,896]{2,1,0:T(8,128)(2,1)} %broadcast_in_dim.40, bf16[4,224,896]{2,1,0:T(8,128)(2,1)S(1)} %copy-done.2, s32[]{:T(128)S(6)} %select_n.32), kind=kLoop, calls=%fused_computation.21 | loop fusion | bytes 3211268 | tf_op jit(solution)/shard_map/dynamic_update_slice | solution.py:122
  52.0 2.7 %constant_dynamic-update-slice_fusion.2 = bf16[4,896,896]{2,1,0:T(8,128)(2,1)} fusion(bf16[4,896,896]{2,1,0:T(8,128)(2,1)} %constant_dynamic-update-slice_fusion.3, bf16[4,224,896]{2,1,0:T(8,128)(2,1)} %collective-permute-done, s32[]{:T(128)S(6)} %select_n.36), kind=kLoop, calls=%fused_computation.20 | loop fusion | bytes 3211268 | tf_op jit(solution)/shard_map/dynamic_update_slice | solution.py:122
  54.8 0.0 collective-permute-done.1
  54.8 2.7 %constant_dynamic-update-slice_fusion.1 = bf16[4,896,896]{2,1,0:T(8,128)(2,1)} fusion(bf16[4,896,896]{2,1,0:T(8,128)(2,1)} %constant_dynamic-update-slice_fusion.2, bf16[4,224,896]{2,1,0:T(8,128)(2,1)} %collective-permute-done.1, s32[]{:T(128)S(6)} %select_n.37), kind=kLoop, calls=%fused_computation.19 | loop fusion | bytes 3211268 | tf_op jit(solution)/shard_map/dynamic_update_slice | solution.py:122
  57.5 0.0 collective-permute-done.2
  57.5 2.7 %constant_dynamic-update-slice_fusion.w_ref = bf16[4,896,896]{2,1,0:T(8,128)(2,1)} fusion(bf16[4,896,896]{2,1,0:T(8,128)(2,1)} %constant_dynamic-update-slice_fusion.1, bf16[4,224,896]{2,1,0:T(8,128)(2,1)} %collective-permute-done.2, s32[]{:T(128)S(6)} %select_n.38), kind=kLoop, calls=%fused_computation.18 | loop fusion | bytes 3211268 | tf_op jit(solution)/shard_map/dynamic_update_slice | solution.py:122
  60.2 3.7 %all-to-all-done.1 = bf16[8,2,64,896]{3,2,1,0:T(8,128)(2,1)S(1)} async-done(((bf16[8,2,64,896]{3,2,1,0:T(8,128)(2,1)}), bf16[8,2,64,896]{3,2,1,0:T(8,128)(2,1)S(1)}, u32[]{:S(2)}, u32[]{:S(2)}) %all-to-all-start.1) | async-done | bytes 1835040 | tf_op jit(solution)/shard_map/all_to_all | solution.py:145
  63.9 2.0 %gather_fusion.1 = bf16[16,64,896]{2,1,0:T(8,128)(2,1)} fusion(bf16[16,64,896]{2,1,0:T(8,128)(2,1)S(1)} %bitcast.33, s32[1024]{0:T(1024)S(1)} %pad_clamp_fusion), kind=kCustom, calls=%fused_computation.1 | custom fusion | bytes 3670080 | tf_op jit(solution)/shard_map/jit(_take)/gather | solution.py:147
  65.8 16.0 %shard_map.73 = bf16[1024,896]{1,0:T(8,128)(2,1)} custom-call(bf16[1024,896]{1,0:T(8,128)(2,1)} %bitcast.35, f32[1,896]{1,0:T(1,128)} %reshape.40.gain_ref, bf16[4,896,896]{2,1,0:T(8,128)(2,1)} %constant_dynamic-update-slice_fusion.w_ref), custom_call_target="tpu_custom_call" | custom-call | tf_op jit(solution)/shard_map/pallas_call | solution.py:58
  81.9 0.0 copy-start.1
  81.9 9.2 %convert_bitcast_fusion.kt_ref = bf16[2048,1024]{1,0:T(8,128)(2,1)} fusion(bf16[1024,896]{1,0:T(8,128)(2,1)} %shard_map.73, bf16[2,896,2048]{2,1,0:T(8,128)(2,1)} %param.13), kind=kOutput, calls=%fused_computation.2 | convolution fusion | flops 3760193536 | bytes 9699328 | tf_op jit(solution)/shard_map/ef,re->fr/dot_general | solution.py:149
  91.1 0.0 copy-done.1
  91.1 8.1 %convolution_convert_fusion.v_ref = bf16[1024,2048]{1,0:T(8,128)(2,1)} fusion(bf16[1024,896]{1,0:T(8,128)(2,1)S(1)} %copy-done.1, bf16[2,896,2048]{2,1,0:T(8,128)(2,1)} %param.13), kind=kOutput, calls=%fused_computation.3 | convolution fusion | flops 3760193536 | bytes 9699328 | tf_op jit(solution)/shard_map/dot_general | solution.py:152
  99.2 8.2 %shard_map.74 = bf16[512,2048]{1,0:T(8,128)(2,1)} custom-call(bf16[512,2048]{1,0:T(8,128)(2,1)} %bitcast.36, bf16[2048,1024]{1,0:T(8,128)(2,1)} %convert_bitcast_fusion.kt_ref, bf16[1024,2048]{1,0:T(8,128)(2,1)} %convolution_convert_fusion.v_ref), custom_call_target="tpu_custom_call" | custom-call | tf_op jit(solution)/shard_map/pallas_call | solution.py:96
  (7 shorter events, 0.1 us)
Async XLA Ops:
  0.0 16.8 %copy-start = (bf16[1,4,64,896]{3,2,1,0:T(8,128)(2,1)S(1)}, bf16[1,4,64,896]{3,2,1,0:T(8,128)(2,1)}, u32[]{:S(2)}) copy-start(bf16[1,4,64,896]{3,2,1,0:T(8,128)(2,1)} %param.8) | copy-start | bytes 1376260
  2.6 13.9 %all-to-all-start = ((s32[8,3,16]{2,1,0:T(4,128)}), s32[8,3,16]{2,1,0:T(4,128)S(1)}, u32[]{:S(2)}, u32[]{:S(2)}) async-start(s32[8,3,16]{2,1,0:T(4,128)} %broadcast_in_dim.35), calls=%async_computation | async-start | bytes 32768 | tf_op jit(solution)/shard_map/all_to_all | solution.py:139
  9.9 36.9 %collective-permute-start = (bf16[4,224,896]{2,1,0:T(8,128)(2,1)}, bf16[4,224,896]{2,1,0:T(8,128)(2,1)}, u32[]{:S(2)}, u32[]{:S(2)}) collective-permute-start(bf16[4,224,896]{2,1,0:T(8,128)(2,1)} %param.12), channel_id=1, source_target_pairs={{0,16},{8,24},{16,0},{24,8},{1,17},{9,25},{17,1},{25,9},{2,18},{10... | collective-permute-start | bytes 4816904 | tf_op jit(solution)/shard_map/ppermute | solution.py:116
  16.8 29.9 %copy-start.3 = (s32[1,8,2]{1,2,0:T(2,128)S(1)}, s32[1,8,2]{1,2,0:T(2,128)}, u32[]{:S(2)}) copy-start(s32[1,8,2]{1,2,0:T(2,128)} %param.9) | copy-start | bytes 196
  16.9 30.1 %copy-start.4 = (f32[896]{0:T(1024)S(1)}, f32[896]{0:T(1024)}, u32[]{:S(2)}) copy-start(f32[896]{0:T(1024)} %param.11) | copy-start | bytes 10756
  18.9 45.0 %all-to-all-start.1 = ((bf16[8,2,64,896]{3,2,1,0:T(8,128)(2,1)}), bf16[8,2,64,896]{3,2,1,0:T(8,128)(2,1)S(1)}, u32[]{:S(2)}, u32[]{:S(2)}) async-start(bf16[8,2,64,896]{3,2,1,0:T(8,128)(2,1)} %bitcast.34), calls=%async_computation.1 | async-start | bytes 3670016 | tf_op jit(solution)/shard_map/all_to_all | solution.py:145
  22.5 32.3 %collective-permute-start.1 = (bf16[4,224,896]{2,1,0:T(8,128)(2,1)}, bf16[4,224,896]{2,1,0:T(8,128)(2,1)}, u32[]{:S(2)}, u32[]{:S(2)}) collective-permute-start(bf16[4,224,896]{2,1,0:T(8,128)(2,1)} %param.12), channel_id=1, source_target_pairs={{0,8},{8,0},{16,24},{24,16},{1,9},{9,1},{17,25},{25,17},{2,10},{10... | collective-permute-start | bytes 4816904 | tf_op jit(solution)/shard_map/ppermute | solution.py:118
  46.8 10.7 %collective-permute-start.2 = (bf16[4,224,896]{2,1,0:T(8,128)(2,1)}, bf16[4,224,896]{2,1,0:T(8,128)(2,1)}, u32[]{:S(2)}, u32[]{:S(2)}) collective-permute-start(bf16[4,224,896]{2,1,0:T(8,128)(2,1)} %collective-permute-done), channel_id=1, source_target_pairs={{0,8},{8,0},{16,24},{24,16},{1,9},{9,1},{17,25},{25,17},{2,10},{10... | collective-permute-start | bytes 4816904 | tf_op jit(solution)/shard_map/ppermute | solution.py:118
  47.6 3.2 %copy-start.2 = (bf16[4,224,896]{2,1,0:T(8,128)(2,1)S(1)}, bf16[4,224,896]{2,1,0:T(8,128)(2,1)}, u32[]{:S(2)}) copy-start(bf16[4,224,896]{2,1,0:T(8,128)(2,1)} %param.12) | copy-start | bytes 4816900
  81.9 9.2 %copy-start.1 = (bf16[1024,896]{1,0:T(8,128)(2,1)S(1)}, bf16[1024,896]{1,0:T(8,128)(2,1)}, u32[]{:S(2)}) copy-start(bf16[1024,896]{1,0:T(8,128)(2,1)} %shard_map.73) | copy-start | bytes 5505028

commit v9 on v8

--- a/solution.py
+++ b/solution.py
@@ -142,10 +142,16 @@
         picks = jnp.sum(jnp.where(match, asked[:, 1, None, :], 0), axis=-1)
         sent = jnp.take(neighbour_input[0], picks.reshape(-1), axis=0, mode="clip")
         sent = sent.reshape(n_seq, per_owner, NLEN, neighbour_input.shape[-1])
-        got = lax.all_to_all(sent, "seq", 0, 0, tiled=True)
-        got = got.reshape(n_seq * per_owner, NLEN, neighbour_input.shape[-1])
-        chosen_raw = jnp.take(got, owners * per_owner + rank, axis=0, mode="clip")
-        chosen = encode_blocks(chosen_raw, enc_gain, full_weights)
+        encoded = []
+        for slot in range(per_owner):
+            part = sent[:, slot]
+            if encoded:
+                part, _ = lax.optimization_barrier((part, got))
+            got = lax.all_to_all(part, "seq", 0, 0, tiled=True)
+            encoded.append(encode_blocks(got, enc_gain, full_weights))
+        encoded = jnp.stack(encoded).reshape(per_owner * n_seq, NLEN, neighbour_input.shape[-1])
+        chosen = jnp.take(encoded, rank * n_seq + owners, axis=0, mode="clip")
+        chosen = chosen.reshape(refs * NLEN, neighbour_input.shape[-1])
         keys_t = jnp.einsum(
             "ef,re->fr", kv_weight[0], chosen, preferred_element_type=jnp.float32
         ).astype(jnp.bfloat16)

time: 108 us -> 117 us (1.083)
  starting transfers between devices: 12.4 us -> 18.3 us
  Pallas kernels: 24.3 us -> 28.4 us
  waiting for transfers between devices: 33 us -> 29.2 us
  other arithmetic: 0.37 us -> 1.73 us
  local copies, waits for them, and re-layouts: 20 us -> 21.3 us
    all_to_all x1 -> x2, starting transfers between devices: 3.59 us -> 9.41 us  [shards(): got = lax.all_to_all(part, 'seq', 0, 0, tiled=True)]
    pallas_call x1 -> x2, Pallas kernels: 16 us -> 20.1 us  [encode_blocks(): pl.pallas_call(_encoder_kernel, out_shape=jax.ShapeDtypeStruct(flat.shape...]
    all_to_all x1 -> x2, waiting for transfers between devices: 3.65 us -> 0.16 us  [shards(): got = lax.all_to_all(part, 'seq', 0, 0, tiled=True)]
    squeeze x0 -> x1, local copies, waits for them, and re-layouts: none -> 1.39 us  [shards(): part = sent[:, slot]]
    another operation x0 -> x1, other arithmetic: none -> 1.36 us  [shards(): jnp.stack(encoded)]
    unnamed x12 -> x16, local copies, waits for them, and re-layouts: 1.59 us -> 2.51 us
  transfers between devices with their start and end apart: 5 -> 6, of which waited for: 3 -> 3; matrix products, arithmetic and copies ran while one was open for 15% -> 14% of each run, Pallas kernels for 0% -> 9%
where the time goes in v9:
time: 117 us; the launch traced here: 116 us
  waiting for transfers between devices  29.2 us (25%)
  Pallas kernels  28.4 us (24%)
  local copies, waits for them, and re-layouts  21.3 us (18%)
  starting transfers between devices  18.3 us (16%)
  matrix products  17.3 us (15%)
  other arithmetic  1.73 us (1%)
    ppermute x1, waiting for transfers between devices, gather_weights(): lax.ppermute(shard, 'dp', ring)  23.9 us
    pallas_call x2, Pallas kernels, encode_blocks(): pl.pallas_call(_encoder_kernel, out_shape=jax.ShapeDtypeStruct(flat.shape...  20.1 us
    dynamic_update_slice x4, local copies, waits for them, and re-layouts, gather_weights(): full = lax.dynamic_update_slice(full, piece, (0, owner * rows, 0))  9.52 us
    all_to_all x2, starting transfers between devices, shards(): got = lax.all_to_all(part, 'seq', 0, 0, tiled=True)  9.41 us
    dot_general x1, matrix products, shards(): jnp.einsum('ef,re->fr', kv_weight[0], chosen, preferred_element_type=jnp....  9.23 us
    pallas_call x1, Pallas kernels, cross_attend(): pl.pallas_call(_cross_kernel, out_shape=jax.ShapeDtypeStruct(queries.shap...  8.25 us
    dot_general x1, matrix products, shards(): jnp.dot(chosen, kv_weight[1], preferred_element_type=jnp.float32)  8.06 us
    all_to_all x1, starting transfers between devices, shards(): asked = lax.all_to_all(asks, 'seq', 0, 0, tiled=True)  7.28 us
  transfers between devices with their start and end apart: 6, of which 3 were waited for; matrix products, arithmetic and copies ran while one was open for 14% of the time, Pallas kernels for 9%

profile of v9, /device:TPU:0, one launch (start us, length us, event | category | flops | bytes accessed | tf_op | source)
XLA Modules:
  0.0 116.2 jit_solution(1368033114873177675)
XLA Ops:
  0.0 0.0 copy-start
  0.0 0.8 copy.32
  0.8 0.1 eq.39
  0.9 0.1 stack_reshape.6
  1.0 0.2 convert_reduce_fusion
  1.2 0.8 copy.33
  1.9 0.1 stack_reshape.7
  2.0 0.6 broadcast_in_dim.35
  2.6 7.3 %all-to-all-start = ((s32[8,3,16]{2,1,0:T(4,128)}), s32[8,3,16]{2,1,0:T(4,128)S(1)}, u32[]{:S(2)}, u32[]{:S(2)}) async-start(s32[8,3,16]{2,1,0:T(4,128)} %broadcast_in_dim.35), calls=%async_computation | async-start | bytes 32768 | tf_op jit(solution)/shard_map/all_to_all | solution.py:139
  9.9 1.5 %collective-permute-start = (bf16[4,224,896]{2,1,0:T(8,128)(2,1)}, bf16[4,224,896]{2,1,0:T(8,128)(2,1)}, u32[]{:S(2)}, u32[]{:S(2)}) collective-permute-start(bf16[4,224,896]{2,1,0:T(8,128)(2,1)} %param.12), channel_id=1, source_target_pairs={{0,16},{8,24},{16,0},{24,8},{1,17},{9,25},{17,1},{25,9},{2,18},{10... | collective-permute-start | bytes 4816904 | tf_op jit(solution)/shard_map/ppermute | solution.py:116
  11.4 5.1 %all-to-all-done = s32[8,3,16]{2,1,0:T(4,128)S(1)} async-done(((s32[8,3,16]{2,1,0:T(4,128)}), s32[8,3,16]{2,1,0:T(4,128)S(1)}, u32[]{:S(2)}, u32[]{:S(2)}) %all-to-all-start) | async-done | bytes 1568 | tf_op jit(solution)/shard_map/all_to_all | solution.py:139
  16.5 0.1 select_reduce_fusion
  16.7 0.1 copy.38
  16.7 0.1 reshape.55
  16.8 0.0 copy-done
  16.8 0.8 gather_fusion
  17.7 1.4 %slice_bitcast_fusion.1 = (bf16[8,64,896]{2,1,0:T(8,128)(2,1)}, bf16[8,64,896]{2,1,0:T(8,128)(2,1)}) fusion(bf16[8,2,64,896]{3,2,1,0:T(8,128)(2,1)S(1)} %bitcast.45), kind=kLoop, calls=%fused_computation.10 | loop fusion | bytes 3670016 | tf_op jit(solution)/shard_map/squeeze | solution.py:147
  19.1 0.0 copy-start.6
  19.1 3.7 %all-to-all-start.1 = ((bf16[8,64,896]{2,1,0:T(8,128)(2,1)}), bf16[8,64,896]{2,1,0:T(8,128)(2,1)S(1)}, u32[]{:S(2)}, u32[]{:S(2)}) async-start(bf16[8,64,896]{2,1,0:T(8,128)(2,1)} %get-tuple-element.7), calls=%async_computation.1 | async-start | bytes 1835008 | tf_op jit(solution)/shard_map/all_to_all | solution.py:150
  22.8 0.1 collective-permute-start.1
  22.9 23.9 %collective-permute-done = bf16[4,224,896]{2,1,0:T(8,128)(2,1)} collective-permute-done((bf16[4,224,896]{2,1,0:T(8,128)(2,1)}, bf16[4,224,896]{2,1,0:T(8,128)(2,1)}, u32[]{:S(2)}, u32[]{:S(2)}) %collective-permute-start) | collective-permute-done | bytes 1605664 | tf_op jit(solution)/shard_map/ppermute | solution.py:116
  46.8 0.0 collective-permute-start.2
  46.8 0.0 all-to-all-done.1
  46.8 5.7 %all-to-all-start.2 = ((bf16[8,64,896]{2,1,0:T(8,128)(2,1)}), bf16[8,64,896]{2,1,0:T(8,128)(2,1)S(1)}, u32[]{:S(2)}, u32[]{:S(2)}) async-start(bf16[8,64,896]{2,1,0:T(8,128)(2,1)} %get-tuple-element.6), calls=%async_computation.2 | async-start | bytes 1835008 | tf_op jit(solution)/shard_map/all_to_all | solution.py:150
  52.5 0.1 reshape.51
  52.6 0.0 copy-done.6
  52.6 0.6 reshape.48.gain_ref
  53.2 0.0 copy-start.5
  53.2 3.2 %broadcast_in_dim.40 = bf16[4,896,896]{2,1,0:T(8,128)(2,1)} broadcast(bf16[]{:T(256)} %constant.39.clone.1), dimensions={} | broadcast | bytes 6422530 | tf_op jit(solution)/shard_map/broadcast_in_dim | solution.py:120
  56.4 0.0 copy-done.2
  56.4 0.0 copy-done.5
  56.4 1.3 %constant_dynamic-update-slice_fusion.3 = bf16[4,896,896]{2,1,0:T(8,128)(2,1)} fusion(bf16[4,896,896]{2,1,0:T(8,128)(2,1)} %broadcast_in_dim.40, bf16[4,224,896]{2,1,0:T(8,128)(2,1)S(1)} %copy-done.5, s32[]{:T(128)S(6)} %select_n.32), kind=kLoop, calls=%fused_computation.24 | loop fusion | bytes 3211268 | tf_op jit(solution)/shard_map/dynamic_update_slice | solution.py:122
  57.7 2.8 %constant_dynamic-update-slice_fusion.2 = bf16[4,896,896]{2,1,0:T(8,128)(2,1)} fusion(bf16[4,896,896]{2,1,0:T(8,128)(2,1)} %constant_dynamic-update-slice_fusion.3, bf16[4,224,896]{2,1,0:T(8,128)(2,1)} %collective-permute-done, s32[]{:T(128)S(6)} %select_n.36), kind=kLoop, calls=%fused_computation.23 | loop fusion | bytes 3211268 | tf_op jit(solution)/shard_map/dynamic_update_slice | solution.py:122
  60.5 0.0 collective-permute-done.1
  60.5 2.7 %constant_dynamic-update-slice_fusion.1 = bf16[4,896,896]{2,1,0:T(8,128)(2,1)} fusion(bf16[4,896,896]{2,1,0:T(8,128)(2,1)} %constant_dynamic-update-slice_fusion.2, bf16[4,224,896]{2,1,0:T(8,128)(2,1)} %collective-permute-done.1, s32[]{:T(128)S(6)} %select_n.37), kind=kLoop, calls=%fused_computation.22 | loop fusion | bytes 3211268 | tf_op jit(solution)/shard_map/dynamic_update_slice | solution.py:122
  63.2 0.0 collective-permute-done.2
  63.2 2.7 %constant_dynamic-update-slice_fusion.w_ref = bf16[4,896,896]{2,1,0:T(8,128)(2,1)} fusion(bf16[4,896,896]{2,1,0:T(8,128)(2,1)} %constant_dynamic-update-slice_fusion.1, bf16[4,224,896]{2,1,0:T(8,128)(2,1)} %collective-permute-done.2, s32[]{:T(128)S(6)} %select_n.38), kind=kLoop, calls=%fused_computation.21 | loop fusion | bytes 3211268 | tf_op jit(solution)/shard_map/dynamic_update_slice | solution.py:122
  65.9 10.0 %shard_map.73 = bf16[512,896]{1,0:T(8,128)(2,1)} custom-call(bf16[512,896]{1,0:T(8,128)(2,1)} %bitcast.49, f32[1,896]{1,0:T(1,128)} %reshape.48.gain_ref, bf16[4,896,896]{2,1,0:T(8,128)(2,1)} %constant_dynamic-update-slice_fusion.w_ref), custom_call_target="tpu_custom_call" | custom-call | tf_op jit(solution)/shard_map/pallas_call | solution.py:58
  76.0 0.2 all-to-all-done.2
  76.1 0.9 copy-done.3
  77.1 10.1 %shard_map.74 = bf16[512,896]{1,0:T(8,128)(2,1)} custom-call(bf16[512,896]{1,0:T(8,128)(2,1)} %bitcast.50, f32[1,896]{1,0:T(1,128)} %reshape.48.gain_ref, bf16[4,896,896]{2,1,0:T(8,128)(2,1)} %constant_dynamic-update-slice_fusion.w_ref), custom_call_target="tpu_custom_call" | custom-call | tf_op jit(solution)/shard_map/pallas_call | solution.py:58
  87.2 0.0 copy-done.1
  87.2 1.4 %pad_maximum_fusion = bf16[2,512,896]{2,1,0:T(8,128)(2,1)S(1)} fusion(bf16[1,512,896]{2,1,0:T(8,128)(2,1)} %bitcast.48, bf16[1,512,896]{2,1,0:T(8,128)(2,1)S(1)} %bitcast.47), kind=kLoop, calls=%fused_computation.8 | loop fusion | flops 917504 | bytes 3670016 | tf_op jit(solution)/shard_map/stack | solution.py:152
  88.5 2.2 %gather_fusion.1 = bf16[16,64,896]{2,1,0:T(8,128)(2,1)} fusion(bf16[16,64,896]{2,1,0:T(8,128)(2,1)S(1)} %bitcast.46, s32[1024]{0:T(1024)S(1)} %pad_clamp_fusion), kind=kCustom, calls=%fused_computation.1 | custom fusion | bytes 3670080 | tf_op jit(solution)/shard_map/jit(_take)/gather | solution.py:153
  90.7 9.2 %convert_bitcast_fusion.kt_ref = bf16[2048,1024]{1,0:T(8,128)(2,1)} fusion(bf16[1024,896]{1,0:T(8,128)(2,1)} %bitcast.52, bf16[2,896,2048]{2,1,0:T(8,128)(2,1)} %param.13), kind=kOutput, calls=%fused_computation.2 | convolution fusion | flops 3760193536 | bytes 9699328 | tf_op jit(solution)/shard_map/ef,re->fr/dot_general | solution.py:155
  99.9 0.0 copy-done.4
  99.9 8.1 %convolution_convert_fusion.v_ref = bf16[1024,2048]{1,0:T(8,128)(2,1)} fusion(bf16[1024,896]{1,0:T(8,128)(2,1)S(1)} %bitcast.53, bf16[2,896,2048]{2,1,0:T(8,128)(2,1)} %param.13), kind=kOutput, calls=%fused_computation.3 | convolution fusion | flops 3760193536 | bytes 9699328 | tf_op jit(solution)/shard_map/dot_general | solution.py:158
  108.0 8.2 %shard_map.75 = bf16[512,2048]{1,0:T(8,128)(2,1)} custom-call(bf16[512,2048]{1,0:T(8,128)(2,1)} %bitcast.51, bf16[2048,1024]{1,0:T(8,128)(2,1)} %convert_bitcast_fusion.kt_ref, bf16[1024,2048]{1,0:T(8,128)(2,1)} %convolution_convert_fusion.v_ref), custom_call_target="tpu_custom_call" | custom-call | tf_op jit(solution)/shard_map/pallas_call | solution.py:96
  (10 shorter events, 0.1 us)
Async XLA Ops:
  0.0 16.8 %copy-start = (bf16[1,4,64,896]{3,2,1,0:T(8,128)(2,1)S(1)}, bf16[1,4,64,896]{3,2,1,0:T(8,128)(2,1)}, u32[]{:S(2)}) copy-start(bf16[1,4,64,896]{3,2,1,0:T(8,128)(2,1)} %param.8) | copy-start | bytes 1376260
  2.6 13.9 %all-to-all-start = ((s32[8,3,16]{2,1,0:T(4,128)}), s32[8,3,16]{2,1,0:T(4,128)S(1)}, u32[]{:S(2)}, u32[]{:S(2)}) async-start(s32[8,3,16]{2,1,0:T(4,128)} %broadcast_in_dim.35), calls=%async_computation | async-start | bytes 32768 | tf_op jit(solution)/shard_map/all_to_all | solution.py:139
  9.9 36.9 %collective-permute-start = (bf16[4,224,896]{2,1,0:T(8,128)(2,1)}, bf16[4,224,896]{2,1,0:T(8,128)(2,1)}, u32[]{:S(2)}, u32[]{:S(2)}) collective-permute-start(bf16[4,224,896]{2,1,0:T(8,128)(2,1)} %param.12), channel_id=1, source_target_pairs={{0,16},{8,24},{16,0},{24,8},{1,17},{9,25},{17,1},{25,9},{2,18},{10... | collective-permute-start | bytes 4816904 | tf_op jit(solution)/shard_map/ppermute | solution.py:116
  19.1 33.5 %copy-start.6 = (f32[896]{0:T(1024)S(1)}, f32[896]{0:T(1024)}, u32[]{:S(2)}) copy-start(f32[896]{0:T(1024)} %param.11) | copy-start | bytes 10756
  19.1 27.7 %all-to-all-start.1 = ((bf16[8,64,896]{2,1,0:T(8,128)(2,1)}), bf16[8,64,896]{2,1,0:T(8,128)(2,1)S(1)}, u32[]{:S(2)}, u32[]{:S(2)}) async-start(bf16[8,64,896]{2,1,0:T(8,128)(2,1)} %get-tuple-element.7), calls=%async_computation.1 | async-start | bytes 1835008 | tf_op jit(solution)/shard_map/all_to_all | solution.py:150
  22.8 37.7 %collective-permute-start.1 = (bf16[4,224,896]{2,1,0:T(8,128)(2,1)}, bf16[4,224,896]{2,1,0:T(8,128)(2,1)}, u32[]{:S(2)}, u32[]{:S(2)}) collective-permute-start(bf16[4,224,896]{2,1,0:T(8,128)(2,1)} %param.12), channel_id=1, source_target_pairs={{0,8},{8,0},{16,24},{24,16},{1,9},{9,1},{17,25},{25,17},{2,10},{10... | collective-permute-start | bytes 4816904 | tf_op jit(solution)/shard_map/ppermute | solution.py:118
  46.8 16.4 %collective-permute-start.2 = (bf16[4,224,896]{2,1,0:T(8,128)(2,1)}, bf16[4,224,896]{2,1,0:T(8,128)(2,1)}, u32[]{:S(2)}, u32[]{:S(2)}) collective-permute-start(bf16[4,224,896]{2,1,0:T(8,128)(2,1)} %collective-permute-done), channel_id=1, source_target_pairs={{0,8},{8,0},{16,24},{24,16},{1,9},{9,1},{17,25},{25,17},{2,10},{10... | collective-permute-start | bytes 4816904 | tf_op jit(solution)/shard_map/ppermute | solution.py:118
  46.8 9.6 %copy-start.2 = (bf16[8,64,896]{2,1,0:T(8,128)(2,1)}, bf16[8,64,896]{2,1,0:T(8,128)(2,1)S(1)}, u32[]{:S(2)}) copy-start(bf16[8,64,896]{2,1,0:T(8,128)(2,1)S(1)} %all-to-all-done.1) | copy-start | bytes 2752516
  46.8 29.3 %all-to-all-start.2 = ((bf16[8,64,896]{2,1,0:T(8,128)(2,1)}), bf16[8,64,896]{2,1,0:T(8,128)(2,1)S(1)}, u32[]{:S(2)}, u32[]{:S(2)}) async-start(bf16[8,64,896]{2,1,0:T(8,128)(2,1)} %get-tuple-element.6), calls=%async_computation.2 | async-start | bytes 1835008 | tf_op jit(solution)/shard_map/all_to_all | solution.py:150
  53.2 3.2 %copy-start.5 = (bf16[4,224,896]{2,1,0:T(8,128)(2,1)S(1)}, bf16[4,224,896]{2,1,0:T(8,128)(2,1)}, u32[]{:S(2)}) copy-start(bf16[4,224,896]{2,1,0:T(8,128)(2,1)} %param.12) | copy-start | bytes 4816900
  76.1 0.9 copy-start.3
  77.1 10.1 %copy-start.1 = (bf16[512,896]{1,0:T(8,128)(2,1)S(1)}, bf16[512,896]{1,0:T(8,128)(2,1)}, u32[]{:S(2)}) copy-start(bf16[512,896]{1,0:T(8,128)(2,1)} %shard_map.73) | copy-start | bytes 2752516
  90.7 9.2 %copy-start.4 = (bf16[16,64,896]{2,1,0:T(8,128)(2,1)S(1)}, bf16[16,64,896]{2,1,0:T(8,128)(2,1)}, u32[]{:S(2)}) copy-start(bf16[16,64,896]{2,1,0:T(8,128)(2,1)} %gather_fusion.1) | copy-start | bytes 5505028

commit v10 on v8

--- a/solution.py
+++ b/solution.py
@@ -23,7 +23,12 @@
     return (raised * (1.0 / jnp.sum(raised, axis=-1, keepdims=True))).astype(jnp.bfloat16)
 
 
-def _encoder_kernel(x_ref, gain_ref, w_ref, out_ref, q_ref, kt_ref, v_ref, mix_ref):
+def _encoder_kernel(order_ref, *refs):
+    group = len(refs) - 8
+    block_refs = refs[:group]
+    gain_ref, w_ref, out_ref, q_ref, kt_ref, v_ref, mix_ref, x_ref = refs[group:]
+    for b in range(group):
+        x_ref[pl.ds(b * NLEN, NLEN), :] = block_refs[b][0]
     inputs = x_ref[...].astype(jnp.float32)
     spread = jnp.mean(inputs * inputs, axis=-1, keepdims=True)
     normed = (inputs * lax.rsqrt(spread + epsilon) * gain_ref[...]).astype(jnp.bfloat16)
@@ -50,28 +55,38 @@
     out_ref[...] = (inputs + output).astype(jnp.bfloat16)
 
 
-def encode_blocks(blocks, gain, attention, group=8):
-    count, length, width = blocks.shape
+def encode_blocks(blocks, order, gain, attention, group=8):
+    count = order.shape[0]
+    _, length, width = blocks.shape
     group = min(group, count)
     rows = group * length
-    flat = blocks.reshape(count * length, width)
-    return pl.pallas_call(
-        _encoder_kernel,
-        out_shape=jax.ShapeDtypeStruct(flat.shape, jnp.bfloat16),
+    order = jnp.clip(order, 0, blocks.shape[0] - 1).astype(jnp.int32)
+
+    def block_spec(j):
+        return pl.BlockSpec((1, length, width), lambda i, order_ref: (order_ref[i * group + j], 0, 0))
+
+    grid_spec = pltpu.PrefetchScalarGridSpec(
+        num_scalar_prefetch=1,
         grid=(count // group,),
-        in_specs=[
-            pl.BlockSpec((rows, width), lambda i: (i, 0)),
-            pl.BlockSpec((1, width), lambda i: (0, 0)),
-            pl.BlockSpec(attention.shape, lambda i: (0, 0, 0)),
+        in_specs=[block_spec(j) for j in range(group)]
+        + [
+            pl.BlockSpec((1, width), lambda i, order_ref: (0, 0)),
+            pl.BlockSpec(attention.shape, lambda i, order_ref: (0, 0, 0)),
         ],
-        out_specs=pl.BlockSpec((rows, width), lambda i: (i, 0)),
+        out_specs=pl.BlockSpec((rows, width), lambda i, order_ref: (i, 0)),
         scratch_shapes=[
             pltpu.VMEM((rows, width), jnp.bfloat16),
             pltpu.VMEM((width, rows), jnp.bfloat16),
             pltpu.VMEM((rows, width), jnp.bfloat16),
             pltpu.VMEM((rows, width), jnp.bfloat16),
+            pltpu.VMEM((rows, width), blocks.dtype),
         ],
-    )(flat, gain.reshape(1, width), attention)
+    )
+    return pl.pallas_call(
+        _encoder_kernel,
+        out_shape=jax.ShapeDtypeStruct((count * length, width), jnp.bfloat16),
+        grid_spec=grid_spec,
+    )(order, *([blocks] * group), gain.reshape(1, width), attention)
 
 
 def _cross_kernel(q_ref, kt_ref, v_ref, out_ref):
@@ -144,8 +159,7 @@
         sent = sent.reshape(n_seq, per_owner, NLEN, neighbour_input.shape[-1])
         got = lax.all_to_all(sent, "seq", 0, 0, tiled=True)
         got = got.reshape(n_seq * per_owner, NLEN, neighbour_input.shape[-1])
-        chosen_raw = jnp.take(got, owners * per_owner + rank, axis=0, mode="clip")
-        chosen = encode_blocks(chosen_raw, enc_gain, full_weights)
+        chosen = encode_blocks(got, owners * per_owner + rank, enc_gain, full_weights)
         keys_t = jnp.einsum(
             "ef,re->fr", kv_weight[0], chosen, preferred_element_type=jnp.float32
         ).astype(jnp.bfloat16)

time: 108 us -> 108 us (level)
  Pallas kernels: 24.3 us -> 25.4 us
    gather x1 -> x0, local copies, waits for them, and re-layouts: 1.98 us -> none  [shards(): chosen_raw = jnp.take(got, owners * per_owner + rank, axis=0, mode='clip')]
    unnamed x12, local copies, waits for them, and re-layouts: 1.59 us -> 2.81 us
    pallas_call x1, Pallas kernels: 16 us -> 17.1 us  [encode_blocks(): pl.pallas_call(_encoder_kernel, out_shape=jax.ShapeDtypeStruct((count * l...]
where the time goes in v10:
time: 108 us
  waiting for transfers between devices  32.6 us (30%)
  Pallas kernels  25.4 us (24%)
  local copies, waits for them, and re-layouts  19.1 us (18%)
  matrix products  17.3 us (16%)
  starting transfers between devices  12.4 us (11%)
    ppermute x1, waiting for transfers between devices, gather_weights(): lax.ppermute(shard, 'dp', ring)  24.2 us
    pallas_call x1, Pallas kernels, encode_blocks(): pl.pallas_call(_encoder_kernel, out_shape=jax.ShapeDtypeStruct((count * l...  17.1 us
    dynamic_update_slice x4, local copies, waits for them, and re-layouts, gather_weights(): full = lax.dynamic_update_slice(full, piece, (0, owner * rows, 0))  9.45 us
    dot_general x1, matrix products, shards(): jnp.einsum('ef,re->fr', kv_weight[0], chosen, preferred_element_type=jnp....  9.22 us
    pallas_call x1, Pallas kernels, cross_attend(): pl.pallas_call(_cross_kernel, out_shape=jax.ShapeDtypeStruct(queries.shap...  8.25 us
    dot_general x1, matrix products, shards(): jnp.dot(chosen, kv_weight[1], preferred_element_type=jnp.float32)  8.08 us
    all_to_all x1, starting transfers between devices, shards(): asked = lax.all_to_all(asks, 'seq', 0, 0, tiled=True)  7.28 us
    all_to_all x1, waiting for transfers between devices, shards(): asked = lax.all_to_all(asks, 'seq', 0, 0, tiled=True)  5.08 us
  transfers between devices with their start and end apart: 5, of which 3 were waited for; matrix products, arithmetic and copies ran while one was open for 15% of the time, Pallas kernels for 0%

profile of v10, /device:TPU:0, one launch (start us, length us, event | category | flops | bytes accessed | tf_op | source)
XLA Modules:
  0.0 107.8 jit_solution(6137037134513294586)
XLA Ops:
  0.0 0.0 copy-start
  0.0 0.8 copy.23
  0.8 0.1 reshape.17
  0.9 0.1 broadcast_in_dim_reshape.4
  1.0 0.2 convert_reduce_fusion
  1.2 0.8 copy.25
  1.9 0.1 stack_reshape.4
  2.0 0.6 broadcast_in_dim.33
  2.6 7.3 %all-to-all-start = ((s32[8,3,16]{2,1,0:T(4,128)}), s32[8,3,16]{2,1,0:T(4,128)S(1)}, u32[]{:S(2)}, u32[]{:S(2)}) async-start(s32[8,3,16]{2,1,0:T(4,128)} %broadcast_in_dim.33), calls=%async_computation | async-start | bytes 32768 | tf_op jit(solution)/shard_map/all_to_all | solution.py:154
  9.9 1.5 %collective-permute-start = (bf16[4,224,896]{2,1,0:T(8,128)(2,1)}, bf16[4,224,896]{2,1,0:T(8,128)(2,1)}, u32[]{:S(2)}, u32[]{:S(2)}) collective-permute-start(bf16[4,224,896]{2,1,0:T(8,128)(2,1)} %param.12), channel_id=1, source_target_pairs={{0,16},{8,24},{16,0},{24,8},{1,17},{9,25},{17,1},{25,9},{2,18},{10... | collective-permute-start | bytes 4816904 | tf_op jit(solution)/shard_map/ppermute | solution.py:131
  11.4 5.1 %all-to-all-done = s32[8,3,16]{2,1,0:T(4,128)S(1)} async-done(((s32[8,3,16]{2,1,0:T(4,128)}), s32[8,3,16]{2,1,0:T(4,128)S(1)}, u32[]{:S(2)}, u32[]{:S(2)}) %all-to-all-start) | async-done | bytes 1568 | tf_op jit(solution)/shard_map/all_to_all | solution.py:154
  16.5 0.1 select_reduce_fusion
  16.7 0.1 copy.29
  16.7 0.1 reshape.23
  16.8 0.0 copy-done
  16.8 0.0 copy-start.4
  16.9 2.0 %gather_fusion = bf16[16,64,896]{2,1,0:T(8,128)(2,1)} fusion(bf16[4,64,896]{2,1,0:T(8,128)(2,1)S(1)} %bitcast.25, s32[1024]{0:T(1024)S(1)} %pad_clamp_fusion), kind=kCustom, calls=%fused_computation | custom fusion | bytes 3670080 | tf_op jit(solution)/shard_map/jit(_take)/gather | solution.py:158
  18.8 3.6 %all-to-all-start.1 = ((bf16[8,2,64,896]{3,2,1,0:T(8,128)(2,1)}), bf16[8,2,64,896]{3,2,1,0:T(8,128)(2,1)S(1)}, u32[]{:S(2)}, u32[]{:S(2)}) async-start(bf16[8,2,64,896]{3,2,1,0:T(8,128)(2,1)} %bitcast.34), calls=%async_computation.1 | async-start | bytes 3670016 | tf_op jit(solution)/shard_map/all_to_all | solution.py:160
  22.4 0.1 collective-permute-start.1
  22.5 24.2 %collective-permute-done = bf16[4,224,896]{2,1,0:T(8,128)(2,1)} collective-permute-done((bf16[4,224,896]{2,1,0:T(8,128)(2,1)}, bf16[4,224,896]{2,1,0:T(8,128)(2,1)}, u32[]{:S(2)}, u32[]{:S(2)}) %collective-permute-start) | collective-permute-done | bytes 1605664 | tf_op jit(solution)/shard_map/ppermute | solution.py:131
  46.8 0.0 collective-permute-start.2
  46.8 0.0 copy-done.4
  46.8 0.6 reshape.20.refs_8_
  47.4 0.0 copy-start.3
  47.4 3.2 %broadcast_in_dim.38 = bf16[4,896,896]{2,1,0:T(8,128)(2,1)} broadcast(bf16[]{:T(256)} %constant.42.clone.1), dimensions={} | broadcast | bytes 6422530 | tf_op jit(solution)/shard_map/broadcast_in_dim | solution.py:135
  50.6 0.0 copy-done.3
  50.6 1.3 %constant_dynamic-update-slice_fusion.3 = bf16[4,896,896]{2,1,0:T(8,128)(2,1)} fusion(bf16[4,896,896]{2,1,0:T(8,128)(2,1)} %broadcast_in_dim.38, bf16[4,224,896]{2,1,0:T(8,128)(2,1)S(1)} %copy-done.3, s32[]{:T(128)S(6)} %select_n.32), kind=kLoop, calls=%fused_computation.19 | loop fusion | bytes 3211268 | tf_op jit(solution)/shard_map/dynamic_update_slice | solution.py:137
  51.9 0.6 add_clamp_fusion.order_ref
  52.4 2.7 %constant_dynamic-update-slice_fusion.2 = bf16[4,896,896]{2,1,0:T(8,128)(2,1)} fusion(bf16[4,896,896]{2,1,0:T(8,128)(2,1)} %constant_dynamic-update-slice_fusion.3, bf16[4,224,896]{2,1,0:T(8,128)(2,1)} %collective-permute-done, s32[]{:T(128)S(6)} %select_n.36), kind=kLoop, calls=%fused_computation.18 | loop fusion | bytes 3211268 | tf_op jit(solution)/shard_map/dynamic_update_slice | solution.py:137
  55.1 0.0 collective-permute-done.1
  55.1 2.7 %constant_dynamic-update-slice_fusion.1 = bf16[4,896,896]{2,1,0:T(8,128)(2,1)} fusion(bf16[4,896,896]{2,1,0:T(8,128)(2,1)} %constant_dynamic-update-slice_fusion.2, bf16[4,224,896]{2,1,0:T(8,128)(2,1)} %collective-permute-done.1, s32[]{:T(128)S(6)} %select_n.37), kind=kLoop, calls=%fused_computation.17 | loop fusion | bytes 3211268 | tf_op jit(solution)/shard_map/dynamic_update_slice | solution.py:137
  57.9 0.0 collective-permute-done.2
  57.9 2.7 %constant_dynamic-update-slice_fusion.refs_9_ = bf16[4,896,896]{2,1,0:T(8,128)(2,1)} fusion(bf16[4,896,896]{2,1,0:T(8,128)(2,1)} %constant_dynamic-update-slice_fusion.1, bf16[4,224,896]{2,1,0:T(8,128)(2,1)} %collective-permute-done.2, s32[]{:T(128)S(6)} %select_n.38), kind=kLoop, calls=%fused_computation.16 | loop fusion | bytes 3211268 | tf_op jit(solution)/shard_map/dynamic_update_slice | solution.py:137
  60.6 3.3 %all-to-all-done.1 = bf16[8,2,64,896]{3,2,1,0:T(8,128)(2,1)S(1)} async-done(((bf16[8,2,64,896]{3,2,1,0:T(8,128)(2,1)}), bf16[8,2,64,896]{3,2,1,0:T(8,128)(2,1)S(1)}, u32[]{:S(2)}, u32[]{:S(2)}) %all-to-all-start.1) | async-done | bytes 1835040 | tf_op jit(solution)/shard_map/all_to_all | solution.py:160
  63.9 0.0 copy-start.1
  63.9 1.2 %copy-done.1 = bf16[8,2,64,896]{3,2,1,0:T(8,128)(2,1)} copy-done((bf16[8,2,64,896]{3,2,1,0:T(8,128)(2,1)}, bf16[8,2,64,896]{3,2,1,0:T(8,128)(2,1)S(1)}, u32[]{:S(2)}) %copy-start.1) | copy-done | bytes 1835032
  65.1 17.1 %shard_map.73 = bf16[1024,896]{1,0:T(8,128)(2,1)} custom-call(s32[16]{0:T(128)} %add_clamp_fusion.order_ref, bf16[16,64,896]{2,1,0:T(8,128)(2,1)} %bitcast.26, bf16[16,64,896]{2,1,0:T(8,128)(2,1)} %bitcast.27, bf16[16,64,896]{2,1,0:T(8,128)(2,1)} %bitcast.28, bf16[16,64,896]{2,1,0:T(8,128)(2,1)} %bitcast.29, bf16[16,64,896]{2,1,0:T(8,128)(2,1)} %bitcast.30, ...), custom_call_target="tpu_custom_call" | custom-call | tf_op jit(solution)/shard_map/pallas_call | solution.py:85
  82.2 0.0 copy-start.2
  82.2 9.2 %convert_bitcast_fusion.kt_ref = bf16[2048,1024]{1,0:T(8,128)(2,1)} fusion(bf16[1024,896]{1,0:T(8,128)(2,1)} %shard_map.73, bf16[2,896,2048]{2,1,0:T(8,128)(2,1)} %param.13), kind=kOutput, calls=%fused_computation.1 | convolution fusion | flops 3760193536 | bytes 9699328 | tf_op jit(solution)/shard_map/ef,re->fr/dot_general | solution.py:163
  91.4 0.0 copy-done.2
  91.5 8.1 %convolution_convert_fusion.v_ref = bf16[1024,2048]{1,0:T(8,128)(2,1)} fusion(bf16[1024,896]{1,0:T(8,128)(2,1)S(1)} %copy-done.2, bf16[2,896,2048]{2,1,0:T(8,128)(2,1)} %param.13), kind=kOutput, calls=%fused_computation.2 | convolution fusion | flops 3760193536 | bytes 9699328 | tf_op jit(solution)/shard_map/dot_general | solution.py:166
  99.5 8.2 %shard_map.74 = bf16[512,2048]{1,0:T(8,128)(2,1)} custom-call(bf16[512,2048]{1,0:T(8,128)(2,1)} %bitcast.35, bf16[2048,1024]{1,0:T(8,128)(2,1)} %convert_bitcast_fusion.kt_ref, bf16[1024,2048]{1,0:T(8,128)(2,1)} %convolution_convert_fusion.v_ref), custom_call_target="tpu_custom_call" | custom-call | tf_op jit(solution)/shard_map/pallas_call | solution.py:111
  (4 shorter events, 0.0 us)
Async XLA Ops:
  0.0 16.8 %copy-start = (bf16[1,4,64,896]{3,2,1,0:T(8,128)(2,1)S(1)}, bf16[1,4,64,896]{3,2,1,0:T(8,128)(2,1)}, u32[]{:S(2)}) copy-start(bf16[1,4,64,896]{3,2,1,0:T(8,128)(2,1)} %param.8) | copy-start | bytes 1376260
  2.6 13.9 %all-to-all-start = ((s32[8,3,16]{2,1,0:T(4,128)}), s32[8,3,16]{2,1,0:T(4,128)S(1)}, u32[]{:S(2)}, u32[]{:S(2)}) async-start(s32[8,3,16]{2,1,0:T(4,128)} %broadcast_in_dim.33), calls=%async_computation | async-start | bytes 32768 | tf_op jit(solution)/shard_map/all_to_all | solution.py:154
  9.9 36.9 %collective-permute-start = (bf16[4,224,896]{2,1,0:T(8,128)(2,1)}, bf16[4,224,896]{2,1,0:T(8,128)(2,1)}, u32[]{:S(2)}, u32[]{:S(2)}) collective-permute-start(bf16[4,224,896]{2,1,0:T(8,128)(2,1)} %param.12), channel_id=1, source_target_pairs={{0,16},{8,24},{16,0},{24,8},{1,17},{9,25},{17,1},{25,9},{2,18},{10... | collective-permute-start | bytes 4816904 | tf_op jit(solution)/shard_map/ppermute | solution.py:131
  16.8 29.9 %copy-start.4 = (f32[896]{0:T(1024)S(1)}, f32[896]{0:T(1024)}, u32[]{:S(2)}) copy-start(f32[896]{0:T(1024)} %param.11) | copy-start | bytes 10756
  18.8 45.0 %all-to-all-start.1 = ((bf16[8,2,64,896]{3,2,1,0:T(8,128)(2,1)}), bf16[8,2,64,896]{3,2,1,0:T(8,128)(2,1)S(1)}, u32[]{:S(2)}, u32[]{:S(2)}) async-start(bf16[8,2,64,896]{3,2,1,0:T(8,128)(2,1)} %bitcast.34), calls=%async_computation.1 | async-start | bytes 3670016 | tf_op jit(solution)/shard_map/all_to_all | solution.py:160
  22.4 32.7 %collective-permute-start.1 = (bf16[4,224,896]{2,1,0:T(8,128)(2,1)}, bf16[4,224,896]{2,1,0:T(8,128)(2,1)}, u32[]{:S(2)}, u32[]{:S(2)}) collective-permute-start(bf16[4,224,896]{2,1,0:T(8,128)(2,1)} %param.12), channel_id=1, source_target_pairs={{0,8},{8,0},{16,24},{24,16},{1,9},{9,1},{17,25},{25,17},{2,10},{10... | collective-permute-start | bytes 4816904 | tf_op jit(solution)/shard_map/ppermute | solution.py:133
  46.8 11.1 %collective-permute-start.2 = (bf16[4,224,896]{2,1,0:T(8,128)(2,1)}, bf16[4,224,896]{2,1,0:T(8,128)(2,1)}, u32[]{:S(2)}, u32[]{:S(2)}) collective-permute-start(bf16[4,224,896]{2,1,0:T(8,128)(2,1)} %collective-permute-done), channel_id=1, source_target_pairs={{0,8},{8,0},{16,24},{24,16},{1,9},{9,1},{17,25},{25,17},{2,10},{10... | collective-permute-start | bytes 4816904 | tf_op jit(solution)/shard_map/ppermute | solution.py:133
  47.4 3.2 %copy-start.3 = (bf16[4,224,896]{2,1,0:T(8,128)(2,1)S(1)}, bf16[4,224,896]{2,1,0:T(8,128)(2,1)}, u32[]{:S(2)}) copy-start(bf16[4,224,896]{2,1,0:T(8,128)(2,1)} %param.12) | copy-start | bytes 4816900
  63.9 1.2 %copy-start.1 = (bf16[8,2,64,896]{3,2,1,0:T(8,128)(2,1)}, bf16[8,2,64,896]{3,2,1,0:T(8,128)(2,1)S(1)}, u32[]{:S(2)}) copy-start(bf16[8,2,64,896]{3,2,1,0:T(8,128)(2,1)S(1)} %all-to-all-done.1) | copy-start | bytes 5505028
  82.2 9.2 %copy-start.2 = (bf16[1024,896]{1,0:T(8,128)(2,1)S(1)}, bf16[1024,896]{1,0:T(8,128)(2,1)}, u32[]{:S(2)}) copy-start(bf16[1024,896]{1,0:T(8,128)(2,1)} %shard_map.73) | copy-start | bytes 5505028

commit v11 on v8

--- a/solution.py
+++ b/solution.py
@@ -74,36 +74,44 @@
     )(flat, gain.reshape(1, width), attention)
 
 
-def _cross_kernel(q_ref, kt_ref, v_ref, out_ref):
+def _cross_kernel(qt_ref, kv_ref, out_ref):
     scale = HEAD_DIM ** (-0.5)
-    memory = NEIGH * NLEN
-    for s in range(q_ref.shape[0] // SPAN):
-        rq = pl.ds(s * SPAN, SPAN)
-        rk = pl.ds(s * memory, memory)
-        for h in range(q_ref.shape[-1] // HEAD_DIM):
+    spans, memory = 2 * SPAN, 2 * NEIGH * NLEN
+    key_of = lax.broadcasted_iota(jnp.int32, (memory, spans), 0) // (NEIGH * NLEN)
+    query_of = lax.broadcasted_iota(jnp.int32, (memory, spans), 1) // SPAN
+    same = key_of == query_of
+    half = kv_ref.shape[-1] // 2
+    for p in range(qt_ref.shape[-1] // spans):
+        rq = pl.ds(p * spans, spans)
+        rk = pl.ds(p * memory, memory)
+        for h in range(half // HEAD_DIM):
             cols = pl.ds(h * HEAD_DIM, HEAD_DIM)
-            scores = jnp.dot(q_ref[rq, cols], kt_ref[cols, rk], preferred_element_type=jnp.float32) * scale
-            weights = _softmax_bf16(scores)
-            out_ref[rq, cols] = jnp.dot(
-                weights, v_ref[rk, cols], preferred_element_type=jnp.float32
+            scores = jnp.dot(kv_ref[rk, cols], qt_ref[cols, rq], preferred_element_type=jnp.float32) * scale
+            scores = jnp.where(same, scores, -jnp.inf)
+            highest = jnp.max(scores, axis=0, keepdims=True)
+            raised = jnp.exp(scores - highest)
+            weights = (raised * (1.0 / jnp.sum(raised, axis=0, keepdims=True))).astype(jnp.bfloat16)
+            out_ref[rq, cols] = lax.dot_general(
+                weights, kv_ref[rk, pl.ds(half + h * HEAD_DIM, HEAD_DIM)],
+                (((0,), (0,)), ((), ())), preferred_element_type=jnp.float32,
             ).astype(jnp.bfloat16)
 
 
-def cross_attend(queries, keys_t, values, group=4):
-    length, width = queries.shape
-    memory = NEIGH * NLEN
-    group = min(group, length // SPAN)
+def cross_attend(queries_t, keys_values, group=2):
+    width, length = queries_t.shape
+    spans = 2 * SPAN
+    memory = 2 * NEIGH * NLEN
+    group = min(group, length // spans)
     return pl.pallas_call(
         _cross_kernel,
-        out_shape=jax.ShapeDtypeStruct(queries.shape, jnp.bfloat16),
-        grid=(length // (SPAN * group),),
+        out_shape=jax.ShapeDtypeStruct((length, width), jnp.bfloat16),
+        grid=(length // (spans * group),),
         in_specs=[
-            pl.BlockSpec((SPAN * group, width), lambda c: (c, 0)),
-            pl.BlockSpec((width, memory * group), lambda c: (0, c)),
-            pl.BlockSpec((memory * group, width), lambda c: (c, 0)),
+            pl.BlockSpec((width, spans * group), lambda c: (0, c)),
+            pl.BlockSpec((memory * group, 2 * width), lambda c: (c, 0)),
         ],
-        out_specs=pl.BlockSpec((SPAN * group, width), lambda c: (c, 0)),
-    )(queries, keys_t, values)
+        out_specs=pl.BlockSpec((spans * group, width), lambda c: (c, 0)),
+    )(queries_t, keys_values)
 
 
 def gather_weights(shard, n_dp):
@@ -146,11 +154,9 @@
         got = got.reshape(n_seq * per_owner, NLEN, neighbour_input.shape[-1])
         chosen_raw = jnp.take(got, owners * per_owner + rank, axis=0, mode="clip")
         chosen = encode_blocks(chosen_raw, enc_gain, full_weights)
-        keys_t = jnp.einsum(
-            "ef,re->fr", kv_weight[0], chosen, preferred_element_type=jnp.float32
-        ).astype(jnp.bfloat16)
-        values = jnp.dot(chosen, kv_weight[1], preferred_element_type=jnp.float32).astype(jnp.bfloat16)
-        return cross_attend(queries[0], keys_t, values)[None]
+        both = jnp.concatenate([kv_weight[0], kv_weight[1]], axis=1)
+        keys_values = jnp.dot(chosen, both, preferred_element_type=jnp.float32).astype(jnp.bfloat16)
+        return cross_attend(queries[0].T, keys_values)[None]
 
     return shards
 

time: 108 us -> 113 us (1.046)
  local copies, waits for them, and re-layouts: 20 us -> 31.4 us
  waiting for transfers between devices: 33 us -> 29.3 us
  matrix products: 17.3 us -> 14.5 us
    squeeze x0 -> x1, local copies, waits for them, and re-layouts: none -> 7.55 us  [shards(): both = jnp.concatenate([kv_weight[0], kv_weight[1]], axis=1)]
    unnamed x12 -> x11, local copies, waits for them, and re-layouts: 1.59 us -> 5.49 us
    all_to_all x1, waiting for transfers between devices: 3.65 us -> 0.01 us  [shards(): got = lax.all_to_all(sent, 'seq', 0, 0, tiled=True)]
    dot_general x2 -> x1, matrix products: 17.3 us -> 14.5 us  [shards(): jnp.dot(chosen, both, preferred_element_type=jnp.float32)]
  transfers between devices with their start and end apart: 5 -> 5, of which waited for: 3 -> 2; matrix products, arithmetic and copies ran while one was open for 15% -> 24% of each run, Pallas kernels for 0% -> 0%
where the time goes in v11:
time: 113 us; the launch traced here: 112 us
  local copies, waits for them, and re-layouts  31.4 us (28%)
  waiting for transfers between devices  29.3 us (26%)
  Pallas kernels  24 us (21%)
  matrix products  14.5 us (13%)
  starting transfers between devices  12.4 us (11%)
    ppermute x1, waiting for transfers between devices, gather_weights(): lax.ppermute(shard, 'dp', ring)  24.2 us
    pallas_call x1, Pallas kernels, encode_blocks(): pl.pallas_call(_encoder_kernel, out_shape=jax.ShapeDtypeStruct(flat.shape...  16 us
    dot_general x1, matrix products, shards(): jnp.dot(chosen, both, preferred_element_type=jnp.float32)  14.5 us
    dynamic_update_slice x4, local copies, waits for them, and re-layouts, gather_weights(): full = lax.dynamic_update_slice(full, piece, (0, owner * rows, 0))  9.45 us
    pallas_call x1, Pallas kernels, cross_attend(): pl.pallas_call(_cross_kernel, out_shape=jax.ShapeDtypeStruct((length, wid...  8.04 us
    squeeze x1, local copies, waits for them, and re-layouts, shards(): both = jnp.concatenate([kv_weight[0], kv_weight[1]], axis=1)  7.55 us
    all_to_all x1, starting transfers between devices, shards(): asked = lax.all_to_all(asks, 'seq', 0, 0, tiled=True)  7.28 us
    unnamed x11, local copies, waits for them, and re-layouts  5.49 us
  transfers between devices with their start and end apart: 5, of which 2 were waited for; matrix products, arithmetic and copies ran while one was open for 24% of the time, Pallas kernels for 0%

profile of v11, /device:TPU:0, one launch (start us, length us, event | category | flops | bytes accessed | tf_op | source)
XLA Modules:
  0.0 112.2 jit_solution(14859827226656702522)
XLA Ops:
  0.0 0.0 copy-start
  0.0 0.8 copy.27
  0.8 0.1 eq.39
  0.9 0.1 stack_reshape.6
  1.0 0.2 convert_reduce_fusion
  1.2 0.8 copy.28
  1.9 0.1 stack_reshape.7
  2.0 0.6 broadcast_in_dim.35
  2.6 7.3 %all-to-all-start = ((s32[8,3,16]{2,1,0:T(4,128)}), s32[8,3,16]{2,1,0:T(4,128)S(1)}, u32[]{:S(2)}, u32[]{:S(2)}) async-start(s32[8,3,16]{2,1,0:T(4,128)} %broadcast_in_dim.35), calls=%async_computation | async-start | bytes 32768 | tf_op jit(solution)/shard_map/all_to_all | solution.py:147
  9.9 1.5 %collective-permute-start = (bf16[4,224,896]{2,1,0:T(8,128)(2,1)}, bf16[4,224,896]{2,1,0:T(8,128)(2,1)}, u32[]{:S(2)}, u32[]{:S(2)}) collective-permute-start(bf16[4,224,896]{2,1,0:T(8,128)(2,1)} %param.12), channel_id=1, source_target_pairs={{0,16},{8,24},{16,0},{24,8},{1,17},{9,25},{17,1},{25,9},{2,18},{10... | collective-permute-start | bytes 4816904 | tf_op jit(solution)/shard_map/ppermute | solution.py:124
  11.4 5.1 %all-to-all-done = s32[8,3,16]{2,1,0:T(4,128)S(1)} async-done(((s32[8,3,16]{2,1,0:T(4,128)}), s32[8,3,16]{2,1,0:T(4,128)S(1)}, u32[]{:S(2)}, u32[]{:S(2)}) %all-to-all-start) | async-done | bytes 1568 | tf_op jit(solution)/shard_map/all_to_all | solution.py:147
  16.5 0.1 select_reduce_fusion
  16.7 0.1 copy.33
  16.7 0.1 reshape.43
  16.8 0.0 copy-done
  16.8 0.0 copy-start.2
  16.9 0.0 copy-start.3
  16.9 2.0 %gather_fusion = bf16[16,64,896]{2,1,0:T(8,128)(2,1)} fusion(bf16[4,64,896]{2,1,0:T(8,128)(2,1)S(1)} %bitcast.29, s32[1024]{0:T(1024)S(1)} %pad_clamp_fusion.1), kind=kCustom, calls=%fused_computation | custom fusion | bytes 3670080 | tf_op jit(solution)/shard_map/jit(_take)/gather | solution.py:151
  18.9 3.6 %all-to-all-start.1 = ((bf16[8,2,64,896]{3,2,1,0:T(8,128)(2,1)}), bf16[8,2,64,896]{3,2,1,0:T(8,128)(2,1)S(1)}, u32[]{:S(2)}, u32[]{:S(2)}) async-start(bf16[8,2,64,896]{3,2,1,0:T(8,128)(2,1)} %bitcast.32), calls=%async_computation.1 | async-start | bytes 3670016 | tf_op jit(solution)/shard_map/all_to_all | solution.py:153
  22.5 0.1 collective-permute-start.1
  22.5 24.2 %collective-permute-done = bf16[4,224,896]{2,1,0:T(8,128)(2,1)} collective-permute-done((bf16[4,224,896]{2,1,0:T(8,128)(2,1)}, bf16[4,224,896]{2,1,0:T(8,128)(2,1)}, u32[]{:S(2)}, u32[]{:S(2)}) %collective-permute-start) | collective-permute-done | bytes 1605664 | tf_op jit(solution)/shard_map/ppermute | solution.py:124
  46.8 0.0 collective-permute-start.2
  46.8 0.0 copy-done.2
  46.8 0.1 copy.34
  46.9 0.1 mul.29
  47.0 0.0 copy-done.3
  47.0 0.6 reshape.40.gain_ref
  47.6 3.9 %copy.26 = bf16[1,512,2048]{1,2,0:T(8,128)(2,1)} copy(bf16[1,512,2048]{2,1,0:T(8,128)(2,1)} %param.7) | data formatting | bytes 4194304 | tf_op args[0]
  51.5 0.0 copy-start.1
  51.5 3.2 %broadcast_in_dim.40 = bf16[4,896,896]{2,1,0:T(8,128)(2,1)} broadcast(bf16[]{:T(256)} %constant.40.clone.1), dimensions={} | broadcast | bytes 6422530 | tf_op jit(solution)/shard_map/broadcast_in_dim | solution.py:128
  54.7 0.0 copy-done.1
  54.7 1.3 %constant_dynamic-update-slice_fusion.3 = bf16[4,896,896]{2,1,0:T(8,128)(2,1)} fusion(bf16[4,896,896]{2,1,0:T(8,128)(2,1)} %broadcast_in_dim.40, bf16[4,224,896]{2,1,0:T(8,128)(2,1)S(1)} %copy-done.1, s32[]{:T(128)S(6)} %select_n.32), kind=kLoop, calls=%fused_computation.21 | loop fusion | bytes 3211268 | tf_op jit(solution)/shard_map/dynamic_update_slice | solution.py:130
  56.0 7.6 %slice_bitcast_fusion.1 = (bf16[896,2048]{1,0:T(8,128)(2,1)}, bf16[896,2048]{1,0:T(8,128)(2,1)}) fusion(bf16[2,896,2048]{2,1,0:T(8,128)(2,1)} %param.13), kind=kLoop, calls=%fused_computation.7 | loop fusion | bytes 14680064 | tf_op jit(solution)/shard_map/squeeze | solution.py:157
  63.6 2.7 %constant_dynamic-update-slice_fusion.2 = bf16[4,896,896]{2,1,0:T(8,128)(2,1)} fusion(bf16[4,896,896]{2,1,0:T(8,128)(2,1)} %constant_dynamic-update-slice_fusion.3, bf16[4,224,896]{2,1,0:T(8,128)(2,1)} %collective-permute-done, s32[]{:T(128)S(6)} %select_n.36), kind=kLoop, calls=%fused_computation.20 | loop fusion | bytes 3211268 | tf_op jit(solution)/shard_map/dynamic_update_slice | solution.py:130
  66.3 0.0 collective-permute-done.1
  66.3 2.7 %constant_dynamic-update-slice_fusion.1 = bf16[4,896,896]{2,1,0:T(8,128)(2,1)} fusion(bf16[4,896,896]{2,1,0:T(8,128)(2,1)} %constant_dynamic-update-slice_fusion.2, bf16[4,224,896]{2,1,0:T(8,128)(2,1)} %collective-permute-done.1, s32[]{:T(128)S(6)} %select_n.37), kind=kLoop, calls=%fused_computation.19 | loop fusion | bytes 3211268 | tf_op jit(solution)/shard_map/dynamic_update_slice | solution.py:130
  69.0 0.0 collective-permute-done.2
  69.0 2.7 %constant_dynamic-update-slice_fusion.w_ref = bf16[4,896,896]{2,1,0:T(8,128)(2,1)} fusion(bf16[4,896,896]{2,1,0:T(8,128)(2,1)} %constant_dynamic-update-slice_fusion.1, bf16[4,224,896]{2,1,0:T(8,128)(2,1)} %collective-permute-done.2, s32[]{:T(128)S(6)} %select_n.38), kind=kLoop, calls=%fused_computation.18 | loop fusion | bytes 3211268 | tf_op jit(solution)/shard_map/dynamic_update_slice | solution.py:130
  71.7 0.0 all-to-all-done.1
  71.7 2.0 %gather_fusion.1 = bf16[16,64,896]{2,1,0:T(8,128)(2,1)} fusion(bf16[16,64,896]{2,1,0:T(8,128)(2,1)S(1)} %bitcast.31, s32[1024]{0:T(1024)S(1)} %pad_clamp_fusion), kind=kCustom, calls=%fused_computation.1 | custom fusion | bytes 3670080 | tf_op jit(solution)/shard_map/jit(_take)/gather | solution.py:155
  73.7 16.0 %shard_map.73 = bf16[1024,896]{1,0:T(8,128)(2,1)} custom-call(bf16[1024,896]{1,0:T(8,128)(2,1)} %bitcast.33, f32[1,896]{1,0:T(1,128)} %reshape.40.gain_ref, bf16[4,896,896]{2,1,0:T(8,128)(2,1)} %constant_dynamic-update-slice_fusion.w_ref), custom_call_target="tpu_custom_call" | custom-call | tf_op jit(solution)/shard_map/pallas_call | solution.py:58
  89.7 14.5 %convolution_convert_fusion.kv_ref = bf16[1024,4096]{1,0:T(8,128)(2,1)} fusion(bf16[1024,896]{1,0:T(8,128)(2,1)} %shard_map.73, bf16[896,2048]{1,0:T(8,128)(2,1)} %get-tuple-element.6, bf16[896,2048]{1,0:T(8,128)(2,1)} %get-tuple-element.5), kind=kOutput, calls=%fused_computation.2 | convolution fusion | flops 7535067136 | bytes 17563648 | tf_op jit(solution)/shard_map/dot_general | solution.py:158
  104.2 8.0 %shard_map.74 = bf16[512,2048]{1,0:T(8,128)(2,1)} custom-call(bf16[2048,512]{1,0:T(8,128)(2,1)} %bitcast.30, bf16[1024,4096]{1,0:T(8,128)(2,1)} %convolution_convert_fusion.kv_ref), custom_call_target="tpu_custom_call" | custom-call | tf_op jit(solution)/shard_map/pallas_call | solution.py:105
  (7 shorter events, 0.1 us)
Async XLA Ops:
  0.0 16.8 %copy-start = (bf16[1,4,64,896]{3,2,1,0:T(8,128)(2,1)S(1)}, bf16[1,4,64,896]{3,2,1,0:T(8,128)(2,1)}, u32[]{:S(2)}) copy-start(bf16[1,4,64,896]{3,2,1,0:T(8,128)(2,1)} %param.8) | copy-start | bytes 1376260
  2.6 13.9 %all-to-all-start = ((s32[8,3,16]{2,1,0:T(4,128)}), s32[8,3,16]{2,1,0:T(4,128)S(1)}, u32[]{:S(2)}, u32[]{:S(2)}) async-start(s32[8,3,16]{2,1,0:T(4,128)} %broadcast_in_dim.35), calls=%async_computation | async-start | bytes 32768 | tf_op jit(solution)/shard_map/all_to_all | solution.py:147
  9.9 36.9 %collective-permute-start = (bf16[4,224,896]{2,1,0:T(8,128)(2,1)}, bf16[4,224,896]{2,1,0:T(8,128)(2,1)}, u32[]{:S(2)}, u32[]{:S(2)}) collective-permute-start(bf16[4,224,896]{2,1,0:T(8,128)(2,1)} %param.12), channel_id=1, source_target_pairs={{0,16},{8,24},{16,0},{24,8},{1,17},{9,25},{17,1},{25,9},{2,18},{10... | collective-permute-start | bytes 4816904 | tf_op jit(solution)/shard_map/ppermute | solution.py:124
  16.8 29.9 %copy-start.2 = (s32[1,8,2]{1,2,0:T(2,128)S(1)}, s32[1,8,2]{1,2,0:T(2,128)}, u32[]{:S(2)}) copy-start(s32[1,8,2]{1,2,0:T(2,128)} %param.9) | copy-start | bytes 196
  16.9 30.1 %copy-start.3 = (f32[896]{0:T(1024)S(1)}, f32[896]{0:T(1024)}, u32[]{:S(2)}) copy-start(f32[896]{0:T(1024)} %param.11) | copy-start | bytes 10756
  18.9 52.9 %all-to-all-start.1 = ((bf16[8,2,64,896]{3,2,1,0:T(8,128)(2,1)}), bf16[8,2,64,896]{3,2,1,0:T(8,128)(2,1)S(1)}, u32[]{:S(2)}, u32[]{:S(2)}) async-start(bf16[8,2,64,896]{3,2,1,0:T(8,128)(2,1)} %bitcast.32), calls=%async_computation.1 | async-start | bytes 3670016 | tf_op jit(solution)/shard_map/all_to_all | solution.py:153
  22.5 43.8 %collective-permute-start.1 = (bf16[4,224,896]{2,1,0:T(8,128)(2,1)}, bf16[4,224,896]{2,1,0:T(8,128)(2,1)}, u32[]{:S(2)}, u32[]{:S(2)}) collective-permute-start(bf16[4,224,896]{2,1,0:T(8,128)(2,1)} %param.12), channel_id=1, source_target_pairs={{0,8},{8,0},{16,24},{24,16},{1,9},{9,1},{17,25},{25,17},{2,10},{10... | collective-permute-start | bytes 4816904 | tf_op jit(solution)/shard_map/ppermute | solution.py:126
  46.8 22.2 %collective-permute-start.2 = (bf16[4,224,896]{2,1,0:T(8,128)(2,1)}, bf16[4,224,896]{2,1,0:T(8,128)(2,1)}, u32[]{:S(2)}, u32[]{:S(2)}) collective-permute-start(bf16[4,224,896]{2,1,0:T(8,128)(2,1)} %collective-permute-done), channel_id=1, source_target_pairs={{0,8},{8,0},{16,24},{24,16},{1,9},{9,1},{17,25},{25,17},{2,10},{10... | collective-permute-start | bytes 4816904 | tf_op jit(solution)/shard_map/ppermute | solution.py:126
  51.5 3.2 %copy-start.1 = (bf16[4,224,896]{2,1,0:T(8,128)(2,1)S(1)}, bf16[4,224,896]{2,1,0:T(8,128)(2,1)}, u32[]{:S(2)}) copy-start(bf16[4,224,896]{2,1,0:T(8,128)(2,1)} %param.12) | copy-start | bytes 4816900

commit v12 on v8

--- a/solution.py
+++ b/solution.py
@@ -50,7 +50,7 @@
     out_ref[...] = (inputs + output).astype(jnp.bfloat16)
 
 
-def encode_blocks(blocks, gain, attention, group=8):
+def encode_blocks(blocks, gain, attention, group=16):
     count, length, width = blocks.shape
     group = min(group, count)
     rows = group * length
@@ -89,7 +89,7 @@
             ).astype(jnp.bfloat16)
 
 
-def cross_attend(queries, keys_t, values, group=4):
+def cross_attend(queries, keys_t, values, group=8):
     length, width = queries.shape
     memory = NEIGH * NLEN
     group = min(group, length // SPAN)

time: 108 us -> 110 us (1.019)
  Pallas kernels: 24.3 us -> 26.1 us
    pallas_call x1, Pallas kernels: 8.25 us -> 9.7 us  [cross_attend(): pl.pallas_call(_cross_kernel, out_shape=jax.ShapeDtypeStruct(queries.shap...]
  transfers between devices with their start and end apart: 5 -> 5, of which waited for: 3 -> 3; matrix products, arithmetic and copies ran while one was open for 15% -> 14% of each run, Pallas kernels for 0% -> 0%
where the time goes in v12:
time: 110 us; the launch traced here: 109 us
  waiting for transfers between devices  33 us (30%)
  Pallas kernels  26.1 us (24%)
  local copies, waits for them, and re-layouts  20 us (18%)
  matrix products  17.5 us (16%)
  starting transfers between devices  12.4 us (11%)
    ppermute x1, waiting for transfers between devices, gather_weights(): lax.ppermute(shard, 'dp', ring)  24.2 us
    pallas_call x1, Pallas kernels, encode_blocks(): pl.pallas_call(_encoder_kernel, out_shape=jax.ShapeDtypeStruct(flat.shape...  16.4 us
    pallas_call x1, Pallas kernels, cross_attend(): pl.pallas_call(_cross_kernel, out_shape=jax.ShapeDtypeStruct(queries.shap...  9.7 us
    dynamic_update_slice x4, local copies, waits for them, and re-layouts, gather_weights(): full = lax.dynamic_update_slice(full, piece, (0, owner * rows, 0))  9.45 us
    dot_general x1, matrix products, shards(): jnp.einsum('ef,re->fr', kv_weight[0], chosen, preferred_element_type=jnp....  9.42 us
    dot_general x1, matrix products, shards(): jnp.dot(chosen, kv_weight[1], preferred_element_type=jnp.float32)  8.08 us
    all_to_all x1, starting transfers between devices, shards(): asked = lax.all_to_all(asks, 'seq', 0, 0, tiled=True)  7.28 us
    all_to_all x1, waiting for transfers between devices, shards(): asked = lax.all_to_all(asks, 'seq', 0, 0, tiled=True)  5.08 us
  transfers between devices with their start and end apart: 5, of which 3 were waited for; matrix products, arithmetic and copies ran while one was open for 14% of the time, Pallas kernels for 0%

profile of v12, /device:TPU:0, one launch (start us, length us, event | category | flops | bytes accessed | tf_op | source)
XLA Modules:
  0.0 109.5 jit_solution(17801152586307225864)
XLA Ops:
  0.0 0.0 copy-start
  0.0 0.8 copy.26
  0.8 0.1 eq.39
  0.9 0.1 stack_reshape.6
  1.0 0.2 convert_reduce_fusion
  1.2 0.8 copy.27
  1.9 0.1 stack_reshape.7
  2.0 0.6 broadcast_in_dim.35
  2.6 7.3 %all-to-all-start = ((s32[8,3,16]{2,1,0:T(4,128)}), s32[8,3,16]{2,1,0:T(4,128)S(1)}, u32[]{:S(2)}, u32[]{:S(2)}) async-start(s32[8,3,16]{2,1,0:T(4,128)} %broadcast_in_dim.35), calls=%async_computation | async-start | bytes 32768 | tf_op jit(solution)/shard_map/all_to_all | solution.py:139
  9.9 1.5 %collective-permute-start = (bf16[4,224,896]{2,1,0:T(8,128)(2,1)}, bf16[4,224,896]{2,1,0:T(8,128)(2,1)}, u32[]{:S(2)}, u32[]{:S(2)}) collective-permute-start(bf16[4,224,896]{2,1,0:T(8,128)(2,1)} %param.12), channel_id=1, source_target_pairs={{0,16},{8,24},{16,0},{24,8},{1,17},{9,25},{17,1},{25,9},{2,18},{10... | collective-permute-start | bytes 4816904 | tf_op jit(solution)/shard_map/ppermute | solution.py:116
  11.4 5.1 %all-to-all-done = s32[8,3,16]{2,1,0:T(4,128)S(1)} async-done(((s32[8,3,16]{2,1,0:T(4,128)}), s32[8,3,16]{2,1,0:T(4,128)S(1)}, u32[]{:S(2)}, u32[]{:S(2)}) %all-to-all-start) | async-done | bytes 1568 | tf_op jit(solution)/shard_map/all_to_all | solution.py:139
  16.5 0.1 select_reduce_fusion
  16.7 0.1 copy.32
  16.7 0.1 reshape.43
  16.8 0.0 copy-done
  16.8 0.0 copy-start.3
  16.9 0.0 copy-start.4
  16.9 2.0 %gather_fusion = bf16[16,64,896]{2,1,0:T(8,128)(2,1)} fusion(bf16[4,64,896]{2,1,0:T(8,128)(2,1)S(1)} %bitcast.32, s32[1024]{0:T(1024)S(1)} %pad_clamp_fusion.1), kind=kCustom, calls=%fused_computation | custom fusion | bytes 3670080 | tf_op jit(solution)/shard_map/jit(_take)/gather | solution.py:143
  18.9 3.6 %all-to-all-start.1 = ((bf16[8,2,64,896]{3,2,1,0:T(8,128)(2,1)}), bf16[8,2,64,896]{3,2,1,0:T(8,128)(2,1)S(1)}, u32[]{:S(2)}, u32[]{:S(2)}) async-start(bf16[8,2,64,896]{3,2,1,0:T(8,128)(2,1)} %bitcast.34), calls=%async_computation.1 | async-start | bytes 3670016 | tf_op jit(solution)/shard_map/all_to_all | solution.py:145
  22.5 0.1 collective-permute-start.1
  22.5 24.2 %collective-permute-done = bf16[4,224,896]{2,1,0:T(8,128)(2,1)} collective-permute-done((bf16[4,224,896]{2,1,0:T(8,128)(2,1)}, bf16[4,224,896]{2,1,0:T(8,128)(2,1)}, u32[]{:S(2)}, u32[]{:S(2)}) %collective-permute-start) | collective-permute-done | bytes 1605664 | tf_op jit(solution)/shard_map/ppermute | solution.py:116
  46.8 0.0 collective-permute-start.2
  46.8 0.0 copy-done.3
  46.8 0.1 copy.33
  46.9 0.1 mul.29
  47.0 0.0 copy-done.4
  47.0 0.6 reshape.40.gain_ref
  47.6 0.0 copy-start.2
  47.6 3.2 %broadcast_in_dim.40 = bf16[4,896,896]{2,1,0:T(8,128)(2,1)} broadcast(bf16[]{:T(256)} %constant.40.clone.1), dimensions={} | broadcast | bytes 6422530 | tf_op jit(solution)/shard_map/broadcast_in_dim | solution.py:120
  50.7 0.0 copy-done.2
  50.7 1.3 %constant_dynamic-update-slice_fusion.3 = bf16[4,896,896]{2,1,0:T(8,128)(2,1)} fusion(bf16[4,896,896]{2,1,0:T(8,128)(2,1)} %broadcast_in_dim.40, bf16[4,224,896]{2,1,0:T(8,128)(2,1)S(1)} %copy-done.2, s32[]{:T(128)S(6)} %select_n.32), kind=kLoop, calls=%fused_computation.21 | loop fusion | bytes 3211268 | tf_op jit(solution)/shard_map/dynamic_update_slice | solution.py:122
  52.0 2.7 %constant_dynamic-update-slice_fusion.2 = bf16[4,896,896]{2,1,0:T(8,128)(2,1)} fusion(bf16[4,896,896]{2,1,0:T(8,128)(2,1)} %constant_dynamic-update-slice_fusion.3, bf16[4,224,896]{2,1,0:T(8,128)(2,1)} %collective-permute-done, s32[]{:T(128)S(6)} %select_n.36), kind=kLoop, calls=%fused_computation.20 | loop fusion | bytes 3211268 | tf_op jit(solution)/shard_map/dynamic_update_slice | solution.py:122
  54.8 0.0 collective-permute-done.1
  54.8 2.7 %constant_dynamic-update-slice_fusion.1 = bf16[4,896,896]{2,1,0:T(8,128)(2,1)} fusion(bf16[4,896,896]{2,1,0:T(8,128)(2,1)} %constant_dynamic-update-slice_fusion.2, bf16[4,224,896]{2,1,0:T(8,128)(2,1)} %collective-permute-done.1, s32[]{:T(128)S(6)} %select_n.37), kind=kLoop, calls=%fused_computation.19 | loop fusion | bytes 3211268 | tf_op jit(solution)/shard_map/dynamic_update_slice | solution.py:122
  57.5 0.0 collective-permute-done.2
  57.5 2.7 %constant_dynamic-update-slice_fusion.w_ref = bf16[4,896,896]{2,1,0:T(8,128)(2,1)} fusion(bf16[4,896,896]{2,1,0:T(8,128)(2,1)} %constant_dynamic-update-slice_fusion.1, bf16[4,224,896]{2,1,0:T(8,128)(2,1)} %collective-permute-done.2, s32[]{:T(128)S(6)} %select_n.38), kind=kLoop, calls=%fused_computation.18 | loop fusion | bytes 3211268 | tf_op jit(solution)/shard_map/dynamic_update_slice | solution.py:122
  60.2 3.7 %all-to-all-done.1 = bf16[8,2,64,896]{3,2,1,0:T(8,128)(2,1)S(1)} async-done(((bf16[8,2,64,896]{3,2,1,0:T(8,128)(2,1)}), bf16[8,2,64,896]{3,2,1,0:T(8,128)(2,1)S(1)}, u32[]{:S(2)}, u32[]{:S(2)}) %all-to-all-start.1) | async-done | bytes 1835040 | tf_op jit(solution)/shard_map/all_to_all | solution.py:145
  63.9 2.0 %gather_fusion.1 = bf16[16,64,896]{2,1,0:T(8,128)(2,1)} fusion(bf16[16,64,896]{2,1,0:T(8,128)(2,1)S(1)} %bitcast.33, s32[1024]{0:T(1024)S(1)} %pad_clamp_fusion), kind=kCustom, calls=%fused_computation.1 | custom fusion | bytes 3670080 | tf_op jit(solution)/shard_map/jit(_take)/gather | solution.py:147
  65.8 16.4 %shard_map.73 = bf16[1024,896]{1,0:T(8,128)(2,1)} custom-call(bf16[1024,896]{1,0:T(8,128)(2,1)} %bitcast.35, f32[1,896]{1,0:T(1,128)} %reshape.40.gain_ref, bf16[4,896,896]{2,1,0:T(8,128)(2,1)} %constant_dynamic-update-slice_fusion.w_ref), custom_call_target="tpu_custom_call" | custom-call | tf_op jit(solution)/shard_map/pallas_call | solution.py:58
  82.3 0.0 copy-start.1
  82.3 9.4 %convert_bitcast_fusion.kt_ref = bf16[2048,1024]{1,0:T(8,128)(2,1)} fusion(bf16[1024,896]{1,0:T(8,128)(2,1)} %shard_map.73, bf16[2,896,2048]{2,1,0:T(8,128)(2,1)} %param.13), kind=kOutput, calls=%fused_computation.2 | convolution fusion | flops 3760193536 | bytes 9699328 | tf_op jit(solution)/shard_map/ef,re->fr/dot_general | solution.py:149
  91.7 0.0 copy-done.1
  91.7 8.1 %convolution_convert_fusion.v_ref = bf16[1024,2048]{1,0:T(8,128)(2,1)} fusion(bf16[1024,896]{1,0:T(8,128)(2,1)S(1)} %copy-done.1, bf16[2,896,2048]{2,1,0:T(8,128)(2,1)} %param.13), kind=kOutput, calls=%fused_computation.3 | convolution fusion | flops 3760193536 | bytes 9699328 | tf_op jit(solution)/shard_map/dot_general | solution.py:152
  99.8 9.7 %shard_map.74 = bf16[512,2048]{1,0:T(8,128)(2,1)} custom-call(bf16[512,2048]{1,0:T(8,128)(2,1)} %bitcast.36, bf16[2048,1024]{1,0:T(8,128)(2,1)} %convert_bitcast_fusion.kt_ref, bf16[1024,2048]{1,0:T(8,128)(2,1)} %convolution_convert_fusion.v_ref), custom_call_target="tpu_custom_call" | custom-call | tf_op jit(solution)/shard_map/pallas_call | solution.py:96
  (7 shorter events, 0.1 us)
Async XLA Ops:
  0.0 16.8 %copy-start = (bf16[1,4,64,896]{3,2,1,0:T(8,128)(2,1)S(1)}, bf16[1,4,64,896]{3,2,1,0:T(8,128)(2,1)}, u32[]{:S(2)}) copy-start(bf16[1,4,64,896]{3,2,1,0:T(8,128)(2,1)} %param.8) | copy-start | bytes 1376260
  2.6 13.9 %all-to-all-start = ((s32[8,3,16]{2,1,0:T(4,128)}), s32[8,3,16]{2,1,0:T(4,128)S(1)}, u32[]{:S(2)}, u32[]{:S(2)}) async-start(s32[8,3,16]{2,1,0:T(4,128)} %broadcast_in_dim.35), calls=%async_computation | async-start | bytes 32768 | tf_op jit(solution)/shard_map/all_to_all | solution.py:139
  9.9 36.9 %collective-permute-start = (bf16[4,224,896]{2,1,0:T(8,128)(2,1)}, bf16[4,224,896]{2,1,0:T(8,128)(2,1)}, u32[]{:S(2)}, u32[]{:S(2)}) collective-permute-start(bf16[4,224,896]{2,1,0:T(8,128)(2,1)} %param.12), channel_id=1, source_target_pairs={{0,16},{8,24},{16,0},{24,8},{1,17},{9,25},{17,1},{25,9},{2,18},{10... | collective-permute-start | bytes 4816904 | tf_op jit(solution)/shard_map/ppermute | solution.py:116
  16.8 29.9 %copy-start.3 = (s32[1,8,2]{1,2,0:T(2,128)S(1)}, s32[1,8,2]{1,2,0:T(2,128)}, u32[]{:S(2)}) copy-start(s32[1,8,2]{1,2,0:T(2,128)} %param.9) | copy-start | bytes 196
  16.9 30.1 %copy-start.4 = (f32[896]{0:T(1024)S(1)}, f32[896]{0:T(1024)}, u32[]{:S(2)}) copy-start(f32[896]{0:T(1024)} %param.11) | copy-start | bytes 10756
  18.9 45.0 %all-to-all-start.1 = ((bf16[8,2,64,896]{3,2,1,0:T(8,128)(2,1)}), bf16[8,2,64,896]{3,2,1,0:T(8,128)(2,1)S(1)}, u32[]{:S(2)}, u32[]{:S(2)}) async-start(bf16[8,2,64,896]{3,2,1,0:T(8,128)(2,1)} %bitcast.34), calls=%async_computation.1 | async-start | bytes 3670016 | tf_op jit(solution)/shard_map/all_to_all | solution.py:145
  22.5 32.3 %collective-permute-start.1 = (bf16[4,224,896]{2,1,0:T(8,128)(2,1)}, bf16[4,224,896]{2,1,0:T(8,128)(2,1)}, u32[]{:S(2)}, u32[]{:S(2)}) collective-permute-start(bf16[4,224,896]{2,1,0:T(8,128)(2,1)} %param.12), channel_id=1, source_target_pairs={{0,8},{8,0},{16,24},{24,16},{1,9},{9,1},{17,25},{25,17},{2,10},{10... | collective-permute-start | bytes 4816904 | tf_op jit(solution)/shard_map/ppermute | solution.py:118
  46.8 10.7 %collective-permute-start.2 = (bf16[4,224,896]{2,1,0:T(8,128)(2,1)}, bf16[4,224,896]{2,1,0:T(8,128)(2,1)}, u32[]{:S(2)}, u32[]{:S(2)}) collective-permute-start(bf16[4,224,896]{2,1,0:T(8,128)(2,1)} %collective-permute-done), channel_id=1, source_target_pairs={{0,8},{8,0},{16,24},{24,16},{1,9},{9,1},{17,25},{25,17},{2,10},{10... | collective-permute-start | bytes 4816904 | tf_op jit(solution)/shard_map/ppermute | solution.py:118
  47.6 3.2 %copy-start.2 = (bf16[4,224,896]{2,1,0:T(8,128)(2,1)S(1)}, bf16[4,224,896]{2,1,0:T(8,128)(2,1)}, u32[]{:S(2)}) copy-start(bf16[4,224,896]{2,1,0:T(8,128)(2,1)} %param.12) | copy-start | bytes 4816900
  82.3 9.4 %copy-start.1 = (bf16[1024,896]{1,0:T(8,128)(2,1)S(1)}, bf16[1024,896]{1,0:T(8,128)(2,1)}, u32[]{:S(2)}) copy-start(bf16[1024,896]{1,0:T(8,128)(2,1)} %shard_map.73) | copy-start | bytes 5505028

commit v13 on v8

--- a/solution.py
+++ b/solution.py
@@ -131,14 +131,18 @@
         indices = block_list.reshape(-1)
         refs = owners.shape[0]
         per_owner = -(-refs // n_seq)
-        same = owners[:, None] == owners[None, :]
+        asks = jnp.stack([owners, indices])
+        asks = jnp.broadcast_to(asks[None], (n_seq, 2, refs))
+        asked = lax.all_to_all(asks, "seq", 0, 0, tiled=True)
         earlier = jnp.arange(refs)[None, :] < jnp.arange(refs)[:, None]
-        rank = jnp.sum(same & earlier, axis=1).astype(jnp.int32)
-        asks = jnp.stack([owners, indices, rank])
-        asks = jnp.broadcast_to(asks[None], (n_seq, 3, refs))
-        asked = lax.all_to_all(asks, "seq", 0, 0, tiled=True)
+
+        def rank_of(names):
+            return jnp.sum((names[..., :, None] == names[..., None, :]) & earlier, axis=-1)
+
+        rank = rank_of(owners).astype(jnp.int32)
+        asked_rank = rank_of(asked[:, 0])
         slots = jnp.arange(per_owner, dtype=jnp.int32)
-        match = (asked[:, 0, None, :] == me) & (asked[:, 2, None, :] == slots[None, :, None])
+        match = (asked[:, 0, None, :] == me) & (asked_rank[:, None, :] == slots[None, :, None])
         picks = jnp.sum(jnp.where(match, asked[:, 1, None, :], 0), axis=-1)
         sent = jnp.take(neighbour_input[0], picks.reshape(-1), axis=0, mode="clip")
         sent = sent.reshape(n_seq, per_owner, NLEN, neighbour_input.shape[-1])

time: 108 us -> 109 us (level)
    ppermute x1, waiting for transfers between devices: 24.2 us -> 14.4 us  [gather_weights(): lax.ppermute(shard, 'dp', ring)]
    all_to_all x1, waiting for transfers between devices: 3.65 us -> 13 us  [shards(): got = lax.all_to_all(sent, 'seq', 0, 0, tiled=True)]
    all_to_all x1, starting transfers between devices: 7.28 us -> 5.83 us  [shards(): asked = lax.all_to_all(asks, 'seq', 0, 0, tiled=True)]
    ppermute x1, starting transfers between devices: 1.49 us -> 2.94 us  [gather_weights(): lax.ppermute(shard, 'dp', ring)]
    all_to_all x1, waiting for transfers between devices: 5.08 us -> 6.5 us  [shards(): asked = lax.all_to_all(asks, 'seq', 0, 0, tiled=True)]
  transfers between devices with their start and end apart: 5 -> 5, of which waited for: 3 -> 3; matrix products, arithmetic and copies ran while one was open for 15% -> 17% of each run, Pallas kernels for 0% -> 0%
where the time goes in v13:
time: 109 us
  waiting for transfers between devices  34 us (31%)
  Pallas kernels  24.3 us (22%)
  local copies, waits for them, and re-layouts  19.9 us (18%)
  matrix products  17.3 us (16%)
  starting transfers between devices  12.4 us (11%)
    pallas_call x1, Pallas kernels, encode_blocks(): pl.pallas_call(_encoder_kernel, out_shape=jax.ShapeDtypeStruct(flat.shape...  16 us
    ppermute x1, waiting for transfers between devices, gather_weights(): lax.ppermute(shard, 'dp', ring)  14.4 us
    all_to_all x1, waiting for transfers between devices, shards(): got = lax.all_to_all(sent, 'seq', 0, 0, tiled=True)  13 us
    dynamic_update_slice x4, local copies, waits for them, and re-layouts, gather_weights(): full = lax.dynamic_update_slice(full, piece, (0, owner * rows, 0))  9.49 us
    dot_general x1, matrix products, shards(): jnp.einsum('ef,re->fr', kv_weight[0], chosen, preferred_element_type=jnp....  9.21 us
    pallas_call x1, Pallas kernels, cross_attend(): pl.pallas_call(_cross_kernel, out_shape=jax.ShapeDtypeStruct(queries.shap...  8.25 us
    dot_general x1, matrix products, shards(): jnp.dot(chosen, kv_weight[1], preferred_element_type=jnp.float32)  8.06 us
    all_to_all x1, waiting for transfers between devices, shards(): asked = lax.all_to_all(asks, 'seq', 0, 0, tiled=True)  6.5 us
  transfers between devices with their start and end apart: 5, of which 3 were waited for; matrix products, arithmetic and copies ran while one was open for 17% of the time, Pallas kernels for 0%

profile of v13, /device:TPU:0, one launch (start us, length us, event | category | flops | bytes accessed | tf_op | source)
XLA Modules:
  0.0 108.6 jit_solution(5843027603976117082)
XLA Ops:
  0.0 0.0 copy-start
  0.0 2.9 %collective-permute-start = (bf16[4,224,896]{2,1,0:T(8,128)(2,1)}, bf16[4,224,896]{2,1,0:T(8,128)(2,1)}, u32[]{:S(2)}, u32[]{:S(2)}) collective-permute-start(bf16[4,224,896]{2,1,0:T(8,128)(2,1)} %param.12), channel_id=1, source_target_pairs={{0,16},{8,24},{16,0},{24,8},{1,17},{9,25},{17,1},{25,9},{2,18},{10... | collective-permute-start | bytes 4816904 | tf_op jit(solution)/shard_map/ppermute | solution.py:116
  2.9 0.8 copy.25
  3.7 0.1 stack_reshape.6
  3.8 0.8 copy.26
  4.5 0.1 stack_reshape.7
  4.6 0.6 broadcast_in_dim.37
  5.2 5.8 %all-to-all-start = ((s32[8,2,16]{2,1,0:T(2,128)}), s32[8,2,16]{2,1,0:T(2,128)S(1)}, u32[]{:S(2)}, u32[]{:S(2)}) async-start(s32[8,2,16]{2,1,0:T(2,128)} %broadcast_in_dim.37), calls=%async_computation | async-start | bytes 16384 | tf_op jit(solution)/shard_map/all_to_all | solution.py:136
  11.1 6.5 %all-to-all-done = s32[8,2,16]{2,1,0:T(2,128)S(1)} async-done(((s32[8,2,16]{2,1,0:T(2,128)}), s32[8,2,16]{2,1,0:T(2,128)S(1)}, u32[]{:S(2)}, u32[]{:S(2)}) %all-to-all-start) | async-done | bytes 1056 | tf_op jit(solution)/shard_map/all_to_all | solution.py:136
  17.6 0.3 convert_reduce_fusion
  17.9 0.2 select_reduce_fusion
  18.0 0.1 copy.29
  18.1 0.1 reshape.57
  18.2 0.0 copy-done
  18.2 0.0 copy-start.3
  18.3 0.0 copy-start.4
  18.3 2.0 %gather_fusion = bf16[16,64,896]{2,1,0:T(8,128)(2,1)} fusion(bf16[4,64,896]{2,1,0:T(8,128)(2,1)S(1)} %bitcast.30, s32[1024]{0:T(1024)S(1)} %pad_clamp_fusion.1), kind=kCustom, calls=%fused_computation | custom fusion | bytes 3670080 | tf_op jit(solution)/shard_map/jit(_take)/gather | solution.py:147
  20.2 3.6 %all-to-all-start.1 = ((bf16[8,2,64,896]{3,2,1,0:T(8,128)(2,1)}), bf16[8,2,64,896]{3,2,1,0:T(8,128)(2,1)S(1)}, u32[]{:S(2)}, u32[]{:S(2)}) async-start(bf16[8,2,64,896]{3,2,1,0:T(8,128)(2,1)} %bitcast.32), calls=%async_computation.1 | async-start | bytes 3670016 | tf_op jit(solution)/shard_map/all_to_all | solution.py:149
  23.9 0.1 collective-permute-start.1
  23.9 14.4 %collective-permute-done = bf16[4,224,896]{2,1,0:T(8,128)(2,1)} collective-permute-done((bf16[4,224,896]{2,1,0:T(8,128)(2,1)}, bf16[4,224,896]{2,1,0:T(8,128)(2,1)}, u32[]{:S(2)}, u32[]{:S(2)}) %collective-permute-start) | collective-permute-done | bytes 1605664 | tf_op jit(solution)/shard_map/ppermute | solution.py:116
  38.4 0.0 collective-permute-start.2
  38.4 0.1 eq.61
  38.4 0.0 copy-done.3
  38.4 0.1 copy.30
  38.5 0.1 mul.29
  38.6 0.0 copy-done.4
  38.6 0.6 reshape.54.gain_ref
  39.2 0.0 copy-start.2
  39.2 0.2 convert_reduce_fusion.1
  39.4 3.2 %broadcast_in_dim.42 = bf16[4,896,896]{2,1,0:T(8,128)(2,1)} broadcast(bf16[]{:T(256)} %constant.40.clone.1), dimensions={} | broadcast | bytes 6422530 | tf_op jit(solution)/shard_map/broadcast_in_dim | solution.py:120
  42.6 0.0 copy-done.2
  42.6 1.3 %constant_dynamic-update-slice_fusion.3 = bf16[4,896,896]{2,1,0:T(8,128)(2,1)} fusion(bf16[4,896,896]{2,1,0:T(8,128)(2,1)} %broadcast_in_dim.42, bf16[4,224,896]{2,1,0:T(8,128)(2,1)S(1)} %copy-done.2, s32[]{:T(128)S(6)} %select_n.32), kind=kLoop, calls=%fused_computation.21 | loop fusion | bytes 3211268 | tf_op jit(solution)/shard_map/dynamic_update_slice | solution.py:122
  43.9 2.8 %constant_dynamic-update-slice_fusion.2 = bf16[4,896,896]{2,1,0:T(8,128)(2,1)} fusion(bf16[4,896,896]{2,1,0:T(8,128)(2,1)} %constant_dynamic-update-slice_fusion.3, bf16[4,224,896]{2,1,0:T(8,128)(2,1)} %collective-permute-done, s32[]{:T(128)S(6)} %select_n.36), kind=kLoop, calls=%fused_computation.20 | loop fusion | bytes 3211268 | tf_op jit(solution)/shard_map/dynamic_update_slice | solution.py:122
  46.7 0.0 collective-permute-done.1
  46.7 2.7 %constant_dynamic-update-slice_fusion.1 = bf16[4,896,896]{2,1,0:T(8,128)(2,1)} fusion(bf16[4,896,896]{2,1,0:T(8,128)(2,1)} %constant_dynamic-update-slice_fusion.2, bf16[4,224,896]{2,1,0:T(8,128)(2,1)} %collective-permute-done.1, s32[]{:T(128)S(6)} %select_n.37), kind=kLoop, calls=%fused_computation.19 | loop fusion | bytes 3211268 | tf_op jit(solution)/shard_map/dynamic_update_slice | solution.py:122
  49.4 0.0 collective-permute-done.2
  49.4 2.7 %constant_dynamic-update-slice_fusion.w_ref = bf16[4,896,896]{2,1,0:T(8,128)(2,1)} fusion(bf16[4,896,896]{2,1,0:T(8,128)(2,1)} %constant_dynamic-update-slice_fusion.1, bf16[4,224,896]{2,1,0:T(8,128)(2,1)} %collective-permute-done.2, s32[]{:T(128)S(6)} %select_n.38), kind=kLoop, calls=%fused_computation.18 | loop fusion | bytes 3211268 | tf_op jit(solution)/shard_map/dynamic_update_slice | solution.py:122
  52.1 13.0 %all-to-all-done.1 = bf16[8,2,64,896]{3,2,1,0:T(8,128)(2,1)S(1)} async-done(((bf16[8,2,64,896]{3,2,1,0:T(8,128)(2,1)}), bf16[8,2,64,896]{3,2,1,0:T(8,128)(2,1)S(1)}, u32[]{:S(2)}, u32[]{:S(2)}) %all-to-all-start.1) | async-done | bytes 1835040 | tf_op jit(solution)/shard_map/all_to_all | solution.py:149
  65.1 2.0 %gather_fusion.1 = bf16[16,64,896]{2,1,0:T(8,128)(2,1)} fusion(bf16[16,64,896]{2,1,0:T(8,128)(2,1)S(1)} %bitcast.31, s32[1024]{0:T(1024)S(1)} %pad_clamp_fusion), kind=kCustom, calls=%fused_computation.1 | custom fusion | bytes 3670080 | tf_op jit(solution)/shard_map/jit(_take)/gather | solution.py:151
  67.1 16.0 %shard_map.73 = bf16[1024,896]{1,0:T(8,128)(2,1)} custom-call(bf16[1024,896]{1,0:T(8,128)(2,1)} %bitcast.33, f32[1,896]{1,0:T(1,128)} %reshape.54.gain_ref, bf16[4,896,896]{2,1,0:T(8,128)(2,1)} %constant_dynamic-update-slice_fusion.w_ref), custom_call_target="tpu_custom_call" | custom-call | tf_op jit(solution)/shard_map/pallas_call | solution.py:58
  83.1 0.0 copy-start.1
  83.1 9.2 %convert_bitcast_fusion.kt_ref = bf16[2048,1024]{1,0:T(8,128)(2,1)} fusion(bf16[1024,896]{1,0:T(8,128)(2,1)} %shard_map.73, bf16[2,896,2048]{2,1,0:T(8,128)(2,1)} %param.13), kind=kOutput, calls=%fused_computation.2 | convolution fusion | flops 3760193536 | bytes 9699328 | tf_op jit(solution)/shard_map/ef,re->fr/dot_general | solution.py:153
  92.3 0.0 copy-done.1
  92.3 8.1 %convolution_convert_fusion.v_ref = bf16[1024,2048]{1,0:T(8,128)(2,1)} fusion(bf16[1024,896]{1,0:T(8,128)(2,1)S(1)} %copy-done.1, bf16[2,896,2048]{2,1,0:T(8,128)(2,1)} %param.13), kind=kOutput, calls=%fused_computation.3 | convolution fusion | flops 3760193536 | bytes 9699328 | tf_op jit(solution)/shard_map/dot_general | solution.py:156
  100.4 8.2 %shard_map.74 = bf16[512,2048]{1,0:T(8,128)(2,1)} custom-call(bf16[512,2048]{1,0:T(8,128)(2,1)} %bitcast.34, bf16[2048,1024]{1,0:T(8,128)(2,1)} %convert_bitcast_fusion.kt_ref, bf16[1024,2048]{1,0:T(8,128)(2,1)} %convolution_convert_fusion.v_ref), custom_call_target="tpu_custom_call" | custom-call | tf_op jit(solution)/shard_map/pallas_call | solution.py:96
  (8 shorter events, 0.1 us)
Async XLA Ops:
  0.0 18.2 %copy-start = (bf16[1,4,64,896]{3,2,1,0:T(8,128)(2,1)S(1)}, bf16[1,4,64,896]{3,2,1,0:T(8,128)(2,1)}, u32[]{:S(2)}) copy-start(bf16[1,4,64,896]{3,2,1,0:T(8,128)(2,1)} %param.8) | copy-start | bytes 1376260
  0.0 38.3 %collective-permute-start = (bf16[4,224,896]{2,1,0:T(8,128)(2,1)}, bf16[4,224,896]{2,1,0:T(8,128)(2,1)}, u32[]{:S(2)}, u32[]{:S(2)}) collective-permute-start(bf16[4,224,896]{2,1,0:T(8,128)(2,1)} %param.12), channel_id=1, source_target_pairs={{0,16},{8,24},{16,0},{24,8},{1,17},{9,25},{17,1},{25,9},{2,18},{10... | collective-permute-start | bytes 4816904 | tf_op jit(solution)/shard_map/ppermute | solution.py:116
  5.2 12.3 %all-to-all-start = ((s32[8,2,16]{2,1,0:T(2,128)}), s32[8,2,16]{2,1,0:T(2,128)S(1)}, u32[]{:S(2)}, u32[]{:S(2)}) async-start(s32[8,2,16]{2,1,0:T(2,128)} %broadcast_in_dim.37), calls=%async_computation | async-start | bytes 16384 | tf_op jit(solution)/shard_map/all_to_all | solution.py:136
  18.2 20.2 %copy-start.3 = (s32[1,8,2]{1,2,0:T(2,128)S(1)}, s32[1,8,2]{1,2,0:T(2,128)}, u32[]{:S(2)}) copy-start(s32[1,8,2]{1,2,0:T(2,128)} %param.9) | copy-start | bytes 196
  18.3 20.4 %copy-start.4 = (f32[896]{0:T(1024)S(1)}, f32[896]{0:T(1024)}, u32[]{:S(2)}) copy-start(f32[896]{0:T(1024)} %param.11) | copy-start | bytes 10756
  20.2 44.9 %all-to-all-start.1 = ((bf16[8,2,64,896]{3,2,1,0:T(8,128)(2,1)}), bf16[8,2,64,896]{3,2,1,0:T(8,128)(2,1)S(1)}, u32[]{:S(2)}, u32[]{:S(2)}) async-start(bf16[8,2,64,896]{3,2,1,0:T(8,128)(2,1)} %bitcast.32), calls=%async_computation.1 | async-start | bytes 3670016 | tf_op jit(solution)/shard_map/all_to_all | solution.py:149
  23.9 22.8 %collective-permute-start.1 = (bf16[4,224,896]{2,1,0:T(8,128)(2,1)}, bf16[4,224,896]{2,1,0:T(8,128)(2,1)}, u32[]{:S(2)}, u32[]{:S(2)}) collective-permute-start(bf16[4,224,896]{2,1,0:T(8,128)(2,1)} %param.12), channel_id=1, source_target_pairs={{0,8},{8,0},{16,24},{24,16},{1,9},{9,1},{17,25},{25,17},{2,10},{10... | collective-permute-start | bytes 4816904 | tf_op jit(solution)/shard_map/ppermute | solution.py:118
  38.4 11.0 %collective-permute-start.2 = (bf16[4,224,896]{2,1,0:T(8,128)(2,1)}, bf16[4,224,896]{2,1,0:T(8,128)(2,1)}, u32[]{:S(2)}, u32[]{:S(2)}) collective-permute-start(bf16[4,224,896]{2,1,0:T(8,128)(2,1)} %collective-permute-done), channel_id=1, source_target_pairs={{0,8},{8,0},{16,24},{24,16},{1,9},{9,1},{17,25},{25,17},{2,10},{10... | collective-permute-start | bytes 4816904 | tf_op jit(solution)/shard_map/ppermute | solution.py:118
  39.2 3.4 %copy-start.2 = (bf16[4,224,896]{2,1,0:T(8,128)(2,1)S(1)}, bf16[4,224,896]{2,1,0:T(8,128)(2,1)}, u32[]{:S(2)}) copy-start(bf16[4,224,896]{2,1,0:T(8,128)(2,1)} %param.12) | copy-start | bytes 4816900
  83.1 9.2 %copy-start.1 = (bf16[1024,896]{1,0:T(8,128)(2,1)S(1)}, bf16[1024,896]{1,0:T(8,128)(2,1)}, u32[]{:S(2)}) copy-start(bf16[1024,896]{1,0:T(8,128)(2,1)} %shard_map.73) | copy-start | bytes 5505028

commit v14 on v8

--- a/solution.py
+++ b/solution.py
@@ -23,13 +23,29 @@
     return (raised * (1.0 / jnp.sum(raised, axis=-1, keepdims=True))).astype(jnp.bfloat16)
 
 
-def _encoder_kernel(x_ref, gain_ref, w_ref, out_ref, q_ref, kt_ref, v_ref, mix_ref):
+def _encoder_kernel(x_ref, gain_ref, w_hbm, out_ref, w_ref, sems, q_ref, kt_ref, v_ref, mix_ref):
+    first = pl.program_id(0) == 0
+    copies = [pltpu.make_async_copy(w_hbm.at[p], w_ref.at[p], sems.at[p]) for p in range(4)]
+
+    @pl.when(first)
+    def _():
+        for copy in copies:
+            copy.start()
+
+    def ready(p):
+        @pl.when(first)
+        def _():
+            copies[p].wait()
+
     inputs = x_ref[...].astype(jnp.float32)
     spread = jnp.mean(inputs * inputs, axis=-1, keepdims=True)
     normed = (inputs * lax.rsqrt(spread + epsilon) * gain_ref[...]).astype(jnp.bfloat16)
+    ready(0)
     q_ref[...] = jnp.dot(normed, w_ref[0], preferred_element_type=jnp.float32).astype(jnp.bfloat16)
+    ready(1)
+    kt_ref[...] = jnp.dot(normed, w_ref[1], preferred_element_type=jnp.float32).T.astype(jnp.bfloat16)
+    ready(2)
     v_ref[...] = jnp.dot(normed, w_ref[2], preferred_element_type=jnp.float32).astype(jnp.bfloat16)
-    kt_ref[...] = jnp.dot(normed, w_ref[1], preferred_element_type=jnp.float32).T.astype(jnp.bfloat16)
     width = inputs.shape[-1]
     head_size = width // ENC_HEADS
     scale = head_size ** (-0.5)
@@ -46,6 +62,7 @@
             mix_ref[rows, cols] = jnp.dot(
                 weights, v_ref[rows, cols], preferred_element_type=jnp.float32
             ).astype(jnp.bfloat16)
+    ready(3)
     output = jnp.dot(mix_ref[...], w_ref[3], preferred_element_type=jnp.float32)
     out_ref[...] = (inputs + output).astype(jnp.bfloat16)
 
@@ -62,15 +79,18 @@
         in_specs=[
             pl.BlockSpec((rows, width), lambda i: (i, 0)),
             pl.BlockSpec((1, width), lambda i: (0, 0)),
-            pl.BlockSpec(attention.shape, lambda i: (0, 0, 0)),
+            pl.BlockSpec(memory_space=pl.ANY),
         ],
         out_specs=pl.BlockSpec((rows, width), lambda i: (i, 0)),
         scratch_shapes=[
+            pltpu.VMEM(attention.shape, attention.dtype),
+            pltpu.SemaphoreType.DMA((4,)),
             pltpu.VMEM((rows, width), jnp.bfloat16),
             pltpu.VMEM((width, rows), jnp.bfloat16),
             pltpu.VMEM((rows, width), jnp.bfloat16),
             pltpu.VMEM((rows, width), jnp.bfloat16),
         ],
+        compiler_params=pltpu.CompilerParams(dimension_semantics=("arbitrary",)),
     )(flat, gain.reshape(1, width), attention)
 
 

time: 108 us -> 109 us (level)
  no operation moved by 1% of the time
where the time goes in v14:
time: 109 us; the launch traced here: 108 us
  waiting for transfers between devices  33 us (30%)
  Pallas kernels  25 us (23%)
  local copies, waits for them, and re-layouts  20 us (18%)
  matrix products  17.3 us (16%)
  starting transfers between devices  12.4 us (11%)
    ppermute x1, waiting for transfers between devices, gather_weights(): lax.ppermute(shard, 'dp', ring)  24.2 us
    pallas_call x1, Pallas kernels, encode_blocks(): pl.pallas_call(_encoder_kernel, out_shape=jax.ShapeDtypeStruct(flat.shape...  16.7 us
    dynamic_update_slice x4, local copies, waits for them, and re-layouts, gather_weights(): full = lax.dynamic_update_slice(full, piece, (0, owner * rows, 0))  9.45 us
    dot_general x1, matrix products, shards(): jnp.einsum('ef,re->fr', kv_weight[0], chosen, preferred_element_type=jnp....  9.22 us
    pallas_call x1, Pallas kernels, cross_attend(): pl.pallas_call(_cross_kernel, out_shape=jax.ShapeDtypeStruct(queries.shap...  8.25 us
    dot_general x1, matrix products, shards(): jnp.dot(chosen, kv_weight[1], preferred_element_type=jnp.float32)  8.08 us
    all_to_all x1, starting transfers between devices, shards(): asked = lax.all_to_all(asks, 'seq', 0, 0, tiled=True)  7.28 us
    all_to_all x1, waiting for transfers between devices, shards(): asked = lax.all_to_all(asks, 'seq', 0, 0, tiled=True)  5.08 us
  transfers between devices with their start and end apart: 5, of which 3 were waited for; matrix products, arithmetic and copies ran while one was open for 15% of the time, Pallas kernels for 0%

profile of v14, /device:TPU:0, one launch (start us, length us, event | category | flops | bytes accessed | tf_op | source)
XLA Modules:
  0.0 108.1 jit_solution(14717762263501421599)
XLA Ops:
  0.0 0.0 copy-start
  0.0 0.8 copy.26
  0.8 0.1 eq.39
  0.9 0.1 stack_reshape.6
  1.0 0.2 convert_reduce_fusion
  1.2 0.8 copy.27
  1.9 0.1 stack_reshape.7
  2.0 0.6 broadcast_in_dim.35
  2.6 7.3 %all-to-all-start = ((s32[8,3,16]{2,1,0:T(4,128)}), s32[8,3,16]{2,1,0:T(4,128)S(1)}, u32[]{:S(2)}, u32[]{:S(2)}) async-start(s32[8,3,16]{2,1,0:T(4,128)} %broadcast_in_dim.35), calls=%async_computation | async-start | bytes 32768 | tf_op jit(solution)/shard_map/all_to_all | solution.py:159
  9.9 1.5 %collective-permute-start = (bf16[4,224,896]{2,1,0:T(8,128)(2,1)}, bf16[4,224,896]{2,1,0:T(8,128)(2,1)}, u32[]{:S(2)}, u32[]{:S(2)}) collective-permute-start(bf16[4,224,896]{2,1,0:T(8,128)(2,1)} %param.12), channel_id=1, source_target_pairs={{0,16},{8,24},{16,0},{24,8},{1,17},{9,25},{17,1},{25,9},{2,18},{10... | collective-permute-start | bytes 4816904 | tf_op jit(solution)/shard_map/ppermute | solution.py:136
  11.4 5.1 %all-to-all-done = s32[8,3,16]{2,1,0:T(4,128)S(1)} async-done(((s32[8,3,16]{2,1,0:T(4,128)}), s32[8,3,16]{2,1,0:T(4,128)S(1)}, u32[]{:S(2)}, u32[]{:S(2)}) %all-to-all-start) | async-done | bytes 1568 | tf_op jit(solution)/shard_map/all_to_all | solution.py:159
  16.5 0.1 select_reduce_fusion
  16.7 0.1 copy.32
  16.7 0.1 reshape.43
  16.8 0.0 copy-done
  16.8 0.0 copy-start.3
  16.9 0.0 copy-start.4
  16.9 2.0 %gather_fusion = bf16[16,64,896]{2,1,0:T(8,128)(2,1)} fusion(bf16[4,64,896]{2,1,0:T(8,128)(2,1)S(1)} %bitcast.32, s32[1024]{0:T(1024)S(1)} %pad_clamp_fusion.1), kind=kCustom, calls=%fused_computation | custom fusion | bytes 3670080 | tf_op jit(solution)/shard_map/jit(_take)/gather | solution.py:163
  18.9 3.6 %all-to-all-start.1 = ((bf16[8,2,64,896]{3,2,1,0:T(8,128)(2,1)}), bf16[8,2,64,896]{3,2,1,0:T(8,128)(2,1)S(1)}, u32[]{:S(2)}, u32[]{:S(2)}) async-start(bf16[8,2,64,896]{3,2,1,0:T(8,128)(2,1)} %bitcast.34), calls=%async_computation.1 | async-start | bytes 3670016 | tf_op jit(solution)/shard_map/all_to_all | solution.py:165
  22.5 0.1 collective-permute-start.1
  22.5 24.2 %collective-permute-done = bf16[4,224,896]{2,1,0:T(8,128)(2,1)} collective-permute-done((bf16[4,224,896]{2,1,0:T(8,128)(2,1)}, bf16[4,224,896]{2,1,0:T(8,128)(2,1)}, u32[]{:S(2)}, u32[]{:S(2)}) %collective-permute-start) | collective-permute-done | bytes 1605664 | tf_op jit(solution)/shard_map/ppermute | solution.py:136
  46.8 0.0 collective-permute-start.2
  46.8 0.0 copy-done.3
  46.8 0.1 copy.33
  46.9 0.1 mul.29
  47.0 0.0 copy-done.4
  47.0 0.6 reshape.40.gain_ref
  47.6 0.0 copy-start.2
  47.6 3.2 %broadcast_in_dim.40 = bf16[4,896,896]{2,1,0:T(8,128)(2,1)} broadcast(bf16[]{:T(256)} %constant.40.clone.1), dimensions={} | broadcast | bytes 6422530 | tf_op jit(solution)/shard_map/broadcast_in_dim | solution.py:140
  50.7 0.0 copy-done.2
  50.7 1.3 %constant_dynamic-update-slice_fusion.3 = bf16[4,896,896]{2,1,0:T(8,128)(2,1)} fusion(bf16[4,896,896]{2,1,0:T(8,128)(2,1)} %broadcast_in_dim.40, bf16[4,224,896]{2,1,0:T(8,128)(2,1)S(1)} %copy-done.2, s32[]{:T(128)S(6)} %select_n.32), kind=kLoop, calls=%fused_computation.21 | loop fusion | bytes 3211268 | tf_op jit(solution)/shard_map/dynamic_update_slice | solution.py:142
  52.0 2.7 %constant_dynamic-update-slice_fusion.2 = bf16[4,896,896]{2,1,0:T(8,128)(2,1)} fusion(bf16[4,896,896]{2,1,0:T(8,128)(2,1)} %constant_dynamic-update-slice_fusion.3, bf16[4,224,896]{2,1,0:T(8,128)(2,1)} %collective-permute-done, s32[]{:T(128)S(6)} %select_n.36), kind=kLoop, calls=%fused_computation.20 | loop fusion | bytes 3211268 | tf_op jit(solution)/shard_map/dynamic_update_slice | solution.py:142
  54.8 0.0 collective-permute-done.1
  54.8 2.7 %constant_dynamic-update-slice_fusion.1 = bf16[4,896,896]{2,1,0:T(8,128)(2,1)} fusion(bf16[4,896,896]{2,1,0:T(8,128)(2,1)} %constant_dynamic-update-slice_fusion.2, bf16[4,224,896]{2,1,0:T(8,128)(2,1)} %collective-permute-done.1, s32[]{:T(128)S(6)} %select_n.37), kind=kLoop, calls=%fused_computation.19 | loop fusion | bytes 3211268 | tf_op jit(solution)/shard_map/dynamic_update_slice | solution.py:142
  57.5 0.0 collective-permute-done.2
  57.5 2.7 %constant_dynamic-update-slice_fusion.w_hbm = bf16[4,896,896]{2,1,0:T(8,128)(2,1)} fusion(bf16[4,896,896]{2,1,0:T(8,128)(2,1)} %constant_dynamic-update-slice_fusion.1, bf16[4,224,896]{2,1,0:T(8,128)(2,1)} %collective-permute-done.2, s32[]{:T(128)S(6)} %select_n.38), kind=kLoop, calls=%fused_computation.18 | loop fusion | bytes 3211268 | tf_op jit(solution)/shard_map/dynamic_update_slice | solution.py:142
  60.2 3.7 %all-to-all-done.1 = bf16[8,2,64,896]{3,2,1,0:T(8,128)(2,1)S(1)} async-done(((bf16[8,2,64,896]{3,2,1,0:T(8,128)(2,1)}), bf16[8,2,64,896]{3,2,1,0:T(8,128)(2,1)S(1)}, u32[]{:S(2)}, u32[]{:S(2)}) %all-to-all-start.1) | async-done | bytes 1835040 | tf_op jit(solution)/shard_map/all_to_all | solution.py:165
  63.9 2.0 %gather_fusion.1 = bf16[16,64,896]{2,1,0:T(8,128)(2,1)} fusion(bf16[16,64,896]{2,1,0:T(8,128)(2,1)S(1)} %bitcast.33, s32[1024]{0:T(1024)S(1)} %pad_clamp_fusion), kind=kCustom, calls=%fused_computation.1 | custom fusion | bytes 3670080 | tf_op jit(solution)/shard_map/jit(_take)/gather | solution.py:167
  65.8 16.7 %shard_map.73 = bf16[1024,896]{1,0:T(8,128)(2,1)} custom-call(bf16[1024,896]{1,0:T(8,128)(2,1)} %bitcast.35, f32[1,896]{1,0:T(1,128)} %reshape.40.gain_ref, bf16[4,896,896]{2,1,0:T(8,128)(2,1)} %constant_dynamic-update-slice_fusion.w_hbm), custom_call_target="tpu_custom_call" | custom-call | tf_op jit(solution)/shard_map/pallas_call | solution.py:75
  82.6 0.0 copy-start.1
  82.6 9.2 %convert_bitcast_fusion.kt_ref = bf16[2048,1024]{1,0:T(8,128)(2,1)} fusion(bf16[1024,896]{1,0:T(8,128)(2,1)} %shard_map.73, bf16[2,896,2048]{2,1,0:T(8,128)(2,1)} %param.13), kind=kOutput, calls=%fused_computation.2 | convolution fusion | flops 3760193536 | bytes 9699328 | tf_op jit(solution)/shard_map/ef,re->fr/dot_general | solution.py:169
  91.8 0.0 copy-done.1
  91.8 8.1 %convolution_convert_fusion.v_ref = bf16[1024,2048]{1,0:T(8,128)(2,1)} fusion(bf16[1024,896]{1,0:T(8,128)(2,1)S(1)} %copy-done.1, bf16[2,896,2048]{2,1,0:T(8,128)(2,1)} %param.13), kind=kOutput, calls=%fused_computation.3 | convolution fusion | flops 3760193536 | bytes 9699328 | tf_op jit(solution)/shard_map/dot_general | solution.py:172
  99.9 8.2 %shard_map.74 = bf16[512,2048]{1,0:T(8,128)(2,1)} custom-call(bf16[512,2048]{1,0:T(8,128)(2,1)} %bitcast.36, bf16[2048,1024]{1,0:T(8,128)(2,1)} %convert_bitcast_fusion.kt_ref, bf16[1024,2048]{1,0:T(8,128)(2,1)} %convolution_convert_fusion.v_ref), custom_call_target="tpu_custom_call" | custom-call | tf_op jit(solution)/shard_map/pallas_call | solution.py:116
  (7 shorter events, 0.1 us)
Async XLA Ops:
  0.0 16.8 %copy-start = (bf16[1,4,64,896]{3,2,1,0:T(8,128)(2,1)S(1)}, bf16[1,4,64,896]{3,2,1,0:T(8,128)(2,1)}, u32[]{:S(2)}) copy-start(bf16[1,4,64,896]{3,2,1,0:T(8,128)(2,1)} %param.8) | copy-start | bytes 1376260
  2.6 13.9 %all-to-all-start = ((s32[8,3,16]{2,1,0:T(4,128)}), s32[8,3,16]{2,1,0:T(4,128)S(1)}, u32[]{:S(2)}, u32[]{:S(2)}) async-start(s32[8,3,16]{2,1,0:T(4,128)} %broadcast_in_dim.35), calls=%async_computation | async-start | bytes 32768 | tf_op jit(solution)/shard_map/all_to_all | solution.py:159
  9.9 36.9 %collective-permute-start = (bf16[4,224,896]{2,1,0:T(8,128)(2,1)}, bf16[4,224,896]{2,1,0:T(8,128)(2,1)}, u32[]{:S(2)}, u32[]{:S(2)}) collective-permute-start(bf16[4,224,896]{2,1,0:T(8,128)(2,1)} %param.12), channel_id=1, source_target_pairs={{0,16},{8,24},{16,0},{24,8},{1,17},{9,25},{17,1},{25,9},{2,18},{10... | collective-permute-start | bytes 4816904 | tf_op jit(solution)/shard_map/ppermute | solution.py:136
  16.8 29.9 %copy-start.3 = (s32[1,8,2]{1,2,0:T(2,128)S(1)}, s32[1,8,2]{1,2,0:T(2,128)}, u32[]{:S(2)}) copy-start(s32[1,8,2]{1,2,0:T(2,128)} %param.9) | copy-start | bytes 196
  16.9 30.1 %copy-start.4 = (f32[896]{0:T(1024)S(1)}, f32[896]{0:T(1024)}, u32[]{:S(2)}) copy-start(f32[896]{0:T(1024)} %param.11) | copy-start | bytes 10756
  18.9 45.0 %all-to-all-start.1 = ((bf16[8,2,64,896]{3,2,1,0:T(8,128)(2,1)}), bf16[8,2,64,896]{3,2,1,0:T(8,128)(2,1)S(1)}, u32[]{:S(2)}, u32[]{:S(2)}) async-start(bf16[8,2,64,896]{3,2,1,0:T(8,128)(2,1)} %bitcast.34), calls=%async_computation.1 | async-start | bytes 3670016 | tf_op jit(solution)/shard_map/all_to_all | solution.py:165
  22.5 32.3 %collective-permute-start.1 = (bf16[4,224,896]{2,1,0:T(8,128)(2,1)}, bf16[4,224,896]{2,1,0:T(8,128)(2,1)}, u32[]{:S(2)}, u32[]{:S(2)}) collective-permute-start(bf16[4,224,896]{2,1,0:T(8,128)(2,1)} %param.12), channel_id=1, source_target_pairs={{0,8},{8,0},{16,24},{24,16},{1,9},{9,1},{17,25},{25,17},{2,10},{10... | collective-permute-start | bytes 4816904 | tf_op jit(solution)/shard_map/ppermute | solution.py:138
  46.8 10.7 %collective-permute-start.2 = (bf16[4,224,896]{2,1,0:T(8,128)(2,1)}, bf16[4,224,896]{2,1,0:T(8,128)(2,1)}, u32[]{:S(2)}, u32[]{:S(2)}) collective-permute-start(bf16[4,224,896]{2,1,0:T(8,128)(2,1)} %collective-permute-done), channel_id=1, source_target_pairs={{0,8},{8,0},{16,24},{24,16},{1,9},{9,1},{17,25},{25,17},{2,10},{10... | collective-permute-start | bytes 4816904 | tf_op jit(solution)/shard_map/ppermute | solution.py:138
  47.6 3.2 %copy-start.2 = (bf16[4,224,896]{2,1,0:T(8,128)(2,1)S(1)}, bf16[4,224,896]{2,1,0:T(8,128)(2,1)}, u32[]{:S(2)}) copy-start(bf16[4,224,896]{2,1,0:T(8,128)(2,1)} %param.12) | copy-start | bytes 4816900
  82.6 9.2 %copy-start.1 = (bf16[1024,896]{1,0:T(8,128)(2,1)S(1)}, bf16[1024,896]{1,0:T(8,128)(2,1)}, u32[]{:S(2)}) copy-start(bf16[1024,896]{1,0:T(8,128)(2,1)} %shard_map.73) | copy-start | bytes 5505028

commit v15 on v8

--- a/solution.py
+++ b/solution.py
@@ -140,8 +140,10 @@
         slots = jnp.arange(per_owner, dtype=jnp.int32)
         match = (asked[:, 0, None, :] == me) & (asked[:, 2, None, :] == slots[None, :, None])
         picks = jnp.sum(jnp.where(match, asked[:, 1, None, :], 0), axis=-1)
-        sent = jnp.take(neighbour_input[0], picks.reshape(-1), axis=0, mode="clip")
-        sent = sent.reshape(n_seq, per_owner, NLEN, neighbour_input.shape[-1])
+        own = neighbour_input[0]
+        sent = jnp.zeros((n_seq, per_owner) + own.shape[1:], own.dtype)
+        for block in range(own.shape[0]):
+            sent = jnp.where((picks == block)[:, :, None, None], own[block], sent)
         got = lax.all_to_all(sent, "seq", 0, 0, tiled=True)
         got = got.reshape(n_seq * per_owner, NLEN, neighbour_input.shape[-1])
         chosen_raw = jnp.take(got, owners * per_owner + rank, axis=0, mode="clip")

time: 108 us -> 109 us (level)
  other arithmetic: 0.37 us -> 2.14 us
    ppermute x1, waiting for transfers between devices: 24.2 us -> 14.3 us  [gather_weights(): lax.ppermute(shard, 'dp', ring)]
    all_to_all x1, waiting for transfers between devices: 3.65 us -> 13.5 us  [shards(): got = lax.all_to_all(sent, 'seq', 0, 0, tiled=True)]
    gather x1 -> x0, local copies, waits for them, and re-layouts: 1.98 us -> none  [shards(): sent = jnp.take(neighbour_input[0], picks.reshape(-1), axis=0, mode='clip')]
    select_n x0 -> x1, other arithmetic: none -> 1.77 us  [shards(): sent = jnp.where((picks == block)[:, :, None, None], own[block], sent)]
    all_to_all x1, starting transfers between devices: 7.28 us -> 5.83 us  [shards(): asked = lax.all_to_all(asks, 'seq', 0, 0, tiled=True)]
    ppermute x1, starting transfers between devices: 1.49 us -> 2.94 us  [gather_weights(): lax.ppermute(shard, 'dp', ring)]
    squeeze x0 -> x1, local copies, waits for them, and re-layouts: none -> 1.1 us  [shards(): sent = jnp.where((picks == block)[:, :, None, None], own[block], sent)]
  transfers between devices with their start and end apart: 5 -> 5, of which waited for: 3 -> 3; matrix products, arithmetic and copies ran while one was open for 15% -> 18% of each run, Pallas kernels for 0% -> 0%
where the time goes in v15:
time: 109 us
  waiting for transfers between devices  33.2 us (30%)
  Pallas kernels  24.3 us (22%)
  local copies, waits for them, and re-layouts  19.3 us (18%)
  matrix products  17.3 us (16%)
  starting transfers between devices  12.6 us (12%)
  other arithmetic  2.14 us (2%)
    pallas_call x1, Pallas kernels, encode_blocks(): pl.pallas_call(_encoder_kernel, out_shape=jax.ShapeDtypeStruct(flat.shape...  16 us
    ppermute x1, waiting for transfers between devices, gather_weights(): lax.ppermute(shard, 'dp', ring)  14.3 us
    all_to_all x1, waiting for transfers between devices, shards(): got = lax.all_to_all(sent, 'seq', 0, 0, tiled=True)  13.5 us
    dynamic_update_slice x4, local copies, waits for them, and re-layouts, gather_weights(): full = lax.dynamic_update_slice(full, piece, (0, owner * rows, 0))  9.47 us
    dot_general x1, matrix products, shards(): jnp.einsum('ef,re->fr', kv_weight[0], chosen, preferred_element_type=jnp....  9.21 us
    pallas_call x1, Pallas kernels, cross_attend(): pl.pallas_call(_cross_kernel, out_shape=jax.ShapeDtypeStruct(queries.shap...  8.25 us
    dot_general x1, matrix products, shards(): jnp.dot(chosen, kv_weight[1], preferred_element_type=jnp.float32)  8.08 us
    all_to_all x1, starting transfers between devices, shards(): asked = lax.all_to_all(asks, 'seq', 0, 0, tiled=True)  5.83 us
  transfers between devices with their start and end apart: 5, of which 3 were waited for; matrix products, arithmetic and copies ran while one was open for 18% of the time, Pallas kernels for 0%

profile of v15, /device:TPU:0, one launch (start us, length us, event | category | flops | bytes accessed | tf_op | source)
XLA Modules:
  0.0 108.8 jit_solution(15967362357342665945)
XLA Ops:
  0.0 2.9 %collective-permute-start = (bf16[4,224,896]{2,1,0:T(8,128)(2,1)}, bf16[4,224,896]{2,1,0:T(8,128)(2,1)}, u32[]{:S(2)}, u32[]{:S(2)}) collective-permute-start(bf16[4,224,896]{2,1,0:T(8,128)(2,1)} %param.12), channel_id=1, source_target_pairs={{0,16},{8,24},{16,0},{24,8},{1,17},{9,25},{17,1},{25,9},{2,18},{10... | collective-permute-start | bytes 4816904 | tf_op jit(solution)/shard_map/ppermute | solution.py:116
  2.9 0.8 copy.26
  3.7 0.1 eq.67
  3.8 0.1 stack_reshape.6
  3.9 0.2 convert_reduce_fusion
  4.0 0.8 copy.27
  4.8 0.1 stack_reshape.7
  4.9 0.6 broadcast_in_dim.74
  5.5 5.8 %all-to-all-start = ((s32[8,3,16]{2,1,0:T(4,128)}), s32[8,3,16]{2,1,0:T(4,128)S(1)}, u32[]{:S(2)}, u32[]{:S(2)}) async-start(s32[8,3,16]{2,1,0:T(4,128)} %broadcast_in_dim.74), calls=%async_computation | async-start | bytes 32768 | tf_op jit(solution)/shard_map/all_to_all | solution.py:139
  11.3 1.1 %slice_bitcast_fusion.3 = (bf16[64,896]{1,0:T(8,128)(2,1)S(1)}, bf16[64,896]{1,0:T(8,128)(2,1)S(1)}, bf16[64,896]{1,0:T(8,128)(2,1)S(1)}, bf16[64,896]{1,0:T(8,128)(2,1)S(1)}) fusion(bf16[1,4,64,896]{3,2,1,0:T(8,128)(2,1)} %param.8), kind=kLoop, calls=%fused_computation.11 | loop fusion | bytes 917504 | tf_op jit(solution)/shard_map/squeeze | solution.py:146
  12.4 5.5 %all-to-all-done = s32[8,3,16]{2,1,0:T(4,128)S(1)} async-done(((s32[8,3,16]{2,1,0:T(4,128)}), s32[8,3,16]{2,1,0:T(4,128)S(1)}, u32[]{:S(2)}, u32[]{:S(2)}) %all-to-all-start) | async-done | bytes 1568 | tf_op jit(solution)/shard_map/all_to_all | solution.py:139
  17.9 0.1 select_reduce_fusion
  18.1 0.1 copy.32
  18.2 0.1 copy.33
  18.3 0.1 copy.34
  18.4 0.1 copy.35
  18.5 1.8 %select_select_fusion = bf16[8,2,64,896]{3,2,1,0:T(8,128)(2,1)} fusion(pred[8,2]{1,0:T(8,128)(4,1)S(1)} %copy.35, pred[8,2]{1,0:T(8,128)(4,1)S(1)} %copy.34, pred[8,2]{1,0:T(8,128)(4,1)S(1)} %copy.33, pred[8,2]{1,0:T(8,128)(4,1)S(1)} %copy.32, bf16[64,896]{1,0:T(8,128)(2,1)S(1)} %get-tuple-element.7, bf16[64,896]{1,0:T(8,128)(2,1)S(1)} %get-tuple-element.8, ...), kind=kLoop, calls=%fused_computation.7 | loop fusion | flops 3670016 | bytes 2293824 | tf_op jit(solution)/shard_map/jit(_where)/select_n | solution.py:146
  20.3 0.0 copy-start.1
  20.3 0.0 copy-start.2
  20.3 0.0 copy-start.3
  20.3 3.7 %all-to-all-start.1 = ((bf16[8,2,64,896]{3,2,1,0:T(8,128)(2,1)}), bf16[8,2,64,896]{3,2,1,0:T(8,128)(2,1)S(1)}, u32[]{:S(2)}, u32[]{:S(2)}) async-start(bf16[8,2,64,896]{3,2,1,0:T(8,128)(2,1)} %select_select_fusion), calls=%async_computation.1 | async-start | bytes 3670016 | tf_op jit(solution)/shard_map/all_to_all | solution.py:147
  24.0 0.0 copy-done.1
  24.0 0.1 collective-permute-start.1
  24.1 14.3 %collective-permute-done = bf16[4,224,896]{2,1,0:T(8,128)(2,1)} collective-permute-done((bf16[4,224,896]{2,1,0:T(8,128)(2,1)}, bf16[4,224,896]{2,1,0:T(8,128)(2,1)}, u32[]{:S(2)}, u32[]{:S(2)}) %collective-permute-start) | collective-permute-done | bytes 1605664 | tf_op jit(solution)/shard_map/ppermute | solution.py:116
  38.3 0.0 collective-permute-start.2
  38.4 0.0 copy-done.2
  38.4 0.1 copy.36
  38.4 0.1 mul.29
  38.5 0.0 copy-done.3
  38.5 0.6 reshape.54.gain_ref
  39.1 3.2 %broadcast_in_dim.87 = bf16[4,896,896]{2,1,0:T(8,128)(2,1)} broadcast(bf16[]{:T(256)} %constant.47.clone.1), dimensions={} | broadcast | bytes 6422530 | tf_op jit(solution)/shard_map/broadcast_in_dim | solution.py:120
  42.3 1.3 %constant_dynamic-update-slice_fusion.3 = bf16[4,896,896]{2,1,0:T(8,128)(2,1)} fusion(bf16[4,896,896]{2,1,0:T(8,128)(2,1)} %broadcast_in_dim.87, bf16[4,224,896]{2,1,0:T(8,128)(2,1)S(1)} %copy-done.1, s32[]{:T(128)S(6)} %select_n.49), kind=kLoop, calls=%fused_computation.24 | loop fusion | bytes 3211268 | tf_op jit(solution)/shard_map/dynamic_update_slice | solution.py:122
  43.6 2.7 %constant_dynamic-update-slice_fusion.2 = bf16[4,896,896]{2,1,0:T(8,128)(2,1)} fusion(bf16[4,896,896]{2,1,0:T(8,128)(2,1)} %constant_dynamic-update-slice_fusion.3, bf16[4,224,896]{2,1,0:T(8,128)(2,1)} %collective-permute-done, s32[]{:T(128)S(6)} %select_n.53), kind=kLoop, calls=%fused_computation.23 | loop fusion | bytes 3211268 | tf_op jit(solution)/shard_map/dynamic_update_slice | solution.py:122
  46.3 0.0 collective-permute-done.1
  46.3 2.7 %constant_dynamic-update-slice_fusion.1 = bf16[4,896,896]{2,1,0:T(8,128)(2,1)} fusion(bf16[4,896,896]{2,1,0:T(8,128)(2,1)} %constant_dynamic-update-slice_fusion.2, bf16[4,224,896]{2,1,0:T(8,128)(2,1)} %collective-permute-done.1, s32[]{:T(128)S(6)} %select_n.54), kind=kLoop, calls=%fused_computation.22 | loop fusion | bytes 3211268 | tf_op jit(solution)/shard_map/dynamic_update_slice | solution.py:122
  49.0 0.0 collective-permute-done.2
  49.0 2.7 %constant_dynamic-update-slice_fusion.w_ref = bf16[4,896,896]{2,1,0:T(8,128)(2,1)} fusion(bf16[4,896,896]{2,1,0:T(8,128)(2,1)} %constant_dynamic-update-slice_fusion.1, bf16[4,224,896]{2,1,0:T(8,128)(2,1)} %collective-permute-done.2, s32[]{:T(128)S(6)} %select_n.55), kind=kLoop, calls=%fused_computation.21 | loop fusion | bytes 3211268 | tf_op jit(solution)/shard_map/dynamic_update_slice | solution.py:122
  51.8 13.5 %all-to-all-done.1 = bf16[8,2,64,896]{3,2,1,0:T(8,128)(2,1)S(1)} async-done(((bf16[8,2,64,896]{3,2,1,0:T(8,128)(2,1)}), bf16[8,2,64,896]{3,2,1,0:T(8,128)(2,1)S(1)}, u32[]{:S(2)}, u32[]{:S(2)}) %all-to-all-start.1) | async-done | bytes 1835040 | tf_op jit(solution)/shard_map/all_to_all | solution.py:147
  65.3 2.0 %gather_fusion = bf16[16,64,896]{2,1,0:T(8,128)(2,1)} fusion(bf16[16,64,896]{2,1,0:T(8,128)(2,1)S(1)} %bitcast.38, s32[1024]{0:T(1024)S(1)} %pad_clamp_fusion), kind=kCustom, calls=%fused_computation | custom fusion | bytes 3670080 | tf_op jit(solution)/shard_map/jit(_take)/gather | solution.py:149
  67.3 16.0 %shard_map.73 = bf16[1024,896]{1,0:T(8,128)(2,1)} custom-call(bf16[1024,896]{1,0:T(8,128)(2,1)} %bitcast.39, f32[1,896]{1,0:T(1,128)} %reshape.54.gain_ref, bf16[4,896,896]{2,1,0:T(8,128)(2,1)} %constant_dynamic-update-slice_fusion.w_ref), custom_call_target="tpu_custom_call" | custom-call | tf_op jit(solution)/shard_map/pallas_call | solution.py:58
  83.3 0.0 copy-start
  83.3 9.2 %convert_bitcast_fusion.kt_ref = bf16[2048,1024]{1,0:T(8,128)(2,1)} fusion(bf16[1024,896]{1,0:T(8,128)(2,1)} %shard_map.73, bf16[2,896,2048]{2,1,0:T(8,128)(2,1)} %param.13), kind=kOutput, calls=%fused_computation.1 | convolution fusion | flops 3760193536 | bytes 9699328 | tf_op jit(solution)/shard_map/ef,re->fr/dot_general | solution.py:151
  92.5 0.0 copy-done
  92.5 8.1 %convolution_convert_fusion.v_ref = bf16[1024,2048]{1,0:T(8,128)(2,1)} fusion(bf16[1024,896]{1,0:T(8,128)(2,1)S(1)} %copy-done, bf16[2,896,2048]{2,1,0:T(8,128)(2,1)} %param.13), kind=kOutput, calls=%fused_computation.2 | convolution fusion | flops 3760193536 | bytes 9699328 | tf_op jit(solution)/shard_map/dot_general | solution.py:154
  100.6 8.2 %shard_map.74 = bf16[512,2048]{1,0:T(8,128)(2,1)} custom-call(bf16[512,2048]{1,0:T(8,128)(2,1)} %bitcast.40, bf16[2048,1024]{1,0:T(8,128)(2,1)} %convert_bitcast_fusion.kt_ref, bf16[1024,2048]{1,0:T(8,128)(2,1)} %convolution_convert_fusion.v_ref), custom_call_target="tpu_custom_call" | custom-call | tf_op jit(solution)/shard_map/pallas_call | solution.py:96
  (7 shorter events, 0.1 us)
Async XLA Ops:
  0.0 38.3 %collective-permute-start = (bf16[4,224,896]{2,1,0:T(8,128)(2,1)}, bf16[4,224,896]{2,1,0:T(8,128)(2,1)}, u32[]{:S(2)}, u32[]{:S(2)}) collective-permute-start(bf16[4,224,896]{2,1,0:T(8,128)(2,1)} %param.12), channel_id=1, source_target_pairs={{0,16},{8,24},{16,0},{24,8},{1,17},{9,25},{17,1},{25,9},{2,18},{10... | collective-permute-start | bytes 4816904 | tf_op jit(solution)/shard_map/ppermute | solution.py:116
  5.5 12.4 %all-to-all-start = ((s32[8,3,16]{2,1,0:T(4,128)}), s32[8,3,16]{2,1,0:T(4,128)S(1)}, u32[]{:S(2)}, u32[]{:S(2)}) async-start(s32[8,3,16]{2,1,0:T(4,128)} %broadcast_in_dim.74), calls=%async_computation | async-start | bytes 32768 | tf_op jit(solution)/shard_map/all_to_all | solution.py:139
  20.3 3.7 %copy-start.1 = (bf16[4,224,896]{2,1,0:T(8,128)(2,1)S(1)}, bf16[4,224,896]{2,1,0:T(8,128)(2,1)}, u32[]{:S(2)}) copy-start(bf16[4,224,896]{2,1,0:T(8,128)(2,1)} %param.12) | copy-start | bytes 4816900
  20.3 18.1 %copy-start.2 = (s32[1,8,2]{1,2,0:T(2,128)S(1)}, s32[1,8,2]{1,2,0:T(2,128)}, u32[]{:S(2)}) copy-start(s32[1,8,2]{1,2,0:T(2,128)} %param.9) | copy-start | bytes 196
  20.3 18.3 %copy-start.3 = (f32[896]{0:T(1024)S(1)}, f32[896]{0:T(1024)}, u32[]{:S(2)}) copy-start(f32[896]{0:T(1024)} %param.11) | copy-start | bytes 10756
  20.3 45.0 %all-to-all-start.1 = ((bf16[8,2,64,896]{3,2,1,0:T(8,128)(2,1)}), bf16[8,2,64,896]{3,2,1,0:T(8,128)(2,1)S(1)}, u32[]{:S(2)}, u32[]{:S(2)}) async-start(bf16[8,2,64,896]{3,2,1,0:T(8,128)(2,1)} %select_select_fusion), calls=%async_computation.1 | async-start | bytes 3670016 | tf_op jit(solution)/shard_map/all_to_all | solution.py:147
  24.0 22.3 %collective-permute-start.1 = (bf16[4,224,896]{2,1,0:T(8,128)(2,1)S(1)}, bf16[4,224,896]{2,1,0:T(8,128)(2,1)}, u32[]{:S(2)}, u32[]{:S(2)}) collective-permute-start(bf16[4,224,896]{2,1,0:T(8,128)(2,1)S(1)} %copy-done.1), channel_id=1, source_target_pairs={{0,8},{8,0},{16,24},{24,16},{1,9},{9,1},{17,25},{25,17},{2,10},{10... | collective-permute-start | bytes 4816904 | tf_op jit(solution)/shard_map/ppermute | solution.py:118
  38.3 10.7 %collective-permute-start.2 = (bf16[4,224,896]{2,1,0:T(8,128)(2,1)}, bf16[4,224,896]{2,1,0:T(8,128)(2,1)}, u32[]{:S(2)}, u32[]{:S(2)}) collective-permute-start(bf16[4,224,896]{2,1,0:T(8,128)(2,1)} %collective-permute-done), channel_id=1, source_target_pairs={{0,8},{8,0},{16,24},{24,16},{1,9},{9,1},{17,25},{25,17},{2,10},{10... | collective-permute-start | bytes 4816904 | tf_op jit(solution)/shard_map/ppermute | solution.py:118
  83.3 9.2 %copy-start = (bf16[1024,896]{1,0:T(8,128)(2,1)S(1)}, bf16[1024,896]{1,0:T(8,128)(2,1)}, u32[]{:S(2)}) copy-start(bf16[1024,896]{1,0:T(8,128)(2,1)} %shard_map.73) | copy-start | bytes 5505028

commit v16 on v11

--- a/solution.py
+++ b/solution.py
@@ -74,30 +74,28 @@
     )(flat, gain.reshape(1, width), attention)
 
 
-def _cross_kernel(qt_ref, kv_ref, out_ref):
+def _cross_kernel(qt_ref, k_ref, v_ref, out_ref):
     scale = HEAD_DIM ** (-0.5)
     spans, memory = 2 * SPAN, 2 * NEIGH * NLEN
     key_of = lax.broadcasted_iota(jnp.int32, (memory, spans), 0) // (NEIGH * NLEN)
     query_of = lax.broadcasted_iota(jnp.int32, (memory, spans), 1) // SPAN
     same = key_of == query_of
-    half = kv_ref.shape[-1] // 2
     for p in range(qt_ref.shape[-1] // spans):
         rq = pl.ds(p * spans, spans)
         rk = pl.ds(p * memory, memory)
-        for h in range(half // HEAD_DIM):
+        for h in range(k_ref.shape[-1] // HEAD_DIM):
             cols = pl.ds(h * HEAD_DIM, HEAD_DIM)
-            scores = jnp.dot(kv_ref[rk, cols], qt_ref[cols, rq], preferred_element_type=jnp.float32) * scale
+            scores = jnp.dot(k_ref[rk, cols], qt_ref[cols, rq], preferred_element_type=jnp.float32) * scale
             scores = jnp.where(same, scores, -jnp.inf)
             highest = jnp.max(scores, axis=0, keepdims=True)
             raised = jnp.exp(scores - highest)
             weights = (raised * (1.0 / jnp.sum(raised, axis=0, keepdims=True))).astype(jnp.bfloat16)
             out_ref[rq, cols] = lax.dot_general(
-                weights, kv_ref[rk, pl.ds(half + h * HEAD_DIM, HEAD_DIM)],
-                (((0,), (0,)), ((), ())), preferred_element_type=jnp.float32,
+                weights, v_ref[rk, cols], (((0,), (0,)), ((), ())), preferred_element_type=jnp.float32
             ).astype(jnp.bfloat16)
 
 
-def cross_attend(queries_t, keys_values, group=2):
+def cross_attend(queries_t, keys, values, group=2):
     width, length = queries_t.shape
     spans = 2 * SPAN
     memory = 2 * NEIGH * NLEN
@@ -108,10 +106,11 @@
         grid=(length // (spans * group),),
         in_specs=[
             pl.BlockSpec((width, spans * group), lambda c: (0, c)),
-            pl.BlockSpec((memory * group, 2 * width), lambda c: (c, 0)),
+            pl.BlockSpec((memory * group, width), lambda c: (c, 0)),
+            pl.BlockSpec((memory * group, width), lambda c: (c, 0)),
         ],
         out_specs=pl.BlockSpec((spans * group, width), lambda c: (c, 0)),
-    )(queries_t, keys_values)
+    )(queries_t, keys, values)
 
 
 def gather_weights(shard, n_dp):
@@ -154,9 +153,9 @@
         got = got.reshape(n_seq * per_owner, NLEN, neighbour_input.shape[-1])
         chosen_raw = jnp.take(got, owners * per_owner + rank, axis=0, mode="clip")
         chosen = encode_blocks(chosen_raw, enc_gain, full_weights)
-        both = jnp.concatenate([kv_weight[0], kv_weight[1]], axis=1)
-        keys_values = jnp.dot(chosen, both, preferred_element_type=jnp.float32).astype(jnp.bfloat16)
-        return cross_attend(queries[0].T, keys_values)[None]
+        keys = jnp.dot(chosen, kv_weight[0], preferred_element_type=jnp.float32).astype(jnp.bfloat16)
+        values = jnp.dot(chosen, kv_weight[1], preferred_element_type=jnp.float32).astype(jnp.bfloat16)
+        return cross_attend(queries[0].T, keys, values)[None]
 
     return shards
 

time: 113 us -> 108 us (0.956)
  local copies, waits for them, and re-layouts: 31.4 us -> 23.9 us
  matrix products: 14.5 us -> 17.3 us
    squeeze x1 -> x0, local copies, waits for them, and re-layouts: 7.55 us -> none  [shards(): both = jnp.concatenate([kv_weight[0], kv_weight[1]], axis=1)]
    dot_general x1 -> x2, matrix products: 14.5 us -> 17.3 us  [the longest x1 9.25 us: shards(): jnp.dot(chosen, kv_weight[1], preferred_element_type=jnp.float32)]
    unnamed x11 -> x13, local copies, waits for them, and re-layouts: 5.49 us -> 5.51 us
  transfers between devices with their start and end apart: 5 -> 5, of which waited for: 2 -> 2; matrix products, arithmetic and copies ran while one was open for 24% -> 18% of each run, Pallas kernels for 0% -> 0%
where the time goes in v16:
time: 108 us
  waiting for transfers between devices  29.3 us (27%)
  Pallas kernels  24.1 us (22%)
  local copies, waits for them, and re-layouts  23.9 us (22%)
  matrix products  17.3 us (16%)
  starting transfers between devices  12.4 us (11%)
    ppermute x1, waiting for transfers between devices, gather_weights(): lax.ppermute(shard, 'dp', ring)  24.2 us
    pallas_call x1, Pallas kernels, encode_blocks(): pl.pallas_call(_encoder_kernel, out_shape=jax.ShapeDtypeStruct(flat.shape...  16 us
    dynamic_update_slice x4, local copies, waits for them, and re-layouts, gather_weights(): full = lax.dynamic_update_slice(full, piece, (0, owner * rows, 0))  9.5 us
    dot_general x1, matrix products, shards(): jnp.dot(chosen, kv_weight[1], preferred_element_type=jnp.float32)  9.25 us
    dot_general x1, matrix products, shards(): jnp.dot(chosen, kv_weight[0], preferred_element_type=jnp.float32)  8.08 us
    pallas_call x1, Pallas kernels, cross_attend(): pl.pallas_call(_cross_kernel, out_shape=jax.ShapeDtypeStruct((length, wid...  8.07 us
    all_to_all x1, starting transfers between devices, shards(): asked = lax.all_to_all(asks, 'seq', 0, 0, tiled=True)  7.28 us
    unnamed x13, local copies, waits for them, and re-layouts  5.51 us
  transfers between devices with their start and end apart: 5, of which 2 were waited for; matrix products, arithmetic and copies ran while one was open for 18% of the time, Pallas kernels for 0%

profile of v16, /device:TPU:0, one launch (start us, length us, event | category | flops | bytes accessed | tf_op | source)
XLA Modules:
  0.0 107.5 jit_solution(1963910435092239652)
XLA Ops:
  0.0 0.0 copy-start
  0.0 0.8 copy.27
  0.8 0.1 eq.39
  0.9 0.1 stack_reshape.6
  1.0 0.2 convert_reduce_fusion
  1.2 0.8 copy.28
  1.9 0.1 stack_reshape.7
  2.0 0.6 broadcast_in_dim.35
  2.6 7.3 %all-to-all-start = ((s32[8,3,16]{2,1,0:T(4,128)}), s32[8,3,16]{2,1,0:T(4,128)S(1)}, u32[]{:S(2)}, u32[]{:S(2)}) async-start(s32[8,3,16]{2,1,0:T(4,128)} %broadcast_in_dim.35), calls=%async_computation | async-start | bytes 32768 | tf_op jit(solution)/shard_map/all_to_all | solution.py:146
  9.9 1.5 %collective-permute-start = (bf16[4,224,896]{2,1,0:T(8,128)(2,1)}, bf16[4,224,896]{2,1,0:T(8,128)(2,1)}, u32[]{:S(2)}, u32[]{:S(2)}) collective-permute-start(bf16[4,224,896]{2,1,0:T(8,128)(2,1)} %param.12), channel_id=1, source_target_pairs={{0,16},{8,24},{16,0},{24,8},{1,17},{9,25},{17,1},{25,9},{2,18},{10... | collective-permute-start | bytes 4816904 | tf_op jit(solution)/shard_map/ppermute | solution.py:123
  11.4 5.1 %all-to-all-done = s32[8,3,16]{2,1,0:T(4,128)S(1)} async-done(((s32[8,3,16]{2,1,0:T(4,128)}), s32[8,3,16]{2,1,0:T(4,128)S(1)}, u32[]{:S(2)}, u32[]{:S(2)}) %all-to-all-start) | async-done | bytes 1568 | tf_op jit(solution)/shard_map/all_to_all | solution.py:146
  16.5 0.1 select_reduce_fusion
  16.7 0.1 copy.33
  16.7 0.1 reshape.43
  16.8 0.0 copy-done
  16.8 0.0 copy-start.3
  16.9 0.0 copy-start.4
  16.9 2.0 %gather_fusion = bf16[16,64,896]{2,1,0:T(8,128)(2,1)} fusion(bf16[4,64,896]{2,1,0:T(8,128)(2,1)S(1)} %bitcast.32, s32[1024]{0:T(1024)S(1)} %pad_clamp_fusion.1), kind=kCustom, calls=%fused_computation | custom fusion | bytes 3670080 | tf_op jit(solution)/shard_map/jit(_take)/gather | solution.py:150
  18.9 3.6 %all-to-all-start.1 = ((bf16[8,2,64,896]{3,2,1,0:T(8,128)(2,1)}), bf16[8,2,64,896]{3,2,1,0:T(8,128)(2,1)S(1)}, u32[]{:S(2)}, u32[]{:S(2)}) async-start(bf16[8,2,64,896]{3,2,1,0:T(8,128)(2,1)} %bitcast.35), calls=%async_computation.1 | async-start | bytes 3670016 | tf_op jit(solution)/shard_map/all_to_all | solution.py:152
  22.5 0.1 collective-permute-start.1
  22.5 24.2 %collective-permute-done = bf16[4,224,896]{2,1,0:T(8,128)(2,1)} collective-permute-done((bf16[4,224,896]{2,1,0:T(8,128)(2,1)}, bf16[4,224,896]{2,1,0:T(8,128)(2,1)}, u32[]{:S(2)}, u32[]{:S(2)}) %collective-permute-start) | collective-permute-done | bytes 1605664 | tf_op jit(solution)/shard_map/ppermute | solution.py:123
  46.8 0.0 collective-permute-start.2
  46.8 0.0 copy-done.3
  46.8 0.1 copy.34
  46.9 0.1 mul.29
  47.0 0.0 copy-done.4
  47.0 0.6 reshape.40.gain_ref
  47.6 3.9 %copy.26 = bf16[1,512,2048]{1,2,0:T(8,128)(2,1)} copy(bf16[1,512,2048]{2,1,0:T(8,128)(2,1)} %param.7) | data formatting | bytes 4194304 | tf_op args[0]
  51.5 0.0 copy-start.2
  51.5 3.1 %broadcast_in_dim.40 = bf16[4,896,896]{2,1,0:T(8,128)(2,1)} broadcast(bf16[]{:T(256)} %constant.40.clone.1), dimensions={} | broadcast | bytes 6422530 | tf_op jit(solution)/shard_map/broadcast_in_dim | solution.py:127
  54.6 0.0 copy-done.2
  54.6 1.3 %constant_dynamic-update-slice_fusion.3 = bf16[4,896,896]{2,1,0:T(8,128)(2,1)} fusion(bf16[4,896,896]{2,1,0:T(8,128)(2,1)} %broadcast_in_dim.40, bf16[4,224,896]{2,1,0:T(8,128)(2,1)S(1)} %copy-done.2, s32[]{:T(128)S(6)} %select_n.32), kind=kLoop, calls=%fused_computation.21 | loop fusion | bytes 3211268 | tf_op jit(solution)/shard_map/dynamic_update_slice | solution.py:129
  55.9 2.7 %constant_dynamic-update-slice_fusion.2 = bf16[4,896,896]{2,1,0:T(8,128)(2,1)} fusion(bf16[4,896,896]{2,1,0:T(8,128)(2,1)} %constant_dynamic-update-slice_fusion.3, bf16[4,224,896]{2,1,0:T(8,128)(2,1)} %collective-permute-done, s32[]{:T(128)S(6)} %select_n.36), kind=kLoop, calls=%fused_computation.20 | loop fusion | bytes 3211268 | tf_op jit(solution)/shard_map/dynamic_update_slice | solution.py:129
  58.6 0.0 collective-permute-done.1
  58.6 2.7 %constant_dynamic-update-slice_fusion.1 = bf16[4,896,896]{2,1,0:T(8,128)(2,1)} fusion(bf16[4,896,896]{2,1,0:T(8,128)(2,1)} %constant_dynamic-update-slice_fusion.2, bf16[4,224,896]{2,1,0:T(8,128)(2,1)} %collective-permute-done.1, s32[]{:T(128)S(6)} %select_n.37), kind=kLoop, calls=%fused_computation.19 | loop fusion | bytes 3211268 | tf_op jit(solution)/shard_map/dynamic_update_slice | solution.py:129
  61.4 0.0 collective-permute-done.2
  61.4 2.7 %constant_dynamic-update-slice_fusion.w_ref = bf16[4,896,896]{2,1,0:T(8,128)(2,1)} fusion(bf16[4,896,896]{2,1,0:T(8,128)(2,1)} %constant_dynamic-update-slice_fusion.1, bf16[4,224,896]{2,1,0:T(8,128)(2,1)} %collective-permute-done.2, s32[]{:T(128)S(6)} %select_n.38), kind=kLoop, calls=%fused_computation.18 | loop fusion | bytes 3211268 | tf_op jit(solution)/shard_map/dynamic_update_slice | solution.py:129
  64.1 0.0 all-to-all-done.1
  64.1 2.0 %gather_fusion.1 = bf16[16,64,896]{2,1,0:T(8,128)(2,1)} fusion(bf16[16,64,896]{2,1,0:T(8,128)(2,1)S(1)} %bitcast.34, s32[1024]{0:T(1024)S(1)} %pad_clamp_fusion), kind=kCustom, calls=%fused_computation.1 | custom fusion | bytes 3670080 | tf_op jit(solution)/shard_map/jit(_take)/gather | solution.py:154
  66.1 16.0 %shard_map.73 = bf16[1024,896]{1,0:T(8,128)(2,1)} custom-call(bf16[1024,896]{1,0:T(8,128)(2,1)} %bitcast.36, f32[1,896]{1,0:T(1,128)} %reshape.40.gain_ref, bf16[4,896,896]{2,1,0:T(8,128)(2,1)} %constant_dynamic-update-slice_fusion.w_ref), custom_call_target="tpu_custom_call" | custom-call | tf_op jit(solution)/shard_map/pallas_call | solution.py:58
  82.1 0.0 copy-start.1
  82.1 9.3 %convolution_convert_fusion.v_ref = bf16[1024,2048]{1,0:T(8,128)(2,1)} fusion(bf16[1024,896]{1,0:T(8,128)(2,1)} %shard_map.73, bf16[2,896,2048]{2,1,0:T(8,128)(2,1)} %param.13), kind=kOutput, calls=%fused_computation.2 | convolution fusion | flops 3760193536 | bytes 9699328 | tf_op jit(solution)/shard_map/dot_general | solution.py:157
  91.4 0.0 copy-done.1
  91.4 8.1 %convolution_convert_fusion.1.k_ref = bf16[1024,2048]{1,0:T(8,128)(2,1)} fusion(bf16[1024,896]{1,0:T(8,128)(2,1)S(1)} %copy-done.1, bf16[2,896,2048]{2,1,0:T(8,128)(2,1)} %param.13), kind=kOutput, calls=%fused_computation.3 | convolution fusion | flops 3760193536 | bytes 9699328 | tf_op jit(solution)/shard_map/dot_general | solution.py:156
  99.5 8.1 %shard_map.74 = bf16[512,2048]{1,0:T(8,128)(2,1)} custom-call(bf16[2048,512]{1,0:T(8,128)(2,1)} %bitcast.33, bf16[1024,2048]{1,0:T(8,128)(2,1)} %convolution_convert_fusion.1.k_ref, bf16[1024,2048]{1,0:T(8,128)(2,1)} %convolution_convert_fusion.v_ref), custom_call_target="tpu_custom_call" | custom-call | tf_op jit(solution)/shard_map/pallas_call | solution.py:103
  (7 shorter events, 0.1 us)
Async XLA Ops:
  0.0 16.8 %copy-start = (bf16[1,4,64,896]{3,2,1,0:T(8,128)(2,1)S(1)}, bf16[1,4,64,896]{3,2,1,0:T(8,128)(2,1)}, u32[]{:S(2)}) copy-start(bf16[1,4,64,896]{3,2,1,0:T(8,128)(2,1)} %param.8) | copy-start | bytes 1376260
  2.6 13.9 %all-to-all-start = ((s32[8,3,16]{2,1,0:T(4,128)}), s32[8,3,16]{2,1,0:T(4,128)S(1)}, u32[]{:S(2)}, u32[]{:S(2)}) async-start(s32[8,3,16]{2,1,0:T(4,128)} %broadcast_in_dim.35), calls=%async_computation | async-start | bytes 32768 | tf_op jit(solution)/shard_map/all_to_all | solution.py:146
  9.9 36.9 %collective-permute-start = (bf16[4,224,896]{2,1,0:T(8,128)(2,1)}, bf16[4,224,896]{2,1,0:T(8,128)(2,1)}, u32[]{:S(2)}, u32[]{:S(2)}) collective-permute-start(bf16[4,224,896]{2,1,0:T(8,128)(2,1)} %param.12), channel_id=1, source_target_pairs={{0,16},{8,24},{16,0},{24,8},{1,17},{9,25},{17,1},{25,9},{2,18},{10... | collective-permute-start | bytes 4816904 | tf_op jit(solution)/shard_map/ppermute | solution.py:123
  16.8 29.9 %copy-start.3 = (s32[1,8,2]{1,2,0:T(2,128)S(1)}, s32[1,8,2]{1,2,0:T(2,128)}, u32[]{:S(2)}) copy-start(s32[1,8,2]{1,2,0:T(2,128)} %param.9) | copy-start | bytes 196
  16.9 30.1 %copy-start.4 = (f32[896]{0:T(1024)S(1)}, f32[896]{0:T(1024)}, u32[]{:S(2)}) copy-start(f32[896]{0:T(1024)} %param.11) | copy-start | bytes 10756
  18.9 45.3 %all-to-all-start.1 = ((bf16[8,2,64,896]{3,2,1,0:T(8,128)(2,1)}), bf16[8,2,64,896]{3,2,1,0:T(8,128)(2,1)S(1)}, u32[]{:S(2)}, u32[]{:S(2)}) async-start(bf16[8,2,64,896]{3,2,1,0:T(8,128)(2,1)} %bitcast.35), calls=%async_computation.1 | async-start | bytes 3670016 | tf_op jit(solution)/shard_map/all_to_all | solution.py:152
  22.5 36.2 %collective-permute-start.1 = (bf16[4,224,896]{2,1,0:T(8,128)(2,1)}, bf16[4,224,896]{2,1,0:T(8,128)(2,1)}, u32[]{:S(2)}, u32[]{:S(2)}) collective-permute-start(bf16[4,224,896]{2,1,0:T(8,128)(2,1)} %param.12), channel_id=1, source_target_pairs={{0,8},{8,0},{16,24},{24,16},{1,9},{9,1},{17,25},{25,17},{2,10},{10... | collective-permute-start | bytes 4816904 | tf_op jit(solution)/shard_map/ppermute | solution.py:125
  46.8 14.6 %collective-permute-start.2 = (bf16[4,224,896]{2,1,0:T(8,128)(2,1)}, bf16[4,224,896]{2,1,0:T(8,128)(2,1)}, u32[]{:S(2)}, u32[]{:S(2)}) collective-permute-start(bf16[4,224,896]{2,1,0:T(8,128)(2,1)} %collective-permute-done), channel_id=1, source_target_pairs={{0,8},{8,0},{16,24},{24,16},{1,9},{9,1},{17,25},{25,17},{2,10},{10... | collective-permute-start | bytes 4816904 | tf_op jit(solution)/shard_map/ppermute | solution.py:125
  51.5 3.1 %copy-start.2 = (bf16[4,224,896]{2,1,0:T(8,128)(2,1)S(1)}, bf16[4,224,896]{2,1,0:T(8,128)(2,1)}, u32[]{:S(2)}) copy-start(bf16[4,224,896]{2,1,0:T(8,128)(2,1)} %param.12) | copy-start | bytes 4816900
  82.1 9.3 %copy-start.1 = (bf16[1024,896]{1,0:T(8,128)(2,1)S(1)}, bf16[1024,896]{1,0:T(8,128)(2,1)}, u32[]{:S(2)}) copy-start(bf16[1024,896]{1,0:T(8,128)(2,1)} %shard_map.73) | copy-start | bytes 5505028

commit v17 on v13

--- a/solution.py
+++ b/solution.py
@@ -131,14 +131,14 @@
         indices = block_list.reshape(-1)
         refs = owners.shape[0]
         per_owner = -(-refs // n_seq)
-        asks = jnp.stack([owners, indices])
-        asks = jnp.broadcast_to(asks[None], (n_seq, 2, refs))
-        asked = lax.all_to_all(asks, "seq", 0, 0, tiled=True)
         earlier = jnp.arange(refs)[None, :] < jnp.arange(refs)[:, None]
 
         def rank_of(names):
             return jnp.sum((names[..., :, None] == names[..., None, :]) & earlier, axis=-1)
 
+        asks = jnp.concatenate([owner_list, block_list], axis=0)
+        asks = jnp.broadcast_to(asks[None], (n_seq,) + asks.shape)
+        asked = lax.all_to_all(asks, "seq", 0, 0, tiled=True).reshape(n_seq, 2, refs)
         rank = rank_of(owners).astype(jnp.int32)
         asked_rank = rank_of(asked[:, 0])
         slots = jnp.arange(per_owner, dtype=jnp.int32)

time: 109 us -> 108 us (level)
  local copies, waits for them, and re-layouts: 19.9 us -> 18.6 us
    unnamed x12, local copies, waits for them, and re-layouts: 1.53 us -> 0.18 us
where the time goes in v17:
time: 108 us
  waiting for transfers between devices  33.9 us (31%)
  Pallas kernels  24.3 us (22%)
  local copies, waits for them, and re-layouts  18.6 us (17%)
  matrix products  17.3 us (16%)
  starting transfers between devices  12.4 us (11%)
  other arithmetic  1.36 us (1%)
    pallas_call x1, Pallas kernels, encode_blocks(): pl.pallas_call(_encoder_kernel, out_shape=jax.ShapeDtypeStruct(flat.shape...  16 us
    ppermute x1, waiting for transfers between devices, gather_weights(): lax.ppermute(shard, 'dp', ring)  15.1 us
    all_to_all x1, waiting for transfers between devices, shards(): got = lax.all_to_all(sent, 'seq', 0, 0, tiled=True)  12.2 us
    dynamic_update_slice x4, local copies, waits for them, and re-layouts, gather_weights(): full = lax.dynamic_update_slice(full, piece, (0, owner * rows, 0))  9.49 us
    dot_general x1, matrix products, shards(): jnp.einsum('ef,re->fr', kv_weight[0], chosen, preferred_element_type=jnp....  9.21 us
    pallas_call x1, Pallas kernels, cross_attend(): pl.pallas_call(_cross_kernel, out_shape=jax.ShapeDtypeStruct(queries.shap...  8.25 us
    dot_general x1, matrix products, shards(): jnp.dot(chosen, kv_weight[1], preferred_element_type=jnp.float32)  8.06 us
    all_to_all x1, waiting for transfers between devices, shards(): lax.all_to_all(asks, 'seq', 0, 0, tiled=True).reshape(n_seq, 2, refs)  6.56 us
  transfers between devices with their start and end apart: 5, of which 3 were waited for; matrix products, arithmetic and copies ran while one was open for 17% of the time, Pallas kernels for 0%

profile of v17, /device:TPU:0, one launch (start us, length us, event | category | flops | bytes accessed | tf_op | source)
XLA Modules:
  0.0 107.9 jit_solution(14150504966699950226)
XLA Ops:
  0.0 0.0 copy-start
  0.0 2.9 %collective-permute-start = (bf16[4,224,896]{2,1,0:T(8,128)(2,1)}, bf16[4,224,896]{2,1,0:T(8,128)(2,1)}, u32[]{:S(2)}, u32[]{:S(2)}) collective-permute-start(bf16[4,224,896]{2,1,0:T(8,128)(2,1)} %param.12), channel_id=1, source_target_pairs={{0,16},{8,24},{16,0},{24,8},{1,17},{9,25},{17,1},{25,9},{2,18},{10... | collective-permute-start | bytes 4816904 | tf_op jit(solution)/shard_map/ppermute | solution.py:116
  2.9 0.7 pad_add_fusion
  3.6 0.6 broadcast_in_dim.37
  4.3 5.8 %all-to-all-start = ((s32[8,2,8,2]{2,3,1,0:T(2,128)}), s32[8,2,8,2]{2,3,1,0:T(2,128)S(1)}, u32[]{:S(2)}, u32[]{:S(2)}) async-start(s32[8,2,8,2]{2,3,1,0:T(2,128)} %broadcast_in_dim.37), calls=%async_computation | async-start | bytes 32768 | tf_op jit(solution)/shard_map/all_to_all | solution.py:141
  10.1 6.6 %all-to-all-done = s32[8,2,8,2]{2,3,1,0:T(2,128)S(1)} async-done(((s32[8,2,8,2]{2,3,1,0:T(2,128)}), s32[8,2,8,2]{2,3,1,0:T(2,128)S(1)}, u32[]{:S(2)}, u32[]{:S(2)}) %all-to-all-start) | async-done | bytes 1056 | tf_op jit(solution)/shard_map/all_to_all | solution.py:141
  16.7 0.1 copy.42
  16.8 0.1 copy.50
  16.8 0.1 copy.44
  16.9 0.3 convert_reduce_fusion
  17.2 0.2 select_reduce_fusion
  17.3 0.1 copy.45
  17.4 0.1 reshape.61
  17.5 0.0 copy-done
  17.5 0.0 copy-start.3
  17.5 0.0 copy-start.4
  17.6 2.0 %gather_fusion = bf16[16,64,896]{2,1,0:T(8,128)(2,1)} fusion(bf16[4,64,896]{2,1,0:T(8,128)(2,1)S(1)} %bitcast.27, s32[1024]{0:T(1024)S(1)} %pad_clamp_fusion.1), kind=kCustom, calls=%fused_computation | custom fusion | bytes 3670080 | tf_op jit(solution)/shard_map/jit(_take)/gather | solution.py:147
  19.5 3.6 %all-to-all-start.1 = ((bf16[8,2,64,896]{3,2,1,0:T(8,128)(2,1)}), bf16[8,2,64,896]{3,2,1,0:T(8,128)(2,1)S(1)}, u32[]{:S(2)}, u32[]{:S(2)}) async-start(bf16[8,2,64,896]{3,2,1,0:T(8,128)(2,1)} %bitcast.29), calls=%async_computation.1 | async-start | bytes 3670016 | tf_op jit(solution)/shard_map/all_to_all | solution.py:149
  23.1 0.1 collective-permute-start.1
  23.2 15.1 %collective-permute-done = bf16[4,224,896]{2,1,0:T(8,128)(2,1)} collective-permute-done((bf16[4,224,896]{2,1,0:T(8,128)(2,1)}, bf16[4,224,896]{2,1,0:T(8,128)(2,1)}, u32[]{:S(2)}, u32[]{:S(2)}) %collective-permute-start) | collective-permute-done | bytes 1605664 | tf_op jit(solution)/shard_map/ppermute | solution.py:116
  38.4 0.0 collective-permute-start.2
  38.4 0.0 copy-done.3
  38.4 0.1 copy.47
  38.4 0.1 copy.46
  38.5 0.1 mul.29
  38.6 0.1 eq.61
  38.7 0.0 copy-done.4
  38.7 0.6 reshape.58.gain_ref
  39.3 0.0 copy-start.2
  39.3 0.2 convert_reduce_fusion.1
  39.5 3.2 %broadcast_in_dim.42 = bf16[4,896,896]{2,1,0:T(8,128)(2,1)} broadcast(bf16[]{:T(256)} %constant.40.clone.1), dimensions={} | broadcast | bytes 6422530 | tf_op jit(solution)/shard_map/broadcast_in_dim | solution.py:120
  42.7 0.0 copy-done.2
  42.7 1.3 %constant_dynamic-update-slice_fusion.3 = bf16[4,896,896]{2,1,0:T(8,128)(2,1)} fusion(bf16[4,896,896]{2,1,0:T(8,128)(2,1)} %broadcast_in_dim.42, bf16[4,224,896]{2,1,0:T(8,128)(2,1)S(1)} %copy-done.2, s32[]{:T(128)S(6)} %select_n.32), kind=kLoop, calls=%fused_computation.21 | loop fusion | bytes 3211268 | tf_op jit(solution)/shard_map/dynamic_update_slice | solution.py:122
  44.0 2.8 %constant_dynamic-update-slice_fusion.2 = bf16[4,896,896]{2,1,0:T(8,128)(2,1)} fusion(bf16[4,896,896]{2,1,0:T(8,128)(2,1)} %constant_dynamic-update-slice_fusion.3, bf16[4,224,896]{2,1,0:T(8,128)(2,1)} %collective-permute-done, s32[]{:T(128)S(6)} %select_n.36), kind=kLoop, calls=%fused_computation.20 | loop fusion | bytes 3211268 | tf_op jit(solution)/shard_map/dynamic_update_slice | solution.py:122
  46.7 0.0 collective-permute-done.1
  46.7 2.7 %constant_dynamic-update-slice_fusion.1 = bf16[4,896,896]{2,1,0:T(8,128)(2,1)} fusion(bf16[4,896,896]{2,1,0:T(8,128)(2,1)} %constant_dynamic-update-slice_fusion.2, bf16[4,224,896]{2,1,0:T(8,128)(2,1)} %collective-permute-done.1, s32[]{:T(128)S(6)} %select_n.37), kind=kLoop, calls=%fused_computation.19 | loop fusion | bytes 3211268 | tf_op jit(solution)/shard_map/dynamic_update_slice | solution.py:122
  49.5 0.0 collective-permute-done.2
  49.5 2.7 %constant_dynamic-update-slice_fusion.w_ref = bf16[4,896,896]{2,1,0:T(8,128)(2,1)} fusion(bf16[4,896,896]{2,1,0:T(8,128)(2,1)} %constant_dynamic-update-slice_fusion.1, bf16[4,224,896]{2,1,0:T(8,128)(2,1)} %collective-permute-done.2, s32[]{:T(128)S(6)} %select_n.38), kind=kLoop, calls=%fused_computation.18 | loop fusion | bytes 3211268 | tf_op jit(solution)/shard_map/dynamic_update_slice | solution.py:122
  52.2 12.2 %all-to-all-done.1 = bf16[8,2,64,896]{3,2,1,0:T(8,128)(2,1)S(1)} async-done(((bf16[8,2,64,896]{3,2,1,0:T(8,128)(2,1)}), bf16[8,2,64,896]{3,2,1,0:T(8,128)(2,1)S(1)}, u32[]{:S(2)}, u32[]{:S(2)}) %all-to-all-start.1) | async-done | bytes 1835040 | tf_op jit(solution)/shard_map/all_to_all | solution.py:149
  64.4 2.0 %gather_fusion.1 = bf16[16,64,896]{2,1,0:T(8,128)(2,1)} fusion(bf16[16,64,896]{2,1,0:T(8,128)(2,1)S(1)} %bitcast.28, s32[1024]{0:T(1024)S(1)} %pad_clamp_fusion), kind=kCustom, calls=%fused_computation.1 | custom fusion | bytes 3670080 | tf_op jit(solution)/shard_map/jit(_take)/gather | solution.py:151
  66.4 16.0 %shard_map.73 = bf16[1024,896]{1,0:T(8,128)(2,1)} custom-call(bf16[1024,896]{1,0:T(8,128)(2,1)} %bitcast.30, f32[1,896]{1,0:T(1,128)} %reshape.58.gain_ref, bf16[4,896,896]{2,1,0:T(8,128)(2,1)} %constant_dynamic-update-slice_fusion.w_ref), custom_call_target="tpu_custom_call" | custom-call | tf_op jit(solution)/shard_map/pallas_call | solution.py:58
  82.4 0.0 copy-start.1
  82.4 9.2 %convert_bitcast_fusion.kt_ref = bf16[2048,1024]{1,0:T(8,128)(2,1)} fusion(bf16[1024,896]{1,0:T(8,128)(2,1)} %shard_map.73, bf16[2,896,2048]{2,1,0:T(8,128)(2,1)} %param.13), kind=kOutput, calls=%fused_computation.2 | convolution fusion | flops 3760193536 | bytes 9699328 | tf_op jit(solution)/shard_map/ef,re->fr/dot_general | solution.py:153
  91.6 0.0 copy-done.1
  91.6 8.1 %convolution_convert_fusion.v_ref = bf16[1024,2048]{1,0:T(8,128)(2,1)} fusion(bf16[1024,896]{1,0:T(8,128)(2,1)S(1)} %copy-done.1, bf16[2,896,2048]{2,1,0:T(8,128)(2,1)} %param.13), kind=kOutput, calls=%fused_computation.3 | convolution fusion | flops 3760193536 | bytes 9699328 | tf_op jit(solution)/shard_map/dot_general | solution.py:156
  99.7 8.2 %shard_map.74 = bf16[512,2048]{1,0:T(8,128)(2,1)} custom-call(bf16[512,2048]{1,0:T(8,128)(2,1)} %bitcast.31, bf16[2048,1024]{1,0:T(8,128)(2,1)} %convert_bitcast_fusion.kt_ref, bf16[1024,2048]{1,0:T(8,128)(2,1)} %convolution_convert_fusion.v_ref), custom_call_target="tpu_custom_call" | custom-call | tf_op jit(solution)/shard_map/pallas_call | solution.py:96
  (7 shorter events, 0.0 us)
Async XLA Ops:
  0.0 17.5 %copy-start = (bf16[1,4,64,896]{3,2,1,0:T(8,128)(2,1)S(1)}, bf16[1,4,64,896]{3,2,1,0:T(8,128)(2,1)}, u32[]{:S(2)}) copy-start(bf16[1,4,64,896]{3,2,1,0:T(8,128)(2,1)} %param.8) | copy-start | bytes 1376260
  0.0 38.3 %collective-permute-start = (bf16[4,224,896]{2,1,0:T(8,128)(2,1)}, bf16[4,224,896]{2,1,0:T(8,128)(2,1)}, u32[]{:S(2)}, u32[]{:S(2)}) collective-permute-start(bf16[4,224,896]{2,1,0:T(8,128)(2,1)} %param.12), channel_id=1, source_target_pairs={{0,16},{8,24},{16,0},{24,8},{1,17},{9,25},{17,1},{25,9},{2,18},{10... | collective-permute-start | bytes 4816904 | tf_op jit(solution)/shard_map/ppermute | solution.py:116
  4.3 12.4 %all-to-all-start = ((s32[8,2,8,2]{2,3,1,0:T(2,128)}), s32[8,2,8,2]{2,3,1,0:T(2,128)S(1)}, u32[]{:S(2)}, u32[]{:S(2)}) async-start(s32[8,2,8,2]{2,3,1,0:T(2,128)} %broadcast_in_dim.37), calls=%async_computation | async-start | bytes 32768 | tf_op jit(solution)/shard_map/all_to_all | solution.py:141
  17.5 20.8 %copy-start.3 = (s32[1,8,2]{1,2,0:T(2,128)S(1)}, s32[1,8,2]{1,2,0:T(2,128)}, u32[]{:S(2)}) copy-start(s32[1,8,2]{1,2,0:T(2,128)} %param.9) | copy-start | bytes 196
  17.5 21.1 %copy-start.4 = (f32[896]{0:T(1024)S(1)}, f32[896]{0:T(1024)}, u32[]{:S(2)}) copy-start(f32[896]{0:T(1024)} %param.11) | copy-start | bytes 10756
  19.5 44.9 %all-to-all-start.1 = ((bf16[8,2,64,896]{3,2,1,0:T(8,128)(2,1)}), bf16[8,2,64,896]{3,2,1,0:T(8,128)(2,1)S(1)}, u32[]{:S(2)}, u32[]{:S(2)}) async-start(bf16[8,2,64,896]{3,2,1,0:T(8,128)(2,1)} %bitcast.29), calls=%async_computation.1 | async-start | bytes 3670016 | tf_op jit(solution)/shard_map/all_to_all | solution.py:149
  23.1 23.6 %collective-permute-start.1 = (bf16[4,224,896]{2,1,0:T(8,128)(2,1)}, bf16[4,224,896]{2,1,0:T(8,128)(2,1)}, u32[]{:S(2)}, u32[]{:S(2)}) collective-permute-start(bf16[4,224,896]{2,1,0:T(8,128)(2,1)} %param.12), channel_id=1, source_target_pairs={{0,8},{8,0},{16,24},{24,16},{1,9},{9,1},{17,25},{25,17},{2,10},{10... | collective-permute-start | bytes 4816904 | tf_op jit(solution)/shard_map/ppermute | solution.py:118
  38.4 11.1 %collective-permute-start.2 = (bf16[4,224,896]{2,1,0:T(8,128)(2,1)}, bf16[4,224,896]{2,1,0:T(8,128)(2,1)}, u32[]{:S(2)}, u32[]{:S(2)}) collective-permute-start(bf16[4,224,896]{2,1,0:T(8,128)(2,1)} %collective-permute-done), channel_id=1, source_target_pairs={{0,8},{8,0},{16,24},{24,16},{1,9},{9,1},{17,25},{25,17},{2,10},{10... | collective-permute-start | bytes 4816904 | tf_op jit(solution)/shard_map/ppermute | solution.py:118
  39.3 3.4 %copy-start.2 = (bf16[4,224,896]{2,1,0:T(8,128)(2,1)S(1)}, bf16[4,224,896]{2,1,0:T(8,128)(2,1)}, u32[]{:S(2)}) copy-start(bf16[4,224,896]{2,1,0:T(8,128)(2,1)} %param.12) | copy-start | bytes 4816900
  82.4 9.2 %copy-start.1 = (bf16[1024,896]{1,0:T(8,128)(2,1)S(1)}, bf16[1024,896]{1,0:T(8,128)(2,1)}, u32[]{:S(2)}) copy-start(bf16[1024,896]{1,0:T(8,128)(2,1)} %shard_map.73) | copy-start | bytes 5505028

commit v18 on v8

--- a/solution.py
+++ b/solution.py
@@ -29,7 +29,7 @@
     normed = (inputs * lax.rsqrt(spread + epsilon) * gain_ref[...]).astype(jnp.bfloat16)
     q_ref[...] = jnp.dot(normed, w_ref[0], preferred_element_type=jnp.float32).astype(jnp.bfloat16)
     v_ref[...] = jnp.dot(normed, w_ref[2], preferred_element_type=jnp.float32).astype(jnp.bfloat16)
-    kt_ref[...] = jnp.dot(normed, w_ref[1], preferred_element_type=jnp.float32).T.astype(jnp.bfloat16)
+    kt_ref[...] = jnp.dot(normed, w_ref[1], preferred_element_type=jnp.float32).astype(jnp.bfloat16).T
     width = inputs.shape[-1]
     head_size = width // ENC_HEADS
     scale = head_size ** (-0.5)

time: 108 us -> 108 us (level)
  no operation moved by 1% of the time
where the time goes in v18:
time: 108 us; the launch traced here: 107 us
  waiting for transfers between devices  33 us (31%)
  Pallas kernels  24.1 us (22%)
  local copies, waits for them, and re-layouts  20 us (19%)
  matrix products  17.3 us (16%)
  starting transfers between devices  12.4 us (11%)
    ppermute x1, waiting for transfers between devices, gather_weights(): lax.ppermute(shard, 'dp', ring)  24.2 us
    pallas_call x1, Pallas kernels, encode_blocks(): pl.pallas_call(_encoder_kernel, out_shape=jax.ShapeDtypeStruct(flat.shape...  15.9 us
    dynamic_update_slice x4, local copies, waits for them, and re-layouts, gather_weights(): full = lax.dynamic_update_slice(full, piece, (0, owner * rows, 0))  9.45 us
    dot_general x1, matrix products, shards(): jnp.einsum('ef,re->fr', kv_weight[0], chosen, preferred_element_type=jnp....  9.22 us
    pallas_call x1, Pallas kernels, cross_attend(): pl.pallas_call(_cross_kernel, out_shape=jax.ShapeDtypeStruct(queries.shap...  8.25 us
    dot_general x1, matrix products, shards(): jnp.dot(chosen, kv_weight[1], preferred_element_type=jnp.float32)  8.08 us
    all_to_all x1, starting transfers between devices, shards(): asked = lax.all_to_all(asks, 'seq', 0, 0, tiled=True)  7.28 us
    all_to_all x1, waiting for transfers between devices, shards(): asked = lax.all_to_all(asks, 'seq', 0, 0, tiled=True)  5.08 us
  transfers between devices with their start and end apart: 5, of which 3 were waited for; matrix products, arithmetic and copies ran while one was open for 15% of the time, Pallas kernels for 0%

profile of v18, /device:TPU:0, one launch (start us, length us, event | category | flops | bytes accessed | tf_op | source)
XLA Modules:
  0.0 107.3 jit_solution(13427667906566525697)
XLA Ops:
  0.0 0.0 copy-start
  0.0 0.8 copy.26
  0.8 0.1 eq.39
  0.9 0.1 stack_reshape.6
  1.0 0.2 convert_reduce_fusion
  1.2 0.8 copy.27
  1.9 0.1 stack_reshape.7
  2.0 0.6 broadcast_in_dim.35
  2.6 7.3 %all-to-all-start = ((s32[8,3,16]{2,1,0:T(4,128)}), s32[8,3,16]{2,1,0:T(4,128)S(1)}, u32[]{:S(2)}, u32[]{:S(2)}) async-start(s32[8,3,16]{2,1,0:T(4,128)} %broadcast_in_dim.35), calls=%async_computation | async-start | bytes 32768 | tf_op jit(solution)/shard_map/all_to_all | solution.py:139
  9.9 1.5 %collective-permute-start = (bf16[4,224,896]{2,1,0:T(8,128)(2,1)}, bf16[4,224,896]{2,1,0:T(8,128)(2,1)}, u32[]{:S(2)}, u32[]{:S(2)}) collective-permute-start(bf16[4,224,896]{2,1,0:T(8,128)(2,1)} %param.12), channel_id=1, source_target_pairs={{0,16},{8,24},{16,0},{24,8},{1,17},{9,25},{17,1},{25,9},{2,18},{10... | collective-permute-start | bytes 4816904 | tf_op jit(solution)/shard_map/ppermute | solution.py:116
  11.4 5.1 %all-to-all-done = s32[8,3,16]{2,1,0:T(4,128)S(1)} async-done(((s32[8,3,16]{2,1,0:T(4,128)}), s32[8,3,16]{2,1,0:T(4,128)S(1)}, u32[]{:S(2)}, u32[]{:S(2)}) %all-to-all-start) | async-done | bytes 1568 | tf_op jit(solution)/shard_map/all_to_all | solution.py:139
  16.5 0.1 select_reduce_fusion
  16.7 0.1 copy.32
  16.7 0.1 reshape.43
  16.8 0.0 copy-done
  16.8 0.0 copy-start.3
  16.9 0.0 copy-start.4
  16.9 2.0 %gather_fusion = bf16[16,64,896]{2,1,0:T(8,128)(2,1)} fusion(bf16[4,64,896]{2,1,0:T(8,128)(2,1)S(1)} %bitcast.32, s32[1024]{0:T(1024)S(1)} %pad_clamp_fusion.1), kind=kCustom, calls=%fused_computation | custom fusion | bytes 3670080 | tf_op jit(solution)/shard_map/jit(_take)/gather | solution.py:143
  18.9 3.6 %all-to-all-start.1 = ((bf16[8,2,64,896]{3,2,1,0:T(8,128)(2,1)}), bf16[8,2,64,896]{3,2,1,0:T(8,128)(2,1)S(1)}, u32[]{:S(2)}, u32[]{:S(2)}) async-start(bf16[8,2,64,896]{3,2,1,0:T(8,128)(2,1)} %bitcast.34), calls=%async_computation.1 | async-start | bytes 3670016 | tf_op jit(solution)/shard_map/all_to_all | solution.py:145
  22.5 0.1 collective-permute-start.1
  22.5 24.2 %collective-permute-done = bf16[4,224,896]{2,1,0:T(8,128)(2,1)} collective-permute-done((bf16[4,224,896]{2,1,0:T(8,128)(2,1)}, bf16[4,224,896]{2,1,0:T(8,128)(2,1)}, u32[]{:S(2)}, u32[]{:S(2)}) %collective-permute-start) | collective-permute-done | bytes 1605664 | tf_op jit(solution)/shard_map/ppermute | solution.py:116
  46.8 0.0 collective-permute-start.2
  46.8 0.0 copy-done.3
  46.8 0.1 copy.33
  46.9 0.1 mul.29
  47.0 0.0 copy-done.4
  47.0 0.6 reshape.40.gain_ref
  47.6 0.0 copy-start.2
  47.6 3.2 %broadcast_in_dim.40 = bf16[4,896,896]{2,1,0:T(8,128)(2,1)} broadcast(bf16[]{:T(256)} %constant.40.clone.1), dimensions={} | broadcast | bytes 6422530 | tf_op jit(solution)/shard_map/broadcast_in_dim | solution.py:120
  50.7 0.0 copy-done.2
  50.7 1.3 %constant_dynamic-update-slice_fusion.3 = bf16[4,896,896]{2,1,0:T(8,128)(2,1)} fusion(bf16[4,896,896]{2,1,0:T(8,128)(2,1)} %broadcast_in_dim.40, bf16[4,224,896]{2,1,0:T(8,128)(2,1)S(1)} %copy-done.2, s32[]{:T(128)S(6)} %select_n.32), kind=kLoop, calls=%fused_computation.21 | loop fusion | bytes 3211268 | tf_op jit(solution)/shard_map/dynamic_update_slice | solution.py:122
  52.0 2.7 %constant_dynamic-update-slice_fusion.2 = bf16[4,896,896]{2,1,0:T(8,128)(2,1)} fusion(bf16[4,896,896]{2,1,0:T(8,128)(2,1)} %constant_dynamic-update-slice_fusion.3, bf16[4,224,896]{2,1,0:T(8,128)(2,1)} %collective-permute-done, s32[]{:T(128)S(6)} %select_n.36), kind=kLoop, calls=%fused_computation.20 | loop fusion | bytes 3211268 | tf_op jit(solution)/shard_map/dynamic_update_slice | solution.py:122
  54.8 0.0 collective-permute-done.1
  54.8 2.7 %constant_dynamic-update-slice_fusion.1 = bf16[4,896,896]{2,1,0:T(8,128)(2,1)} fusion(bf16[4,896,896]{2,1,0:T(8,128)(2,1)} %constant_dynamic-update-slice_fusion.2, bf16[4,224,896]{2,1,0:T(8,128)(2,1)} %collective-permute-done.1, s32[]{:T(128)S(6)} %select_n.37), kind=kLoop, calls=%fused_computation.19 | loop fusion | bytes 3211268 | tf_op jit(solution)/shard_map/dynamic_update_slice | solution.py:122
  57.5 0.0 collective-permute-done.2
  57.5 2.7 %constant_dynamic-update-slice_fusion.w_ref = bf16[4,896,896]{2,1,0:T(8,128)(2,1)} fusion(bf16[4,896,896]{2,1,0:T(8,128)(2,1)} %constant_dynamic-update-slice_fusion.1, bf16[4,224,896]{2,1,0:T(8,128)(2,1)} %collective-permute-done.2, s32[]{:T(128)S(6)} %select_n.38), kind=kLoop, calls=%fused_computation.18 | loop fusion | bytes 3211268 | tf_op jit(solution)/shard_map/dynamic_update_slice | solution.py:122
  60.2 3.7 %all-to-all-done.1 = bf16[8,2,64,896]{3,2,1,0:T(8,128)(2,1)S(1)} async-done(((bf16[8,2,64,896]{3,2,1,0:T(8,128)(2,1)}), bf16[8,2,64,896]{3,2,1,0:T(8,128)(2,1)S(1)}, u32[]{:S(2)}, u32[]{:S(2)}) %all-to-all-start.1) | async-done | bytes 1835040 | tf_op jit(solution)/shard_map/all_to_all | solution.py:145
  63.9 2.0 %gather_fusion.1 = bf16[16,64,896]{2,1,0:T(8,128)(2,1)} fusion(bf16[16,64,896]{2,1,0:T(8,128)(2,1)S(1)} %bitcast.33, s32[1024]{0:T(1024)S(1)} %pad_clamp_fusion), kind=kCustom, calls=%fused_computation.1 | custom fusion | bytes 3670080 | tf_op jit(solution)/shard_map/jit(_take)/gather | solution.py:147
  65.8 15.9 %shard_map.73 = bf16[1024,896]{1,0:T(8,128)(2,1)} custom-call(bf16[1024,896]{1,0:T(8,128)(2,1)} %bitcast.35, f32[1,896]{1,0:T(1,128)} %reshape.40.gain_ref, bf16[4,896,896]{2,1,0:T(8,128)(2,1)} %constant_dynamic-update-slice_fusion.w_ref), custom_call_target="tpu_custom_call" | custom-call | tf_op jit(solution)/shard_map/pallas_call | solution.py:58
  81.7 0.0 copy-start.1
  81.7 9.2 %convert_bitcast_fusion.kt_ref = bf16[2048,1024]{1,0:T(8,128)(2,1)} fusion(bf16[1024,896]{1,0:T(8,128)(2,1)} %shard_map.73, bf16[2,896,2048]{2,1,0:T(8,128)(2,1)} %param.13), kind=kOutput, calls=%fused_computation.2 | convolution fusion | flops 3760193536 | bytes 9699328 | tf_op jit(solution)/shard_map/ef,re->fr/dot_general | solution.py:149
  90.9 0.0 copy-done.1
  90.9 8.1 %convolution_convert_fusion.v_ref = bf16[1024,2048]{1,0:T(8,128)(2,1)} fusion(bf16[1024,896]{1,0:T(8,128)(2,1)S(1)} %copy-done.1, bf16[2,896,2048]{2,1,0:T(8,128)(2,1)} %param.13), kind=kOutput, calls=%fused_computation.3 | convolution fusion | flops 3760193536 | bytes 9699328 | tf_op jit(solution)/shard_map/dot_general | solution.py:152
  99.0 8.2 %shard_map.74 = bf16[512,2048]{1,0:T(8,128)(2,1)} custom-call(bf16[512,2048]{1,0:T(8,128)(2,1)} %bitcast.36, bf16[2048,1024]{1,0:T(8,128)(2,1)} %convert_bitcast_fusion.kt_ref, bf16[1024,2048]{1,0:T(8,128)(2,1)} %convolution_convert_fusion.v_ref), custom_call_target="tpu_custom_call" | custom-call | tf_op jit(solution)/shard_map/pallas_call | solution.py:96
  (7 shorter events, 0.1 us)
Async XLA Ops:
  0.0 16.8 %copy-start = (bf16[1,4,64,896]{3,2,1,0:T(8,128)(2,1)S(1)}, bf16[1,4,64,896]{3,2,1,0:T(8,128)(2,1)}, u32[]{:S(2)}) copy-start(bf16[1,4,64,896]{3,2,1,0:T(8,128)(2,1)} %param.8) | copy-start | bytes 1376260
  2.6 13.9 %all-to-all-start = ((s32[8,3,16]{2,1,0:T(4,128)}), s32[8,3,16]{2,1,0:T(4,128)S(1)}, u32[]{:S(2)}, u32[]{:S(2)}) async-start(s32[8,3,16]{2,1,0:T(4,128)} %broadcast_in_dim.35), calls=%async_computation | async-start | bytes 32768 | tf_op jit(solution)/shard_map/all_to_all | solution.py:139
  9.9 36.9 %collective-permute-start = (bf16[4,224,896]{2,1,0:T(8,128)(2,1)}, bf16[4,224,896]{2,1,0:T(8,128)(2,1)}, u32[]{:S(2)}, u32[]{:S(2)}) collective-permute-start(bf16[4,224,896]{2,1,0:T(8,128)(2,1)} %param.12), channel_id=1, source_target_pairs={{0,16},{8,24},{16,0},{24,8},{1,17},{9,25},{17,1},{25,9},{2,18},{10... | collective-permute-start | bytes 4816904 | tf_op jit(solution)/shard_map/ppermute | solution.py:116
  16.8 29.9 %copy-start.3 = (s32[1,8,2]{1,2,0:T(2,128)S(1)}, s32[1,8,2]{1,2,0:T(2,128)}, u32[]{:S(2)}) copy-start(s32[1,8,2]{1,2,0:T(2,128)} %param.9) | copy-start | bytes 196
  16.9 30.1 %copy-start.4 = (f32[896]{0:T(1024)S(1)}, f32[896]{0:T(1024)}, u32[]{:S(2)}) copy-start(f32[896]{0:T(1024)} %param.11) | copy-start | bytes 10756
  18.9 45.0 %all-to-all-start.1 = ((bf16[8,2,64,896]{3,2,1,0:T(8,128)(2,1)}), bf16[8,2,64,896]{3,2,1,0:T(8,128)(2,1)S(1)}, u32[]{:S(2)}, u32[]{:S(2)}) async-start(bf16[8,2,64,896]{3,2,1,0:T(8,128)(2,1)} %bitcast.34), calls=%async_computation.1 | async-start | bytes 3670016 | tf_op jit(solution)/shard_map/all_to_all | solution.py:145
  22.5 32.3 %collective-permute-start.1 = (bf16[4,224,896]{2,1,0:T(8,128)(2,1)}, bf16[4,224,896]{2,1,0:T(8,128)(2,1)}, u32[]{:S(2)}, u32[]{:S(2)}) collective-permute-start(bf16[4,224,896]{2,1,0:T(8,128)(2,1)} %param.12), channel_id=1, source_target_pairs={{0,8},{8,0},{16,24},{24,16},{1,9},{9,1},{17,25},{25,17},{2,10},{10... | collective-permute-start | bytes 4816904 | tf_op jit(solution)/shard_map/ppermute | solution.py:118
  46.8 10.7 %collective-permute-start.2 = (bf16[4,224,896]{2,1,0:T(8,128)(2,1)}, bf16[4,224,896]{2,1,0:T(8,128)(2,1)}, u32[]{:S(2)}, u32[]{:S(2)}) collective-permute-start(bf16[4,224,896]{2,1,0:T(8,128)(2,1)} %collective-permute-done), channel_id=1, source_target_pairs={{0,8},{8,0},{16,24},{24,16},{1,9},{9,1},{17,25},{25,17},{2,10},{10... | collective-permute-start | bytes 4816904 | tf_op jit(solution)/shard_map/ppermute | solution.py:118
  47.6 3.2 %copy-start.2 = (bf16[4,224,896]{2,1,0:T(8,128)(2,1)S(1)}, bf16[4,224,896]{2,1,0:T(8,128)(2,1)}, u32[]{:S(2)}) copy-start(bf16[4,224,896]{2,1,0:T(8,128)(2,1)} %param.12) | copy-start | bytes 4816900
  81.7 9.2 %copy-start.1 = (bf16[1024,896]{1,0:T(8,128)(2,1)S(1)}, bf16[1024,896]{1,0:T(8,128)(2,1)}, u32[]{:S(2)}) copy-start(bf16[1024,896]{1,0:T(8,128)(2,1)} %shard_map.73) | copy-start | bytes 5505028

commit v19 on v16

--- a/solution.py
+++ b/solution.py
@@ -29,7 +29,7 @@
     normed = (inputs * lax.rsqrt(spread + epsilon) * gain_ref[...]).astype(jnp.bfloat16)
     q_ref[...] = jnp.dot(normed, w_ref[0], preferred_element_type=jnp.float32).astype(jnp.bfloat16)
     v_ref[...] = jnp.dot(normed, w_ref[2], preferred_element_type=jnp.float32).astype(jnp.bfloat16)
-    kt_ref[...] = jnp.dot(normed, w_ref[1], preferred_element_type=jnp.float32).T.astype(jnp.bfloat16)
+    kt_ref[...] = jnp.dot(normed, w_ref[1], preferred_element_type=jnp.float32).astype(jnp.bfloat16).T
     width = inputs.shape[-1]
     head_size = width // ENC_HEADS
     scale = head_size ** (-0.5)
@@ -74,43 +74,57 @@
     )(flat, gain.reshape(1, width), attention)
 
 
-def _cross_kernel(qt_ref, k_ref, v_ref, out_ref):
+def _cross_kernel(slot_ref, qt_ref, *refs):
+    count = (len(refs) - 1) // 2
+    k_refs, v_refs, out_ref = refs[:count], refs[count:2 * count], refs[-1]
     scale = HEAD_DIM ** (-0.5)
     spans, memory = 2 * SPAN, 2 * NEIGH * NLEN
     key_of = lax.broadcasted_iota(jnp.int32, (memory, spans), 0) // (NEIGH * NLEN)
     query_of = lax.broadcasted_iota(jnp.int32, (memory, spans), 1) // SPAN
     same = key_of == query_of
-    for p in range(qt_ref.shape[-1] // spans):
-        rq = pl.ds(p * spans, spans)
-        rk = pl.ds(p * memory, memory)
-        for h in range(k_ref.shape[-1] // HEAD_DIM):
-            cols = pl.ds(h * HEAD_DIM, HEAD_DIM)
-            scores = jnp.dot(k_ref[rk, cols], qt_ref[cols, rq], preferred_element_type=jnp.float32) * scale
-            scores = jnp.where(same, scores, -jnp.inf)
-            highest = jnp.max(scores, axis=0, keepdims=True)
-            raised = jnp.exp(scores - highest)
-            weights = (raised * (1.0 / jnp.sum(raised, axis=0, keepdims=True))).astype(jnp.bfloat16)
-            out_ref[rq, cols] = lax.dot_general(
-                weights, v_ref[rk, cols], (((0,), (0,)), ((), ())), preferred_element_type=jnp.float32
-            ).astype(jnp.bfloat16)
+    for h in range(qt_ref.shape[0] // HEAD_DIM):
+        cols = pl.ds(h * HEAD_DIM, HEAD_DIM)
+        queries_t = qt_ref[cols, :]
+        scores = jnp.concatenate(
+            [jnp.dot(k[0, :, cols], queries_t, preferred_element_type=jnp.float32) for k in k_refs], axis=0
+        ) * scale
+        scores = jnp.where(same, scores, -jnp.inf)
+        highest = jnp.max(scores, axis=0, keepdims=True)
+        raised = jnp.exp(scores - highest)
+        weights = (raised * (1.0 / jnp.sum(raised, axis=0, keepdims=True))).astype(jnp.bfloat16)
+        mixed = lax.dot_general(
+            weights[:NLEN], v_refs[0][0, :, cols], (((0,), (0,)), ((), ())), preferred_element_type=jnp.float32
+        )
+        for j in range(1, count):
+            mixed = mixed + lax.dot_general(
+                weights[j * NLEN:(j + 1) * NLEN], v_refs[j][0, :, cols],
+                (((0,), (0,)), ((), ())), preferred_element_type=jnp.float32,
+            )
+        out_ref[:, cols] = mixed.astype(jnp.bfloat16)
 
 
-def cross_attend(queries_t, keys, values, group=2):
+def cross_attend(queries_t, keys, values, slots):
     width, length = queries_t.shape
     spans = 2 * SPAN
-    memory = 2 * NEIGH * NLEN
-    group = min(group, length // spans)
+    count = 2 * NEIGH
+    slots = jnp.clip(slots, 0, keys.shape[0] - 1).astype(jnp.int32)
+
+    def block_spec(j):
+        return pl.BlockSpec((1, NLEN, width), lambda c, slot_ref: (slot_ref[c * count + j], 0, 0))
+
+    grid_spec = pltpu.PrefetchScalarGridSpec(
+        num_scalar_prefetch=1,
+        grid=(length // spans,),
+        in_specs=[pl.BlockSpec((width, spans), lambda c, slot_ref: (0, c))]
+        + [block_spec(j) for j in range(count)]
+        + [block_spec(j) for j in range(count)],
+        out_specs=pl.BlockSpec((spans, width), lambda c, slot_ref: (c, 0)),
+    )
     return pl.pallas_call(
         _cross_kernel,
         out_shape=jax.ShapeDtypeStruct((length, width), jnp.bfloat16),
-        grid=(length // (spans * group),),
-        in_specs=[
-            pl.BlockSpec((width, spans * group), lambda c: (0, c)),
-            pl.BlockSpec((memory * group, width), lambda c: (c, 0)),
-            pl.BlockSpec((memory * group, width), lambda c: (c, 0)),
-        ],
-        out_specs=pl.BlockSpec((spans * group, width), lambda c: (c, 0)),
-    )(queries_t, keys, values)
+        grid_spec=grid_spec,
+    )(slots, queries_t, *([keys] * count), *([values] * count))
 
 
 def gather_weights(shard, n_dp):
@@ -151,11 +165,15 @@
         sent = sent.reshape(n_seq, per_owner, NLEN, neighbour_input.shape[-1])
         got = lax.all_to_all(sent, "seq", 0, 0, tiled=True)
         got = got.reshape(n_seq * per_owner, NLEN, neighbour_input.shape[-1])
-        chosen_raw = jnp.take(got, owners * per_owner + rank, axis=0, mode="clip")
-        chosen = encode_blocks(chosen_raw, enc_gain, full_weights)
+        slots = owners * per_owner + rank
+        if got.shape[0] > refs:
+            got = jnp.take(got, slots, axis=0, mode="clip")
+            slots = jnp.arange(refs, dtype=jnp.int32)
+        chosen = encode_blocks(got, enc_gain, full_weights)
         keys = jnp.dot(chosen, kv_weight[0], preferred_element_type=jnp.float32).astype(jnp.bfloat16)
         values = jnp.dot(chosen, kv_weight[1], preferred_element_type=jnp.float32).astype(jnp.bfloat16)
-        return cross_attend(queries[0].T, keys, values)[None]
+        blocks = (got.shape[0], NLEN, keys.shape[-1])
+        return cross_attend(queries[0].T, keys.reshape(blocks), values.reshape(blocks), slots)[None]
 
     return shards
 

time: 108 us -> 109 us (level)
  Pallas kernels: 24.1 us -> 25.7 us
    gather x1 -> x0, local copies, waits for them, and re-layouts: 1.98 us -> none  [shards(): chosen_raw = jnp.take(got, owners * per_owner + rank, axis=0, mode='clip')]
    pallas_call x1, Pallas kernels: 8.07 us -> 9.87 us  [cross_attend(): pl.pallas_call(_cross_kernel, out_shape=jax.ShapeDtypeStruct((length, wid...]
    unnamed x13, local copies, waits for them, and re-layouts: 5.51 us -> 6.73 us
    dot_general x1, matrix products: 8.08 us -> 9.27 us  [shards(): jnp.dot(chosen, kv_weight[0], preferred_element_type=jnp.float32)]
    dot_general x1, matrix products: 9.25 us -> 8.09 us  [shards(): jnp.dot(chosen, kv_weight[1], preferred_element_type=jnp.float32)]
where the time goes in v19:
time: 109 us
  waiting for transfers between devices  29.3 us (27%)
  Pallas kernels  25.7 us (24%)
  local copies, waits for them, and re-layouts  23 us (21%)
  matrix products  17.4 us (16%)
  starting transfers between devices  12.4 us (11%)
    ppermute x1, waiting for transfers between devices, gather_weights(): lax.ppermute(shard, 'dp', ring)  24.2 us
    pallas_call x1, Pallas kernels, encode_blocks(): pl.pallas_call(_encoder_kernel, out_shape=jax.ShapeDtypeStruct(flat.shape...  15.9 us
    pallas_call x1, Pallas kernels, cross_attend(): pl.pallas_call(_cross_kernel, out_shape=jax.ShapeDtypeStruct((length, wid...  9.87 us
    dynamic_update_slice x4, local copies, waits for them, and re-layouts, gather_weights(): full = lax.dynamic_update_slice(full, piece, (0, owner * rows, 0))  9.55 us
    dot_general x1, matrix products, shards(): jnp.dot(chosen, kv_weight[0], preferred_element_type=jnp.float32)  9.27 us
    dot_general x1, matrix products, shards(): jnp.dot(chosen, kv_weight[1], preferred_element_type=jnp.float32)  8.09 us
    all_to_all x1, starting transfers between devices, shards(): asked = lax.all_to_all(asks, 'seq', 0, 0, tiled=True)  7.28 us
    unnamed x13, local copies, waits for them, and re-layouts  6.73 us
  transfers between devices with their start and end apart: 5, of which 2 were waited for; matrix products, arithmetic and copies ran while one was open for 18% of the time, Pallas kernels for 0%

profile of v19, /device:TPU:0, one launch (start us, length us, event | category | flops | bytes accessed | tf_op | source)
XLA Modules:
  0.0 108.9 jit_solution(11565625227226633699)
XLA Ops:
  0.0 0.0 copy-start
  0.0 0.8 copy.23
  0.8 0.1 reshape.20
  0.9 0.1 broadcast_in_dim_reshape.4
  1.0 0.2 convert_reduce_fusion
  1.2 0.8 copy.26
  1.9 0.1 stack_reshape.4
  2.0 0.6 broadcast_in_dim.33
  2.6 7.3 %all-to-all-start = ((s32[8,3,16]{2,1,0:T(4,128)}), s32[8,3,16]{2,1,0:T(4,128)S(1)}, u32[]{:S(2)}, u32[]{:S(2)}) async-start(s32[8,3,16]{2,1,0:T(4,128)} %broadcast_in_dim.33), calls=%async_computation | async-start | bytes 32768 | tf_op jit(solution)/shard_map/all_to_all | solution.py:160
  9.9 1.5 %collective-permute-start = (bf16[4,224,896]{2,1,0:T(8,128)(2,1)}, bf16[4,224,896]{2,1,0:T(8,128)(2,1)}, u32[]{:S(2)}, u32[]{:S(2)}) collective-permute-start(bf16[4,224,896]{2,1,0:T(8,128)(2,1)} %param.12), channel_id=1, source_target_pairs={{0,16},{8,24},{16,0},{24,8},{1,17},{9,25},{17,1},{25,9},{2,18},{10... | collective-permute-start | bytes 4816904 | tf_op jit(solution)/shard_map/ppermute | solution.py:137
  11.4 5.1 %all-to-all-done = s32[8,3,16]{2,1,0:T(4,128)S(1)} async-done(((s32[8,3,16]{2,1,0:T(4,128)}), s32[8,3,16]{2,1,0:T(4,128)S(1)}, u32[]{:S(2)}, u32[]{:S(2)}) %all-to-all-start) | async-done | bytes 1568 | tf_op jit(solution)/shard_map/all_to_all | solution.py:160
  16.5 0.1 select_reduce_fusion
  16.7 0.1 copy.30
  16.7 0.1 reshape.27
  16.8 0.0 copy-done
  16.8 0.0 copy-start.4
  16.9 2.0 %gather_fusion = bf16[16,64,896]{2,1,0:T(8,128)(2,1)} fusion(bf16[4,64,896]{2,1,0:T(8,128)(2,1)S(1)} %bitcast.27, s32[1024]{0:T(1024)S(1)} %pad_clamp_fusion), kind=kCustom, calls=%fused_computation | custom fusion | bytes 3670080 | tf_op jit(solution)/shard_map/jit(_take)/gather | solution.py:164
  18.8 3.6 %all-to-all-start.1 = ((bf16[8,2,64,896]{3,2,1,0:T(8,128)(2,1)}), bf16[8,2,64,896]{3,2,1,0:T(8,128)(2,1)S(1)}, u32[]{:S(2)}, u32[]{:S(2)}) async-start(bf16[8,2,64,896]{3,2,1,0:T(8,128)(2,1)} %bitcast.7), calls=%async_computation.1 | async-start | bytes 3670016 | tf_op jit(solution)/shard_map/all_to_all | solution.py:166
  22.4 0.1 collective-permute-start.1
  22.5 24.2 %collective-permute-done = bf16[4,224,896]{2,1,0:T(8,128)(2,1)} collective-permute-done((bf16[4,224,896]{2,1,0:T(8,128)(2,1)}, bf16[4,224,896]{2,1,0:T(8,128)(2,1)}, u32[]{:S(2)}, u32[]{:S(2)}) %collective-permute-start) | collective-permute-done | bytes 1605664 | tf_op jit(solution)/shard_map/ppermute | solution.py:137
  46.8 0.0 collective-permute-start.2
  46.8 0.0 copy-done.4
  46.8 0.6 reshape.22.gain_ref
  47.4 3.9 %copy.24 = bf16[1,512,2048]{1,2,0:T(8,128)(2,1)} copy(bf16[1,512,2048]{2,1,0:T(8,128)(2,1)} %param.7) | data formatting | bytes 4194304 | tf_op args[0]
  51.3 0.0 copy-start.3
  51.3 3.1 %broadcast_in_dim.38 = bf16[4,896,896]{2,1,0:T(8,128)(2,1)} broadcast(bf16[]{:T(256)} %constant.42.clone.1), dimensions={} | broadcast | bytes 6422530 | tf_op jit(solution)/shard_map/broadcast_in_dim | solution.py:141
  54.4 0.0 copy-done.3
  54.4 1.3 %constant_dynamic-update-slice_fusion.3 = bf16[4,896,896]{2,1,0:T(8,128)(2,1)} fusion(bf16[4,896,896]{2,1,0:T(8,128)(2,1)} %broadcast_in_dim.38, bf16[4,224,896]{2,1,0:T(8,128)(2,1)S(1)} %copy-done.3, s32[]{:T(128)S(6)} %select_n.32), kind=kLoop, calls=%fused_computation.19 | loop fusion | bytes 3211268 | tf_op jit(solution)/shard_map/dynamic_update_slice | solution.py:143
  55.7 0.6 add_clamp_fusion.slot_ref
  56.3 2.7 %constant_dynamic-update-slice_fusion.2 = bf16[4,896,896]{2,1,0:T(8,128)(2,1)} fusion(bf16[4,896,896]{2,1,0:T(8,128)(2,1)} %constant_dynamic-update-slice_fusion.3, bf16[4,224,896]{2,1,0:T(8,128)(2,1)} %collective-permute-done, s32[]{:T(128)S(6)} %select_n.36), kind=kLoop, calls=%fused_computation.18 | loop fusion | bytes 3211268 | tf_op jit(solution)/shard_map/dynamic_update_slice | solution.py:143
  59.1 0.0 collective-permute-done.1
  59.1 2.7 %constant_dynamic-update-slice_fusion.1 = bf16[4,896,896]{2,1,0:T(8,128)(2,1)} fusion(bf16[4,896,896]{2,1,0:T(8,128)(2,1)} %constant_dynamic-update-slice_fusion.2, bf16[4,224,896]{2,1,0:T(8,128)(2,1)} %collective-permute-done.1, s32[]{:T(128)S(6)} %select_n.37), kind=kLoop, calls=%fused_computation.17 | loop fusion | bytes 3211268 | tf_op jit(solution)/shard_map/dynamic_update_slice | solution.py:143
  61.8 0.0 collective-permute-done.2
  61.8 2.8 %constant_dynamic-update-slice_fusion.w_ref = bf16[4,896,896]{2,1,0:T(8,128)(2,1)} fusion(bf16[4,896,896]{2,1,0:T(8,128)(2,1)} %constant_dynamic-update-slice_fusion.1, bf16[4,224,896]{2,1,0:T(8,128)(2,1)} %collective-permute-done.2, s32[]{:T(128)S(6)} %select_n.38), kind=kLoop, calls=%fused_computation.16 | loop fusion | bytes 3211268 | tf_op jit(solution)/shard_map/dynamic_update_slice | solution.py:143
  64.6 0.0 all-to-all-done.1
  64.6 0.0 copy-start.1
  64.6 1.2 %copy-done.1 = bf16[8,2,64,896]{3,2,1,0:T(8,128)(2,1)} copy-done((bf16[8,2,64,896]{3,2,1,0:T(8,128)(2,1)}, bf16[8,2,64,896]{3,2,1,0:T(8,128)(2,1)S(1)}, u32[]{:S(2)}) %copy-start.1) | copy-done | bytes 1835032
  65.8 15.9 %shard_map.73 = bf16[1024,896]{1,0:T(8,128)(2,1)} custom-call(bf16[1024,896]{1,0:T(8,128)(2,1)} %bitcast.37, f32[1,896]{1,0:T(1,128)} %reshape.22.gain_ref, bf16[4,896,896]{2,1,0:T(8,128)(2,1)} %constant_dynamic-update-slice_fusion.w_ref), custom_call_target="tpu_custom_call" | custom-call | tf_op jit(solution)/shard_map/pallas_call | solution.py:58
  81.7 0.0 copy-start.2
  81.7 9.3 %convolution_convert_fusion.1 = bf16[1024,2048]{1,0:T(8,128)(2,1)} fusion(bf16[1024,896]{1,0:T(8,128)(2,1)} %shard_map.73, bf16[2,896,2048]{2,1,0:T(8,128)(2,1)} %param.13), kind=kOutput, calls=%fused_computation.2 | convolution fusion | flops 3760193536 | bytes 9699328 | tf_op jit(solution)/shard_map/dot_general | solution.py:173
  90.9 0.0 copy-done.2
  90.9 8.1 %convolution_convert_fusion = bf16[1024,2048]{1,0:T(8,128)(2,1)} fusion(bf16[1024,896]{1,0:T(8,128)(2,1)S(1)} %copy-done.2, bf16[2,896,2048]{2,1,0:T(8,128)(2,1)} %param.13), kind=kOutput, calls=%fused_computation.1 | convolution fusion | flops 3760193536 | bytes 9699328 | tf_op jit(solution)/shard_map/dot_general | solution.py:174
  99.0 9.9 %shard_map.74 = bf16[512,2048]{1,0:T(8,128)(2,1)} custom-call(s32[16]{0:T(128)} %add_clamp_fusion.slot_ref, bf16[2048,512]{1,0:T(8,128)(2,1)} %bitcast.36, bf16[16,64,2048]{2,1,0:T(8,128)(2,1)} %bitcast.28, bf16[16,64,2048]{2,1,0:T(8,128)(2,1)} %bitcast.29, bf16[16,64,2048]{2,1,0:T(8,128)(2,1)} %bitcast.30, bf16[16,64,2048]{2,1,0:T(8,128)(2,1)} %bitcast.31, ...), custom_call_target="tpu_custom_call" | custom-call | tf_op jit(solution)/shard_map/pallas_call | solution.py:123
  (4 shorter events, 0.0 us)
Async XLA Ops:
  0.0 16.8 %copy-start = (bf16[1,4,64,896]{3,2,1,0:T(8,128)(2,1)S(1)}, bf16[1,4,64,896]{3,2,1,0:T(8,128)(2,1)}, u32[]{:S(2)}) copy-start(bf16[1,4,64,896]{3,2,1,0:T(8,128)(2,1)} %param.8) | copy-start | bytes 1376260
  2.6 13.9 %all-to-all-start = ((s32[8,3,16]{2,1,0:T(4,128)}), s32[8,3,16]{2,1,0:T(4,128)S(1)}, u32[]{:S(2)}, u32[]{:S(2)}) async-start(s32[8,3,16]{2,1,0:T(4,128)} %broadcast_in_dim.33), calls=%async_computation | async-start | bytes 32768 | tf_op jit(solution)/shard_map/all_to_all | solution.py:160
  9.9 36.9 %collective-permute-start = (bf16[4,224,896]{2,1,0:T(8,128)(2,1)}, bf16[4,224,896]{2,1,0:T(8,128)(2,1)}, u32[]{:S(2)}, u32[]{:S(2)}) collective-permute-start(bf16[4,224,896]{2,1,0:T(8,128)(2,1)} %param.12), channel_id=1, source_target_pairs={{0,16},{8,24},{16,0},{24,8},{1,17},{9,25},{17,1},{25,9},{2,18},{10... | collective-permute-start | bytes 4816904 | tf_op jit(solution)/shard_map/ppermute | solution.py:137
  16.8 29.9 %copy-start.4 = (f32[896]{0:T(1024)S(1)}, f32[896]{0:T(1024)}, u32[]{:S(2)}) copy-start(f32[896]{0:T(1024)} %param.11) | copy-start | bytes 10756
  18.8 45.7 %all-to-all-start.1 = ((bf16[8,2,64,896]{3,2,1,0:T(8,128)(2,1)}), bf16[8,2,64,896]{3,2,1,0:T(8,128)(2,1)S(1)}, u32[]{:S(2)}, u32[]{:S(2)}) async-start(bf16[8,2,64,896]{3,2,1,0:T(8,128)(2,1)} %bitcast.7), calls=%async_computation.1 | async-start | bytes 3670016 | tf_op jit(solution)/shard_map/all_to_all | solution.py:166
  22.4 36.6 %collective-permute-start.1 = (bf16[4,224,896]{2,1,0:T(8,128)(2,1)}, bf16[4,224,896]{2,1,0:T(8,128)(2,1)}, u32[]{:S(2)}, u32[]{:S(2)}) collective-permute-start(bf16[4,224,896]{2,1,0:T(8,128)(2,1)} %param.12), channel_id=1, source_target_pairs={{0,8},{8,0},{16,24},{24,16},{1,9},{9,1},{17,25},{25,17},{2,10},{10... | collective-permute-start | bytes 4816904 | tf_op jit(solution)/shard_map/ppermute | solution.py:139
  46.8 15.0 %collective-permute-start.2 = (bf16[4,224,896]{2,1,0:T(8,128)(2,1)}, bf16[4,224,896]{2,1,0:T(8,128)(2,1)}, u32[]{:S(2)}, u32[]{:S(2)}) collective-permute-start(bf16[4,224,896]{2,1,0:T(8,128)(2,1)} %collective-permute-done), channel_id=1, source_target_pairs={{0,8},{8,0},{16,24},{24,16},{1,9},{9,1},{17,25},{25,17},{2,10},{10... | collective-permute-start | bytes 4816904 | tf_op jit(solution)/shard_map/ppermute | solution.py:139
  51.3 3.1 %copy-start.3 = (bf16[4,224,896]{2,1,0:T(8,128)(2,1)S(1)}, bf16[4,224,896]{2,1,0:T(8,128)(2,1)}, u32[]{:S(2)}) copy-start(bf16[4,224,896]{2,1,0:T(8,128)(2,1)} %param.12) | copy-start | bytes 4816900
  64.6 1.2 %copy-start.1 = (bf16[8,2,64,896]{3,2,1,0:T(8,128)(2,1)}, bf16[8,2,64,896]{3,2,1,0:T(8,128)(2,1)S(1)}, u32[]{:S(2)}) copy-start(bf16[8,2,64,896]{3,2,1,0:T(8,128)(2,1)S(1)} %all-to-all-done.1) | copy-start | bytes 5505028
  81.7 9.3 %copy-start.2 = (bf16[1024,896]{1,0:T(8,128)(2,1)S(1)}, bf16[1024,896]{1,0:T(8,128)(2,1)}, u32[]{:S(2)}) copy-start(bf16[1024,896]{1,0:T(8,128)(2,1)} %shard_map.73) | copy-start | bytes 5505028

commit v20 on v18

--- a/solution.py
+++ b/solution.py
@@ -74,7 +74,8 @@
     )(flat, gain.reshape(1, width), attention)
 
 
-def _cross_kernel(q_ref, kt_ref, v_ref, out_ref):
+def _cross_kernel(q_ref, kt_ref, enc_ref, wv_ref, out_ref, v_ref):
+    v_ref[...] = jnp.dot(enc_ref[...], wv_ref[...], preferred_element_type=jnp.float32).astype(jnp.bfloat16)
     scale = HEAD_DIM ** (-0.5)
     memory = NEIGH * NLEN
     for s in range(q_ref.shape[0] // SPAN):
@@ -89,8 +90,9 @@
             ).astype(jnp.bfloat16)
 
 
-def cross_attend(queries, keys_t, values, group=4):
+def cross_attend(queries, keys_t, encoded, value_weight, group=4):
     length, width = queries.shape
+    enc_width = encoded.shape[-1]
     memory = NEIGH * NLEN
     group = min(group, length // SPAN)
     return pl.pallas_call(
@@ -100,10 +102,12 @@
         in_specs=[
             pl.BlockSpec((SPAN * group, width), lambda c: (c, 0)),
             pl.BlockSpec((width, memory * group), lambda c: (0, c)),
-            pl.BlockSpec((memory * group, width), lambda c: (c, 0)),
+            pl.BlockSpec((memory * group, enc_width), lambda c: (c, 0)),
+            pl.BlockSpec(value_weight.shape, lambda c: (0, 0)),
         ],
         out_specs=pl.BlockSpec((SPAN * group, width), lambda c: (c, 0)),
-    )(queries, keys_t, values)
+        scratch_shapes=[pltpu.VMEM((memory * group, width), jnp.bfloat16)],
+    )(queries, keys_t, encoded, value_weight)
 
 
 def gather_weights(shard, n_dp):
@@ -149,8 +153,7 @@
         keys_t = jnp.einsum(
             "ef,re->fr", kv_weight[0], chosen, preferred_element_type=jnp.float32
         ).astype(jnp.bfloat16)
-        values = jnp.dot(chosen, kv_weight[1], preferred_element_type=jnp.float32).astype(jnp.bfloat16)
-        return cross_attend(queries[0], keys_t, values)[None]
+        return cross_attend(queries[0], keys_t, chosen, kv_weight[1])[None]
 
     return shards
 

time: 108 us -> 106 us (0.981)
  matrix products: 17.3 us -> 9.09 us
  Pallas kernels: 24.1 us -> 29.9 us
  local copies, waits for them, and re-layouts: 20 us -> 24.4 us
  waiting for transfers between devices: 33 us -> 29.3 us
    dot_general x1 -> x0, matrix products: 8.08 us -> none  [shards(): jnp.dot(chosen, kv_weight[1], preferred_element_type=jnp.float32)]
    pallas_call x1, Pallas kernels: 8.25 us -> 14 us  [cross_attend(): pl.pallas_call(_cross_kernel, out_shape=jax.ShapeDtypeStruct(queries.shap...]
    squeeze x0 -> x1, local copies, waits for them, and re-layouts: none -> 4.4 us  [shards(): return cross_attend(queries[0], keys_t, chosen, kv_weight[1])[None]]
    all_to_all x1, waiting for transfers between devices: 3.65 us -> 0.01 us  [shards(): got = lax.all_to_all(sent, 'seq', 0, 0, tiled=True)]
  transfers between devices with their start and end apart: 5 -> 5, of which waited for: 3 -> 2; matrix products, arithmetic and copies ran while one was open for 15% -> 19% of each run, Pallas kernels for 0% -> 0%
where the time goes in v20:
time: 106 us
  Pallas kernels  29.9 us (28%)
  waiting for transfers between devices  29.3 us (28%)
  local copies, waits for them, and re-layouts  24.4 us (23%)
  starting transfers between devices  12.4 us (12%)
  matrix products  9.09 us (9%)
    ppermute x1, waiting for transfers between devices, gather_weights(): lax.ppermute(shard, 'dp', ring)  24.2 us
    pallas_call x1, Pallas kernels, encode_blocks(): pl.pallas_call(_encoder_kernel, out_shape=jax.ShapeDtypeStruct(flat.shape...  15.9 us
    pallas_call x1, Pallas kernels, cross_attend(): pl.pallas_call(_cross_kernel, out_shape=jax.ShapeDtypeStruct(queries.shap...  14 us
    dynamic_update_slice x4, local copies, waits for them, and re-layouts, gather_weights(): full = lax.dynamic_update_slice(full, piece, (0, owner * rows, 0))  9.46 us
    dot_general x1, matrix products, shards(): jnp.einsum('ef,re->fr', kv_weight[0], chosen, preferred_element_type=jnp....  9.09 us
    all_to_all x1, starting transfers between devices, shards(): asked = lax.all_to_all(asks, 'seq', 0, 0, tiled=True)  7.28 us
    all_to_all x1, waiting for transfers between devices, shards(): asked = lax.all_to_all(asks, 'seq', 0, 0, tiled=True)  5.08 us
    squeeze x1, local copies, waits for them, and re-layouts, shards(): return cross_attend(queries[0], keys_t, chosen, kv_weight[1])[None]  4.4 us
  transfers between devices with their start and end apart: 5, of which 2 were waited for; matrix products, arithmetic and copies ran while one was open for 19% of the time, Pallas kernels for 0%

profile of v20, /device:TPU:0, one launch (start us, length us, event | category | flops | bytes accessed | tf_op | source)
XLA Modules:
  0.0 105.5 jit_solution(5648050359179072685)
XLA Ops:
  0.0 0.0 copy-start
  0.0 0.8 copy.26
  0.8 0.1 eq.39
  0.9 0.1 stack_reshape.6
  1.0 0.2 convert_reduce_fusion
  1.2 0.8 copy.27
  1.9 0.1 stack_reshape.7
  2.0 0.6 broadcast_in_dim.35
  2.6 7.3 %all-to-all-start = ((s32[8,3,16]{2,1,0:T(4,128)}), s32[8,3,16]{2,1,0:T(4,128)S(1)}, u32[]{:S(2)}, u32[]{:S(2)}) async-start(s32[8,3,16]{2,1,0:T(4,128)} %broadcast_in_dim.35), calls=%async_computation | async-start | bytes 32768 | tf_op jit(solution)/shard_map/all_to_all | solution.py:143
  9.9 1.5 %collective-permute-start = (bf16[4,224,896]{2,1,0:T(8,128)(2,1)}, bf16[4,224,896]{2,1,0:T(8,128)(2,1)}, u32[]{:S(2)}, u32[]{:S(2)}) collective-permute-start(bf16[4,224,896]{2,1,0:T(8,128)(2,1)} %param.12), channel_id=1, source_target_pairs={{0,16},{8,24},{16,0},{24,8},{1,17},{9,25},{17,1},{25,9},{2,18},{10... | collective-permute-start | bytes 4816904 | tf_op jit(solution)/shard_map/ppermute | solution.py:120
  11.4 5.1 %all-to-all-done = s32[8,3,16]{2,1,0:T(4,128)S(1)} async-done(((s32[8,3,16]{2,1,0:T(4,128)}), s32[8,3,16]{2,1,0:T(4,128)S(1)}, u32[]{:S(2)}, u32[]{:S(2)}) %all-to-all-start) | async-done | bytes 1568 | tf_op jit(solution)/shard_map/all_to_all | solution.py:143
  16.5 0.1 select_reduce_fusion
  16.7 0.1 copy.32
  16.7 0.1 reshape.43
  16.8 0.0 copy-done
  16.8 0.0 copy-start.2
  16.9 0.0 copy-start.3
  16.9 2.0 %gather_fusion = bf16[16,64,896]{2,1,0:T(8,128)(2,1)} fusion(bf16[4,64,896]{2,1,0:T(8,128)(2,1)S(1)} %bitcast.30, s32[1024]{0:T(1024)S(1)} %pad_clamp_fusion.1), kind=kCustom, calls=%fused_computation | custom fusion | bytes 3670080 | tf_op jit(solution)/shard_map/jit(_take)/gather | solution.py:147
  18.9 3.6 %all-to-all-start.1 = ((bf16[8,2,64,896]{3,2,1,0:T(8,128)(2,1)}), bf16[8,2,64,896]{3,2,1,0:T(8,128)(2,1)S(1)}, u32[]{:S(2)}, u32[]{:S(2)}) async-start(bf16[8,2,64,896]{3,2,1,0:T(8,128)(2,1)} %bitcast.32), calls=%async_computation.1 | async-start | bytes 3670016 | tf_op jit(solution)/shard_map/all_to_all | solution.py:149
  22.5 0.1 collective-permute-start.1
  22.6 24.2 %collective-permute-done = bf16[4,224,896]{2,1,0:T(8,128)(2,1)} collective-permute-done((bf16[4,224,896]{2,1,0:T(8,128)(2,1)}, bf16[4,224,896]{2,1,0:T(8,128)(2,1)}, u32[]{:S(2)}, u32[]{:S(2)}) %collective-permute-start) | collective-permute-done | bytes 1605664 | tf_op jit(solution)/shard_map/ppermute | solution.py:120
  46.8 0.0 collective-permute-start.2
  46.8 0.0 copy-done.2
  46.8 0.1 copy.33
  46.9 0.1 mul.29
  47.0 0.0 copy-done.3
  47.0 0.6 reshape.40.gain_ref
  47.6 0.0 copy-start.1
  47.6 3.2 %broadcast_in_dim.40 = bf16[4,896,896]{2,1,0:T(8,128)(2,1)} broadcast(bf16[]{:T(256)} %constant.40.clone.1), dimensions={} | broadcast | bytes 6422530 | tf_op jit(solution)/shard_map/broadcast_in_dim | solution.py:124
  50.7 0.0 copy-done.1
  50.7 1.3 %constant_dynamic-update-slice_fusion.3 = bf16[4,896,896]{2,1,0:T(8,128)(2,1)} fusion(bf16[4,896,896]{2,1,0:T(8,128)(2,1)} %broadcast_in_dim.40, bf16[4,224,896]{2,1,0:T(8,128)(2,1)S(1)} %copy-done.1, s32[]{:T(128)S(6)} %select_n.32), kind=kLoop, calls=%fused_computation.19 | loop fusion | bytes 3211268 | tf_op jit(solution)/shard_map/dynamic_update_slice | solution.py:126
  52.0 4.4 %slice_bitcast_fusion.wv_ref = bf16[896,2048]{1,0:T(8,128)(2,1)} fusion(bf16[2,896,2048]{2,1,0:T(8,128)(2,1)} %param.13), kind=kLoop, calls=%fused_computation.4 | loop fusion | bytes 7340032 | tf_op jit(solution)/shard_map/squeeze | solution.py:156
  56.4 2.7 %constant_dynamic-update-slice_fusion.2 = bf16[4,896,896]{2,1,0:T(8,128)(2,1)} fusion(bf16[4,896,896]{2,1,0:T(8,128)(2,1)} %constant_dynamic-update-slice_fusion.3, bf16[4,224,896]{2,1,0:T(8,128)(2,1)} %collective-permute-done, s32[]{:T(128)S(6)} %select_n.36), kind=kLoop, calls=%fused_computation.18 | loop fusion | bytes 3211268 | tf_op jit(solution)/shard_map/dynamic_update_slice | solution.py:126
  59.2 0.0 collective-permute-done.1
  59.2 2.7 %constant_dynamic-update-slice_fusion.1 = bf16[4,896,896]{2,1,0:T(8,128)(2,1)} fusion(bf16[4,896,896]{2,1,0:T(8,128)(2,1)} %constant_dynamic-update-slice_fusion.2, bf16[4,224,896]{2,1,0:T(8,128)(2,1)} %collective-permute-done.1, s32[]{:T(128)S(6)} %select_n.37), kind=kLoop, calls=%fused_computation.17 | loop fusion | bytes 3211268 | tf_op jit(solution)/shard_map/dynamic_update_slice | solution.py:126
  61.9 0.0 collective-permute-done.2
  61.9 2.7 %constant_dynamic-update-slice_fusion.w_ref = bf16[4,896,896]{2,1,0:T(8,128)(2,1)} fusion(bf16[4,896,896]{2,1,0:T(8,128)(2,1)} %constant_dynamic-update-slice_fusion.1, bf16[4,224,896]{2,1,0:T(8,128)(2,1)} %collective-permute-done.2, s32[]{:T(128)S(6)} %select_n.38), kind=kLoop, calls=%fused_computation.16 | loop fusion | bytes 3211268 | tf_op jit(solution)/shard_map/dynamic_update_slice | solution.py:126
  64.6 0.0 all-to-all-done.1
  64.6 2.0 %gather_fusion.1 = bf16[16,64,896]{2,1,0:T(8,128)(2,1)} fusion(bf16[16,64,896]{2,1,0:T(8,128)(2,1)S(1)} %bitcast.31, s32[1024]{0:T(1024)S(1)} %pad_clamp_fusion), kind=kCustom, calls=%fused_computation.1 | custom fusion | bytes 3670080 | tf_op jit(solution)/shard_map/jit(_take)/gather | solution.py:151
  66.6 15.9 %shard_map.73.enc_ref = bf16[1024,896]{1,0:T(8,128)(2,1)} custom-call(bf16[1024,896]{1,0:T(8,128)(2,1)} %bitcast.33, f32[1,896]{1,0:T(1,128)} %reshape.40.gain_ref, bf16[4,896,896]{2,1,0:T(8,128)(2,1)} %constant_dynamic-update-slice_fusion.w_ref), custom_call_target="tpu_custom_call" | custom-call | tf_op jit(solution)/shard_map/pallas_call | solution.py:58
  82.4 9.1 %convert_bitcast_fusion.kt_ref = bf16[2048,1024]{1,0:T(8,128)(2,1)} fusion(bf16[1024,896]{1,0:T(8,128)(2,1)} %shard_map.73.enc_ref, bf16[2,896,2048]{2,1,0:T(8,128)(2,1)} %param.13), kind=kOutput, calls=%fused_computation.2 | convolution fusion | flops 3760193536 | bytes 9699328 | tf_op jit(solution)/shard_map/ef,re->fr/dot_general | solution.py:153
  91.5 14.0 %shard_map.74 = bf16[512,2048]{1,0:T(8,128)(2,1)} custom-call(bf16[512,2048]{1,0:T(8,128)(2,1)} %bitcast.34, bf16[2048,1024]{1,0:T(8,128)(2,1)} %convert_bitcast_fusion.kt_ref, bf16[1024,896]{1,0:T(8,128)(2,1)} %shard_map.73.enc_ref, bf16[896,2048]{1,0:T(8,128)(2,1)} %slice_bitcast_fusion.wv_ref), custom_call_target="tpu_custom_call" | custom-call | tf_op jit(solution)/shard_map/pallas_call | solution.py:98
  (7 shorter events, 0.1 us)
Async XLA Ops:
  0.0 16.8 %copy-start = (bf16[1,4,64,896]{3,2,1,0:T(8,128)(2,1)S(1)}, bf16[1,4,64,896]{3,2,1,0:T(8,128)(2,1)}, u32[]{:S(2)}) copy-start(bf16[1,4,64,896]{3,2,1,0:T(8,128)(2,1)} %param.8) | copy-start | bytes 1376260
  2.6 13.9 %all-to-all-start = ((s32[8,3,16]{2,1,0:T(4,128)}), s32[8,3,16]{2,1,0:T(4,128)S(1)}, u32[]{:S(2)}, u32[]{:S(2)}) async-start(s32[8,3,16]{2,1,0:T(4,128)} %broadcast_in_dim.35), calls=%async_computation | async-start | bytes 32768 | tf_op jit(solution)/shard_map/all_to_all | solution.py:143
  9.9 36.9 %collective-permute-start = (bf16[4,224,896]{2,1,0:T(8,128)(2,1)}, bf16[4,224,896]{2,1,0:T(8,128)(2,1)}, u32[]{:S(2)}, u32[]{:S(2)}) collective-permute-start(bf16[4,224,896]{2,1,0:T(8,128)(2,1)} %param.12), channel_id=1, source_target_pairs={{0,16},{8,24},{16,0},{24,8},{1,17},{9,25},{17,1},{25,9},{2,18},{10... | collective-permute-start | bytes 4816904 | tf_op jit(solution)/shard_map/ppermute | solution.py:120
  16.8 29.9 %copy-start.2 = (s32[1,8,2]{1,2,0:T(2,128)S(1)}, s32[1,8,2]{1,2,0:T(2,128)}, u32[]{:S(2)}) copy-start(s32[1,8,2]{1,2,0:T(2,128)} %param.9) | copy-start | bytes 196
  16.9 30.1 %copy-start.3 = (f32[896]{0:T(1024)S(1)}, f32[896]{0:T(1024)}, u32[]{:S(2)}) copy-start(f32[896]{0:T(1024)} %param.11) | copy-start | bytes 10756
  18.9 45.7 %all-to-all-start.1 = ((bf16[8,2,64,896]{3,2,1,0:T(8,128)(2,1)}), bf16[8,2,64,896]{3,2,1,0:T(8,128)(2,1)S(1)}, u32[]{:S(2)}, u32[]{:S(2)}) async-start(bf16[8,2,64,896]{3,2,1,0:T(8,128)(2,1)} %bitcast.32), calls=%async_computation.1 | async-start | bytes 3670016 | tf_op jit(solution)/shard_map/all_to_all | solution.py:149
  22.5 36.7 %collective-permute-start.1 = (bf16[4,224,896]{2,1,0:T(8,128)(2,1)}, bf16[4,224,896]{2,1,0:T(8,128)(2,1)}, u32[]{:S(2)}, u32[]{:S(2)}) collective-permute-start(bf16[4,224,896]{2,1,0:T(8,128)(2,1)} %param.12), channel_id=1, source_target_pairs={{0,8},{8,0},{16,24},{24,16},{1,9},{9,1},{17,25},{25,17},{2,10},{10... | collective-permute-start | bytes 4816904 | tf_op jit(solution)/shard_map/ppermute | solution.py:122
  46.8 15.1 %collective-permute-start.2 = (bf16[4,224,896]{2,1,0:T(8,128)(2,1)}, bf16[4,224,896]{2,1,0:T(8,128)(2,1)}, u32[]{:S(2)}, u32[]{:S(2)}) collective-permute-start(bf16[4,224,896]{2,1,0:T(8,128)(2,1)} %collective-permute-done), channel_id=1, source_target_pairs={{0,8},{8,0},{16,24},{24,16},{1,9},{9,1},{17,25},{25,17},{2,10},{10... | collective-permute-start | bytes 4816904 | tf_op jit(solution)/shard_map/ppermute | solution.py:122
  47.6 3.2 %copy-start.1 = (bf16[4,224,896]{2,1,0:T(8,128)(2,1)S(1)}, bf16[4,224,896]{2,1,0:T(8,128)(2,1)}, u32[]{:S(2)}) copy-start(bf16[4,224,896]{2,1,0:T(8,128)(2,1)} %param.12) | copy-start | bytes 4816900

commit v21 on v20

--- a/solution.py
+++ b/solution.py
@@ -74,8 +74,10 @@
     )(flat, gain.reshape(1, width), attention)
 
 
-def _cross_kernel(q_ref, kt_ref, enc_ref, wv_ref, out_ref, v_ref):
-    v_ref[...] = jnp.dot(enc_ref[...], wv_ref[...], preferred_element_type=jnp.float32).astype(jnp.bfloat16)
+def _cross_kernel(q_ref, enc_ref, wk_ref, wv_ref, out_ref, kt_ref, v_ref):
+    encoded = enc_ref[...]
+    kt_ref[...] = jnp.dot(encoded, wk_ref[...], preferred_element_type=jnp.float32).astype(jnp.bfloat16).T
+    v_ref[...] = jnp.dot(encoded, wv_ref[...], preferred_element_type=jnp.float32).astype(jnp.bfloat16)
     scale = HEAD_DIM ** (-0.5)
     memory = NEIGH * NLEN
     for s in range(q_ref.shape[0] // SPAN):
@@ -90,7 +92,7 @@
             ).astype(jnp.bfloat16)
 
 
-def cross_attend(queries, keys_t, encoded, value_weight, group=4):
+def cross_attend(queries, encoded, key_weight, value_weight, group=4):
     length, width = queries.shape
     enc_width = encoded.shape[-1]
     memory = NEIGH * NLEN
@@ -101,13 +103,16 @@
         grid=(length // (SPAN * group),),
         in_specs=[
             pl.BlockSpec((SPAN * group, width), lambda c: (c, 0)),
-            pl.BlockSpec((width, memory * group), lambda c: (0, c)),
             pl.BlockSpec((memory * group, enc_width), lambda c: (c, 0)),
+            pl.BlockSpec(key_weight.shape, lambda c: (0, 0)),
             pl.BlockSpec(value_weight.shape, lambda c: (0, 0)),
         ],
         out_specs=pl.BlockSpec((SPAN * group, width), lambda c: (c, 0)),
-        scratch_shapes=[pltpu.VMEM((memory * group, width), jnp.bfloat16)],
-    )(queries, keys_t, encoded, value_weight)
+        scratch_shapes=[
+            pltpu.VMEM((width, memory * group), jnp.bfloat16),
+            pltpu.VMEM((memory * group, width), jnp.bfloat16),
+        ],
+    )(queries, encoded, key_weight, value_weight)
 
 
 def gather_weights(shard, n_dp):
@@ -150,10 +155,7 @@
         got = got.reshape(n_seq * per_owner, NLEN, neighbour_input.shape[-1])
         chosen_raw = jnp.take(got, owners * per_owner + rank, axis=0, mode="clip")
         chosen = encode_blocks(chosen_raw, enc_gain, full_weights)
-        keys_t = jnp.einsum(
-            "ef,re->fr", kv_weight[0], chosen, preferred_element_type=jnp.float32
-        ).astype(jnp.bfloat16)
-        return cross_attend(queries[0], keys_t, chosen, kv_weight[1])[None]
+        return cross_attend(queries[0], chosen, kv_weight[0], kv_weight[1])[None]
 
     return shards
 

time: 106 us -> 104 us (0.981)
  matrix products: 9.09 us -> 0 us
  Pallas kernels: 29.9 us -> 33.9 us
  local copies, waits for them, and re-layouts: 24.4 us -> 27.6 us
    dot_general x1 -> x0, matrix products: 9.09 us -> none  [shards(): jnp.einsum('ef,re->fr', kv_weight[0], chosen, preferred_element_type=jnp....]
    pallas_call x1, Pallas kernels: 14 us -> 18 us  [cross_attend(): pl.pallas_call(_cross_kernel, out_shape=jax.ShapeDtypeStruct(queries.shap...]
    squeeze x1, local copies, waits for them, and re-layouts: 4.4 us -> 7.59 us  [shards(): return cross_attend(queries[0], chosen, kv_weight[0], kv_weight[1])[None]]
  transfers between devices with their start and end apart: 5 -> 5, of which waited for: 2 -> 2; matrix products, arithmetic and copies ran while one was open for 19% -> 22% of each run, Pallas kernels for 0% -> 0%
where the time goes in v21:
time: 104 us
  Pallas kernels  33.9 us (33%)
  waiting for transfers between devices  29.2 us (28%)
  local copies, waits for them, and re-layouts  27.6 us (27%)
  starting transfers between devices  12.6 us (12%)
    ppermute x1, waiting for transfers between devices, gather_weights(): lax.ppermute(shard, 'dp', ring)  24.1 us
    pallas_call x1, Pallas kernels, cross_attend(): pl.pallas_call(_cross_kernel, out_shape=jax.ShapeDtypeStruct(queries.shap...  18 us
    pallas_call x1, Pallas kernels, encode_blocks(): pl.pallas_call(_encoder_kernel, out_shape=jax.ShapeDtypeStruct(flat.shape...  15.9 us
    dynamic_update_slice x4, local copies, waits for them, and re-layouts, gather_weights(): full = lax.dynamic_update_slice(full, piece, (0, owner * rows, 0))  9.45 us
    squeeze x1, local copies, waits for them, and re-layouts, shards(): return cross_attend(queries[0], chosen, kv_weight[0], kv_weight[1])[None]  7.59 us
    all_to_all x1, starting transfers between devices, shards(): asked = lax.all_to_all(asks, 'seq', 0, 0, tiled=True)  7.28 us
    all_to_all x1, waiting for transfers between devices, shards(): asked = lax.all_to_all(asks, 'seq', 0, 0, tiled=True)  5.08 us
    all_to_all x1, starting transfers between devices, shards(): got = lax.all_to_all(sent, 'seq', 0, 0, tiled=True)  3.72 us
  transfers between devices with their start and end apart: 5, of which 2 were waited for; matrix products, arithmetic and copies ran while one was open for 22% of the time, Pallas kernels for 0%

profile of v21, /device:TPU:0, one launch (start us, length us, event | category | flops | bytes accessed | tf_op | source)
XLA Modules:
  0.0 103.8 jit_solution(15574989641573664202)
XLA Ops:
  0.0 0.0 copy-start
  0.0 0.8 copy.23
  0.8 0.1 eq.39
  0.9 0.1 stack_reshape.6
  1.0 0.2 convert_reduce_fusion
  1.2 0.8 copy.24
  1.9 0.1 stack_reshape.7
  2.0 0.6 broadcast_in_dim.35
  2.6 7.3 %all-to-all-start = ((s32[8,3,16]{2,1,0:T(4,128)}), s32[8,3,16]{2,1,0:T(4,128)S(1)}, u32[]{:S(2)}, u32[]{:S(2)}) async-start(s32[8,3,16]{2,1,0:T(4,128)} %broadcast_in_dim.35), calls=%async_computation | async-start | bytes 32768 | tf_op jit(solution)/shard_map/all_to_all | solution.py:148
  9.9 1.5 %collective-permute-start = (bf16[4,224,896]{2,1,0:T(8,128)(2,1)}, bf16[4,224,896]{2,1,0:T(8,128)(2,1)}, u32[]{:S(2)}, u32[]{:S(2)}) collective-permute-start(bf16[4,224,896]{2,1,0:T(8,128)(2,1)} %param.12), channel_id=1, source_target_pairs={{0,16},{8,24},{16,0},{24,8},{1,17},{9,25},{17,1},{25,9},{2,18},{10... | collective-permute-start | bytes 4816904 | tf_op jit(solution)/shard_map/ppermute | solution.py:125
  11.4 5.1 %all-to-all-done = s32[8,3,16]{2,1,0:T(4,128)S(1)} async-done(((s32[8,3,16]{2,1,0:T(4,128)}), s32[8,3,16]{2,1,0:T(4,128)S(1)}, u32[]{:S(2)}, u32[]{:S(2)}) %all-to-all-start) | async-done | bytes 1568 | tf_op jit(solution)/shard_map/all_to_all | solution.py:148
  16.5 0.1 select_reduce_fusion
  16.7 0.1 copy.29
  16.7 0.1 reshape.43
  16.8 0.0 copy-done
  16.8 2.0 %gather_fusion = bf16[16,64,896]{2,1,0:T(8,128)(2,1)} fusion(bf16[4,64,896]{2,1,0:T(8,128)(2,1)S(1)} %bitcast.26, s32[1024]{0:T(1024)S(1)} %pad_clamp_fusion.1), kind=kCustom, calls=%fused_computation | custom fusion | bytes 3670080 | tf_op jit(solution)/shard_map/jit(_take)/gather | solution.py:152
  18.8 0.0 copy-start.2
  18.8 0.0 copy-start.3
  18.8 3.7 %all-to-all-start.1 = ((bf16[8,2,64,896]{3,2,1,0:T(8,128)(2,1)}), bf16[8,2,64,896]{3,2,1,0:T(8,128)(2,1)S(1)}, u32[]{:S(2)}, u32[]{:S(2)}) async-start(bf16[8,2,64,896]{3,2,1,0:T(8,128)(2,1)} %bitcast.28), calls=%async_computation.1 | async-start | bytes 3670016 | tf_op jit(solution)/shard_map/all_to_all | solution.py:154
  22.6 0.1 collective-permute-start.1
  22.7 24.1 %collective-permute-done = bf16[4,224,896]{2,1,0:T(8,128)(2,1)} collective-permute-done((bf16[4,224,896]{2,1,0:T(8,128)(2,1)}, bf16[4,224,896]{2,1,0:T(8,128)(2,1)}, u32[]{:S(2)}, u32[]{:S(2)}) %collective-permute-start) | collective-permute-done | bytes 1605664 | tf_op jit(solution)/shard_map/ppermute | solution.py:125
  46.8 0.0 collective-permute-start.2
  46.8 0.0 copy-done.2
  46.8 0.1 copy.30
  46.9 0.1 mul.29
  47.0 0.0 copy-done.3
  47.0 0.6 reshape.40.gain_ref
  47.6 0.0 copy-start.1
  47.6 3.2 %broadcast_in_dim.40 = bf16[4,896,896]{2,1,0:T(8,128)(2,1)} broadcast(bf16[]{:T(256)} %constant.40.clone.1), dimensions={} | broadcast | bytes 6422530 | tf_op jit(solution)/shard_map/broadcast_in_dim | solution.py:129
  50.8 0.0 copy-done.1
  50.8 1.3 %constant_dynamic-update-slice_fusion.3 = bf16[4,896,896]{2,1,0:T(8,128)(2,1)} fusion(bf16[4,896,896]{2,1,0:T(8,128)(2,1)} %broadcast_in_dim.40, bf16[4,224,896]{2,1,0:T(8,128)(2,1)S(1)} %copy-done.1, s32[]{:T(128)S(6)} %select_n.32), kind=kLoop, calls=%fused_computation.17 | loop fusion | bytes 3211268 | tf_op jit(solution)/shard_map/dynamic_update_slice | solution.py:131
  52.1 7.6 %slice_bitcast_fusion = (bf16[896,2048]{1,0:T(8,128)(2,1)}, bf16[896,2048]{1,0:T(8,128)(2,1)}) fusion(bf16[2,896,2048]{2,1,0:T(8,128)(2,1)} %param.13), kind=kLoop, calls=%fused_computation.2 | loop fusion | bytes 14680064 | tf_op jit(solution)/shard_map/squeeze | solution.py:158
  59.7 2.7 %constant_dynamic-update-slice_fusion.2 = bf16[4,896,896]{2,1,0:T(8,128)(2,1)} fusion(bf16[4,896,896]{2,1,0:T(8,128)(2,1)} %constant_dynamic-update-slice_fusion.3, bf16[4,224,896]{2,1,0:T(8,128)(2,1)} %collective-permute-done, s32[]{:T(128)S(6)} %select_n.36), kind=kLoop, calls=%fused_computation.16 | loop fusion | bytes 3211268 | tf_op jit(solution)/shard_map/dynamic_update_slice | solution.py:131
  62.4 0.0 collective-permute-done.1
  62.4 2.7 %constant_dynamic-update-slice_fusion.1 = bf16[4,896,896]{2,1,0:T(8,128)(2,1)} fusion(bf16[4,896,896]{2,1,0:T(8,128)(2,1)} %constant_dynamic-update-slice_fusion.2, bf16[4,224,896]{2,1,0:T(8,128)(2,1)} %collective-permute-done.1, s32[]{:T(128)S(6)} %select_n.37), kind=kLoop, calls=%fused_computation.15 | loop fusion | bytes 3211268 | tf_op jit(solution)/shard_map/dynamic_update_slice | solution.py:131
  65.1 0.0 collective-permute-done.2
  65.2 2.7 %constant_dynamic-update-slice_fusion.w_ref = bf16[4,896,896]{2,1,0:T(8,128)(2,1)} fusion(bf16[4,896,896]{2,1,0:T(8,128)(2,1)} %constant_dynamic-update-slice_fusion.1, bf16[4,224,896]{2,1,0:T(8,128)(2,1)} %collective-permute-done.2, s32[]{:T(128)S(6)} %select_n.38), kind=kLoop, calls=%fused_computation.14 | loop fusion | bytes 3211268 | tf_op jit(solution)/shard_map/dynamic_update_slice | solution.py:131
  67.9 0.0 all-to-all-done.1
  67.9 2.0 %gather_fusion.1 = bf16[16,64,896]{2,1,0:T(8,128)(2,1)} fusion(bf16[16,64,896]{2,1,0:T(8,128)(2,1)S(1)} %bitcast.27, s32[1024]{0:T(1024)S(1)} %pad_clamp_fusion), kind=kCustom, calls=%fused_computation.1 | custom fusion | bytes 3670080 | tf_op jit(solution)/shard_map/jit(_take)/gather | solution.py:156
  69.9 15.9 %shard_map.73.enc_ref = bf16[1024,896]{1,0:T(8,128)(2,1)} custom-call(bf16[1024,896]{1,0:T(8,128)(2,1)} %bitcast.29, f32[1,896]{1,0:T(1,128)} %reshape.40.gain_ref, bf16[4,896,896]{2,1,0:T(8,128)(2,1)} %constant_dynamic-update-slice_fusion.w_ref), custom_call_target="tpu_custom_call" | custom-call | tf_op jit(solution)/shard_map/pallas_call | solution.py:58
  85.7 18.0 %shard_map.74 = bf16[512,2048]{1,0:T(8,128)(2,1)} custom-call(bf16[512,2048]{1,0:T(8,128)(2,1)} %bitcast.30, bf16[1024,896]{1,0:T(8,128)(2,1)} %shard_map.73.enc_ref, bf16[896,2048]{1,0:T(8,128)(2,1)} %get-tuple-element.6.wk_ref, bf16[896,2048]{1,0:T(8,128)(2,1)} %get-tuple-element.5.wv_ref), custom_call_target="tpu_custom_call" | custom-call | tf_op jit(solution)/shard_map/pallas_call | solution.py:100
  (7 shorter events, 0.1 us)
Async XLA Ops:
  0.0 16.8 %copy-start = (bf16[1,4,64,896]{3,2,1,0:T(8,128)(2,1)S(1)}, bf16[1,4,64,896]{3,2,1,0:T(8,128)(2,1)}, u32[]{:S(2)}) copy-start(bf16[1,4,64,896]{3,2,1,0:T(8,128)(2,1)} %param.8) | copy-start | bytes 1376260
  2.6 13.9 %all-to-all-start = ((s32[8,3,16]{2,1,0:T(4,128)}), s32[8,3,16]{2,1,0:T(4,128)S(1)}, u32[]{:S(2)}, u32[]{:S(2)}) async-start(s32[8,3,16]{2,1,0:T(4,128)} %broadcast_in_dim.35), calls=%async_computation | async-start | bytes 32768 | tf_op jit(solution)/shard_map/all_to_all | solution.py:148
  9.9 36.9 %collective-permute-start = (bf16[4,224,896]{2,1,0:T(8,128)(2,1)}, bf16[4,224,896]{2,1,0:T(8,128)(2,1)}, u32[]{:S(2)}, u32[]{:S(2)}) collective-permute-start(bf16[4,224,896]{2,1,0:T(8,128)(2,1)} %param.12), channel_id=1, source_target_pairs={{0,16},{8,24},{16,0},{24,8},{1,17},{9,25},{17,1},{25,9},{2,18},{10... | collective-permute-start | bytes 4816904 | tf_op jit(solution)/shard_map/ppermute | solution.py:125
  18.8 28.0 %copy-start.2 = (s32[1,8,2]{1,2,0:T(2,128)S(1)}, s32[1,8,2]{1,2,0:T(2,128)}, u32[]{:S(2)}) copy-start(s32[1,8,2]{1,2,0:T(2,128)} %param.9) | copy-start | bytes 196
  18.8 28.2 %copy-start.3 = (f32[896]{0:T(1024)S(1)}, f32[896]{0:T(1024)}, u32[]{:S(2)}) copy-start(f32[896]{0:T(1024)} %param.11) | copy-start | bytes 10756
  18.8 49.0 %all-to-all-start.1 = ((bf16[8,2,64,896]{3,2,1,0:T(8,128)(2,1)}), bf16[8,2,64,896]{3,2,1,0:T(8,128)(2,1)S(1)}, u32[]{:S(2)}, u32[]{:S(2)}) async-start(bf16[8,2,64,896]{3,2,1,0:T(8,128)(2,1)} %bitcast.28), calls=%async_computation.1 | async-start | bytes 3670016 | tf_op jit(solution)/shard_map/all_to_all | solution.py:154
  22.6 39.8 %collective-permute-start.1 = (bf16[4,224,896]{2,1,0:T(8,128)(2,1)}, bf16[4,224,896]{2,1,0:T(8,128)(2,1)}, u32[]{:S(2)}, u32[]{:S(2)}) collective-permute-start(bf16[4,224,896]{2,1,0:T(8,128)(2,1)} %param.12), channel_id=1, source_target_pairs={{0,8},{8,0},{16,24},{24,16},{1,9},{9,1},{17,25},{25,17},{2,10},{10... | collective-permute-start | bytes 4816904 | tf_op jit(solution)/shard_map/ppermute | solution.py:127
  46.8 18.4 %collective-permute-start.2 = (bf16[4,224,896]{2,1,0:T(8,128)(2,1)}, bf16[4,224,896]{2,1,0:T(8,128)(2,1)}, u32[]{:S(2)}, u32[]{:S(2)}) collective-permute-start(bf16[4,224,896]{2,1,0:T(8,128)(2,1)} %collective-permute-done), channel_id=1, source_target_pairs={{0,8},{8,0},{16,24},{24,16},{1,9},{9,1},{17,25},{25,17},{2,10},{10... | collective-permute-start | bytes 4816904 | tf_op jit(solution)/shard_map/ppermute | solution.py:127
  47.6 3.2 %copy-start.1 = (bf16[4,224,896]{2,1,0:T(8,128)(2,1)S(1)}, bf16[4,224,896]{2,1,0:T(8,128)(2,1)}, u32[]{:S(2)}) copy-start(bf16[4,224,896]{2,1,0:T(8,128)(2,1)} %param.12) | copy-start | bytes 4816900

commit v22 on v21

--- a/solution.py
+++ b/solution.py
@@ -92,7 +92,7 @@
             ).astype(jnp.bfloat16)
 
 
-def cross_attend(queries, encoded, key_weight, value_weight, group=4):
+def cross_attend(queries, encoded, key_weight, value_weight, group=2):
     length, width = queries.shape
     enc_width = encoded.shape[-1]
     memory = NEIGH * NLEN

time: 104 us -> 105 us (level)
  no operation moved by 1% of the time
where the time goes in v22:
time: 105 us; the launch traced here: 104 us
  Pallas kernels  34.5 us (33%)
  waiting for transfers between devices  29.2 us (28%)
  local copies, waits for them, and re-layouts  27.6 us (26%)
  starting transfers between devices  12.6 us (12%)
    ppermute x1, waiting for transfers between devices, gather_weights(): lax.ppermute(shard, 'dp', ring)  24.1 us
    pallas_call x1, Pallas kernels, cross_attend(): pl.pallas_call(_cross_kernel, out_shape=jax.ShapeDtypeStruct(queries.shap...  18.7 us
    pallas_call x1, Pallas kernels, encode_blocks(): pl.pallas_call(_encoder_kernel, out_shape=jax.ShapeDtypeStruct(flat.shape...  15.9 us
    dynamic_update_slice x4, local copies, waits for them, and re-layouts, gather_weights(): full = lax.dynamic_update_slice(full, piece, (0, owner * rows, 0))  9.45 us
    squeeze x1, local copies, waits for them, and re-layouts, shards(): return cross_attend(queries[0], chosen, kv_weight[0], kv_weight[1])[None]  7.59 us
    all_to_all x1, starting transfers between devices, shards(): asked = lax.all_to_all(asks, 'seq', 0, 0, tiled=True)  7.28 us
    all_to_all x1, waiting for transfers between devices, shards(): asked = lax.all_to_all(asks, 'seq', 0, 0, tiled=True)  5.08 us
    all_to_all x1, starting transfers between devices, shards(): got = lax.all_to_all(sent, 'seq', 0, 0, tiled=True)  3.72 us
  transfers between devices with their start and end apart: 5, of which 2 were waited for; matrix products, arithmetic and copies ran while one was open for 22% of the time, Pallas kernels for 0%

profile of v22, /device:TPU:0, one launch (start us, length us, event | category | flops | bytes accessed | tf_op | source)
XLA Modules:
  0.0 104.4 jit_solution(14484728432703410769)
XLA Ops:
  0.0 0.0 copy-start
  0.0 0.8 copy.23
  0.8 0.1 eq.39
  0.9 0.1 stack_reshape.6
  1.0 0.2 convert_reduce_fusion
  1.2 0.8 copy.24
  1.9 0.1 stack_reshape.7
  2.0 0.6 broadcast_in_dim.35
  2.6 7.3 %all-to-all-start = ((s32[8,3,16]{2,1,0:T(4,128)}), s32[8,3,16]{2,1,0:T(4,128)S(1)}, u32[]{:S(2)}, u32[]{:S(2)}) async-start(s32[8,3,16]{2,1,0:T(4,128)} %broadcast_in_dim.35), calls=%async_computation | async-start | bytes 32768 | tf_op jit(solution)/shard_map/all_to_all | solution.py:148
  9.9 1.5 %collective-permute-start = (bf16[4,224,896]{2,1,0:T(8,128)(2,1)}, bf16[4,224,896]{2,1,0:T(8,128)(2,1)}, u32[]{:S(2)}, u32[]{:S(2)}) collective-permute-start(bf16[4,224,896]{2,1,0:T(8,128)(2,1)} %param.12), channel_id=1, source_target_pairs={{0,16},{8,24},{16,0},{24,8},{1,17},{9,25},{17,1},{25,9},{2,18},{10... | collective-permute-start | bytes 4816904 | tf_op jit(solution)/shard_map/ppermute | solution.py:125
  11.4 5.1 %all-to-all-done = s32[8,3,16]{2,1,0:T(4,128)S(1)} async-done(((s32[8,3,16]{2,1,0:T(4,128)}), s32[8,3,16]{2,1,0:T(4,128)S(1)}, u32[]{:S(2)}, u32[]{:S(2)}) %all-to-all-start) | async-done | bytes 1568 | tf_op jit(solution)/shard_map/all_to_all | solution.py:148
  16.5 0.1 select_reduce_fusion
  16.7 0.1 copy.29
  16.7 0.1 reshape.43
  16.8 0.0 copy-done
  16.8 2.0 %gather_fusion = bf16[16,64,896]{2,1,0:T(8,128)(2,1)} fusion(bf16[4,64,896]{2,1,0:T(8,128)(2,1)S(1)} %bitcast.26, s32[1024]{0:T(1024)S(1)} %pad_clamp_fusion.1), kind=kCustom, calls=%fused_computation | custom fusion | bytes 3670080 | tf_op jit(solution)/shard_map/jit(_take)/gather | solution.py:152
  18.8 0.0 copy-start.2
  18.8 0.0 copy-start.3
  18.8 3.7 %all-to-all-start.1 = ((bf16[8,2,64,896]{3,2,1,0:T(8,128)(2,1)}), bf16[8,2,64,896]{3,2,1,0:T(8,128)(2,1)S(1)}, u32[]{:S(2)}, u32[]{:S(2)}) async-start(bf16[8,2,64,896]{3,2,1,0:T(8,128)(2,1)} %bitcast.28), calls=%async_computation.1 | async-start | bytes 3670016 | tf_op jit(solution)/shard_map/all_to_all | solution.py:154
  22.6 0.1 collective-permute-start.1
  22.7 24.1 %collective-permute-done = bf16[4,224,896]{2,1,0:T(8,128)(2,1)} collective-permute-done((bf16[4,224,896]{2,1,0:T(8,128)(2,1)}, bf16[4,224,896]{2,1,0:T(8,128)(2,1)}, u32[]{:S(2)}, u32[]{:S(2)}) %collective-permute-start) | collective-permute-done | bytes 1605664 | tf_op jit(solution)/shard_map/ppermute | solution.py:125
  46.8 0.0 collective-permute-start.2
  46.8 0.0 copy-done.2
  46.8 0.1 copy.30
  46.9 0.1 mul.29
  47.0 0.0 copy-done.3
  47.0 0.6 reshape.40.gain_ref
  47.6 0.0 copy-start.1
  47.6 3.2 %broadcast_in_dim.40 = bf16[4,896,896]{2,1,0:T(8,128)(2,1)} broadcast(bf16[]{:T(256)} %constant.40.clone.1), dimensions={} | broadcast | bytes 6422530 | tf_op jit(solution)/shard_map/broadcast_in_dim | solution.py:129
  50.8 0.0 copy-done.1
  50.8 1.3 %constant_dynamic-update-slice_fusion.3 = bf16[4,896,896]{2,1,0:T(8,128)(2,1)} fusion(bf16[4,896,896]{2,1,0:T(8,128)(2,1)} %broadcast_in_dim.40, bf16[4,224,896]{2,1,0:T(8,128)(2,1)S(1)} %copy-done.1, s32[]{:T(128)S(6)} %select_n.32), kind=kLoop, calls=%fused_computation.17 | loop fusion | bytes 3211268 | tf_op jit(solution)/shard_map/dynamic_update_slice | solution.py:131
  52.1 7.6 %slice_bitcast_fusion = (bf16[896,2048]{1,0:T(8,128)(2,1)}, bf16[896,2048]{1,0:T(8,128)(2,1)}) fusion(bf16[2,896,2048]{2,1,0:T(8,128)(2,1)} %param.13), kind=kLoop, calls=%fused_computation.2 | loop fusion | bytes 14680064 | tf_op jit(solution)/shard_map/squeeze | solution.py:158
  59.7 2.7 %constant_dynamic-update-slice_fusion.2 = bf16[4,896,896]{2,1,0:T(8,128)(2,1)} fusion(bf16[4,896,896]{2,1,0:T(8,128)(2,1)} %constant_dynamic-update-slice_fusion.3, bf16[4,224,896]{2,1,0:T(8,128)(2,1)} %collective-permute-done, s32[]{:T(128)S(6)} %select_n.36), kind=kLoop, calls=%fused_computation.16 | loop fusion | bytes 3211268 | tf_op jit(solution)/shard_map/dynamic_update_slice | solution.py:131
  62.4 0.0 collective-permute-done.1
  62.4 2.7 %constant_dynamic-update-slice_fusion.1 = bf16[4,896,896]{2,1,0:T(8,128)(2,1)} fusion(bf16[4,896,896]{2,1,0:T(8,128)(2,1)} %constant_dynamic-update-slice_fusion.2, bf16[4,224,896]{2,1,0:T(8,128)(2,1)} %collective-permute-done.1, s32[]{:T(128)S(6)} %select_n.37), kind=kLoop, calls=%fused_computation.15 | loop fusion | bytes 3211268 | tf_op jit(solution)/shard_map/dynamic_update_slice | solution.py:131
  65.1 0.0 collective-permute-done.2
  65.2 2.7 %constant_dynamic-update-slice_fusion.w_ref = bf16[4,896,896]{2,1,0:T(8,128)(2,1)} fusion(bf16[4,896,896]{2,1,0:T(8,128)(2,1)} %constant_dynamic-update-slice_fusion.1, bf16[4,224,896]{2,1,0:T(8,128)(2,1)} %collective-permute-done.2, s32[]{:T(128)S(6)} %select_n.38), kind=kLoop, calls=%fused_computation.14 | loop fusion | bytes 3211268 | tf_op jit(solution)/shard_map/dynamic_update_slice | solution.py:131
  67.9 0.0 all-to-all-done.1
  67.9 2.0 %gather_fusion.1 = bf16[16,64,896]{2,1,0:T(8,128)(2,1)} fusion(bf16[16,64,896]{2,1,0:T(8,128)(2,1)S(1)} %bitcast.27, s32[1024]{0:T(1024)S(1)} %pad_clamp_fusion), kind=kCustom, calls=%fused_computation.1 | custom fusion | bytes 3670080 | tf_op jit(solution)/shard_map/jit(_take)/gather | solution.py:156
  69.9 15.9 %shard_map.73.enc_ref = bf16[1024,896]{1,0:T(8,128)(2,1)} custom-call(bf16[1024,896]{1,0:T(8,128)(2,1)} %bitcast.29, f32[1,896]{1,0:T(1,128)} %reshape.40.gain_ref, bf16[4,896,896]{2,1,0:T(8,128)(2,1)} %constant_dynamic-update-slice_fusion.w_ref), custom_call_target="tpu_custom_call" | custom-call | tf_op jit(solution)/shard_map/pallas_call | solution.py:58
  85.7 18.7 %shard_map.74 = bf16[512,2048]{1,0:T(8,128)(2,1)} custom-call(bf16[512,2048]{1,0:T(8,128)(2,1)} %bitcast.30, bf16[1024,896]{1,0:T(8,128)(2,1)} %shard_map.73.enc_ref, bf16[896,2048]{1,0:T(8,128)(2,1)} %get-tuple-element.6.wk_ref, bf16[896,2048]{1,0:T(8,128)(2,1)} %get-tuple-element.5.wv_ref), custom_call_target="tpu_custom_call" | custom-call | tf_op jit(solution)/shard_map/pallas_call | solution.py:100
  (7 shorter events, 0.1 us)
Async XLA Ops:
  0.0 16.8 %copy-start = (bf16[1,4,64,896]{3,2,1,0:T(8,128)(2,1)S(1)}, bf16[1,4,64,896]{3,2,1,0:T(8,128)(2,1)}, u32[]{:S(2)}) copy-start(bf16[1,4,64,896]{3,2,1,0:T(8,128)(2,1)} %param.8) | copy-start | bytes 1376260
  2.6 13.9 %all-to-all-start = ((s32[8,3,16]{2,1,0:T(4,128)}), s32[8,3,16]{2,1,0:T(4,128)S(1)}, u32[]{:S(2)}, u32[]{:S(2)}) async-start(s32[8,3,16]{2,1,0:T(4,128)} %broadcast_in_dim.35), calls=%async_computation | async-start | bytes 32768 | tf_op jit(solution)/shard_map/all_to_all | solution.py:148
  9.9 36.9 %collective-permute-start = (bf16[4,224,896]{2,1,0:T(8,128)(2,1)}, bf16[4,224,896]{2,1,0:T(8,128)(2,1)}, u32[]{:S(2)}, u32[]{:S(2)}) collective-permute-start(bf16[4,224,896]{2,1,0:T(8,128)(2,1)} %param.12), channel_id=1, source_target_pairs={{0,16},{8,24},{16,0},{24,8},{1,17},{9,25},{17,1},{25,9},{2,18},{10... | collective-permute-start | bytes 4816904 | tf_op jit(solution)/shard_map/ppermute | solution.py:125
  18.8 28.0 %copy-start.2 = (s32[1,8,2]{1,2,0:T(2,128)S(1)}, s32[1,8,2]{1,2,0:T(2,128)}, u32[]{:S(2)}) copy-start(s32[1,8,2]{1,2,0:T(2,128)} %param.9) | copy-start | bytes 196
  18.8 28.2 %copy-start.3 = (f32[896]{0:T(1024)S(1)}, f32[896]{0:T(1024)}, u32[]{:S(2)}) copy-start(f32[896]{0:T(1024)} %param.11) | copy-start | bytes 10756
  18.8 49.0 %all-to-all-start.1 = ((bf16[8,2,64,896]{3,2,1,0:T(8,128)(2,1)}), bf16[8,2,64,896]{3,2,1,0:T(8,128)(2,1)S(1)}, u32[]{:S(2)}, u32[]{:S(2)}) async-start(bf16[8,2,64,896]{3,2,1,0:T(8,128)(2,1)} %bitcast.28), calls=%async_computation.1 | async-start | bytes 3670016 | tf_op jit(solution)/shard_map/all_to_all | solution.py:154
  22.6 39.8 %collective-permute-start.1 = (bf16[4,224,896]{2,1,0:T(8,128)(2,1)}, bf16[4,224,896]{2,1,0:T(8,128)(2,1)}, u32[]{:S(2)}, u32[]{:S(2)}) collective-permute-start(bf16[4,224,896]{2,1,0:T(8,128)(2,1)} %param.12), channel_id=1, source_target_pairs={{0,8},{8,0},{16,24},{24,16},{1,9},{9,1},{17,25},{25,17},{2,10},{10... | collective-permute-start | bytes 4816904 | tf_op jit(solution)/shard_map/ppermute | solution.py:127
  46.8 18.4 %collective-permute-start.2 = (bf16[4,224,896]{2,1,0:T(8,128)(2,1)}, bf16[4,224,896]{2,1,0:T(8,128)(2,1)}, u32[]{:S(2)}, u32[]{:S(2)}) collective-permute-start(bf16[4,224,896]{2,1,0:T(8,128)(2,1)} %collective-permute-done), channel_id=1, source_target_pairs={{0,8},{8,0},{16,24},{24,16},{1,9},{9,1},{17,25},{25,17},{2,10},{10... | collective-permute-start | bytes 4816904 | tf_op jit(solution)/shard_map/ppermute | solution.py:127
  47.6 3.2 %copy-start.1 = (bf16[4,224,896]{2,1,0:T(8,128)(2,1)S(1)}, bf16[4,224,896]{2,1,0:T(8,128)(2,1)}, u32[]{:S(2)}) copy-start(bf16[4,224,896]{2,1,0:T(8,128)(2,1)} %param.12) | copy-start | bytes 4816900
